TPU v7x, 32 devices: a whole 2x2x4 slice. The times are simulated.
32 devices in a mesh: mem: 4 (over y, core), row: 8 (over z, x).
Axes of the slice: x: 2, y: 2, z: 4, core: 2. Of those that a mesh axis runs over, the one named last changes fastest.
Arguments:
- starting_states: float32 [8, 8, 64, 512], P('mem', None, 'row'), may hold values from -6 to 6
- wind_east: float32 [8, 64, 512], P(None, 'row'), may hold values from -0.25 to 0.25
- wind_north: float32 [8, 64, 512], P(None, 'row'), may hold values from -0.25 to 0.25
- diffusivity: float32 [8, 64, 512], P(None, 'row'), may hold values from 0.05 to 0.22
- embed_weight: bfloat16 [8, 64], replicated, may hold values from -2 to 2
- norm_gain: float32 [64], replicated, may hold values from 0.1 to 1.9
- project_weight: bfloat16 [64, 192], replicated, may hold values from -0.75 to 0.75
- head_scale: float32 [4], replicated, may hold values from 1 to 10
- output_weight: bfloat16 [64, 64], replicated, may hold values from -0.75 to 0.75
- readout_weight: bfloat16 [64, 8], replicated, may hold values from -0.75 to 0.75
- first_kernel: bfloat16 [9, 8, 8], replicated, may hold values from -0.75 to 0.75
- second_kernel: bfloat16 [9, 8, 8], replicated, may hold values from -0.75 to 0.75
Outputs:
- postprocessed: bfloat16 [8, 8, 64, 512], P(None, None, 'row', 'mem')
All inputs are finite; a program needn't handle non-finite values.
Results may differ from a plain program's by a relative error of at most 0.0096.
Values may be sent and summed in bfloat16 or wider, within the bound.
No kernel may reach another device: no remote copies, remote signals or barrier semaphores. Data moves between devices by JAX's collectives and lax.ppermute only.
A program may use at most 64 MiB of HBM per device.

v0:
```python
import jax
import jax.numpy as jnp
from jax import lax
from jax.sharding import PartitionSpec as P

STEPS = 4
DILATION_SPAN = 4


def padded(block, sides, width):
    for axis, dim in sides:
        count = lax.axis_size(axis)
        forward = [(i, i + 1) for i in range(count - 1)]
        backward = [(target, source) for source, target in forward]
        low = lax.ppermute(
            lax.slice_in_dim(block, block.shape[dim] - width, None, axis=dim), axis, forward
        )
        high = lax.ppermute(lax.slice_in_dim(block, 0, width, axis=dim), axis, backward)
        block = jnp.concatenate([low, block, high], axis=dim)
    return block


def advance(padded_field, wind_east, wind_north, diffusivity):
    middle = padded_field[..., 1:-1, :]
    northern = padded_field[..., 2:, :]
    southern = padded_field[..., :-2, :]
    widths = [(0, 0)] * (middle.ndim - 1) + [(1, 1)]
    widened = jnp.pad(middle, widths)
    eastern = widened[..., 2:]
    western = widened[..., :-2]
    drifting = 0.2 * jnp.tanh(middle)
    laplace = northern + southern + eastern + western - 4.0 * middle
    return (
        middle
        - (wind_east + drifting) * (eastern - western) * 0.5
        - (wind_north + drifting) * (northern - southern) * 0.5
        + diffusivity * laplace
    )


def post_block(
    vertical_layers,
    embed_weight,
    norm_gain,
    project_weight,
    head_scale,
    output_weight,
    readout_weight,
):
    members, _, points = vertical_layers.shape
    width = embed_weight.shape[1]
    heads = head_scale.shape[0]
    head_size = width // heads
    embedded = jnp.einsum(
        "mlp,le->pme", vertical_layers, embed_weight, preferred_element_type=jnp.float32
    )
    meansq = jnp.mean(embedded * embedded, axis=-1, keepdims=True)
    normed = (embedded * lax.rsqrt(meansq + 1e-05) * norm_gain).astype(jnp.bfloat16)
    projected = jnp.einsum(
        "pme,ef->pmf", normed, project_weight, preferred_element_type=jnp.float32
    )
    queries = projected[..., :width].reshape(points, members, heads, head_size)
    keys_all = projected[..., width : 2 * width].reshape(points, members, heads, head_size)
    values = (
        projected[..., 2 * width :].astype(jnp.bfloat16).reshape(points, members, heads, head_size)
    )
    queries = (queries * lax.rsqrt(jnp.sum(queries * queries, -1, keepdims=True) + 1.0)).astype(
        jnp.bfloat16
    )
    keys_all = (keys_all * lax.rsqrt(jnp.sum(keys_all * keys_all, -1, keepdims=True) + 1.0)).astype(
        jnp.bfloat16
    )
    scores = jnp.einsum("pmhd,pnhd->phmn", queries, keys_all, preferred_element_type=jnp.float32)
    scores = scores * head_scale[:, None, None]
    weights = jnp.exp(scores)
    probs = (weights / jnp.sum(weights, -1, keepdims=True)).astype(jnp.bfloat16)
    mixed = jnp.einsum("phmn,pnhd->pmhd", probs, values, preferred_element_type=jnp.float32)
    mixed = mixed.astype(jnp.bfloat16).reshape(points, members, width)
    attended = jnp.einsum("pme,ef->pmf", mixed, output_weight, preferred_element_type=jnp.float32)
    residual = (embedded + attended).astype(jnp.bfloat16)
    step_result = jnp.einsum(
        "pme,ef->mfp", residual, readout_weight, preferred_element_type=jnp.float32
    )
    return step_result.astype(jnp.bfloat16)


def convolve(padded_field, kernel):
    row_total = padded_field.shape[2] - 2 * DILATION_SPAN
    column_total = padded_field.shape[3] - 2 * DILATION_SPAN
    summed = jnp.zeros(
        (padded_field.shape[0], kernel.shape[1], row_total, column_total), jnp.float32
    )
    for row_stencil in range(3):
        for column_stencil in range(3):
            shifted_field = padded_field[
                :,
                :,
                row_stencil * DILATION_SPAN : row_stencil * DILATION_SPAN + row_total,
                column_stencil * DILATION_SPAN : column_stencil * DILATION_SPAN + column_total,
            ]
            summed = summed + jnp.einsum(
                "oc,mcij->moij",
                kernel[row_stencil * 3 + column_stencil],
                shifted_field,
                preferred_element_type=jnp.float32,
            )
    return summed


def on_device(
    starting_states,
    wind_east,
    wind_north,
    diffusivity,
    embed_weight,
    norm_gain,
    project_weight,
    head_scale,
    output_weight,
    readout_weight,
    first_kernel,
    second_kernel,
):
    members_here = starting_states.shape[0]
    row_total = starting_states.shape[2]
    coefficients = jnp.stack([wind_east, wind_north, diffusivity])
    joined = jnp.concatenate([starting_states, coefficients], 0)
    widened = padded(joined, (("row", 2),), STEPS)
    gridded_quantity_list = widened[:members_here]
    coef_rows = widened[members_here:]
    first_row = lax.axis_index("row") * row_total - STEPS
    all_rows = lax.axis_size("row") * row_total
    for section in range(STEPS):
        out_rows = row_total + 2 * (STEPS - section - 1)
        offset = section + 1
        window = coef_rows[:, :, offset : offset + out_rows]
        gridded_quantity_list = advance(gridded_quantity_list, window[0], window[1], window[2])
        row_ids = first_row + offset + jnp.arange(out_rows)
        inside = (row_ids >= 0) & (row_ids < all_rows)
        gridded_quantity_list = jnp.where(inside[None, None, :, None], gridded_quantity_list, 0.0)
    predicted_states = gridded_quantity_list.astype(jnp.bfloat16)
    blockwise_quantity = lax.all_to_all(
        predicted_states, "mem", split_axis=3, concat_axis=0, tiled=True
    )
    members, levels_count, tile_rows, tile_cols = blockwise_quantity.shape
    count = tile_rows * tile_cols
    flattened = blockwise_quantity.reshape(members, levels_count, count)
    block = 256

    def one_block(block_index):
        vertical_layers = lax.dynamic_slice_in_dim(flattened, block_index * block, block, 2)
        return post_block(
            vertical_layers,
            embed_weight,
            norm_gain,
            project_weight,
            head_scale,
            output_weight,
            readout_weight,
        )

    blocks = lax.map(one_block, jnp.arange(count // block))
    step_result = jnp.moveaxis(blocks, 0, 2)
    features = step_result.reshape(members, readout_weight.shape[1], tile_rows, tile_cols)
    tile_cols = features.shape[3]
    padded_feature = padded(features, (("mem", 3), ("row", 2)), DILATION_SPAN)
    interior_cells = jax.nn.silu(convolve(padded_feature, first_kernel)).astype(jnp.bfloat16)
    activated_output = padded(interior_cells, (("mem", 3), ("row", 2)), DILATION_SPAN)
    return (features.astype(jnp.float32) + convolve(activated_output, second_kernel)).astype(
        jnp.bfloat16
    )


def solution(mesh):
    return jax.shard_map(
        on_device,
        mesh=mesh,
        in_specs=(
            P("mem", None, "row", None),
            P(None, "row", None),
            P(None, "row", None),
            P(None, "row", None),
            P(),
            P(),
            P(),
            P(),
            P(),
            P(),
            P(),
            P(),
        ),
        out_specs=P(None, None, "row", "mem"),
        check_vma=False,
    )
```

profile of v0, /device:TPU:9, one launch (start us, length us, event | category | flops | bytes accessed | tf_op | source)
XLA Modules:
  0.0 219.3 jit_solution(953675717168693512)
XLA Ops:
  0.0 1.0 copy.200
  1.0 1.1 copy.121
  2.1 1.1 fusion.90
  3.4 3.1 %collective-permute-start = (f32[5,8,4,512]{3,1,2,0:T(8,128)S(1)}, f32[5,8,4,512]{3,1,2,0:T(8,128)S(1)}, u32[]{:S(2)}, u32[]{:S(2)}) collective-permute-start(f32[5,8,4,512]{3,1,2,0:T(8,128)S(1)} %get-tuple-element.115), channel_id=1, source_target_pairs={{0,1},{1,2},{2,3},{3,4},{4,5},{5,6},{6,7},{8,9},{9,10},{10,11},{11... | collective-permute-start | bytes 983048 | tf_op jit(solution)/shard_map/ppermute | solution.py:15
  6.5 3.1 %collective-permute-start.1 = (f32[5,8,4,512]{3,1,2,0:T(8,128)S(1)}, f32[5,8,4,512]{3,1,2,0:T(8,128)S(1)}, u32[]{:S(2)}, u32[]{:S(2)}) collective-permute-start(f32[5,8,4,512]{3,1,2,0:T(8,128)S(1)} %get-tuple-element.116), channel_id=1, source_target_pairs={{1,0},{2,1},{3,2},{4,3},{5,4},{6,5},{7,6},{9,8},{10,9},{11,10},{12... | collective-permute-start | bytes 983048 | tf_op jit(solution)/shard_map/ppermute | solution.py:18
  9.7 10.1 %collective-permute-done = f32[5,8,4,512]{3,1,2,0:T(8,128)S(1)} collective-permute-done((f32[5,8,4,512]{3,1,2,0:T(8,128)S(1)}, f32[5,8,4,512]{3,1,2,0:T(8,128)S(1)}, u32[]{:S(2)}, u32[]{:S(2)}) %collective-permute-start) | collective-permute-done | bytes 327712 | tf_op jit(solution)/shard_map/ppermute | solution.py:15
  19.9 2.9 %collective-permute-done.1 = f32[5,8,4,512]{3,1,2,0:T(8,128)S(1)} collective-permute-done((f32[5,8,4,512]{3,1,2,0:T(8,128)S(1)}, f32[5,8,4,512]{3,1,2,0:T(8,128)S(1)}, u32[]{:S(2)}, u32[]{:S(2)}) %collective-permute-start.1) | collective-permute-done | bytes 327712 | tf_op jit(solution)/shard_map/ppermute | solution.py:18
  24.8 2.0 copy.125
  26.8 2.8 %reshape.99 = bf16[4,2,8192]{2,1,0:T(2,128)(2,1)} reshape(bf16[512,2,8,8]{3,2,1,0:T(8,128)(2,1)S(1)} %bitcast.241) | data formatting | bytes 262144
  29.7 3.8 %all-to-all-start = ((bf16[4,2,8192]{2,1,0:T(2,128)(2,1)}), bf16[4,2,8192]{2,1,0:T(2,128)(2,1)S(1)}, u32[]{:S(2)}, u32[]{:S(2)}) async-start(bf16[4,2,8192]{2,1,0:T(2,128)(2,1)} %reshape.99), calls=%async_computation | async-start | bytes 262144 | tf_op jit(solution)/shard_map/all_to_all | solution.py:142
  36.2 0.9 all-to-all-done
  37.0 2.4 %reshape.100 = bf16[512,2,8,8]{3,2,1,0:T(8,128)(2,1)S(1)} reshape(bf16[4,2,8192]{2,1,0:T(2,128)(2,1)S(1)} %all-to-all-done) | data formatting | bytes 262144
  39.5 1.7 copy.126
  41.2 135.4 %while.10 = (s32[]{:T(128)}, bf16[4,8,8,256]{3,2,1,0:T(8,128)(2,1)S(1)}, s32[4]{0:T(128)S(1)}, bf16[8,8,1024]{2,1,0:T(8,128)(2,1)S(1)}, bf16[8,64]{1,0:T(8,128)(...) while((s32[]{:T(128)}, ...), condition=%wide.region_5.6_spmd, body=%wide.region_0.5_spmd.sunk | while | flops 77932544 | bytes 12530179 | solution.py:162
  41.4 0.6 dynamic_slice.14
  43.8 3.7 %copy.208 = bf16[256,8,4,16]{3,1,2,0:T(8,128)(2,1)} copy(bf16[256,8,4,16]{0,3,2,1:T(8,128)(2,1)S(1)} %get-tuple-element.230) | data formatting | bytes 524288 | tf_op jit(solution)/shard_map/while/body/eval_jaxpr/convert_element_type | solution.py:67
  47.5 3.8 %copy.209 = bf16[256,8,4,16]{3,1,2,0:T(8,128)(2,1)} copy(bf16[256,8,4,16]{0,3,2,1:T(8,128)(2,1)S(1)} %get-tuple-element.231) | data formatting | bytes 524288 | tf_op jit(solution)/shard_map/while/body/eval_jaxpr/convert_element_type | solution.py:70
  51.4 5.4 %fusion.123 = f32[256,4,8,8]{2,3,1,0:T(8,128)} fusion(bf16[256,8,4,16]{3,1,2,0:T(8,128)(2,1)} %copy.208, bf16[256,8,4,16]{3,1,2,0:T(8,128)(2,1)} %copy.209), kind=kOutput, calls=%fused_computation.154.clone.1 | convolution fusion | flops 2097152 | bytes 786432 | tf_op jit(solution)/shard_map/while/body/eval_jaxpr/pmhd,pnhd->phmn/dot_general | solution.py:73
  56.8 3.6 %copy.210 = f32[256,4,8,8]{0,3,2,1:T(8,128)S(1)} copy(f32[256,4,8,8]{2,3,1,0:T(8,128)} %fusion.123) | data formatting | bytes 524288 | tf_op jit(solution)/shard_map/while/body/eval_jaxpr/pmhd,pnhd->phmn/dot_general | solution.py:73
  60.6 3.7 %copy.211 = bf16[256,4,8,8]{3,2,1,0:T(8,128)(2,1)} copy(bf16[256,4,8,8]{0,3,2,1:T(8,128)(2,1)S(1)} %divide_convert_fusion.2) | data formatting | bytes 262144 | tf_op jit(solution)/shard_map/while/body/eval_jaxpr/convert_element_type | solution.py:76
  64.3 3.7 %copy.207 = bf16[256,8,4,16]{3,1,2,0:T(8,128)(2,1)} copy(bf16[256,8,4,16]{0,3,2,1:T(8,128)(2,1)S(1)} %bitcast.240) | data formatting | bytes 524288 | tf_op jit(solution)/shard_map/while/body/eval_jaxpr/reshape | solution.py:65
  68.0 4.1 %convert_bitcast_fusion.2 = bf16[256,8,4,16]{3,1,2,0:T(8,128)(2,1)} fusion(bf16[256,8,4,16]{3,1,2,0:T(8,128)(2,1)} %copy.207, bf16[256,4,8,8]{3,2,1,0:T(8,128)(2,1)S(1)} %copy-done), kind=kOutput, calls=%fused_computation.clone.1 | convolution fusion | flops 2228224 | bytes 655360 | tf_op jit(solution)/shard_map/while/body/eval_jaxpr/phmn,pnhd->pmhd/dot_general | solution.py:77
  72.1 2.7 %copy.212 = bf16[256,8,4,16]{0,3,2,1:T(8,128)(2,1)S(1)} copy(bf16[256,8,4,16]{3,1,2,0:T(8,128)(2,1)} %convert_bitcast_fusion.2) | data formatting | bytes 524288 | tf_op jit(solution)/shard_map/while/body/eval_jaxpr/convert_element_type | solution.py:78
  75.2 0.6 dynamic_slice.14
  77.6 3.7 %copy.208 = bf16[256,8,4,16]{3,1,2,0:T(8,128)(2,1)} copy(bf16[256,8,4,16]{0,3,2,1:T(8,128)(2,1)S(1)} %get-tuple-element.230) | data formatting | bytes 524288 | tf_op jit(solution)/shard_map/while/body/eval_jaxpr/convert_element_type | solution.py:67
  81.3 3.8 %copy.209 = bf16[256,8,4,16]{3,1,2,0:T(8,128)(2,1)} copy(bf16[256,8,4,16]{0,3,2,1:T(8,128)(2,1)S(1)} %get-tuple-element.231) | data formatting | bytes 524288 | tf_op jit(solution)/shard_map/while/body/eval_jaxpr/convert_element_type | solution.py:70
  85.1 5.4 %fusion.123 = f32[256,4,8,8]{2,3,1,0:T(8,128)} fusion(bf16[256,8,4,16]{3,1,2,0:T(8,128)(2,1)} %copy.208, bf16[256,8,4,16]{3,1,2,0:T(8,128)(2,1)} %copy.209), kind=kOutput, calls=%fused_computation.154.clone.1 | convolution fusion | flops 2097152 | bytes 786432 | tf_op jit(solution)/shard_map/while/body/eval_jaxpr/pmhd,pnhd->phmn/dot_general | solution.py:73
  90.5 3.6 %copy.210 = f32[256,4,8,8]{0,3,2,1:T(8,128)S(1)} copy(f32[256,4,8,8]{2,3,1,0:T(8,128)} %fusion.123) | data formatting | bytes 524288 | tf_op jit(solution)/shard_map/while/body/eval_jaxpr/pmhd,pnhd->phmn/dot_general | solution.py:73
  94.4 3.7 %copy.211 = bf16[256,4,8,8]{3,2,1,0:T(8,128)(2,1)} copy(bf16[256,4,8,8]{0,3,2,1:T(8,128)(2,1)S(1)} %divide_convert_fusion.2) | data formatting | bytes 262144 | tf_op jit(solution)/shard_map/while/body/eval_jaxpr/convert_element_type | solution.py:76
  98.1 3.7 %copy.207 = bf16[256,8,4,16]{3,1,2,0:T(8,128)(2,1)} copy(bf16[256,8,4,16]{0,3,2,1:T(8,128)(2,1)S(1)} %bitcast.240) | data formatting | bytes 524288 | tf_op jit(solution)/shard_map/while/body/eval_jaxpr/reshape | solution.py:65
  101.8 4.1 %convert_bitcast_fusion.2 = bf16[256,8,4,16]{3,1,2,0:T(8,128)(2,1)} fusion(bf16[256,8,4,16]{3,1,2,0:T(8,128)(2,1)} %copy.207, bf16[256,4,8,8]{3,2,1,0:T(8,128)(2,1)S(1)} %copy-done), kind=kOutput, calls=%fused_computation.clone.1 | convolution fusion | flops 2228224 | bytes 655360 | tf_op jit(solution)/shard_map/while/body/eval_jaxpr/phmn,pnhd->pmhd/dot_general | solution.py:77
  105.9 2.7 %copy.212 = bf16[256,8,4,16]{0,3,2,1:T(8,128)(2,1)S(1)} copy(bf16[256,8,4,16]{3,1,2,0:T(8,128)(2,1)} %convert_bitcast_fusion.2) | data formatting | bytes 524288 | tf_op jit(solution)/shard_map/while/body/eval_jaxpr/convert_element_type | solution.py:78
  109.0 0.6 dynamic_slice.14
  111.4 3.7 %copy.208 = bf16[256,8,4,16]{3,1,2,0:T(8,128)(2,1)} copy(bf16[256,8,4,16]{0,3,2,1:T(8,128)(2,1)S(1)} %get-tuple-element.230) | data formatting | bytes 524288 | tf_op jit(solution)/shard_map/while/body/eval_jaxpr/convert_element_type | solution.py:67
  115.1 3.8 %copy.209 = bf16[256,8,4,16]{3,1,2,0:T(8,128)(2,1)} copy(bf16[256,8,4,16]{0,3,2,1:T(8,128)(2,1)S(1)} %get-tuple-element.231) | data formatting | bytes 524288 | tf_op jit(solution)/shard_map/while/body/eval_jaxpr/convert_element_type | solution.py:70
  118.9 5.4 %fusion.123 = f32[256,4,8,8]{2,3,1,0:T(8,128)} fusion(bf16[256,8,4,16]{3,1,2,0:T(8,128)(2,1)} %copy.208, bf16[256,8,4,16]{3,1,2,0:T(8,128)(2,1)} %copy.209), kind=kOutput, calls=%fused_computation.154.clone.1 | convolution fusion | flops 2097152 | bytes 786432 | tf_op jit(solution)/shard_map/while/body/eval_jaxpr/pmhd,pnhd->phmn/dot_general | solution.py:73
  124.3 3.6 %copy.210 = f32[256,4,8,8]{0,3,2,1:T(8,128)S(1)} copy(f32[256,4,8,8]{2,3,1,0:T(8,128)} %fusion.123) | data formatting | bytes 524288 | tf_op jit(solution)/shard_map/while/body/eval_jaxpr/pmhd,pnhd->phmn/dot_general | solution.py:73
  128.2 3.7 %copy.211 = bf16[256,4,8,8]{3,2,1,0:T(8,128)(2,1)} copy(bf16[256,4,8,8]{0,3,2,1:T(8,128)(2,1)S(1)} %divide_convert_fusion.2) | data formatting | bytes 262144 | tf_op jit(solution)/shard_map/while/body/eval_jaxpr/convert_element_type | solution.py:76
  131.9 3.7 %copy.207 = bf16[256,8,4,16]{3,1,2,0:T(8,128)(2,1)} copy(bf16[256,8,4,16]{0,3,2,1:T(8,128)(2,1)S(1)} %bitcast.240) | data formatting | bytes 524288 | tf_op jit(solution)/shard_map/while/body/eval_jaxpr/reshape | solution.py:65
  135.6 4.1 %convert_bitcast_fusion.2 = bf16[256,8,4,16]{3,1,2,0:T(8,128)(2,1)} fusion(bf16[256,8,4,16]{3,1,2,0:T(8,128)(2,1)} %copy.207, bf16[256,4,8,8]{3,2,1,0:T(8,128)(2,1)S(1)} %copy-done), kind=kOutput, calls=%fused_computation.clone.1 | convolution fusion | flops 2228224 | bytes 655360 | tf_op jit(solution)/shard_map/while/body/eval_jaxpr/phmn,pnhd->pmhd/dot_general | solution.py:77
  139.7 2.7 %copy.212 = bf16[256,8,4,16]{0,3,2,1:T(8,128)(2,1)S(1)} copy(bf16[256,8,4,16]{3,1,2,0:T(8,128)(2,1)} %convert_bitcast_fusion.2) | data formatting | bytes 524288 | tf_op jit(solution)/shard_map/while/body/eval_jaxpr/convert_element_type | solution.py:78
  142.8 0.6 dynamic_slice.14
  145.2 3.7 %copy.208 = bf16[256,8,4,16]{3,1,2,0:T(8,128)(2,1)} copy(bf16[256,8,4,16]{0,3,2,1:T(8,128)(2,1)S(1)} %get-tuple-element.230) | data formatting | bytes 524288 | tf_op jit(solution)/shard_map/while/body/eval_jaxpr/convert_element_type | solution.py:67
  148.9 3.8 %copy.209 = bf16[256,8,4,16]{3,1,2,0:T(8,128)(2,1)} copy(bf16[256,8,4,16]{0,3,2,1:T(8,128)(2,1)S(1)} %get-tuple-element.231) | data formatting | bytes 524288 | tf_op jit(solution)/shard_map/while/body/eval_jaxpr/convert_element_type | solution.py:70
  152.7 5.4 %fusion.123 = f32[256,4,8,8]{2,3,1,0:T(8,128)} fusion(bf16[256,8,4,16]{3,1,2,0:T(8,128)(2,1)} %copy.208, bf16[256,8,4,16]{3,1,2,0:T(8,128)(2,1)} %copy.209), kind=kOutput, calls=%fused_computation.154.clone.1 | convolution fusion | flops 2097152 | bytes 786432 | tf_op jit(solution)/shard_map/while/body/eval_jaxpr/pmhd,pnhd->phmn/dot_general | solution.py:73
  158.1 3.6 %copy.210 = f32[256,4,8,8]{0,3,2,1:T(8,128)S(1)} copy(f32[256,4,8,8]{2,3,1,0:T(8,128)} %fusion.123) | data formatting | bytes 524288 | tf_op jit(solution)/shard_map/while/body/eval_jaxpr/pmhd,pnhd->phmn/dot_general | solution.py:73
  162.0 3.7 %copy.211 = bf16[256,4,8,8]{3,2,1,0:T(8,128)(2,1)} copy(bf16[256,4,8,8]{0,3,2,1:T(8,128)(2,1)S(1)} %divide_convert_fusion.2) | data formatting | bytes 262144 | tf_op jit(solution)/shard_map/while/body/eval_jaxpr/convert_element_type | solution.py:76
  165.7 3.7 %copy.207 = bf16[256,8,4,16]{3,1,2,0:T(8,128)(2,1)} copy(bf16[256,8,4,16]{0,3,2,1:T(8,128)(2,1)S(1)} %bitcast.240) | data formatting | bytes 524288 | tf_op jit(solution)/shard_map/while/body/eval_jaxpr/reshape | solution.py:65
  169.4 4.1 %convert_bitcast_fusion.2 = bf16[256,8,4,16]{3,1,2,0:T(8,128)(2,1)} fusion(bf16[256,8,4,16]{3,1,2,0:T(8,128)(2,1)} %copy.207, bf16[256,4,8,8]{3,2,1,0:T(8,128)(2,1)S(1)} %copy-done), kind=kOutput, calls=%fused_computation.clone.1 | convolution fusion | flops 2228224 | bytes 655360 | tf_op jit(solution)/shard_map/while/body/eval_jaxpr/phmn,pnhd->pmhd/dot_general | solution.py:77
  173.5 2.7 %copy.212 = bf16[256,8,4,16]{0,3,2,1:T(8,128)(2,1)S(1)} copy(bf16[256,8,4,16]{3,1,2,0:T(8,128)(2,1)} %convert_bitcast_fusion.2) | data formatting | bytes 524288 | tf_op jit(solution)/shard_map/while/body/eval_jaxpr/convert_element_type | solution.py:78
  176.9 2.9 %collective-permute-start.2 = (bf16[8,8,8,4]{3,1,2,0:T(8,128)(2,1)S(1)}, bf16[8,8,8,4]{3,1,2,0:T(8,128)(2,1)S(1)}, u32[]{:S(2)}, u32[]{:S(2)}) collective-permute-start(bf16[8,8,8,4]{3,1,2,0:T(8,128)(2,1)S(1)} %get-tuple-element.127), channel_id=1, source_target_pairs={{0,8},{8,16},{16,24},{1,9},{9,17},{17,25},{2,10},{10,18},{18,26},{... | collective-permute-start | bytes 12296 | tf_op jit(solution)/shard_map/ppermute | solution.py:15
  179.8 1.9 collective-permute-start.3
  181.9 4.2 %collective-permute-done.3 = bf16[8,8,8,4]{3,1,2,0:T(8,128)(2,1)S(1)} collective-permute-done((bf16[8,8,8,4]{3,1,2,0:T(8,128)(2,1)S(1)}, bf16[8,8,8,4]{3,1,2,0:T(8,128)(2,1)S(1)}, u32[]{:S(2)}, u32[]{:S(2)}) %collective-permute-start.3) | collective-permute-done | bytes 4128 | tf_op jit(solution)/shard_map/ppermute | solution.py:18
  186.3 2.2 %collective-permute-start.4 = (bf16[8,8,4,136]{3,1,2,0:T(8,128)(2,1)S(1)}, bf16[8,8,4,136]{3,1,2,0:T(8,128)(2,1)S(1)}, u32[]{:S(2)}, u32[]{:S(2)}) collective-permute-start(bf16[8,8,4,136]{3,1,2,0:T(8,128)(2,1)S(1)} %get-tuple-element.123), channel_id=1, source_target_pairs={{0,1},{1,2},{2,3},{3,4},{4,5},{5,6},{6,7},{8,9},{9,10},{10,11},{11... | collective-permute-start | bytes 208904 | tf_op jit(solution)/shard_map/ppermute | solution.py:15
  188.6 4.2 %collective-permute-start.5 = (bf16[8,8,4,136]{3,1,2,0:T(8,128)(2,1)S(1)}, bf16[8,8,4,136]{3,1,2,0:T(8,128)(2,1)S(1)}, u32[]{:S(2)}, u32[]{:S(2)}) collective-permute-start(bf16[8,8,4,136]{3,1,2,0:T(8,128)(2,1)S(1)} %get-tuple-element.124), channel_id=1, source_target_pairs={{1,0},{2,1},{3,2},{4,3},{5,4},{6,5},{7,6},{9,8},{10,9},{11,10},{12... | collective-permute-start | bytes 208904 | tf_op jit(solution)/shard_map/ppermute | solution.py:18
  193.0 2.2 collective-permute-done.5
  197.3 2.7 %collective-permute-start.6 = (bf16[8,8,8,4]{3,1,2,0:T(8,128)(2,1)S(1)}, bf16[8,8,8,4]{3,1,2,0:T(8,128)(2,1)S(1)}, u32[]{:S(2)}, u32[]{:S(2)}) collective-permute-start(bf16[8,8,8,4]{3,1,2,0:T(8,128)(2,1)S(1)} %get-tuple-element.125), channel_id=1, source_target_pairs={{0,8},{8,16},{16,24},{1,9},{9,17},{17,25},{2,10},{10,18},{18,26},{... | collective-permute-start | bytes 12296 | tf_op jit(solution)/shard_map/ppermute | solution.py:15
  200.0 1.9 collective-permute-start.7
  202.1 4.2 %collective-permute-done.7 = bf16[8,8,8,4]{3,1,2,0:T(8,128)(2,1)S(1)} collective-permute-done((bf16[8,8,8,4]{3,1,2,0:T(8,128)(2,1)S(1)}, bf16[8,8,8,4]{3,1,2,0:T(8,128)(2,1)S(1)}, u32[]{:S(2)}, u32[]{:S(2)}) %collective-permute-start.7) | collective-permute-done | bytes 4128 | tf_op jit(solution)/shard_map/ppermute | solution.py:18
  206.5 4.5 %collective-permute-start.8 = (bf16[8,8,4,136]{3,1,2,0:T(8,128)(2,1)S(1)}, bf16[8,8,4,136]{3,1,2,0:T(8,128)(2,1)S(1)}, u32[]{:S(2)}, u32[]{:S(2)}) collective-permute-start(bf16[8,8,4,136]{3,1,2,0:T(8,128)(2,1)S(1)} %get-tuple-element.121), channel_id=1, source_target_pairs={{0,1},{1,2},{2,3},{3,4},{4,5},{5,6},{6,7},{8,9},{9,10},{10,11},{11... | collective-permute-start | bytes 208904 | tf_op jit(solution)/shard_map/ppermute | solution.py:15
  211.0 1.9 collective-permute-start.9
  213.2 1.1 collective-permute-done.8
  214.3 2.4 %collective-permute-done.9 = bf16[8,8,4,136]{3,1,2,0:T(8,128)(2,1)S(1)} collective-permute-done((bf16[8,8,4,136]{3,1,2,0:T(8,128)(2,1)S(1)}, bf16[8,8,4,136]{3,1,2,0:T(8,128)(2,1)S(1)}, u32[]{:S(2)}, u32[]{:S(2)}) %collective-permute-start.9) | collective-permute-done | bytes 69664 | tf_op jit(solution)/shard_map/ppermute | solution.py:18
  218.6 0.7 copy.154
  (137 shorter events, 17.3 us)
Async XLA Ops:
  0.0 9.6 %copy-start.1 = (bf16[9,8,8]{0,2,1:T(8,128)(2,1)S(1)}, bf16[9,8,8]{0,2,1:T(8,128)(2,1)}, u32[]{:S(2)}) copy-start(bf16[9,8,8]{0,2,1:T(8,128)(2,1)} %param.24) | copy-start | bytes 3460
  3.4 16.5 %collective-permute-start = (f32[5,8,4,512]{3,1,2,0:T(8,128)S(1)}, f32[5,8,4,512]{3,1,2,0:T(8,128)S(1)}, u32[]{:S(2)}, u32[]{:S(2)}) collective-permute-start(f32[5,8,4,512]{3,1,2,0:T(8,128)S(1)} %get-tuple-element.115), channel_id=1, source_target_pairs={{0,1},{1,2},{2,3},{3,4},{4,5},{5,6},{6,7},{8,9},{9,10},{10,11},{11... | collective-permute-start | bytes 983048 | tf_op jit(solution)/shard_map/ppermute | solution.py:15
  6.5 16.3 %collective-permute-start.1 = (f32[5,8,4,512]{3,1,2,0:T(8,128)S(1)}, f32[5,8,4,512]{3,1,2,0:T(8,128)S(1)}, u32[]{:S(2)}, u32[]{:S(2)}) collective-permute-start(f32[5,8,4,512]{3,1,2,0:T(8,128)S(1)} %get-tuple-element.116), channel_id=1, source_target_pairs={{1,0},{2,1},{3,2},{4,3},{5,4},{6,5},{7,6},{9,8},{10,9},{11,10},{12... | collective-permute-start | bytes 983048 | tf_op jit(solution)/shard_map/ppermute | solution.py:18
  24.8 8.7 %copy-start.2 = (bf16[9,8,8]{0,2,1:T(8,128)(2,1)S(1)}, bf16[9,8,8]{0,2,1:T(8,128)(2,1)}, u32[]{:S(2)}) copy-start(bf16[9,8,8]{0,2,1:T(8,128)(2,1)} %param.25) | copy-start | bytes 3460
  24.8 8.8 %copy-start.7 = (bf16[64,64]{1,0:T(8,128)(2,1)S(1)}, bf16[64,64]{1,0:T(8,128)(2,1)}, u32[]{:S(2)}) copy-start(bf16[64,64]{1,0:T(8,128)(2,1)} %param.22) | copy-start | bytes 24580
  29.7 7.4 %all-to-all-start = ((bf16[4,2,8192]{2,1,0:T(2,128)(2,1)}), bf16[4,2,8192]{2,1,0:T(2,128)(2,1)S(1)}, u32[]{:S(2)}, u32[]{:S(2)}) async-start(bf16[4,2,8192]{2,1,0:T(2,128)(2,1)} %reshape.99), calls=%async_computation | async-start | bytes 262144 | tf_op jit(solution)/shard_map/all_to_all | solution.py:142
  36.1 5.1 %copy-start.3 = (bf16[64,192]{1,0:T(8,128)(2,1)S(1)}, bf16[64,192]{1,0:T(8,128)(2,1)}, u32[]{:S(2)}) copy-start(bf16[64,192]{1,0:T(8,128)(2,1)} %param.20) | copy-start | bytes 73732
  36.1 5.1 %copy-start.4 = (bf16[64,8]{0,1:T(8,128)(2,1)S(1)}, bf16[64,8]{0,1:T(8,128)(2,1)}, u32[]{:S(2)}) copy-start(bf16[64,8]{0,1:T(8,128)(2,1)} %param.23) | copy-start | bytes 3076
  36.1 5.1 %copy-start.5 = (f32[4]{0:T(128)S(1)}, f32[4]{0:T(128)}, u32[]{:S(2)}) copy-start(f32[4]{0:T(128)} %param.21) | copy-start | bytes 52
  36.1 5.1 %copy-start.6 = (bf16[8,64]{1,0:T(8,128)(2,1)S(1)}, bf16[8,64]{1,0:T(8,128)(2,1)}, u32[]{:S(2)}) copy-start(bf16[8,64]{1,0:T(8,128)(2,1)} %param.18) | copy-start | bytes 3076
  36.1 5.1 %copy-start.8 = (f32[64]{0:T(128)S(1)}, f32[64]{0:T(128)}, u32[]{:S(2)}) copy-start(f32[64]{0:T(128)} %param.19) | copy-start | bytes 772
  64.3 3.7 %copy-start = (bf16[256,4,8,8]{3,2,1,0:T(8,128)(2,1)S(1)}, bf16[256,4,8,8]{3,2,1,0:T(8,128)(2,1)}, u32[]{:S(2)}) copy-start(bf16[256,4,8,8]{3,2,1,0:T(8,128)(2,1)} %copy.211) | copy-start | bytes 393220 | tf_op jit(solution)/shard_map/while
  98.1 3.7 %copy-start = (bf16[256,4,8,8]{3,2,1,0:T(8,128)(2,1)S(1)}, bf16[256,4,8,8]{3,2,1,0:T(8,128)(2,1)}, u32[]{:S(2)}) copy-start(bf16[256,4,8,8]{3,2,1,0:T(8,128)(2,1)} %copy.211) | copy-start | bytes 393220 | tf_op jit(solution)/shard_map/while
  131.9 3.7 %copy-start = (bf16[256,4,8,8]{3,2,1,0:T(8,128)(2,1)S(1)}, bf16[256,4,8,8]{3,2,1,0:T(8,128)(2,1)}, u32[]{:S(2)}) copy-start(bf16[256,4,8,8]{3,2,1,0:T(8,128)(2,1)} %copy.211) | copy-start | bytes 393220 | tf_op jit(solution)/shard_map/while
  165.7 3.7 %copy-start = (bf16[256,4,8,8]{3,2,1,0:T(8,128)(2,1)S(1)}, bf16[256,4,8,8]{3,2,1,0:T(8,128)(2,1)}, u32[]{:S(2)}) copy-start(bf16[256,4,8,8]{3,2,1,0:T(8,128)(2,1)} %copy.211) | copy-start | bytes 393220 | tf_op jit(solution)/shard_map/while
  176.9 5.0 %collective-permute-start.2 = (bf16[8,8,8,4]{3,1,2,0:T(8,128)(2,1)S(1)}, bf16[8,8,8,4]{3,1,2,0:T(8,128)(2,1)S(1)}, u32[]{:S(2)}, u32[]{:S(2)}) collective-permute-start(bf16[8,8,8,4]{3,1,2,0:T(8,128)(2,1)S(1)} %get-tuple-element.127), channel_id=1, source_target_pairs={{0,8},{8,16},{16,24},{1,9},{9,17},{17,25},{2,10},{10,18},{18,26},{... | collective-permute-start | bytes 12296 | tf_op jit(solution)/shard_map/ppermute | solution.py:15
  179.8 6.3 %collective-permute-start.3 = (bf16[8,8,8,4]{3,1,2,0:T(8,128)(2,1)S(1)}, bf16[8,8,8,4]{3,1,2,0:T(8,128)(2,1)S(1)}, u32[]{:S(2)}, u32[]{:S(2)}) collective-permute-start(bf16[8,8,8,4]{3,1,2,0:T(8,128)(2,1)S(1)} %get-tuple-element.128), channel_id=1, source_target_pairs={{8,0},{16,8},{24,16},{9,1},{17,9},{25,17},{10,2},{18,10},{26,18},{... | collective-permute-start | bytes 12296 | tf_op jit(solution)/shard_map/ppermute | solution.py:18
  186.3 6.7 %collective-permute-start.4 = (bf16[8,8,4,136]{3,1,2,0:T(8,128)(2,1)S(1)}, bf16[8,8,4,136]{3,1,2,0:T(8,128)(2,1)S(1)}, u32[]{:S(2)}, u32[]{:S(2)}) collective-permute-start(bf16[8,8,4,136]{3,1,2,0:T(8,128)(2,1)S(1)} %get-tuple-element.123), channel_id=1, source_target_pairs={{0,1},{1,2},{2,3},{3,4},{4,5},{5,6},{6,7},{8,9},{9,10},{10,11},{11... | collective-permute-start | bytes 208904 | tf_op jit(solution)/shard_map/ppermute | solution.py:15
  188.6 6.7 %collective-permute-start.5 = (bf16[8,8,4,136]{3,1,2,0:T(8,128)(2,1)S(1)}, bf16[8,8,4,136]{3,1,2,0:T(8,128)(2,1)S(1)}, u32[]{:S(2)}, u32[]{:S(2)}) collective-permute-start(bf16[8,8,4,136]{3,1,2,0:T(8,128)(2,1)S(1)} %get-tuple-element.124), channel_id=1, source_target_pairs={{1,0},{2,1},{3,2},{4,3},{5,4},{6,5},{7,6},{9,8},{10,9},{11,10},{12... | collective-permute-start | bytes 208904 | tf_op jit(solution)/shard_map/ppermute | solution.py:18
  197.3 4.8 %collective-permute-start.6 = (bf16[8,8,8,4]{3,1,2,0:T(8,128)(2,1)S(1)}, bf16[8,8,8,4]{3,1,2,0:T(8,128)(2,1)S(1)}, u32[]{:S(2)}, u32[]{:S(2)}) collective-permute-start(bf16[8,8,8,4]{3,1,2,0:T(8,128)(2,1)S(1)} %get-tuple-element.125), channel_id=1, source_target_pairs={{0,8},{8,16},{16,24},{1,9},{9,17},{17,25},{2,10},{10,18},{18,26},{... | collective-permute-start | bytes 12296 | tf_op jit(solution)/shard_map/ppermute | solution.py:15
  200.0 6.3 %collective-permute-start.7 = (bf16[8,8,8,4]{3,1,2,0:T(8,128)(2,1)S(1)}, bf16[8,8,8,4]{3,1,2,0:T(8,128)(2,1)S(1)}, u32[]{:S(2)}, u32[]{:S(2)}) collective-permute-start(bf16[8,8,8,4]{3,1,2,0:T(8,128)(2,1)S(1)} %get-tuple-element.126), channel_id=1, source_target_pairs={{8,0},{16,8},{24,16},{9,1},{17,9},{25,17},{10,2},{18,10},{26,18},{... | collective-permute-start | bytes 12296 | tf_op jit(solution)/shard_map/ppermute | solution.py:18
  206.5 7.8 %collective-permute-start.8 = (bf16[8,8,4,136]{3,1,2,0:T(8,128)(2,1)S(1)}, bf16[8,8,4,136]{3,1,2,0:T(8,128)(2,1)S(1)}, u32[]{:S(2)}, u32[]{:S(2)}) collective-permute-start(bf16[8,8,4,136]{3,1,2,0:T(8,128)(2,1)S(1)} %get-tuple-element.121), channel_id=1, source_target_pairs={{0,1},{1,2},{2,3},{3,4},{4,5},{5,6},{6,7},{8,9},{9,10},{10,11},{11... | collective-permute-start | bytes 208904 | tf_op jit(solution)/shard_map/ppermute | solution.py:15
  211.0 5.7 %collective-permute-start.9 = (bf16[8,8,4,136]{3,1,2,0:T(8,128)(2,1)S(1)}, bf16[8,8,4,136]{3,1,2,0:T(8,128)(2,1)S(1)}, u32[]{:S(2)}, u32[]{:S(2)}) collective-permute-start(bf16[8,8,4,136]{3,1,2,0:T(8,128)(2,1)S(1)} %get-tuple-element.122), channel_id=1, source_target_pairs={{1,0},{2,1},{3,2},{4,3},{5,4},{6,5},{7,6},{9,8},{10,9},{11,10},{12... | collective-permute-start | bytes 208904 | tf_op jit(solution)/shard_map/ppermute | solution.py:18
where the time goes:
time: 221 us; the launch traced here: 219 us
  local copies, waits for them, and re-layouts  104 us (47%)
  matrix products  46 us (21%)
  starting transfers between devices  32.3 us (15%)
  waiting for transfers between devices  28.1 us (13%)
  other arithmetic  5.64 us (3%)
  loops' own time  3.16 us (1%)
    dot_general x4, matrix products, post_block(): jnp.einsum('pmhd,pnhd->phmn', queries, keys_all, preferred_element_type=j...  21.6 us
    dot_general x4, matrix products, post_block(): jnp.einsum('phmn,pnhd->pmhd', probs, values, preferred_element_type=jnp.f...  16.5 us
    ppermute x5, waiting for transfers between devices, padded(): lax.ppermute(lax.slice_in_dim(block, 0, width, axis=dim), axis, backward)  15.9 us
    ppermute x5, starting transfers between devices, padded(): lax.ppermute(lax.slice_in_dim(block, block.shape[dim] - width, None, axis...  15.5 us
    convert_element_type x4, local copies, waits for them, and re-layouts, post_block(): (keys_all * lax.rsqrt(jnp.sum(keys_all * keys_all, -1, keepdims=True) + 1...  15.2 us
    convert_element_type x4, local copies, waits for them, and re-layouts, post_block(): (queries * lax.rsqrt(jnp.sum(queries * queries, -1, keepdims=True) + 1.0)...  14.9 us
    reshape x4, local copies, waits for them, and re-layouts, post_block(): projected[..., 2 * width:].astype(jnp.bfloat16)  14.8 us
    convert_element_type x4, local copies, waits for them, and re-layouts, post_block(): probs = (weights / jnp.sum(weights, -1, keepdims=True)).astype(jnp.bfloat16)  14.6 us
  transfers between devices with their start and end apart: 11, of which 9 were waited for; matrix products, arithmetic and copies ran while one was open for 2% of the time, Pallas kernels for 0%

commit v1 on v0

--- a/solution.py
+++ b/solution.py
@@ -2,6 +2,8 @@
 import jax.numpy as jnp
 from jax import lax
 from jax.sharding import PartitionSpec as P
+from jax.experimental import pallas as pl
+from jax.experimental.pallas import tpu as pltpu
 
 STEPS = 4
 DILATION_SPAN = 4
@@ -38,8 +40,56 @@
     )
 
 
+def attention_kernel(
+    hs_ref, x_ref, w1_ref, gain_ref, pw_ref, ow_ref, rw_ref, out_ref
+):
+    width = w1_ref.shape[0]
+    heads = hs_ref.shape[0]
+    head_size = width // heads
+    lanes = x_ref.shape[2]
+    chunk = 128
+    members = lanes // chunk
+    layers = x_ref[0].astype(jnp.bfloat16)
+    embedded = jnp.dot(w1_ref[...], layers, preferred_element_type=jnp.float32)
+    meansq = jnp.sum(embedded * embedded, axis=0, keepdims=True) * (1.0 / width)
+    normed = (embedded * lax.rsqrt(meansq + 1e-05) * gain_ref[...]).astype(jnp.bfloat16)
+    projected = jnp.dot(pw_ref[...], normed, preferred_element_type=jnp.float32)
+    mixed_heads = []
+    for h in range(heads):
+        q = projected[h * head_size : (h + 1) * head_size]
+        k = projected[width + h * head_size : width + (h + 1) * head_size]
+        v = projected[2 * width + h * head_size : 2 * width + (h + 1) * head_size]
+        v = v.astype(jnp.bfloat16).astype(jnp.float32)
+        q = (q * lax.rsqrt(jnp.sum(q * q, 0, keepdims=True) + 1.0)).astype(jnp.bfloat16)
+        k = (k * lax.rsqrt(jnp.sum(k * k, 0, keepdims=True) + 1.0)).astype(jnp.bfloat16)
+        q = q.astype(jnp.float32)
+        k = k.astype(jnp.float32)
+        scale = hs_ref[h]
+        weights = []
+        for n in range(members):
+            k_n = k[:, n * chunk : (n + 1) * chunk]
+            k_wide = jnp.concatenate([k_n] * members, axis=1)
+            score = jnp.sum(q * k_wide, axis=0, keepdims=True) * scale
+            weights.append(jnp.exp(score))
+        total = weights[0]
+        for n in range(1, members):
+            total = total + weights[n]
+        mixed = jnp.zeros(q.shape, jnp.float32)
+        for n in range(members):
+            prob = (weights[n] / total).astype(jnp.bfloat16).astype(jnp.float32)
+            v_n = v[:, n * chunk : (n + 1) * chunk]
+            v_wide = jnp.concatenate([v_n] * members, axis=1)
+            mixed = mixed + prob * v_wide
+        mixed_heads.append(mixed.astype(jnp.bfloat16))
+    mixed_all = jnp.concatenate(mixed_heads, axis=0)
+    attended = jnp.dot(ow_ref[...], mixed_all, preferred_element_type=jnp.float32)
+    residual = (embedded + attended).astype(jnp.bfloat16)
+    features = jnp.dot(rw_ref[...], residual, preferred_element_type=jnp.float32)
+    out_ref[0] = features.astype(out_ref.dtype)
+
+
 def post_block(
-    vertical_layers,
+    rows_first,
     embed_weight,
     norm_gain,
     project_weight,
@@ -47,41 +97,33 @@
     output_weight,
     readout_weight,
 ):
-    members, _, points = vertical_layers.shape
+    row_count, levels_count, lanes = rows_first.shape
     width = embed_weight.shape[1]
-    heads = head_scale.shape[0]
-    head_size = width // heads
-    embedded = jnp.einsum(
-        "mlp,le->pme", vertical_layers, embed_weight, preferred_element_type=jnp.float32
-    )
-    meansq = jnp.mean(embedded * embedded, axis=-1, keepdims=True)
-    normed = (embedded * lax.rsqrt(meansq + 1e-05) * norm_gain).astype(jnp.bfloat16)
-    projected = jnp.einsum(
-        "pme,ef->pmf", normed, project_weight, preferred_element_type=jnp.float32
-    )
-    queries = projected[..., :width].reshape(points, members, heads, head_size)
-    keys_all = projected[..., width : 2 * width].reshape(points, members, heads, head_size)
-    values = (
-        projected[..., 2 * width :].astype(jnp.bfloat16).reshape(points, members, heads, head_size)
-    )
-    queries = (queries * lax.rsqrt(jnp.sum(queries * queries, -1, keepdims=True) + 1.0)).astype(
-        jnp.bfloat16
-    )
-    keys_all = (keys_all * lax.rsqrt(jnp.sum(keys_all * keys_all, -1, keepdims=True) + 1.0)).astype(
-        jnp.bfloat16
-    )
-    scores = jnp.einsum("pmhd,pnhd->phmn", queries, keys_all, preferred_element_type=jnp.float32)
-    scores = scores * head_scale[:, None, None]
-    weights = jnp.exp(scores)
-    probs = (weights / jnp.sum(weights, -1, keepdims=True)).astype(jnp.bfloat16)
-    mixed = jnp.einsum("phmn,pnhd->pmhd", probs, values, preferred_element_type=jnp.float32)
-    mixed = mixed.astype(jnp.bfloat16).reshape(points, members, width)
-    attended = jnp.einsum("pme,ef->pmf", mixed, output_weight, preferred_element_type=jnp.float32)
-    residual = (embedded + attended).astype(jnp.bfloat16)
-    step_result = jnp.einsum(
-        "pme,ef->mfp", residual, readout_weight, preferred_element_type=jnp.float32
-    )
-    return step_result.astype(jnp.bfloat16)
+    feat = readout_weight.shape[1]
+    full = lambda r: (0, 0)
+    return pl.pallas_call(
+        attention_kernel,
+        grid=(row_count,),
+        in_specs=[
+            pl.BlockSpec(memory_space=pltpu.SMEM),
+            pl.BlockSpec((1, levels_count, lanes), lambda r: (r, 0, 0)),
+            pl.BlockSpec((width, levels_count), full),
+            pl.BlockSpec((width, 1), full),
+            pl.BlockSpec((3 * width, width), full),
+            pl.BlockSpec((width, width), full),
+            pl.BlockSpec((feat, width), full),
+        ],
+        out_specs=pl.BlockSpec((1, feat, lanes), lambda r: (r, 0, 0)),
+        out_shape=jax.ShapeDtypeStruct((row_count, feat, lanes), jnp.bfloat16),
+    )(
+        head_scale,
+        rows_first,
+        embed_weight.T,
+        norm_gain.reshape(width, 1),
+        project_weight.T,
+        output_weight.T,
+        readout_weight.T,
+    )
 
 
 def convolve(padded_field, kernel):
@@ -143,25 +185,20 @@
         predicted_states, "mem", split_axis=3, concat_axis=0, tiled=True
     )
     members, levels_count, tile_rows, tile_cols = blockwise_quantity.shape
-    count = tile_rows * tile_cols
-    flattened = blockwise_quantity.reshape(members, levels_count, count)
-    block = 256
-
-    def one_block(block_index):
-        vertical_layers = lax.dynamic_slice_in_dim(flattened, block_index * block, block, 2)
-        return post_block(
-            vertical_layers,
-            embed_weight,
-            norm_gain,
-            project_weight,
-            head_scale,
-            output_weight,
-            readout_weight,
-        )
-
-    blocks = lax.map(one_block, jnp.arange(count // block))
-    step_result = jnp.moveaxis(blocks, 0, 2)
-    features = step_result.reshape(members, readout_weight.shape[1], tile_rows, tile_cols)
+    rows_first = jnp.transpose(blockwise_quantity, (2, 1, 0, 3)).astype(jnp.float32)
+    rows_first = rows_first.reshape(tile_rows, levels_count, members * tile_cols)
+    step_result = post_block(
+        rows_first,
+        embed_weight,
+        norm_gain,
+        project_weight,
+        head_scale,
+        output_weight,
+        readout_weight,
+    )
+    feat = readout_weight.shape[1]
+    step_result = step_result.reshape(tile_rows, feat, members, tile_cols)
+    features = jnp.transpose(step_result, (2, 1, 0, 3))
     tile_cols = features.shape[3]
     padded_feature = padded(features, (("mem", 3), ("row", 2)), DILATION_SPAN)
     interior_cells = jax.nn.silu(convolve(padded_feature, first_kernel)).astype(jnp.bfloat16)

time: 221 us -> 106 us (0.48)
  local copies, waits for them, and re-layouts: 104 us -> 22 us
  matrix products: 46 us -> 4.75 us
  Pallas kernels: 0 us -> 12.9 us
  loops' own time: 3.16 us -> 0 us
    convert_element_type x16 -> x0, local copies, waits for them, and re-layouts: 55.7 us -> none  [the longest x4 15.2 us: post_block(): (keys_all * lax.rsqrt(jnp.sum(keys_all * keys_all, -1, keepdims=True) + 1...]
    dot_general x20 -> x0, matrix products: 42.2 us -> none  [the longest x4 21.6 us: post_block(): jnp.einsum('pmhd,pnhd->phmn', queries, keys_all, preferred_element_type=j...]
    dot_general x4 -> x0, local copies, waits for them, and re-layouts: 14.3 us -> none  [post_block(): jnp.einsum('pmhd,pnhd->phmn', queries, keys_all, preferred_element_type=j...]
    pallas_call x0 -> x1, Pallas kernels: none -> 12.9 us  [post_block(): pl.pallas_call(attention_kernel, grid=(row_count,), in_specs=[pl.BlockSpe...]
    reshape x6 -> x2, local copies, waits for them, and re-layouts: 14.8 us -> 4.46 us  [the longest x1 3.75 us: on_device(): rows_first.reshape(tile_rows, levels_count, members * tile_cols)]
    another operation x1 -> x0, loops' own time: 3.16 us -> none  [on_device(): blocks = lax.map(one_block, jnp.arange(count // block))]
    dynamic_slice x4 -> x0, local copies, waits for them, and re-layouts: 2.35 us -> none  [on_device(): blocks = lax.map(one_block, jnp.arange(count // block))]
    reshape x0 -> x1, other arithmetic: none -> 2.33 us  [on_device(): rows_first.reshape(tile_rows, levels_count, members * tile_cols)]
  transfers between devices with their start and end apart: 11 -> 11, of which waited for: 9 -> 8; matrix products, arithmetic and copies ran while one was open for 2% -> 7% of each run, Pallas kernels for 0% -> 0%
where the time goes in v1:
time: 106 us; the launch traced here: 105 us
  starting transfers between devices  32.7 us (31%)
  waiting for transfers between devices  26.5 us (25%)
  local copies, waits for them, and re-layouts  22 us (21%)
  Pallas kernels  12.9 us (12%)
  other arithmetic  5.13 us (5%)
  matrix products  4.75 us (4%)
    ppermute x5, starting transfers between devices, padded(): lax.ppermute(lax.slice_in_dim(block, block.shape[dim] - width, None, axis...  16.1 us
    ppermute x5, waiting for transfers between devices, padded(): lax.ppermute(lax.slice_in_dim(block, 0, width, axis=dim), axis, backward)  15 us
    unnamed x40, local copies, waits for them, and re-layouts  13.2 us
    pallas_call x1, Pallas kernels, post_block(): pl.pallas_call(attention_kernel, grid=(row_count,), in_specs=[pl.BlockSpe...  12.9 us
    ppermute x5, starting transfers between devices, padded(): lax.ppermute(lax.slice_in_dim(block, 0, width, axis=dim), axis, backward)  12.8 us
    ppermute x5, waiting for transfers between devices, padded(): lax.ppermute(lax.slice_in_dim(block, block.shape[dim] - width, None, axis...  11.5 us
    dot_general x18, matrix products, convolve(): jnp.einsum('oc,mcij->moij', kernel[row_stencil * 3 + column_stencil], shi...  4.75 us
    all_to_all x1, starting transfers between devices, on_device(): lax.all_to_all(predicted_states, 'mem', split_axis=3, concat_axis=0, tile...  3.79 us
  transfers between devices with their start and end apart: 11, of which 8 were waited for; matrix products, arithmetic and copies ran while one was open for 7% of the time, Pallas kernels for 0%

profile of v1, /device:TPU:9, one launch (start us, length us, event | category | flops | bytes accessed | tf_op | source)
XLA Modules:
  0.0 104.5 jit_solution(6736299339299293805)
XLA Ops:
  0.0 1.0 copy.117
  1.0 1.1 %copy.41 = f32[2,8,8,512]{3,1,2,0:T(8,128)S(1)} copy(f32[2,8,8,512]{3,2,1,0:T(8,128)} %param.12) | data formatting | bytes 524288 | tf_op args[0]
  2.1 1.1 %fusion.73 = (f32[8,8,512]{2,0,1:T(8,128)S(1)}, f32[1,8,8,512]{3,1,2,0:T(8,128)S(1)}, f32[1,8,8,512]{3,1,2,0:T(8,128)S(1)}, f32[8,8,512]{2,0,1:T(8,128)S(1)}) fusion(f32[8,8,512]{2,1,0:T(8,128)} %param.13, f32[8,8,512]{2,1,0:T(8,128)} %param.14), kind=kLoop, calls=%fused_computation.120 | loop fusion | bytes 786432 | tf_op args[1]
  3.4 3.1 %collective-permute-start = (f32[5,8,4,512]{3,1,2,0:T(8,128)S(1)}, f32[5,8,4,512]{3,1,2,0:T(8,128)S(1)}, u32[]{:S(2)}, u32[]{:S(2)}) collective-permute-start(f32[5,8,4,512]{3,1,2,0:T(8,128)S(1)} %get-tuple-element.14), channel_id=1, source_target_pairs={{0,1},{1,2},{2,3},{3,4},{4,5},{5,6},{6,7},{8,9},{9,10},{10,11},{11... | collective-permute-start | bytes 983048 | tf_op jit(solution)/shard_map/ppermute | solution.py:17
  6.5 3.1 %collective-permute-start.1 = (f32[5,8,4,512]{3,1,2,0:T(8,128)S(1)}, f32[5,8,4,512]{3,1,2,0:T(8,128)S(1)}, u32[]{:S(2)}, u32[]{:S(2)}) collective-permute-start(f32[5,8,4,512]{3,1,2,0:T(8,128)S(1)} %get-tuple-element.15), channel_id=1, source_target_pairs={{1,0},{2,1},{3,2},{4,3},{5,4},{6,5},{7,6},{9,8},{10,9},{11,10},{12... | collective-permute-start | bytes 983048 | tf_op jit(solution)/shard_map/ppermute | solution.py:20
  9.7 10.1 %collective-permute-done = f32[5,8,4,512]{3,1,2,0:T(8,128)S(1)} collective-permute-done((f32[5,8,4,512]{3,1,2,0:T(8,128)S(1)}, f32[5,8,4,512]{3,1,2,0:T(8,128)S(1)}, u32[]{:S(2)}, u32[]{:S(2)}) %collective-permute-start) | collective-permute-done | bytes 327712 | tf_op jit(solution)/shard_map/ppermute | solution.py:17
  19.9 2.9 %collective-permute-done.1 = f32[5,8,4,512]{3,1,2,0:T(8,128)S(1)} collective-permute-done((f32[5,8,4,512]{3,1,2,0:T(8,128)S(1)}, f32[5,8,4,512]{3,1,2,0:T(8,128)S(1)}, u32[]{:S(2)}, u32[]{:S(2)}) %collective-permute-start.1) | collective-permute-done | bytes 327712 | tf_op jit(solution)/shard_map/ppermute | solution.py:20
  23.1 0.5 add_select_fusion
  23.6 0.4 add_select_fusion.1
  24.1 0.4 add_select_fusion.2
  24.5 0.3 select_convert_fusion
  24.8 2.0 %copy.45 = bf16[2,8,8,512]{2,1,0,3:T(8,128)(2,1)S(1)} copy(bf16[2,8,8,512]{3,1,2,0:T(8,128)(2,1)S(1)} %select_convert_fusion) | data formatting | bytes 262144 | tf_op jit(solution)/shard_map/convert_element_type | solution.py:183
  26.9 2.8 %reshape.76 = bf16[4,2,8192]{2,1,0:T(2,128)(2,1)} reshape(bf16[512,2,8,8]{3,2,1,0:T(8,128)(2,1)S(1)} %bitcast.191) | data formatting | bytes 262144
  29.7 3.8 %all-to-all-start = ((bf16[4,2,8192]{2,1,0:T(2,128)(2,1)}), bf16[4,2,8192]{2,1,0:T(2,128)(2,1)S(1)}, u32[]{:S(2)}, u32[]{:S(2)}) async-start(bf16[4,2,8192]{2,1,0:T(2,128)(2,1)} %reshape.76), calls=%async_computation | async-start | bytes 262144 | tf_op jit(solution)/shard_map/all_to_all | solution.py:184
  33.6 0.7 copy.48
  34.3 0.7 copy.50.gain_ref
  35.0 0.7 copy.47
  35.7 0.7 copy.49
  37.1 0.1 copy.97
  37.2 0.1 copy.96
  37.4 0.1 copy.95
  37.5 0.1 copy.94
  38.9 2.5 %reshape.77 = bf16[512,2,8,8]{3,2,1,0:T(8,128)(2,1)S(1)} reshape(bf16[4,2,8192]{2,1,0:T(2,128)(2,1)S(1)} %all-to-all-done) | data formatting | bytes 262144
  41.3 2.3 %convert_bitcast_fusion = f32[4,2,8,8,128]{3,2,1,4,0:T(8,128)} fusion(bf16[2,8,8,4,128]{2,1,0,4,3:T(8,128)(2,1)S(1)} %bitcast.190), kind=kLoop, calls=%fused_computation | loop fusion | flops 65536 | bytes 393216 | tf_op jit(solution)/shard_map/reshape | solution.py:189
  43.7 3.8 %copy.46 = f32[4,2,8,8,128]{4,2,1,0,3:T(8,128)} copy(f32[4,2,8,8,128]{3,2,1,4,0:T(8,128)} %convert_bitcast_fusion) | data formatting | bytes 524288 | tf_op jit(solution)/shard_map/reshape | solution.py:189
  47.4 12.9 %shard_map.118 = bf16[8,8,1024]{2,1,0:T(8,128)(2,1)} custom-call(f32[4]{0:T(128)} %hs_ref.1, f32[8,8,1024]{2,1,0:T(8,128)} %bitcast.194, bf16[64,8]{1,0:T(8,128)(2,1)} %bitcast.196, f32[64,1]{1,0:T(8,128)} %copy.50.gain_ref, bf16[192,64]{1,0:T(8,128)(2,1)} %bitcast.195, bf16[64,64]{1,0:T(8,128)(2,1)} %bitcast.197, bf16[8,64]{1,0:T(8,128)(2,1)} %bitcast.198), custom_call_target="tpu_custom_call" | custom-call | tf_op jit(solution)/shard_map/pallas_call | solution.py:104
  60.3 0.9 copy_bitcast_fusion
  61.4 3.5 %collective-permute-start.2 = (bf16[8,8,8,4]{3,1,2,0:T(8,128)(2,1)S(1)}, bf16[8,8,8,4]{3,1,2,0:T(8,128)(2,1)S(1)}, u32[]{:S(2)}, u32[]{:S(2)}) collective-permute-start(bf16[8,8,8,4]{3,1,2,0:T(8,128)(2,1)S(1)} %get-tuple-element.26), channel_id=1, source_target_pairs={{0,8},{8,16},{16,24},{1,9},{9,17},{17,25},{2,10},{10,18},{18,26},{... | collective-permute-start | bytes 12296 | tf_op jit(solution)/shard_map/ppermute | solution.py:17
  64.9 1.9 %collective-permute-start.3 = (bf16[8,8,8,4]{3,1,2,0:T(8,128)(2,1)S(1)}, bf16[8,8,8,4]{3,1,2,0:T(8,128)(2,1)S(1)}, u32[]{:S(2)}, u32[]{:S(2)}) collective-permute-start(bf16[8,8,8,4]{3,1,2,0:T(8,128)(2,1)S(1)} %get-tuple-element.27), channel_id=1, source_target_pairs={{8,0},{16,8},{24,16},{9,1},{17,9},{25,17},{10,2},{18,10},{26,18},{... | collective-permute-start | bytes 12296 | tf_op jit(solution)/shard_map/ppermute | solution.py:20
  66.9 1.1 %fusion.58 = f32[8,8,128,8]{2,3,1,0:T(8,128)S(1)} fusion(bf16[1,8,8]{2,1,0:T(8,128)(2,1)S(1)} %copy.93, bf16[8,8,1024]{2,1,0:T(8,128)(2,1)} %shard_map.118), kind=kOutput, calls=%fused_computation.98 | convolution fusion | flops 1048576 | bytes 393344 | tf_op jit(solution)/shard_map/oc,mcij->moij/dot_general | solution.py:143
  67.9 3.3 %collective-permute-done.3 = bf16[8,8,8,4]{3,1,2,0:T(8,128)(2,1)S(1)} collective-permute-done((bf16[8,8,8,4]{3,1,2,0:T(8,128)(2,1)S(1)}, bf16[8,8,8,4]{3,1,2,0:T(8,128)(2,1)S(1)}, u32[]{:S(2)}, u32[]{:S(2)}) %collective-permute-start.3) | collective-permute-done | bytes 4128 | tf_op jit(solution)/shard_map/ppermute | solution.py:20
  71.2 0.2 pad_maximum_fusion.4
  71.4 2.2 %collective-permute-start.4 = (bf16[8,8,4,136]{3,1,2,0:T(8,128)(2,1)S(1)}, bf16[8,8,4,136]{3,1,2,0:T(8,128)(2,1)S(1)}, u32[]{:S(2)}, u32[]{:S(2)}) collective-permute-start(bf16[8,8,4,136]{3,1,2,0:T(8,128)(2,1)S(1)} %get-tuple-element.22), channel_id=1, source_target_pairs={{0,1},{1,2},{2,3},{3,4},{4,5},{5,6},{6,7},{8,9},{9,10},{10,11},{11... | collective-permute-start | bytes 208904 | tf_op jit(solution)/shard_map/ppermute | solution.py:17
  73.7 3.9 %collective-permute-start.5 = (bf16[8,8,4,136]{3,1,2,0:T(8,128)(2,1)S(1)}, bf16[8,8,4,136]{3,1,2,0:T(8,128)(2,1)S(1)}, u32[]{:S(2)}, u32[]{:S(2)}) collective-permute-start(bf16[8,8,4,136]{3,1,2,0:T(8,128)(2,1)S(1)} %get-tuple-element.23), channel_id=1, source_target_pairs={{1,0},{2,1},{3,2},{4,3},{5,4},{6,5},{7,6},{9,8},{10,9},{11,10},{12... | collective-permute-start | bytes 208904 | tf_op jit(solution)/shard_map/ppermute | solution.py:20
  77.6 0.2 fusion.37
  77.9 0.3 collective-permute-done.4
  78.2 2.2 %collective-permute-done.5 = bf16[8,8,4,136]{3,1,2,0:T(8,128)(2,1)S(1)} collective-permute-done((bf16[8,8,4,136]{3,1,2,0:T(8,128)(2,1)S(1)}, bf16[8,8,4,136]{3,1,2,0:T(8,128)(2,1)S(1)}, u32[]{:S(2)}, u32[]{:S(2)}) %collective-permute-start.5) | collective-permute-done | bytes 69664 | tf_op jit(solution)/shard_map/ppermute | solution.py:20
  80.3 0.3 maximum_maximum_fusion
  80.7 0.2 fusion.39
  80.9 0.2 fusion.41
  81.1 0.2 fusion.30
  81.4 0.2 fusion.32
  81.6 0.2 fusion.34
  81.8 0.2 fusion.14
  82.0 0.3 multiply_convert_fusion
  82.4 2.7 %collective-permute-start.6 = (bf16[8,8,8,4]{3,1,2,0:T(8,128)(2,1)S(1)}, bf16[8,8,8,4]{3,1,2,0:T(8,128)(2,1)S(1)}, u32[]{:S(2)}, u32[]{:S(2)}) collective-permute-start(bf16[8,8,8,4]{3,1,2,0:T(8,128)(2,1)S(1)} %get-tuple-element.24), channel_id=1, source_target_pairs={{0,8},{8,16},{16,24},{1,9},{9,17},{17,25},{2,10},{10,18},{18,26},{... | collective-permute-start | bytes 12296 | tf_op jit(solution)/shard_map/ppermute | solution.py:17
  85.1 1.9 %collective-permute-start.7 = (bf16[8,8,8,4]{3,1,2,0:T(8,128)(2,1)S(1)}, bf16[8,8,8,4]{3,1,2,0:T(8,128)(2,1)S(1)}, u32[]{:S(2)}, u32[]{:S(2)}) collective-permute-start(bf16[8,8,8,4]{3,1,2,0:T(8,128)(2,1)S(1)} %get-tuple-element.25), channel_id=1, source_target_pairs={{8,0},{16,8},{24,16},{9,1},{17,9},{25,17},{10,2},{18,10},{26,18},{... | collective-permute-start | bytes 12296 | tf_op jit(solution)/shard_map/ppermute | solution.py:20
  87.0 0.2 fusion.48
  87.2 4.2 %collective-permute-done.7 = bf16[8,8,8,4]{3,1,2,0:T(8,128)(2,1)S(1)} collective-permute-done((bf16[8,8,8,4]{3,1,2,0:T(8,128)(2,1)S(1)}, bf16[8,8,8,4]{3,1,2,0:T(8,128)(2,1)S(1)}, u32[]{:S(2)}, u32[]{:S(2)}) %collective-permute-start.7) | collective-permute-done | bytes 4128 | tf_op jit(solution)/shard_map/ppermute | solution.py:20
  91.4 0.2 pad_maximum_fusion.5
  91.6 4.5 %collective-permute-start.8 = (bf16[8,8,4,136]{3,1,2,0:T(8,128)(2,1)S(1)}, bf16[8,8,4,136]{3,1,2,0:T(8,128)(2,1)S(1)}, u32[]{:S(2)}, u32[]{:S(2)}) collective-permute-start(bf16[8,8,4,136]{3,1,2,0:T(8,128)(2,1)S(1)} %get-tuple-element.20), channel_id=1, source_target_pairs={{0,1},{1,2},{2,3},{3,4},{4,5},{5,6},{6,7},{8,9},{9,10},{10,11},{11... | collective-permute-start | bytes 208904 | tf_op jit(solution)/shard_map/ppermute | solution.py:17
  96.1 1.9 %collective-permute-start.9 = (bf16[8,8,4,136]{3,1,2,0:T(8,128)(2,1)S(1)}, bf16[8,8,4,136]{3,1,2,0:T(8,128)(2,1)S(1)}, u32[]{:S(2)}, u32[]{:S(2)}) collective-permute-start(bf16[8,8,4,136]{3,1,2,0:T(8,128)(2,1)S(1)} %get-tuple-element.21), channel_id=1, source_target_pairs={{1,0},{2,1},{3,2},{4,3},{5,4},{6,5},{7,6},{9,8},{10,9},{11,10},{12... | collective-permute-start | bytes 208904 | tf_op jit(solution)/shard_map/ppermute | solution.py:20
  98.1 0.2 fusion.23
  98.3 1.1 %collective-permute-done.8 = bf16[8,8,4,136]{3,1,2,0:T(8,128)(2,1)S(1)} collective-permute-done((bf16[8,8,4,136]{3,1,2,0:T(8,128)(2,1)S(1)}, bf16[8,8,4,136]{3,1,2,0:T(8,128)(2,1)S(1)}, u32[]{:S(2)}, u32[]{:S(2)}) %collective-permute-start.8) | collective-permute-done | bytes 69664 | tf_op jit(solution)/shard_map/ppermute | solution.py:17
  99.4 2.4 %collective-permute-done.9 = bf16[8,8,4,136]{3,1,2,0:T(8,128)(2,1)S(1)} collective-permute-done((bf16[8,8,4,136]{3,1,2,0:T(8,128)(2,1)S(1)}, bf16[8,8,4,136]{3,1,2,0:T(8,128)(2,1)S(1)}, u32[]{:S(2)}, u32[]{:S(2)}) %collective-permute-start.9) | collective-permute-done | bytes 69664 | tf_op jit(solution)/shard_map/ppermute | solution.py:20
  101.9 0.3 maximum_maximum_fusion.1
  102.2 0.2 fusion.25
  102.4 0.2 fusion.27
  102.7 0.2 fusion.16
  102.9 0.2 fusion.18
  103.1 0.2 fusion.20
  103.3 0.2 fusion.7
  103.6 0.3 fusion.15
  103.8 0.7 copy.70
  (51 shorter events, 2.9 us)
Async XLA Ops:
  3.2 6.4 %copy-start.1 = (bf16[9,8,8]{0,2,1:T(8,128)(2,1)S(1)}, bf16[9,8,8]{0,2,1:T(8,128)(2,1)}, u32[]{:S(2)}) copy-start(bf16[9,8,8]{0,2,1:T(8,128)(2,1)} %param.22) | copy-start | bytes 3460
  3.4 16.5 %collective-permute-start = (f32[5,8,4,512]{3,1,2,0:T(8,128)S(1)}, f32[5,8,4,512]{3,1,2,0:T(8,128)S(1)}, u32[]{:S(2)}, u32[]{:S(2)}) collective-permute-start(f32[5,8,4,512]{3,1,2,0:T(8,128)S(1)} %get-tuple-element.14), channel_id=1, source_target_pairs={{0,1},{1,2},{2,3},{3,4},{4,5},{5,6},{6,7},{8,9},{9,10},{10,11},{11... | collective-permute-start | bytes 983048 | tf_op jit(solution)/shard_map/ppermute | solution.py:17
  6.5 16.3 %collective-permute-start.1 = (f32[5,8,4,512]{3,1,2,0:T(8,128)S(1)}, f32[5,8,4,512]{3,1,2,0:T(8,128)S(1)}, u32[]{:S(2)}, u32[]{:S(2)}) collective-permute-start(f32[5,8,4,512]{3,1,2,0:T(8,128)S(1)} %get-tuple-element.15), channel_id=1, source_target_pairs={{1,0},{2,1},{3,2},{4,3},{5,4},{6,5},{7,6},{9,8},{10,9},{11,10},{12... | collective-permute-start | bytes 983048 | tf_op jit(solution)/shard_map/ppermute | solution.py:20
  26.8 6.7 %copy-start.2 = (bf16[9,8,8]{0,2,1:T(8,128)(2,1)S(1)}, bf16[9,8,8]{0,2,1:T(8,128)(2,1)}, u32[]{:S(2)}) copy-start(bf16[9,8,8]{0,2,1:T(8,128)(2,1)} %param.23) | copy-start | bytes 3460
  26.8 6.8 %copy-start.3 = (bf16[64,192]{1,0:T(8,128)(2,1)S(1)}, bf16[64,192]{1,0:T(8,128)(2,1)}, u32[]{:S(2)}) copy-start(bf16[64,192]{1,0:T(8,128)(2,1)} %param.18) | copy-start | bytes 73732
  26.8 7.5 %copy-start.6 = (f32[64]{0:T(128)S(1)}, f32[64]{0:T(128)}, u32[]{:S(2)}) copy-start(f32[64]{0:T(128)} %param.17) | copy-start | bytes 772
  26.8 8.2 %copy-start.5 = (bf16[8,64]{1,0:T(8,128)(2,1)S(1)}, bf16[8,64]{1,0:T(8,128)(2,1)}, u32[]{:S(2)}) copy-start(bf16[8,64]{1,0:T(8,128)(2,1)} %param.16) | copy-start | bytes 3076
  26.8 8.9 %copy-start.4 = (bf16[64,64]{1,0:T(8,128)(2,1)S(1)}, bf16[64,64]{1,0:T(8,128)(2,1)}, u32[]{:S(2)}) copy-start(bf16[64,64]{1,0:T(8,128)(2,1)} %param.20) | copy-start | bytes 24580
  29.7 9.2 %all-to-all-start = ((bf16[4,2,8192]{2,1,0:T(2,128)(2,1)}), bf16[4,2,8192]{2,1,0:T(2,128)(2,1)S(1)}, u32[]{:S(2)}, u32[]{:S(2)}) async-start(bf16[4,2,8192]{2,1,0:T(2,128)(2,1)} %reshape.76), calls=%async_computation | async-start | bytes 262144 | tf_op jit(solution)/shard_map/all_to_all | solution.py:184
  61.4 6.6 %collective-permute-start.2 = (bf16[8,8,8,4]{3,1,2,0:T(8,128)(2,1)S(1)}, bf16[8,8,8,4]{3,1,2,0:T(8,128)(2,1)S(1)}, u32[]{:S(2)}, u32[]{:S(2)}) collective-permute-start(bf16[8,8,8,4]{3,1,2,0:T(8,128)(2,1)S(1)} %get-tuple-element.26), channel_id=1, source_target_pairs={{0,8},{8,16},{16,24},{1,9},{9,17},{17,25},{2,10},{10,18},{18,26},{... | collective-permute-start | bytes 12296 | tf_op jit(solution)/shard_map/ppermute | solution.py:17
  64.9 6.3 %collective-permute-start.3 = (bf16[8,8,8,4]{3,1,2,0:T(8,128)(2,1)S(1)}, bf16[8,8,8,4]{3,1,2,0:T(8,128)(2,1)S(1)}, u32[]{:S(2)}, u32[]{:S(2)}) collective-permute-start(bf16[8,8,8,4]{3,1,2,0:T(8,128)(2,1)S(1)} %get-tuple-element.27), channel_id=1, source_target_pairs={{8,0},{16,8},{24,16},{9,1},{17,9},{25,17},{10,2},{18,10},{26,18},{... | collective-permute-start | bytes 12296 | tf_op jit(solution)/shard_map/ppermute | solution.py:20
  71.4 6.7 %collective-permute-start.4 = (bf16[8,8,4,136]{3,1,2,0:T(8,128)(2,1)S(1)}, bf16[8,8,4,136]{3,1,2,0:T(8,128)(2,1)S(1)}, u32[]{:S(2)}, u32[]{:S(2)}) collective-permute-start(bf16[8,8,4,136]{3,1,2,0:T(8,128)(2,1)S(1)} %get-tuple-element.22), channel_id=1, source_target_pairs={{0,1},{1,2},{2,3},{3,4},{4,5},{5,6},{6,7},{8,9},{9,10},{10,11},{11... | collective-permute-start | bytes 208904 | tf_op jit(solution)/shard_map/ppermute | solution.py:17
  73.7 6.7 %collective-permute-start.5 = (bf16[8,8,4,136]{3,1,2,0:T(8,128)(2,1)S(1)}, bf16[8,8,4,136]{3,1,2,0:T(8,128)(2,1)S(1)}, u32[]{:S(2)}, u32[]{:S(2)}) collective-permute-start(bf16[8,8,4,136]{3,1,2,0:T(8,128)(2,1)S(1)} %get-tuple-element.23), channel_id=1, source_target_pairs={{1,0},{2,1},{3,2},{4,3},{5,4},{6,5},{7,6},{9,8},{10,9},{11,10},{12... | collective-permute-start | bytes 208904 | tf_op jit(solution)/shard_map/ppermute | solution.py:20
  82.4 4.8 %collective-permute-start.6 = (bf16[8,8,8,4]{3,1,2,0:T(8,128)(2,1)S(1)}, bf16[8,8,8,4]{3,1,2,0:T(8,128)(2,1)S(1)}, u32[]{:S(2)}, u32[]{:S(2)}) collective-permute-start(bf16[8,8,8,4]{3,1,2,0:T(8,128)(2,1)S(1)} %get-tuple-element.24), channel_id=1, source_target_pairs={{0,8},{8,16},{16,24},{1,9},{9,17},{17,25},{2,10},{10,18},{18,26},{... | collective-permute-start | bytes 12296 | tf_op jit(solution)/shard_map/ppermute | solution.py:17
  85.1 6.3 %collective-permute-start.7 = (bf16[8,8,8,4]{3,1,2,0:T(8,128)(2,1)S(1)}, bf16[8,8,8,4]{3,1,2,0:T(8,128)(2,1)S(1)}, u32[]{:S(2)}, u32[]{:S(2)}) collective-permute-start(bf16[8,8,8,4]{3,1,2,0:T(8,128)(2,1)S(1)} %get-tuple-element.25), channel_id=1, source_target_pairs={{8,0},{16,8},{24,16},{9,1},{17,9},{25,17},{10,2},{18,10},{26,18},{... | collective-permute-start | bytes 12296 | tf_op jit(solution)/shard_map/ppermute | solution.py:20
  91.6 7.8 %collective-permute-start.8 = (bf16[8,8,4,136]{3,1,2,0:T(8,128)(2,1)S(1)}, bf16[8,8,4,136]{3,1,2,0:T(8,128)(2,1)S(1)}, u32[]{:S(2)}, u32[]{:S(2)}) collective-permute-start(bf16[8,8,4,136]{3,1,2,0:T(8,128)(2,1)S(1)} %get-tuple-element.20), channel_id=1, source_target_pairs={{0,1},{1,2},{2,3},{3,4},{4,5},{5,6},{6,7},{8,9},{9,10},{10,11},{11... | collective-permute-start | bytes 208904 | tf_op jit(solution)/shard_map/ppermute | solution.py:17
  96.1 5.7 %collective-permute-start.9 = (bf16[8,8,4,136]{3,1,2,0:T(8,128)(2,1)S(1)}, bf16[8,8,4,136]{3,1,2,0:T(8,128)(2,1)S(1)}, u32[]{:S(2)}, u32[]{:S(2)}) collective-permute-start(bf16[8,8,4,136]{3,1,2,0:T(8,128)(2,1)S(1)} %get-tuple-element.21), channel_id=1, source_target_pairs={{1,0},{2,1},{3,2},{4,3},{5,4},{6,5},{7,6},{9,8},{10,9},{11,10},{12... | collective-permute-start | bytes 208904 | tf_op jit(solution)/shard_map/ppermute | solution.py:20
  102.7 0.9 copy-start

commit v2 on v1

--- a/solution.py
+++ b/solution.py
@@ -200,9 +200,15 @@
     step_result = step_result.reshape(tile_rows, feat, members, tile_cols)
     features = jnp.transpose(step_result, (2, 1, 0, 3))
     tile_cols = features.shape[3]
-    padded_feature = padded(features, (("mem", 3), ("row", 2)), DILATION_SPAN)
-    interior_cells = jax.nn.silu(convolve(padded_feature, first_kernel)).astype(jnp.bfloat16)
-    activated_output = padded(interior_cells, (("mem", 3), ("row", 2)), DILATION_SPAN)
+    span = DILATION_SPAN
+    padded_feature = padded(features, (("mem", 3), ("row", 2)), 2 * span)
+    first = jax.nn.silu(convolve(padded_feature, first_kernel))
+    row_ids = lax.axis_index("row") * tile_rows - span + jnp.arange(tile_rows + 2 * span)
+    col_ids = lax.axis_index("mem") * tile_cols - span + jnp.arange(tile_cols + 2 * span)
+    row_in = (row_ids >= 0) & (row_ids < lax.axis_size("row") * tile_rows)
+    col_in = (col_ids >= 0) & (col_ids < lax.axis_size("mem") * tile_cols)
+    inside = row_in[:, None] & col_in[None, :]
+    activated_output = jnp.where(inside[None, None], first, 0.0).astype(jnp.bfloat16)
     return (features.astype(jnp.float32) + convolve(activated_output, second_kernel)).astype(
         jnp.bfloat16
     )

time: 106 us -> 90.4 us (0.85)
  starting transfers between devices: 32.7 us -> 21.2 us
  waiting for transfers between devices: 26.5 us -> 23.3 us
    ppermute x5 -> x3, starting transfers between devices: 16.1 us -> 8.26 us  [padded(): lax.ppermute(lax.slice_in_dim(block, block.shape[dim] - width, None, axis...]
    ppermute x5 -> x3, waiting for transfers between devices: 15 us -> 7.54 us  [padded(): lax.ppermute(lax.slice_in_dim(block, 0, width, axis=dim), axis, backward)]
    ppermute x5 -> x3, starting transfers between devices: 12.8 us -> 9.12 us  [padded(): lax.ppermute(lax.slice_in_dim(block, 0, width, axis=dim), axis, backward)]
    all_to_all x1, waiting for transfers between devices: 0.01 us -> 3.59 us  [on_device(): lax.all_to_all(predicted_states, 'mem', split_axis=3, concat_axis=0, tile...]
    ppermute x5 -> x3, waiting for transfers between devices: 11.5 us -> 12.1 us  [padded(): lax.ppermute(lax.slice_in_dim(block, block.shape[dim] - width, None, axis...]
  transfers between devices with their start and end apart: 11 -> 7, of which waited for: 8 -> 6; matrix products, arithmetic and copies ran while one was open for 7% -> 6% of each run, Pallas kernels for 0% -> 0%
where the time goes in v2:
time: 90.4 us; the launch traced here: 89.8 us
  waiting for transfers between devices  23.3 us (26%)
  local copies, waits for them, and re-layouts  21.7 us (24%)
  starting transfers between devices  21.2 us (23%)
  Pallas kernels  12.9 us (14%)
  matrix products  5.36 us (6%)
  other arithmetic  4.94 us (5%)
    unnamed x40, local copies, waits for them, and re-layouts  13.1 us
    pallas_call x1, Pallas kernels, post_block(): pl.pallas_call(attention_kernel, grid=(row_count,), in_specs=[pl.BlockSpe...  12.9 us
    ppermute x3, waiting for transfers between devices, padded(): lax.ppermute(lax.slice_in_dim(block, block.shape[dim] - width, None, axis...  12.1 us
    ppermute x3, starting transfers between devices, padded(): lax.ppermute(lax.slice_in_dim(block, 0, width, axis=dim), axis, backward)  9.12 us
    ppermute x3, starting transfers between devices, padded(): lax.ppermute(lax.slice_in_dim(block, block.shape[dim] - width, None, axis...  8.26 us
    ppermute x3, waiting for transfers between devices, padded(): lax.ppermute(lax.slice_in_dim(block, 0, width, axis=dim), axis, backward)  7.54 us
    dot_general x18, matrix products, convolve(): jnp.einsum('oc,mcij->moij', kernel[row_stencil * 3 + column_stencil], shi...  5.36 us
    all_to_all x1, starting transfers between devices, on_device(): lax.all_to_all(predicted_states, 'mem', split_axis=3, concat_axis=0, tile...  3.79 us
  transfers between devices with their start and end apart: 7, of which 6 were waited for; matrix products, arithmetic and copies ran while one was open for 6% of the time, Pallas kernels for 0%

profile of v2, /device:TPU:9, one launch (start us, length us, event | category | flops | bytes accessed | tf_op | source)
XLA Modules:
  0.0 89.8 jit_solution(4645954242418742563)
XLA Ops:
  0.0 1.0 %copy.116 = f32[8,8,512]{2,0,1:T(8,128)S(1)} copy(f32[8,8,512]{2,1,0:T(8,128)} %param.15) | data formatting | bytes 262144 | tf_op args[3]
  1.0 1.1 %copy.41 = f32[2,8,8,512]{3,1,2,0:T(8,128)S(1)} copy(f32[2,8,8,512]{3,2,1,0:T(8,128)} %param.12) | data formatting | bytes 524288 | tf_op args[0]
  2.1 1.1 %fusion.58 = (f32[8,8,512]{2,0,1:T(8,128)S(1)}, f32[1,8,8,512]{3,1,2,0:T(8,128)S(1)}, f32[1,8,8,512]{3,1,2,0:T(8,128)S(1)}, f32[8,8,512]{2,0,1:T(8,128)S(1)}) fusion(f32[8,8,512]{2,1,0:T(8,128)} %param.13, f32[8,8,512]{2,1,0:T(8,128)} %param.14), kind=kLoop, calls=%fused_computation.107 | loop fusion | bytes 786432 | tf_op args[1]
  3.4 3.1 %collective-permute-start = (f32[5,8,4,512]{3,1,2,0:T(8,128)S(1)}, f32[5,8,4,512]{3,1,2,0:T(8,128)S(1)}, u32[]{:S(2)}, u32[]{:S(2)}) collective-permute-start(f32[5,8,4,512]{3,1,2,0:T(8,128)S(1)} %get-tuple-element.14), channel_id=1, source_target_pairs={{0,1},{1,2},{2,3},{3,4},{4,5},{5,6},{6,7},{8,9},{9,10},{10,11},{11... | collective-permute-start | bytes 983048 | tf_op jit(solution)/shard_map/ppermute | solution.py:17
  6.5 3.1 %collective-permute-start.1 = (f32[5,8,4,512]{3,1,2,0:T(8,128)S(1)}, f32[5,8,4,512]{3,1,2,0:T(8,128)S(1)}, u32[]{:S(2)}, u32[]{:S(2)}) collective-permute-start(f32[5,8,4,512]{3,1,2,0:T(8,128)S(1)} %get-tuple-element.15), channel_id=1, source_target_pairs={{1,0},{2,1},{3,2},{4,3},{5,4},{6,5},{7,6},{9,8},{10,9},{11,10},{12... | collective-permute-start | bytes 983048 | tf_op jit(solution)/shard_map/ppermute | solution.py:20
  9.7 0.7 copy.48
  10.4 0.7 copy.50.gain_ref
  11.1 0.7 copy.47
  11.8 0.7 copy.49
  12.7 7.2 %collective-permute-done = f32[5,8,4,512]{3,1,2,0:T(8,128)S(1)} collective-permute-done((f32[5,8,4,512]{3,1,2,0:T(8,128)S(1)}, f32[5,8,4,512]{3,1,2,0:T(8,128)S(1)}, u32[]{:S(2)}, u32[]{:S(2)}) %collective-permute-start) | collective-permute-done | bytes 327712 | tf_op jit(solution)/shard_map/ppermute | solution.py:17
  19.9 2.9 %collective-permute-done.1 = f32[5,8,4,512]{3,1,2,0:T(8,128)S(1)} collective-permute-done((f32[5,8,4,512]{3,1,2,0:T(8,128)S(1)}, f32[5,8,4,512]{3,1,2,0:T(8,128)S(1)}, u32[]{:S(2)}, u32[]{:S(2)}) %collective-permute-start.1) | collective-permute-done | bytes 327712 | tf_op jit(solution)/shard_map/ppermute | solution.py:20
  23.1 0.5 add_select_fusion
  23.7 0.4 add_select_fusion.1
  24.1 0.4 add_select_fusion.2
  24.5 0.3 select_convert_fusion.1
  24.8 2.0 %copy.45 = bf16[2,8,8,512]{2,1,0,3:T(8,128)(2,1)S(1)} copy(bf16[2,8,8,512]{3,1,2,0:T(8,128)(2,1)S(1)} %select_convert_fusion.1) | data formatting | bytes 262144 | tf_op jit(solution)/shard_map/convert_element_type | solution.py:183
  26.8 2.8 %reshape.117 = bf16[4,2,8192]{2,1,0:T(2,128)(2,1)} reshape(bf16[512,2,8,8]{3,2,1,0:T(8,128)(2,1)S(1)} %bitcast.186) | data formatting | bytes 262144
  29.7 3.8 %all-to-all-start = ((bf16[4,2,8192]{2,1,0:T(2,128)(2,1)}), bf16[4,2,8192]{2,1,0:T(2,128)(2,1)S(1)}, u32[]{:S(2)}, u32[]{:S(2)}) async-start(bf16[4,2,8192]{2,1,0:T(2,128)(2,1)} %reshape.117), calls=%async_computation | async-start | bytes 262144 | tf_op jit(solution)/shard_map/all_to_all | solution.py:184
  33.5 3.6 %all-to-all-done = bf16[4,2,8192]{2,1,0:T(2,128)(2,1)S(1)} async-done(((bf16[4,2,8192]{2,1,0:T(2,128)(2,1)}), bf16[4,2,8192]{2,1,0:T(2,128)(2,1)S(1)}, u32[]{:S(2)}, u32[]{:S(2)}) %all-to-all-start) | async-done | bytes 131104 | tf_op jit(solution)/shard_map/all_to_all | solution.py:184
  37.1 2.4 %reshape.118 = bf16[512,2,8,8]{3,2,1,0:T(8,128)(2,1)S(1)} reshape(bf16[4,2,8192]{2,1,0:T(2,128)(2,1)S(1)} %all-to-all-done) | data formatting | bytes 262144
  39.5 2.3 %convert_bitcast_fusion = f32[4,2,8,8,128]{3,2,1,4,0:T(8,128)} fusion(bf16[2,8,8,4,128]{2,1,0,4,3:T(8,128)(2,1)S(1)} %bitcast.185), kind=kLoop, calls=%fused_computation | loop fusion | flops 65536 | bytes 393216 | tf_op jit(solution)/shard_map/reshape | solution.py:189
  41.8 3.8 %copy.46 = f32[4,2,8,8,128]{4,2,1,0,3:T(8,128)} copy(f32[4,2,8,8,128]{3,2,1,4,0:T(8,128)} %convert_bitcast_fusion) | data formatting | bytes 524288 | tf_op jit(solution)/shard_map/reshape | solution.py:189
  45.6 12.9 %shard_map.118 = bf16[8,8,1024]{2,1,0:T(8,128)(2,1)} custom-call(f32[4]{0:T(128)} %hs_ref.1, f32[8,8,1024]{2,1,0:T(8,128)} %bitcast.189, bf16[64,8]{1,0:T(8,128)(2,1)} %bitcast.191, f32[64,1]{1,0:T(8,128)} %copy.50.gain_ref, bf16[192,64]{1,0:T(8,128)(2,1)} %bitcast.190, bf16[64,64]{1,0:T(8,128)(2,1)} %bitcast.192, bf16[8,64]{1,0:T(8,128)(2,1)} %bitcast.193), custom_call_target="tpu_custom_call" | custom-call | tf_op jit(solution)/shard_map/pallas_call | solution.py:104
  58.5 0.9 %copy_bitcast_fusion = bf16[8,8,8,128]{3,1,2,0:T(8,128)(2,1)S(1)} fusion(bf16[8,8,1024]{2,1,0:T(8,128)(2,1)} %shard_map.118), kind=kLoop, calls=%fused_computation.76 | loop fusion | bytes 262144 | tf_op jit(solution)/shard_map/transpose | solution.py:201
  59.5 2.9 %collective-permute-start.2 = (bf16[8,8,8,8]{3,1,2,0:T(8,128)(2,1)S(1)}, bf16[8,8,8,8]{3,1,2,0:T(8,128)(2,1)S(1)}, u32[]{:S(2)}, u32[]{:S(2)}) collective-permute-start(bf16[8,8,8,8]{3,1,2,0:T(8,128)(2,1)S(1)} %get-tuple-element.18), channel_id=1, source_target_pairs={{0,8},{8,16},{16,24},{1,9},{9,17},{17,25},{2,10},{10,18},{18,26},{... | collective-permute-start | bytes 24584 | tf_op jit(solution)/shard_map/ppermute | solution.py:17
  62.5 1.9 %collective-permute-start.3 = (bf16[8,8,8,8]{3,1,2,0:T(8,128)(2,1)S(1)}, bf16[8,8,8,8]{3,1,2,0:T(8,128)(2,1)S(1)}, u32[]{:S(2)}, u32[]{:S(2)}) collective-permute-start(bf16[8,8,8,8]{3,1,2,0:T(8,128)(2,1)S(1)} %get-tuple-element.19), channel_id=1, source_target_pairs={{8,0},{16,8},{24,16},{9,1},{17,9},{25,17},{10,2},{18,10},{26,18},{... | collective-permute-start | bytes 24584 | tf_op jit(solution)/shard_map/ppermute | solution.py:20
  65.1 0.1 copy.95
  65.2 0.1 copy.91
  65.3 0.1 copy.90
  65.5 0.1 copy.89
  65.6 0.1 copy.98
  65.7 0.1 copy.99
  65.9 0.1 copy.100
  66.0 0.1 copy.101
  66.1 0.1 copy.102
  66.3 0.1 copy.103
  66.6 0.1 copy.105
  66.8 1.9 %collective-permute-done.3 = bf16[8,8,8,8]{3,1,2,0:T(8,128)(2,1)S(1)} collective-permute-done((bf16[8,8,8,8]{3,1,2,0:T(8,128)(2,1)S(1)}, bf16[8,8,8,8]{3,1,2,0:T(8,128)(2,1)S(1)}, u32[]{:S(2)}, u32[]{:S(2)}) %collective-permute-start.3) | collective-permute-done | bytes 8224 | tf_op jit(solution)/shard_map/ppermute | solution.py:20
  68.8 0.2 pad_maximum_fusion.4
  68.9 2.2 %collective-permute-start.4 = (bf16[8,8,8,144]{3,1,2,0:T(8,128)(2,1)S(1)}, bf16[8,8,8,144]{3,1,2,0:T(8,128)(2,1)S(1)}, u32[]{:S(2)}, u32[]{:S(2)}) collective-permute-start(bf16[8,8,8,144]{3,1,2,0:T(8,128)(2,1)S(1)} %pad_maximum_fusion.4), channel_id=1, source_target_pairs={{0,1},{1,2},{2,3},{3,4},{4,5},{5,6},{6,7},{8,9},{9,10},{10,11},{11... | collective-permute-start | bytes 442376 | tf_op jit(solution)/shard_map/ppermute | solution.py:17
  71.2 4.1 %collective-permute-start.5 = (bf16[8,8,8,144]{3,1,2,0:T(8,128)(2,1)S(1)}, bf16[8,8,8,144]{3,1,2,0:T(8,128)(2,1)S(1)}, u32[]{:S(2)}, u32[]{:S(2)}) collective-permute-start(bf16[8,8,8,144]{3,1,2,0:T(8,128)(2,1)S(1)} %pad_maximum_fusion.4), channel_id=1, source_target_pairs={{1,0},{2,1},{3,2},{4,3},{5,4},{6,5},{7,6},{9,8},{10,9},{11,10},{12... | collective-permute-start | bytes 442376 | tf_op jit(solution)/shard_map/ppermute | solution.py:20
  75.4 4.9 %collective-permute-done.4 = bf16[8,8,8,144]{3,1,2,0:T(8,128)(2,1)S(1)} collective-permute-done((bf16[8,8,8,144]{3,1,2,0:T(8,128)(2,1)S(1)}, bf16[8,8,8,144]{3,1,2,0:T(8,128)(2,1)S(1)}, u32[]{:S(2)}, u32[]{:S(2)}) %collective-permute-start.4) | collective-permute-done | bytes 147488 | tf_op jit(solution)/shard_map/ppermute | solution.py:17
  80.3 2.7 %collective-permute-done.5 = bf16[8,8,8,144]{3,1,2,0:T(8,128)(2,1)S(1)} collective-permute-done((bf16[8,8,8,144]{3,1,2,0:T(8,128)(2,1)S(1)}, bf16[8,8,8,144]{3,1,2,0:T(8,128)(2,1)S(1)}, u32[]{:S(2)}, u32[]{:S(2)}) %collective-permute-start.5) | collective-permute-done | bytes 147488 | tf_op jit(solution)/shard_map/ppermute | solution.py:20
  83.0 0.2 pad_maximum_fusion.1
  83.3 0.4 fusion.19
  83.6 0.3 fusion.21
  83.9 0.3 fusion.17
  84.3 0.4 maximum_maximum_fusion
  84.6 0.3 fusion.11
  85.0 0.3 fusion.13
  85.4 0.3 fusion.15
  85.6 0.4 fusion.23
  86.0 0.4 fusion.25
  86.4 0.8 select_convert_fusion
  87.2 0.2 fusion.36
  87.4 0.2 convolution_add_fusion.8
  87.6 0.2 convolution_add_fusion.7
  87.8 0.2 convolution_add_fusion.6
  88.0 0.2 convolution_add_fusion.5
  88.2 0.2 convolution_add_fusion.4
  88.5 0.2 convolution_add_fusion.3
  88.7 0.2 convolution_add_fusion.2
  88.9 0.2 fusion.10
  89.1 0.7 copy.70
  (42 shorter events, 1.8 us)
Async XLA Ops:
  3.2 6.4 %copy-start.3 = (bf16[64,192]{1,0:T(8,128)(2,1)S(1)}, bf16[64,192]{1,0:T(8,128)(2,1)}, u32[]{:S(2)}) copy-start(bf16[64,192]{1,0:T(8,128)(2,1)} %param.18) | copy-start | bytes 73732
  3.2 7.2 %copy-start.6 = (f32[64]{0:T(128)S(1)}, f32[64]{0:T(128)}, u32[]{:S(2)}) copy-start(f32[64]{0:T(128)} %param.17) | copy-start | bytes 772
  3.2 7.9 %copy-start.5 = (bf16[8,64]{1,0:T(8,128)(2,1)S(1)}, bf16[8,64]{1,0:T(8,128)(2,1)}, u32[]{:S(2)}) copy-start(bf16[8,64]{1,0:T(8,128)(2,1)} %param.16) | copy-start | bytes 3076
  3.3 8.5 %copy-start.4 = (bf16[64,64]{1,0:T(8,128)(2,1)S(1)}, bf16[64,64]{1,0:T(8,128)(2,1)}, u32[]{:S(2)}) copy-start(bf16[64,64]{1,0:T(8,128)(2,1)} %param.20) | copy-start | bytes 24580
  3.3 9.2 %copy-start = (bf16[9,8,8]{0,2,1:T(8,128)(2,1)S(1)}, bf16[9,8,8]{0,2,1:T(8,128)(2,1)}, u32[]{:S(2)}) copy-start(bf16[9,8,8]{0,2,1:T(8,128)(2,1)} %param.22) | copy-start | bytes 3460
  3.3 9.3 %copy-start.1 = (bf16[9,8,8]{0,2,1:T(8,128)(2,1)S(1)}, bf16[9,8,8]{0,2,1:T(8,128)(2,1)}, u32[]{:S(2)}) copy-start(bf16[9,8,8]{0,2,1:T(8,128)(2,1)} %param.23) | copy-start | bytes 3460
  3.4 16.5 %collective-permute-start = (f32[5,8,4,512]{3,1,2,0:T(8,128)S(1)}, f32[5,8,4,512]{3,1,2,0:T(8,128)S(1)}, u32[]{:S(2)}, u32[]{:S(2)}) collective-permute-start(f32[5,8,4,512]{3,1,2,0:T(8,128)S(1)} %get-tuple-element.14), channel_id=1, source_target_pairs={{0,1},{1,2},{2,3},{3,4},{4,5},{5,6},{6,7},{8,9},{9,10},{10,11},{11... | collective-permute-start | bytes 983048 | tf_op jit(solution)/shard_map/ppermute | solution.py:17
  6.5 16.3 %collective-permute-start.1 = (f32[5,8,4,512]{3,1,2,0:T(8,128)S(1)}, f32[5,8,4,512]{3,1,2,0:T(8,128)S(1)}, u32[]{:S(2)}, u32[]{:S(2)}) collective-permute-start(f32[5,8,4,512]{3,1,2,0:T(8,128)S(1)} %get-tuple-element.15), channel_id=1, source_target_pairs={{1,0},{2,1},{3,2},{4,3},{5,4},{6,5},{7,6},{9,8},{10,9},{11,10},{12... | collective-permute-start | bytes 983048 | tf_op jit(solution)/shard_map/ppermute | solution.py:20
  29.7 7.4 %all-to-all-start = ((bf16[4,2,8192]{2,1,0:T(2,128)(2,1)}), bf16[4,2,8192]{2,1,0:T(2,128)(2,1)S(1)}, u32[]{:S(2)}, u32[]{:S(2)}) async-start(bf16[4,2,8192]{2,1,0:T(2,128)(2,1)} %reshape.117), calls=%async_computation | async-start | bytes 262144 | tf_op jit(solution)/shard_map/all_to_all | solution.py:184
  59.5 7.3 %collective-permute-start.2 = (bf16[8,8,8,8]{3,1,2,0:T(8,128)(2,1)S(1)}, bf16[8,8,8,8]{3,1,2,0:T(8,128)(2,1)S(1)}, u32[]{:S(2)}, u32[]{:S(2)}) collective-permute-start(bf16[8,8,8,8]{3,1,2,0:T(8,128)(2,1)S(1)} %get-tuple-element.18), channel_id=1, source_target_pairs={{0,8},{8,16},{16,24},{1,9},{9,17},{17,25},{2,10},{10,18},{18,26},{... | collective-permute-start | bytes 24584 | tf_op jit(solution)/shard_map/ppermute | solution.py:17
  62.5 6.3 %collective-permute-start.3 = (bf16[8,8,8,8]{3,1,2,0:T(8,128)(2,1)S(1)}, bf16[8,8,8,8]{3,1,2,0:T(8,128)(2,1)S(1)}, u32[]{:S(2)}, u32[]{:S(2)}) collective-permute-start(bf16[8,8,8,8]{3,1,2,0:T(8,128)(2,1)S(1)} %get-tuple-element.19), channel_id=1, source_target_pairs={{8,0},{16,8},{24,16},{9,1},{17,9},{25,17},{10,2},{18,10},{26,18},{... | collective-permute-start | bytes 24584 | tf_op jit(solution)/shard_map/ppermute | solution.py:20
  68.9 11.4 %collective-permute-start.4 = (bf16[8,8,8,144]{3,1,2,0:T(8,128)(2,1)S(1)}, bf16[8,8,8,144]{3,1,2,0:T(8,128)(2,1)S(1)}, u32[]{:S(2)}, u32[]{:S(2)}) collective-permute-start(bf16[8,8,8,144]{3,1,2,0:T(8,128)(2,1)S(1)} %pad_maximum_fusion.4), channel_id=1, source_target_pairs={{0,1},{1,2},{2,3},{3,4},{4,5},{5,6},{6,7},{8,9},{9,10},{10,11},{11... | collective-permute-start | bytes 442376 | tf_op jit(solution)/shard_map/ppermute | solution.py:17
  71.2 11.9 %collective-permute-start.5 = (bf16[8,8,8,144]{3,1,2,0:T(8,128)(2,1)S(1)}, bf16[8,8,8,144]{3,1,2,0:T(8,128)(2,1)S(1)}, u32[]{:S(2)}, u32[]{:S(2)}) collective-permute-start(bf16[8,8,8,144]{3,1,2,0:T(8,128)(2,1)S(1)} %pad_maximum_fusion.4), channel_id=1, source_target_pairs={{1,0},{2,1},{3,2},{4,3},{5,4},{6,5},{7,6},{9,8},{10,9},{11,10},{12... | collective-permute-start | bytes 442376 | tf_op jit(solution)/shard_map/ppermute | solution.py:20
  88.0 0.9 %copy-start.2 = (bf16[8,8,1024]{2,1,0:T(8,128)(2,1)S(1)}, bf16[8,8,1024]{2,1,0:T(8,128)(2,1)}, u32[]{:S(2)}) copy-start(bf16[8,8,1024]{2,1,0:T(8,128)(2,1)} %shard_map.118) | copy-start | bytes 393220

commit v3 on v2

--- a/solution.py
+++ b/solution.py
@@ -1,3 +1,5 @@
+import functools
+
 import jax
 import jax.numpy as jnp
 from jax import lax
@@ -41,15 +43,14 @@
 
 
 def attention_kernel(
-    hs_ref, x_ref, w1_ref, gain_ref, pw_ref, ow_ref, rw_ref, out_ref
+    hs_ref, x_ref, w1_ref, gain_ref, pw_ref, ow_ref, rw_ref, out_ref, *, chunk
 ):
     width = w1_ref.shape[0]
     heads = hs_ref.shape[0]
     head_size = width // heads
-    lanes = x_ref.shape[2]
-    chunk = 128
-    members = lanes // chunk
-    layers = x_ref[0].astype(jnp.bfloat16)
+    sources = x_ref.shape[0]
+    layers = jnp.concatenate([x_ref[s, 0] for s in range(sources)], axis=1)
+    members = layers.shape[1] // chunk
     embedded = jnp.dot(w1_ref[...], layers, preferred_element_type=jnp.float32)
     meansq = jnp.sum(embedded * embedded, axis=0, keepdims=True) * (1.0 / width)
     normed = (embedded * lax.rsqrt(meansq + 1e-05) * gain_ref[...]).astype(jnp.bfloat16)
@@ -89,7 +90,8 @@
 
 
 def post_block(
-    rows_first,
+    by_source,
+    chunk,
     embed_weight,
     norm_gain,
     project_weight,
@@ -97,16 +99,17 @@
     output_weight,
     readout_weight,
 ):
-    row_count, levels_count, lanes = rows_first.shape
+    sources, row_count, levels_count, source_lanes = by_source.shape
+    lanes = sources * source_lanes
     width = embed_weight.shape[1]
     feat = readout_weight.shape[1]
     full = lambda r: (0, 0)
     return pl.pallas_call(
-        attention_kernel,
+        functools.partial(attention_kernel, chunk=chunk),
         grid=(row_count,),
         in_specs=[
             pl.BlockSpec(memory_space=pltpu.SMEM),
-            pl.BlockSpec((1, levels_count, lanes), lambda r: (r, 0, 0)),
+            pl.BlockSpec((sources, 1, levels_count, source_lanes), lambda r: (0, r, 0, 0)),
             pl.BlockSpec((width, levels_count), full),
             pl.BlockSpec((width, 1), full),
             pl.BlockSpec((3 * width, width), full),
@@ -117,7 +120,7 @@
         out_shape=jax.ShapeDtypeStruct((row_count, feat, lanes), jnp.bfloat16),
     )(
         head_scale,
-        rows_first,
+        by_source,
         embed_weight.T,
         norm_gain.reshape(width, 1),
         project_weight.T,
@@ -181,14 +184,18 @@
         inside = (row_ids >= 0) & (row_ids < all_rows)
         gridded_quantity_list = jnp.where(inside[None, None, :, None], gridded_quantity_list, 0.0)
     predicted_states = gridded_quantity_list.astype(jnp.bfloat16)
-    blockwise_quantity = lax.all_to_all(
-        predicted_states, "mem", split_axis=3, concat_axis=0, tiled=True
-    )
-    members, levels_count, tile_rows, tile_cols = blockwise_quantity.shape
-    rows_first = jnp.transpose(blockwise_quantity, (2, 1, 0, 3)).astype(jnp.float32)
-    rows_first = rows_first.reshape(tile_rows, levels_count, members * tile_cols)
+    chunks = lax.axis_size("mem")
+    _, levels_count, tile_rows, cols_all = predicted_states.shape
+    tile_cols = cols_all // chunks
+    by_chunk = predicted_states.reshape(members_here, levels_count, tile_rows, chunks, tile_cols)
+    by_chunk = jnp.transpose(by_chunk, (3, 2, 1, 0, 4)).reshape(
+        chunks, tile_rows, levels_count, members_here * tile_cols
+    )
+    by_source = lax.all_to_all(by_chunk, "mem", split_axis=0, concat_axis=0, tiled=True)
+    members = chunks * members_here
     step_result = post_block(
-        rows_first,
+        by_source,
+        tile_cols,
         embed_weight,
         norm_gain,
         project_weight,

time: 90.4 us -> 78.3 us (0.87)
  local copies, waits for them, and re-layouts: 21.7 us -> 11.3 us
  other arithmetic: 4.94 us -> 3.27 us
    unnamed x40, local copies, waits for them, and re-layouts: 13.1 us -> 8.44 us
    reshape x1 -> x0, local copies, waits for them, and re-layouts: 3.75 us -> none  [on_device(): rows_first.reshape(tile_rows, levels_count, members * tile_cols)]
    convert_element_type x1 -> x0, local copies, waits for them, and re-layouts: 2.01 us -> none  [on_device(): predicted_states = gridded_quantity_list.astype(jnp.bfloat16)]
    reshape x1, other arithmetic: 2.3 us -> 0.93 us  [on_device(): jnp.transpose(by_chunk, (3, 2, 1, 0, 4))]
  transfers between devices with their start and end apart: 7 -> 7, of which waited for: 6 -> 6; matrix products, arithmetic and copies ran while one was open for 6% -> 7% of each run, Pallas kernels for 0% -> 0%
where the time goes in v3:
time: 78.3 us; the launch traced here: 77.8 us
  waiting for transfers between devices  23.5 us (30%)
  starting transfers between devices  21 us (27%)
  Pallas kernels  13 us (17%)
  local copies, waits for them, and re-layouts  11.3 us (14%)
  matrix products  5.36 us (7%)
  other arithmetic  3.27 us (4%)
    pallas_call x1, Pallas kernels, post_block(): pl.pallas_call(functools.partial(attention_kernel, chunk=chunk), grid=(ro...  13 us
    ppermute x3, waiting for transfers between devices, padded(): lax.ppermute(lax.slice_in_dim(block, block.shape[dim] - width, None, axis...  12.3 us
    ppermute x3, starting transfers between devices, padded(): lax.ppermute(lax.slice_in_dim(block, 0, width, axis=dim), axis, backward)  8.93 us
    unnamed x40, local copies, waits for them, and re-layouts  8.44 us
    ppermute x3, starting transfers between devices, padded(): lax.ppermute(lax.slice_in_dim(block, block.shape[dim] - width, None, axis...  8.27 us
    ppermute x3, waiting for transfers between devices, padded(): lax.ppermute(lax.slice_in_dim(block, 0, width, axis=dim), axis, backward)  7.54 us
    dot_general x18, matrix products, convolve(): jnp.einsum('oc,mcij->moij', kernel[row_stencil * 3 + column_stencil], shi...  5.36 us
    all_to_all x1, starting transfers between devices, on_device(): lax.all_to_all(by_chunk, 'mem', split_axis=0, concat_axis=0, tiled=True)  3.79 us
  transfers between devices with their start and end apart: 7, of which 6 were waited for; matrix products, arithmetic and copies ran while one was open for 7% of the time, Pallas kernels for 0%

profile of v3, /device:TPU:9, one launch (start us, length us, event | category | flops | bytes accessed | tf_op | source)
XLA Modules:
  0.0 77.8 jit_solution(156277045685577884)
XLA Ops:
  0.0 1.0 %copy.116 = f32[8,8,512]{2,0,1:T(8,128)S(1)} copy(f32[8,8,512]{2,1,0:T(8,128)} %param.15) | data formatting | bytes 262144 | tf_op args[3]
  1.0 1.1 %copy.41 = f32[2,8,8,512]{3,1,2,0:T(8,128)S(1)} copy(f32[2,8,8,512]{3,2,1,0:T(8,128)} %param.12) | data formatting | bytes 524288 | tf_op args[0]
  2.1 1.1 %fusion.59 = (f32[8,8,512]{2,0,1:T(8,128)S(1)}, f32[1,8,8,512]{3,1,2,0:T(8,128)S(1)}, f32[1,8,8,512]{3,1,2,0:T(8,128)S(1)}, f32[8,8,512]{2,0,1:T(8,128)S(1)}) fusion(f32[8,8,512]{2,1,0:T(8,128)} %param.13, f32[8,8,512]{2,1,0:T(8,128)} %param.14), kind=kLoop, calls=%fused_computation.108 | loop fusion | bytes 786432 | tf_op args[1]
  3.4 3.1 %collective-permute-start = (f32[5,8,4,512]{3,1,2,0:T(8,128)S(1)}, f32[5,8,4,512]{3,1,2,0:T(8,128)S(1)}, u32[]{:S(2)}, u32[]{:S(2)}) collective-permute-start(f32[5,8,4,512]{3,1,2,0:T(8,128)S(1)} %get-tuple-element.14), channel_id=1, source_target_pairs={{0,1},{1,2},{2,3},{3,4},{4,5},{5,6},{6,7},{8,9},{9,10},{10,11},{11... | collective-permute-start | bytes 983048 | tf_op jit(solution)/shard_map/ppermute | solution.py:19
  6.5 3.1 %collective-permute-start.1 = (f32[5,8,4,512]{3,1,2,0:T(8,128)S(1)}, f32[5,8,4,512]{3,1,2,0:T(8,128)S(1)}, u32[]{:S(2)}, u32[]{:S(2)}) collective-permute-start(f32[5,8,4,512]{3,1,2,0:T(8,128)S(1)} %get-tuple-element.15), channel_id=1, source_target_pairs={{1,0},{2,1},{3,2},{4,3},{5,4},{6,5},{7,6},{9,8},{10,9},{11,10},{12... | collective-permute-start | bytes 983048 | tf_op jit(solution)/shard_map/ppermute | solution.py:22
  9.7 0.7 copy.47
  10.4 0.7 copy.49.gain_ref
  11.1 0.7 copy.46
  11.8 0.7 copy.48
  12.7 7.2 %collective-permute-done = f32[5,8,4,512]{3,1,2,0:T(8,128)S(1)} collective-permute-done((f32[5,8,4,512]{3,1,2,0:T(8,128)S(1)}, f32[5,8,4,512]{3,1,2,0:T(8,128)S(1)}, u32[]{:S(2)}, u32[]{:S(2)}) %collective-permute-start) | collective-permute-done | bytes 327712 | tf_op jit(solution)/shard_map/ppermute | solution.py:19
  19.9 2.9 %collective-permute-done.1 = f32[5,8,4,512]{3,1,2,0:T(8,128)S(1)} collective-permute-done((f32[5,8,4,512]{3,1,2,0:T(8,128)S(1)}, f32[5,8,4,512]{3,1,2,0:T(8,128)S(1)}, u32[]{:S(2)}, u32[]{:S(2)}) %collective-permute-start.1) | collective-permute-done | bytes 327712 | tf_op jit(solution)/shard_map/ppermute | solution.py:22
  23.1 0.5 add_select_fusion
  23.7 0.4 add_select_fusion.1
  24.1 0.4 add_select_fusion.2
  24.5 0.9 %copy_bitcast_fusion.1 = bf16[4,8,8,256]{3,2,1,0:T(8,128)(2,1)} fusion(f32[2,8,8,512]{3,1,2,0:T(8,128)S(1)} %slice.333, f32[8,8,512]{2,0,1:T(8,128)S(1)} %copy.116, f32[2,8,10,512]{3,1,2,0:T(8,128)S(1)} %add_select_fusion.2, f32[8,8,512]{2,0,1:T(8,128)S(1)} %get-tuple-element.45, f32[8,8,512]{2,0,1:T(8,128)S(1)} %get-tuple-element.20, ...), kind=kLoop, calls=%fused_computation.76 | loop fusion | flops 1310720 | bytes 1311232 | tf_op jit(solution)/shard_map/reshape | solution.py:191
  25.5 3.8 %all-to-all-start = ((bf16[4,8,8,256]{3,2,1,0:T(8,128)(2,1)}), bf16[4,8,8,256]{3,2,1,0:T(8,128)(2,1)S(1)}, u32[]{:S(2)}, u32[]{:S(2)}) async-start(bf16[4,8,8,256]{3,2,1,0:T(8,128)(2,1)} %copy_bitcast_fusion.1), calls=%async_computation | async-start | bytes 262144 | tf_op jit(solution)/shard_map/all_to_all | solution.py:194
  29.2 3.6 %all-to-all-done.x_ref = bf16[4,8,8,256]{3,2,1,0:T(8,128)(2,1)S(1)} async-done(((bf16[4,8,8,256]{3,2,1,0:T(8,128)(2,1)}), bf16[4,8,8,256]{3,2,1,0:T(8,128)(2,1)S(1)}, u32[]{:S(2)}, u32[]{:S(2)}) %all-to-all-start) | async-done | bytes 131104 | tf_op jit(solution)/shard_map/all_to_all | solution.py:194
  32.8 0.7 copy-done.3
  33.5 13.0 %shard_map.118 = bf16[8,8,1024]{2,1,0:T(8,128)(2,1)} custom-call(f32[4]{0:T(128)} %hs_ref.1, bf16[4,8,8,256]{3,2,1,0:T(8,128)(2,1)} %copy-done.3, bf16[64,8]{1,0:T(8,128)(2,1)} %bitcast.184, f32[64,1]{1,0:T(8,128)} %copy.49.gain_ref, bf16[192,64]{1,0:T(8,128)(2,1)} %bitcast.183, bf16[64,64]{1,0:T(8,128)(2,1)} %bitcast.185, bf16[8,64]{1,0:T(8,128)(2,1)} %bitcast.186), custom_call_target="tpu_custom_call" | custom-call | tf_op jit(solution)/shard_map/pallas_call | solution.py:107
  46.5 0.9 %copy_bitcast_fusion = bf16[8,8,8,128]{3,1,2,0:T(8,128)(2,1)S(1)} fusion(bf16[8,8,1024]{2,1,0:T(8,128)(2,1)} %shard_map.118), kind=kLoop, calls=%fused_computation.75 | loop fusion | bytes 262144 | tf_op jit(solution)/shard_map/transpose | solution.py:208
  47.5 2.9 %collective-permute-start.2 = (bf16[8,8,8,8]{3,1,2,0:T(8,128)(2,1)S(1)}, bf16[8,8,8,8]{3,1,2,0:T(8,128)(2,1)S(1)}, u32[]{:S(2)}, u32[]{:S(2)}) collective-permute-start(bf16[8,8,8,8]{3,1,2,0:T(8,128)(2,1)S(1)} %get-tuple-element.18), channel_id=1, source_target_pairs={{0,8},{8,16},{16,24},{1,9},{9,17},{17,25},{2,10},{10,18},{18,26},{... | collective-permute-start | bytes 24584 | tf_op jit(solution)/shard_map/ppermute | solution.py:19
  50.4 1.9 %collective-permute-start.3 = (bf16[8,8,8,8]{3,1,2,0:T(8,128)(2,1)S(1)}, bf16[8,8,8,8]{3,1,2,0:T(8,128)(2,1)S(1)}, u32[]{:S(2)}, u32[]{:S(2)}) collective-permute-start(bf16[8,8,8,8]{3,1,2,0:T(8,128)(2,1)S(1)} %get-tuple-element.19), channel_id=1, source_target_pairs={{8,0},{16,8},{24,16},{9,1},{17,9},{25,17},{10,2},{18,10},{26,18},{... | collective-permute-start | bytes 24584 | tf_op jit(solution)/shard_map/ppermute | solution.py:22
  52.4 0.1 copy.92
  52.9 0.1 copy.95
  53.0 0.1 copy.94
  53.2 0.1 copy.90
  53.3 0.1 copy.89
  53.4 0.1 copy.88
  53.6 0.1 copy.97
  53.7 0.1 copy.98
  53.9 0.1 copy.99
  54.0 0.1 copy.100
  54.1 0.1 copy.101
  54.3 0.1 copy.102
  54.4 0.1 copy.103
  54.5 0.1 copy.104
  54.7 0.1 copy.105
  54.8 1.9 %collective-permute-done.3 = bf16[8,8,8,8]{3,1,2,0:T(8,128)(2,1)S(1)} collective-permute-done((bf16[8,8,8,8]{3,1,2,0:T(8,128)(2,1)S(1)}, bf16[8,8,8,8]{3,1,2,0:T(8,128)(2,1)S(1)}, u32[]{:S(2)}, u32[]{:S(2)}) %collective-permute-start.3) | collective-permute-done | bytes 8224 | tf_op jit(solution)/shard_map/ppermute | solution.py:22
  56.7 0.2 pad_maximum_fusion.4
  56.9 2.2 %collective-permute-start.4 = (bf16[8,8,8,144]{3,1,2,0:T(8,128)(2,1)S(1)}, bf16[8,8,8,144]{3,1,2,0:T(8,128)(2,1)S(1)}, u32[]{:S(2)}, u32[]{:S(2)}) collective-permute-start(bf16[8,8,8,144]{3,1,2,0:T(8,128)(2,1)S(1)} %pad_maximum_fusion.4), channel_id=1, source_target_pairs={{0,1},{1,2},{2,3},{3,4},{4,5},{5,6},{6,7},{8,9},{9,10},{10,11},{11... | collective-permute-start | bytes 442376 | tf_op jit(solution)/shard_map/ppermute | solution.py:19
  59.2 3.9 %collective-permute-start.5 = (bf16[8,8,8,144]{3,1,2,0:T(8,128)(2,1)S(1)}, bf16[8,8,8,144]{3,1,2,0:T(8,128)(2,1)S(1)}, u32[]{:S(2)}, u32[]{:S(2)}) collective-permute-start(bf16[8,8,8,144]{3,1,2,0:T(8,128)(2,1)S(1)} %pad_maximum_fusion.4), channel_id=1, source_target_pairs={{1,0},{2,1},{3,2},{4,3},{5,4},{6,5},{7,6},{9,8},{10,9},{11,10},{12... | collective-permute-start | bytes 442376 | tf_op jit(solution)/shard_map/ppermute | solution.py:22
  63.2 5.1 %collective-permute-done.4 = bf16[8,8,8,144]{3,1,2,0:T(8,128)(2,1)S(1)} collective-permute-done((bf16[8,8,8,144]{3,1,2,0:T(8,128)(2,1)S(1)}, bf16[8,8,8,144]{3,1,2,0:T(8,128)(2,1)S(1)}, u32[]{:S(2)}, u32[]{:S(2)}) %collective-permute-start.4) | collective-permute-done | bytes 147488 | tf_op jit(solution)/shard_map/ppermute | solution.py:19
  68.3 2.7 %collective-permute-done.5 = bf16[8,8,8,144]{3,1,2,0:T(8,128)(2,1)S(1)} collective-permute-done((bf16[8,8,8,144]{3,1,2,0:T(8,128)(2,1)S(1)}, bf16[8,8,8,144]{3,1,2,0:T(8,128)(2,1)S(1)}, u32[]{:S(2)}, u32[]{:S(2)}) %collective-permute-start.5) | collective-permute-done | bytes 147488 | tf_op jit(solution)/shard_map/ppermute | solution.py:22
  71.0 0.2 pad_maximum_fusion.1
  71.2 0.4 fusion.19
  71.6 0.3 fusion.21
  71.9 0.4 fusion.17
  72.2 0.4 maximum_maximum_fusion
  72.6 0.3 fusion.11
  73.0 0.3 fusion.13
  73.3 0.3 fusion.15
  73.6 0.4 fusion.23
  74.0 0.4 fusion.25
  74.3 0.8 %select_convert_fusion = bf16[8,8,16,136]{3,1,2,0:T(8,128)(2,1)S(1)} fusion(f32[8,16,136,8]{2,3,1,0:T(8,128)S(1)} %fusion.11, f32[8,16,136,8]{2,3,1,0:T(8,128)S(1)} %fusion.13, f32[8,16,136,8]{2,3,1,0:T(8,128)S(1)} %fusion.15, f32[8,16,136,8]{2,3,1,0:T(8,128)S(1)} %fusion.17, f32[8,16,136,8]{2,3,1,0:T(8,128)S(1)} %fusion.19, ...), kind=kOutput, calls=%fused_computation.21 | convolution fusion | flops 4177920 | bytes 5032192 | tf_op jit(solution)/shard_map/oc,mcij->moij/dot_general | solution.py:146
  75.2 0.2 fusion.36
  75.3 0.2 convolution_add_fusion.8
  75.6 0.2 convolution_add_fusion.7
  75.8 0.2 convolution_add_fusion.6
  76.0 0.2 convolution_add_fusion.5
  76.2 0.2 convolution_add_fusion.4
  76.5 0.2 convolution_add_fusion.3
  76.6 0.2 convolution_add_fusion.2
  76.9 0.2 fusion.10
  77.1 0.7 copy.69
  (39 shorter events, 1.3 us)
Async XLA Ops:
  3.2 6.4 %copy-start.4 = (bf16[64,192]{1,0:T(8,128)(2,1)S(1)}, bf16[64,192]{1,0:T(8,128)(2,1)}, u32[]{:S(2)}) copy-start(bf16[64,192]{1,0:T(8,128)(2,1)} %param.18) | copy-start | bytes 73732
  3.2 7.2 %copy-start.7 = (f32[64]{0:T(128)S(1)}, f32[64]{0:T(128)}, u32[]{:S(2)}) copy-start(f32[64]{0:T(128)} %param.17) | copy-start | bytes 772
  3.2 7.9 %copy-start.6 = (bf16[8,64]{1,0:T(8,128)(2,1)S(1)}, bf16[8,64]{1,0:T(8,128)(2,1)}, u32[]{:S(2)}) copy-start(bf16[8,64]{1,0:T(8,128)(2,1)} %param.16) | copy-start | bytes 3076
  3.3 8.5 %copy-start.5 = (bf16[64,64]{1,0:T(8,128)(2,1)S(1)}, bf16[64,64]{1,0:T(8,128)(2,1)}, u32[]{:S(2)}) copy-start(bf16[64,64]{1,0:T(8,128)(2,1)} %param.20) | copy-start | bytes 24580
  3.3 9.2 %copy-start = (bf16[9,8,8]{0,2,1:T(8,128)(2,1)S(1)}, bf16[9,8,8]{0,2,1:T(8,128)(2,1)}, u32[]{:S(2)}) copy-start(bf16[9,8,8]{0,2,1:T(8,128)(2,1)} %param.22) | copy-start | bytes 3460
  3.3 9.3 %copy-start.1 = (bf16[9,8,8]{0,2,1:T(8,128)(2,1)S(1)}, bf16[9,8,8]{0,2,1:T(8,128)(2,1)}, u32[]{:S(2)}) copy-start(bf16[9,8,8]{0,2,1:T(8,128)(2,1)} %param.23) | copy-start | bytes 3460
  3.4 16.5 %collective-permute-start = (f32[5,8,4,512]{3,1,2,0:T(8,128)S(1)}, f32[5,8,4,512]{3,1,2,0:T(8,128)S(1)}, u32[]{:S(2)}, u32[]{:S(2)}) collective-permute-start(f32[5,8,4,512]{3,1,2,0:T(8,128)S(1)} %get-tuple-element.14), channel_id=1, source_target_pairs={{0,1},{1,2},{2,3},{3,4},{4,5},{5,6},{6,7},{8,9},{9,10},{10,11},{11... | collective-permute-start | bytes 983048 | tf_op jit(solution)/shard_map/ppermute | solution.py:19
  6.5 16.3 %collective-permute-start.1 = (f32[5,8,4,512]{3,1,2,0:T(8,128)S(1)}, f32[5,8,4,512]{3,1,2,0:T(8,128)S(1)}, u32[]{:S(2)}, u32[]{:S(2)}) collective-permute-start(f32[5,8,4,512]{3,1,2,0:T(8,128)S(1)} %get-tuple-element.15), channel_id=1, source_target_pairs={{1,0},{2,1},{3,2},{4,3},{5,4},{6,5},{7,6},{9,8},{10,9},{11,10},{12... | collective-permute-start | bytes 983048 | tf_op jit(solution)/shard_map/ppermute | solution.py:22
  25.5 7.4 %all-to-all-start = ((bf16[4,8,8,256]{3,2,1,0:T(8,128)(2,1)}), bf16[4,8,8,256]{3,2,1,0:T(8,128)(2,1)S(1)}, u32[]{:S(2)}, u32[]{:S(2)}) async-start(bf16[4,8,8,256]{3,2,1,0:T(8,128)(2,1)} %copy_bitcast_fusion.1), calls=%async_computation | async-start | bytes 262144 | tf_op jit(solution)/shard_map/all_to_all | solution.py:194
  32.8 0.7 copy-start.3
  47.5 7.3 %collective-permute-start.2 = (bf16[8,8,8,8]{3,1,2,0:T(8,128)(2,1)S(1)}, bf16[8,8,8,8]{3,1,2,0:T(8,128)(2,1)S(1)}, u32[]{:S(2)}, u32[]{:S(2)}) collective-permute-start(bf16[8,8,8,8]{3,1,2,0:T(8,128)(2,1)S(1)} %get-tuple-element.18), channel_id=1, source_target_pairs={{0,8},{8,16},{16,24},{1,9},{9,17},{17,25},{2,10},{10,18},{18,26},{... | collective-permute-start | bytes 24584 | tf_op jit(solution)/shard_map/ppermute | solution.py:19
  50.4 6.3 %collective-permute-start.3 = (bf16[8,8,8,8]{3,1,2,0:T(8,128)(2,1)S(1)}, bf16[8,8,8,8]{3,1,2,0:T(8,128)(2,1)S(1)}, u32[]{:S(2)}, u32[]{:S(2)}) collective-permute-start(bf16[8,8,8,8]{3,1,2,0:T(8,128)(2,1)S(1)} %get-tuple-element.19), channel_id=1, source_target_pairs={{8,0},{16,8},{24,16},{9,1},{17,9},{25,17},{10,2},{18,10},{26,18},{... | collective-permute-start | bytes 24584 | tf_op jit(solution)/shard_map/ppermute | solution.py:22
  56.9 11.4 %collective-permute-start.4 = (bf16[8,8,8,144]{3,1,2,0:T(8,128)(2,1)S(1)}, bf16[8,8,8,144]{3,1,2,0:T(8,128)(2,1)S(1)}, u32[]{:S(2)}, u32[]{:S(2)}) collective-permute-start(bf16[8,8,8,144]{3,1,2,0:T(8,128)(2,1)S(1)} %pad_maximum_fusion.4), channel_id=1, source_target_pairs={{0,1},{1,2},{2,3},{3,4},{4,5},{5,6},{6,7},{8,9},{9,10},{10,11},{11... | collective-permute-start | bytes 442376 | tf_op jit(solution)/shard_map/ppermute | solution.py:19
  59.2 11.8 %collective-permute-start.5 = (bf16[8,8,8,144]{3,1,2,0:T(8,128)(2,1)S(1)}, bf16[8,8,8,144]{3,1,2,0:T(8,128)(2,1)S(1)}, u32[]{:S(2)}, u32[]{:S(2)}) collective-permute-start(bf16[8,8,8,144]{3,1,2,0:T(8,128)(2,1)S(1)} %pad_maximum_fusion.4), channel_id=1, source_target_pairs={{1,0},{2,1},{3,2},{4,3},{5,4},{6,5},{7,6},{9,8},{10,9},{11,10},{12... | collective-permute-start | bytes 442376 | tf_op jit(solution)/shard_map/ppermute | solution.py:22
  76.0 0.9 %copy-start.2 = (bf16[8,8,1024]{2,1,0:T(8,128)(2,1)S(1)}, bf16[8,8,1024]{2,1,0:T(8,128)(2,1)}, u32[]{:S(2)}) copy-start(bf16[8,8,1024]{2,1,0:T(8,128)(2,1)} %shard_map.118) | copy-start | bytes 393220

commit v4 on v3

--- a/solution.py
+++ b/solution.py
@@ -42,48 +42,52 @@
     )
 
 
+def head_sums(x, heads):
+    part = jnp.sum(x, axis=0)
+    shift = heads
+    while shift < part.shape[0]:
+        part = part + pltpu.roll(part, shift, 0)
+        shift *= 2
+    return part
+
+
 def attention_kernel(
-    hs_ref, x_ref, w1_ref, gain_ref, pw_ref, ow_ref, rw_ref, out_ref, *, chunk
+    hs_ref, x_ref, w1_ref, gain_ref, pw_ref, ow_ref, rw_ref, out_ref, *, chunk, heads
 ):
     width = w1_ref.shape[0]
-    heads = hs_ref.shape[0]
-    head_size = width // heads
     sources = x_ref.shape[0]
     layers = jnp.concatenate([x_ref[s, 0] for s in range(sources)], axis=1)
-    members = layers.shape[1] // chunk
+    lanes = layers.shape[1]
+    members = lanes // chunk
     embedded = jnp.dot(w1_ref[...], layers, preferred_element_type=jnp.float32)
     meansq = jnp.sum(embedded * embedded, axis=0, keepdims=True) * (1.0 / width)
     normed = (embedded * lax.rsqrt(meansq + 1e-05) * gain_ref[...]).astype(jnp.bfloat16)
     projected = jnp.dot(pw_ref[...], normed, preferred_element_type=jnp.float32)
-    mixed_heads = []
-    for h in range(heads):
-        q = projected[h * head_size : (h + 1) * head_size]
-        k = projected[width + h * head_size : width + (h + 1) * head_size]
-        v = projected[2 * width + h * head_size : 2 * width + (h + 1) * head_size]
-        v = v.astype(jnp.bfloat16).astype(jnp.float32)
-        q = (q * lax.rsqrt(jnp.sum(q * q, 0, keepdims=True) + 1.0)).astype(jnp.bfloat16)
-        k = (k * lax.rsqrt(jnp.sum(k * k, 0, keepdims=True) + 1.0)).astype(jnp.bfloat16)
-        q = q.astype(jnp.float32)
-        k = k.astype(jnp.float32)
-        scale = hs_ref[h]
-        weights = []
-        for n in range(members):
-            k_n = k[:, n * chunk : (n + 1) * chunk]
-            k_wide = jnp.concatenate([k_n] * members, axis=1)
-            score = jnp.sum(q * k_wide, axis=0, keepdims=True) * scale
-            weights.append(jnp.exp(score))
-        total = weights[0]
-        for n in range(1, members):
-            total = total + weights[n]
-        mixed = jnp.zeros(q.shape, jnp.float32)
-        for n in range(members):
-            prob = (weights[n] / total).astype(jnp.bfloat16).astype(jnp.float32)
-            v_n = v[:, n * chunk : (n + 1) * chunk]
-            v_wide = jnp.concatenate([v_n] * members, axis=1)
-            mixed = mixed + prob * v_wide
-        mixed_heads.append(mixed.astype(jnp.bfloat16))
-    mixed_all = jnp.concatenate(mixed_heads, axis=0)
-    attended = jnp.dot(ow_ref[...], mixed_all, preferred_element_type=jnp.float32)
+    sub = 8
+    tiles = width // sub
+    q = projected[:width].reshape(tiles, sub, lanes)
+    k = projected[width : 2 * width].reshape(tiles, sub, lanes)
+    v = projected[2 * width :].astype(jnp.bfloat16).astype(jnp.float32).reshape(tiles, sub, lanes)
+    q = (q * lax.rsqrt(head_sums(q * q, heads) + 1.0)).astype(jnp.bfloat16).astype(jnp.float32)
+    k = (k * lax.rsqrt(head_sums(k * k, heads) + 1.0)).astype(jnp.bfloat16).astype(jnp.float32)
+    scale = hs_ref[...]
+    weights = []
+    for n in range(members):
+        k_n = k[:, :, n * chunk : (n + 1) * chunk]
+        k_wide = jnp.concatenate([k_n] * members, axis=2)
+        weights.append(jnp.exp(head_sums(q * k_wide, heads) * scale))
+    total = weights[0]
+    for n in range(1, members):
+        total = total + weights[n]
+    inverse = 1.0 / total
+    mixed = jnp.zeros(q.shape, jnp.float32)
+    for n in range(members):
+        prob = (weights[n] * inverse).astype(jnp.bfloat16).astype(jnp.float32)
+        v_n = v[:, :, n * chunk : (n + 1) * chunk]
+        v_wide = jnp.concatenate([v_n] * members, axis=2)
+        mixed = mixed + prob[None] * v_wide
+    mixed = mixed.reshape(width, lanes).astype(jnp.bfloat16)
+    attended = jnp.dot(ow_ref[...], mixed, preferred_element_type=jnp.float32)
     residual = (embedded + attended).astype(jnp.bfloat16)
     features = jnp.dot(rw_ref[...], residual, preferred_element_type=jnp.float32)
     out_ref[0] = features.astype(out_ref.dtype)
@@ -103,12 +107,19 @@
     lanes = sources * source_lanes
     width = embed_weight.shape[1]
     feat = readout_weight.shape[1]
+    heads = head_scale.shape[0]
+    head_size = width // heads
+    sub = 8
+    order = jnp.arange(width).reshape(heads, head_size).T.reshape(width)
+    project_t = project_weight.T.reshape(3, width, width)[:, order].reshape(3 * width, width)
+    output_t = output_weight.T[:, order]
+    scale = jnp.tile(head_scale, sub // heads).reshape(sub, 1)
     full = lambda r: (0, 0)
     return pl.pallas_call(
-        functools.partial(attention_kernel, chunk=chunk),
+        functools.partial(attention_kernel, chunk=chunk, heads=heads),
         grid=(row_count,),
         in_specs=[
-            pl.BlockSpec(memory_space=pltpu.SMEM),
+            pl.BlockSpec((sub, 1), full),
             pl.BlockSpec((sources, 1, levels_count, source_lanes), lambda r: (0, r, 0, 0)),
             pl.BlockSpec((width, levels_count), full),
             pl.BlockSpec((width, 1), full),
@@ -119,12 +130,12 @@
         out_specs=pl.BlockSpec((1, feat, lanes), lambda r: (r, 0, 0)),
         out_shape=jax.ShapeDtypeStruct((row_count, feat, lanes), jnp.bfloat16),
     )(
-        head_scale,
+        scale,
         by_source,
         embed_weight.T,
         norm_gain.reshape(width, 1),
-        project_weight.T,
-        output_weight.T,
+        project_t,
+        output_t,
         readout_weight.T,
     )
 

time: 78.3 us -> 75.2 us (0.960)
  Pallas kernels: 13 us -> 9.79 us
  local copies, waits for them, and re-layouts: 11.3 us -> 13.5 us
  waiting for transfers between devices: 23.5 us -> 21.3 us
    pallas_call x1, Pallas kernels: 13 us -> 9.79 us  [post_block(): pl.pallas_call(functools.partial(attention_kernel, chunk=chunk, heads=hea...]
    gather x0 -> x4, local copies, waits for them, and re-layouts: none -> 2.61 us  [the longest x2 1.33 us: post_block(): output_t = output_weight.T[:, order]]
    ppermute x3, waiting for transfers between devices: 12.3 us -> 10.1 us  [padded(): lax.ppermute(lax.slice_in_dim(block, block.shape[dim] - width, None, axis...]
    unnamed x40 -> x41, local copies, waits for them, and re-layouts: 8.44 us -> 7.15 us
  transfers between devices with their start and end apart: 7 -> 7, of which waited for: 6 -> 6; matrix products, arithmetic and copies ran while one was open for 7% -> 10% of each run, Pallas kernels for 0% -> 0%
where the time goes in v4:
time: 75.2 us; the launch traced here: 74.6 us
  waiting for transfers between devices  21.3 us (28%)
  starting transfers between devices  21 us (28%)
  local copies, waits for them, and re-layouts  13.5 us (18%)
  Pallas kernels  9.79 us (13%)
  matrix products  5.36 us (7%)
  other arithmetic  3.29 us (4%)
    ppermute x3, waiting for transfers between devices, padded(): lax.ppermute(lax.slice_in_dim(block, block.shape[dim] - width, None, axis...  10.1 us
    pallas_call x1, Pallas kernels, post_block(): pl.pallas_call(functools.partial(attention_kernel, chunk=chunk, heads=hea...  9.79 us
    ppermute x3, starting transfers between devices, padded(): lax.ppermute(lax.slice_in_dim(block, 0, width, axis=dim), axis, backward)  8.94 us
    ppermute x3, starting transfers between devices, padded(): lax.ppermute(lax.slice_in_dim(block, block.shape[dim] - width, None, axis...  8.26 us
    ppermute x3, waiting for transfers between devices, padded(): lax.ppermute(lax.slice_in_dim(block, 0, width, axis=dim), axis, backward)  7.54 us
    unnamed x41, local copies, waits for them, and re-layouts  7.15 us
    dot_general x18, matrix products, convolve(): jnp.einsum('oc,mcij->moij', kernel[row_stencil * 3 + column_stencil], shi...  5.36 us
    all_to_all x1, starting transfers between devices, on_device(): lax.all_to_all(by_chunk, 'mem', split_axis=0, concat_axis=0, tiled=True)  3.79 us
  transfers between devices with their start and end apart: 7, of which 6 were waited for; matrix products, arithmetic and copies ran while one was open for 10% of the time, Pallas kernels for 0%

profile of v4, /device:TPU:9, one launch (start us, length us, event | category | flops | bytes accessed | tf_op | source)
XLA Modules:
  0.0 74.6 jit_solution(7467433563100435638)
XLA Ops:
  0.0 1.0 %copy.147 = f32[8,8,512]{2,0,1:T(8,128)S(1)} copy(f32[8,8,512]{2,1,0:T(8,128)} %param.15) | data formatting | bytes 262144 | tf_op args[3]
  1.0 1.1 %copy.69 = f32[2,8,8,512]{3,1,2,0:T(8,128)S(1)} copy(f32[2,8,8,512]{3,2,1,0:T(8,128)} %param.12) | data formatting | bytes 524288 | tf_op args[0]
  2.1 1.1 %fusion.60 = (f32[8,8,512]{2,0,1:T(8,128)S(1)}, f32[1,8,8,512]{3,1,2,0:T(8,128)S(1)}, f32[1,8,8,512]{3,1,2,0:T(8,128)S(1)}, f32[8,8,512]{2,0,1:T(8,128)S(1)}) fusion(f32[8,8,512]{2,1,0:T(8,128)} %param.13, f32[8,8,512]{2,1,0:T(8,128)} %param.14), kind=kLoop, calls=%fused_computation.114 | loop fusion | bytes 786432 | tf_op args[1]
  3.4 3.1 %collective-permute-start = (f32[5,8,4,512]{3,1,2,0:T(8,128)S(1)}, f32[5,8,4,512]{3,1,2,0:T(8,128)S(1)}, u32[]{:S(2)}, u32[]{:S(2)}) collective-permute-start(f32[5,8,4,512]{3,1,2,0:T(8,128)S(1)} %get-tuple-element.14), channel_id=1, source_target_pairs={{0,1},{1,2},{2,3},{3,4},{4,5},{5,6},{6,7},{8,9},{9,10},{10,11},{11... | collective-permute-start | bytes 983048 | tf_op jit(solution)/shard_map/ppermute | solution.py:19
  6.6 3.1 %collective-permute-start.1 = (f32[5,8,4,512]{3,1,2,0:T(8,128)S(1)}, f32[5,8,4,512]{3,1,2,0:T(8,128)S(1)}, u32[]{:S(2)}, u32[]{:S(2)}) collective-permute-start(f32[5,8,4,512]{3,1,2,0:T(8,128)S(1)} %get-tuple-element.15), channel_id=1, source_target_pairs={{1,0},{2,1},{3,2},{4,3},{5,4},{6,5},{7,6},{9,8},{10,9},{11,10},{12... | collective-permute-start | bytes 983048 | tf_op jit(solution)/shard_map/ppermute | solution.py:22
  10.0 0.7 gather_fusion
  10.6 0.6 copy.77
  11.3 0.6 gather_fusion.1
  11.9 0.7 copy.78
  12.6 0.7 copy.80.gain_ref
  13.3 0.7 copy.74
  14.0 0.7 reshape_tile.4.hs_ref
  14.9 5.0 %collective-permute-done = f32[5,8,4,512]{3,1,2,0:T(8,128)S(1)} collective-permute-done((f32[5,8,4,512]{3,1,2,0:T(8,128)S(1)}, f32[5,8,4,512]{3,1,2,0:T(8,128)S(1)}, u32[]{:S(2)}, u32[]{:S(2)}) %collective-permute-start) | collective-permute-done | bytes 327712 | tf_op jit(solution)/shard_map/ppermute | solution.py:19
  19.9 2.9 %collective-permute-done.1 = f32[5,8,4,512]{3,1,2,0:T(8,128)S(1)} collective-permute-done((f32[5,8,4,512]{3,1,2,0:T(8,128)S(1)}, f32[5,8,4,512]{3,1,2,0:T(8,128)S(1)}, u32[]{:S(2)}, u32[]{:S(2)}) %collective-permute-start.1) | collective-permute-done | bytes 327712 | tf_op jit(solution)/shard_map/ppermute | solution.py:22
  23.2 0.5 add_select_fusion
  23.7 0.4 add_select_fusion.1
  24.1 0.4 add_select_fusion.2
  24.5 0.9 %copy_bitcast_fusion.1 = bf16[4,8,8,256]{3,2,1,0:T(8,128)(2,1)} fusion(f32[2,8,8,512]{3,1,2,0:T(8,128)S(1)} %slice.337, f32[8,8,512]{2,0,1:T(8,128)S(1)} %copy.147, f32[2,8,10,512]{3,1,2,0:T(8,128)S(1)} %add_select_fusion.2, f32[8,8,512]{2,0,1:T(8,128)S(1)} %get-tuple-element.45, f32[8,8,512]{2,0,1:T(8,128)S(1)} %get-tuple-element.20, ...), kind=kLoop, calls=%fused_computation.78 | loop fusion | flops 1310720 | bytes 1311232 | tf_op jit(solution)/shard_map/reshape | solution.py:202
  25.5 3.8 %all-to-all-start = ((bf16[4,8,8,256]{3,2,1,0:T(8,128)(2,1)}), bf16[4,8,8,256]{3,2,1,0:T(8,128)(2,1)S(1)}, u32[]{:S(2)}, u32[]{:S(2)}) async-start(bf16[4,8,8,256]{3,2,1,0:T(8,128)(2,1)} %copy_bitcast_fusion.1), calls=%async_computation | async-start | bytes 262144 | tf_op jit(solution)/shard_map/all_to_all | solution.py:205
  29.3 3.6 %all-to-all-done.x_ref = bf16[4,8,8,256]{3,2,1,0:T(8,128)(2,1)S(1)} async-done(((bf16[4,8,8,256]{3,2,1,0:T(8,128)(2,1)}), bf16[4,8,8,256]{3,2,1,0:T(8,128)(2,1)S(1)}, u32[]{:S(2)}, u32[]{:S(2)}) %all-to-all-start) | async-done | bytes 131104 | tf_op jit(solution)/shard_map/all_to_all | solution.py:205
  32.9 0.7 copy-done.4
  33.5 9.8 %shard_map.118 = bf16[8,8,1024]{2,1,0:T(8,128)(2,1)} custom-call(f32[8,1]{1,0:T(8,128)} %reshape_tile.4.hs_ref, bf16[4,8,8,256]{3,2,1,0:T(8,128)(2,1)} %copy-done.4, bf16[64,8]{1,0:T(8,128)(2,1)} %bitcast.195, f32[64,1]{1,0:T(8,128)} %copy.80.gain_ref, bf16[192,64]{1,0:T(8,128)(2,1)} %bitcast.192, bf16[64,64]{1,0:T(8,128)(2,1)} %bitcast.194, ...), custom_call_target="tpu_custom_call" | custom-call | tf_op jit(solution)/shard_map/pallas_call | solution.py:118
  43.3 0.9 %copy_bitcast_fusion = bf16[8,8,8,128]{3,1,2,0:T(8,128)(2,1)S(1)} fusion(bf16[8,8,1024]{2,1,0:T(8,128)(2,1)} %shard_map.118), kind=kLoop, calls=%fused_computation.77 | loop fusion | bytes 262144 | tf_op jit(solution)/shard_map/transpose | solution.py:219
  44.3 2.9 %collective-permute-start.2 = (bf16[8,8,8,8]{3,1,2,0:T(8,128)(2,1)S(1)}, bf16[8,8,8,8]{3,1,2,0:T(8,128)(2,1)S(1)}, u32[]{:S(2)}, u32[]{:S(2)}) collective-permute-start(bf16[8,8,8,8]{3,1,2,0:T(8,128)(2,1)S(1)} %get-tuple-element.18), channel_id=1, source_target_pairs={{0,8},{8,16},{16,24},{1,9},{9,17},{17,25},{2,10},{10,18},{18,26},{... | collective-permute-start | bytes 24584 | tf_op jit(solution)/shard_map/ppermute | solution.py:19
  47.3 1.9 %collective-permute-start.3 = (bf16[8,8,8,8]{3,1,2,0:T(8,128)(2,1)S(1)}, bf16[8,8,8,8]{3,1,2,0:T(8,128)(2,1)S(1)}, u32[]{:S(2)}, u32[]{:S(2)}) collective-permute-start(bf16[8,8,8,8]{3,1,2,0:T(8,128)(2,1)S(1)} %get-tuple-element.19), channel_id=1, source_target_pairs={{8,0},{16,8},{24,16},{9,1},{17,9},{25,17},{10,2},{18,10},{26,18},{... | collective-permute-start | bytes 24584 | tf_op jit(solution)/shard_map/ppermute | solution.py:22
  49.9 0.1 copy.125
  50.0 0.1 copy.121
  50.1 0.1 copy.120
  50.3 0.1 copy.119
  50.4 0.1 copy.128
  50.5 0.1 copy.129
  50.7 0.1 copy.130
  50.8 0.1 copy.131
  51.0 0.1 copy.132
  51.1 0.1 copy.133
  51.2 0.1 copy.134
  51.5 0.1 copy.136
  51.6 1.9 %collective-permute-done.3 = bf16[8,8,8,8]{3,1,2,0:T(8,128)(2,1)S(1)} collective-permute-done((bf16[8,8,8,8]{3,1,2,0:T(8,128)(2,1)S(1)}, bf16[8,8,8,8]{3,1,2,0:T(8,128)(2,1)S(1)}, u32[]{:S(2)}, u32[]{:S(2)}) %collective-permute-start.3) | collective-permute-done | bytes 8224 | tf_op jit(solution)/shard_map/ppermute | solution.py:22
  53.6 0.2 pad_maximum_fusion.4
  53.7 2.2 %collective-permute-start.4 = (bf16[8,8,8,144]{3,1,2,0:T(8,128)(2,1)S(1)}, bf16[8,8,8,144]{3,1,2,0:T(8,128)(2,1)S(1)}, u32[]{:S(2)}, u32[]{:S(2)}) collective-permute-start(bf16[8,8,8,144]{3,1,2,0:T(8,128)(2,1)S(1)} %pad_maximum_fusion.4), channel_id=1, source_target_pairs={{0,1},{1,2},{2,3},{3,4},{4,5},{5,6},{6,7},{8,9},{9,10},{10,11},{11... | collective-permute-start | bytes 442376 | tf_op jit(solution)/shard_map/ppermute | solution.py:19
  56.0 4.0 %collective-permute-start.5 = (bf16[8,8,8,144]{3,1,2,0:T(8,128)(2,1)S(1)}, bf16[8,8,8,144]{3,1,2,0:T(8,128)(2,1)S(1)}, u32[]{:S(2)}, u32[]{:S(2)}) collective-permute-start(bf16[8,8,8,144]{3,1,2,0:T(8,128)(2,1)S(1)} %pad_maximum_fusion.4), channel_id=1, source_target_pairs={{1,0},{2,1},{3,2},{4,3},{5,4},{6,5},{7,6},{9,8},{10,9},{11,10},{12... | collective-permute-start | bytes 442376 | tf_op jit(solution)/shard_map/ppermute | solution.py:22
  60.0 5.1 %collective-permute-done.4 = bf16[8,8,8,144]{3,1,2,0:T(8,128)(2,1)S(1)} collective-permute-done((bf16[8,8,8,144]{3,1,2,0:T(8,128)(2,1)S(1)}, bf16[8,8,8,144]{3,1,2,0:T(8,128)(2,1)S(1)}, u32[]{:S(2)}, u32[]{:S(2)}) %collective-permute-start.4) | collective-permute-done | bytes 147488 | tf_op jit(solution)/shard_map/ppermute | solution.py:19
  65.1 2.7 %collective-permute-done.5 = bf16[8,8,8,144]{3,1,2,0:T(8,128)(2,1)S(1)} collective-permute-done((bf16[8,8,8,144]{3,1,2,0:T(8,128)(2,1)S(1)}, bf16[8,8,8,144]{3,1,2,0:T(8,128)(2,1)S(1)}, u32[]{:S(2)}, u32[]{:S(2)}) %collective-permute-start.5) | collective-permute-done | bytes 147488 | tf_op jit(solution)/shard_map/ppermute | solution.py:22
  67.8 0.2 pad_maximum_fusion.1
  68.1 0.4 fusion.19
  68.4 0.3 fusion.21
  68.7 0.4 fusion.17
  69.1 0.4 maximum_maximum_fusion
  69.5 0.3 fusion.11
  69.8 0.3 fusion.13
  70.2 0.3 fusion.15
  70.4 0.4 fusion.23
  70.8 0.4 fusion.25
  71.2 0.8 %select_convert_fusion = bf16[8,8,16,136]{3,1,2,0:T(8,128)(2,1)S(1)} fusion(f32[8,16,136,8]{2,3,1,0:T(8,128)S(1)} %fusion.11, f32[8,16,136,8]{2,3,1,0:T(8,128)S(1)} %fusion.13, f32[8,16,136,8]{2,3,1,0:T(8,128)S(1)} %fusion.15, f32[8,16,136,8]{2,3,1,0:T(8,128)S(1)} %fusion.17, f32[8,16,136,8]{2,3,1,0:T(8,128)S(1)} %fusion.19, ...), kind=kOutput, calls=%fused_computation.23 | convolution fusion | flops 4177920 | bytes 5032192 | tf_op jit(solution)/shard_map/oc,mcij->moij/dot_general | solution.py:157
  72.0 0.2 fusion.36
  72.2 0.2 convolution_add_fusion.8
  72.4 0.2 convolution_add_fusion.7
  72.6 0.2 convolution_add_fusion.6
  72.8 0.2 convolution_add_fusion.5
  73.1 0.2 convolution_add_fusion.4
  73.3 0.2 convolution_add_fusion.3
  73.5 0.2 convolution_add_fusion.2
  73.7 0.2 fusion.10
  74.0 0.7 copy.100
  (51 shorter events, 2.0 us)
Async XLA Ops:
  0.0 11.3 %copy-start = (bf16[64,64]{1,0:T(8,128)(2,1)S(1)}, bf16[64,64]{1,0:T(8,128)(2,1)}, u32[]{:S(2)}) copy-start(bf16[64,64]{1,0:T(8,128)(2,1)} %param.20) | copy-start | bytes 24580
  3.2 6.6 %copy-start.5 = (bf16[64,192]{1,0:T(8,128)(2,1)S(1)}, bf16[64,192]{1,0:T(8,128)(2,1)}, u32[]{:S(2)}) copy-start(bf16[64,192]{1,0:T(8,128)(2,1)} %param.18) | copy-start | bytes 73732
  3.3 9.4 %copy-start.7 = (f32[64]{0:T(128)S(1)}, f32[64]{0:T(128)}, u32[]{:S(2)}) copy-start(f32[64]{0:T(128)} %param.17) | copy-start | bytes 772
  3.3 10.0 %copy-start.6 = (bf16[8,64]{1,0:T(8,128)(2,1)S(1)}, bf16[8,64]{1,0:T(8,128)(2,1)}, u32[]{:S(2)}) copy-start(bf16[8,64]{1,0:T(8,128)(2,1)} %param.16) | copy-start | bytes 3076
  3.3 10.7 %copy-start.8 = (f32[4]{0:T(128)S(1)}, f32[4]{0:T(128)}, u32[]{:S(2)}) copy-start(f32[4]{0:T(128)} %param.19) | copy-start | bytes 52
  3.4 11.3 %copy-start.1 = (bf16[9,8,8]{0,2,1:T(8,128)(2,1)S(1)}, bf16[9,8,8]{0,2,1:T(8,128)(2,1)}, u32[]{:S(2)}) copy-start(bf16[9,8,8]{0,2,1:T(8,128)(2,1)} %param.22) | copy-start | bytes 3460
  3.4 11.5 %copy-start.2 = (bf16[9,8,8]{0,2,1:T(8,128)(2,1)S(1)}, bf16[9,8,8]{0,2,1:T(8,128)(2,1)}, u32[]{:S(2)}) copy-start(bf16[9,8,8]{0,2,1:T(8,128)(2,1)} %param.23) | copy-start | bytes 3460
  3.4 16.5 %collective-permute-start = (f32[5,8,4,512]{3,1,2,0:T(8,128)S(1)}, f32[5,8,4,512]{3,1,2,0:T(8,128)S(1)}, u32[]{:S(2)}, u32[]{:S(2)}) collective-permute-start(f32[5,8,4,512]{3,1,2,0:T(8,128)S(1)} %get-tuple-element.14), channel_id=1, source_target_pairs={{0,1},{1,2},{2,3},{3,4},{4,5},{5,6},{6,7},{8,9},{9,10},{10,11},{11... | collective-permute-start | bytes 983048 | tf_op jit(solution)/shard_map/ppermute | solution.py:19
  6.6 16.3 %collective-permute-start.1 = (f32[5,8,4,512]{3,1,2,0:T(8,128)S(1)}, f32[5,8,4,512]{3,1,2,0:T(8,128)S(1)}, u32[]{:S(2)}, u32[]{:S(2)}) collective-permute-start(f32[5,8,4,512]{3,1,2,0:T(8,128)S(1)} %get-tuple-element.15), channel_id=1, source_target_pairs={{1,0},{2,1},{3,2},{4,3},{5,4},{6,5},{7,6},{9,8},{10,9},{11,10},{12... | collective-permute-start | bytes 983048 | tf_op jit(solution)/shard_map/ppermute | solution.py:22
  25.5 7.4 %all-to-all-start = ((bf16[4,8,8,256]{3,2,1,0:T(8,128)(2,1)}), bf16[4,8,8,256]{3,2,1,0:T(8,128)(2,1)S(1)}, u32[]{:S(2)}, u32[]{:S(2)}) async-start(bf16[4,8,8,256]{3,2,1,0:T(8,128)(2,1)} %copy_bitcast_fusion.1), calls=%async_computation | async-start | bytes 262144 | tf_op jit(solution)/shard_map/all_to_all | solution.py:205
  32.9 0.7 copy-start.4
  44.3 7.3 %collective-permute-start.2 = (bf16[8,8,8,8]{3,1,2,0:T(8,128)(2,1)S(1)}, bf16[8,8,8,8]{3,1,2,0:T(8,128)(2,1)S(1)}, u32[]{:S(2)}, u32[]{:S(2)}) collective-permute-start(bf16[8,8,8,8]{3,1,2,0:T(8,128)(2,1)S(1)} %get-tuple-element.18), channel_id=1, source_target_pairs={{0,8},{8,16},{16,24},{1,9},{9,17},{17,25},{2,10},{10,18},{18,26},{... | collective-permute-start | bytes 24584 | tf_op jit(solution)/shard_map/ppermute | solution.py:19
  47.3 6.3 %collective-permute-start.3 = (bf16[8,8,8,8]{3,1,2,0:T(8,128)(2,1)S(1)}, bf16[8,8,8,8]{3,1,2,0:T(8,128)(2,1)S(1)}, u32[]{:S(2)}, u32[]{:S(2)}) collective-permute-start(bf16[8,8,8,8]{3,1,2,0:T(8,128)(2,1)S(1)} %get-tuple-element.19), channel_id=1, source_target_pairs={{8,0},{16,8},{24,16},{9,1},{17,9},{25,17},{10,2},{18,10},{26,18},{... | collective-permute-start | bytes 24584 | tf_op jit(solution)/shard_map/ppermute | solution.py:22
  53.7 11.4 %collective-permute-start.4 = (bf16[8,8,8,144]{3,1,2,0:T(8,128)(2,1)S(1)}, bf16[8,8,8,144]{3,1,2,0:T(8,128)(2,1)S(1)}, u32[]{:S(2)}, u32[]{:S(2)}) collective-permute-start(bf16[8,8,8,144]{3,1,2,0:T(8,128)(2,1)S(1)} %pad_maximum_fusion.4), channel_id=1, source_target_pairs={{0,1},{1,2},{2,3},{3,4},{4,5},{5,6},{6,7},{8,9},{9,10},{10,11},{11... | collective-permute-start | bytes 442376 | tf_op jit(solution)/shard_map/ppermute | solution.py:19
  56.0 11.9 %collective-permute-start.5 = (bf16[8,8,8,144]{3,1,2,0:T(8,128)(2,1)S(1)}, bf16[8,8,8,144]{3,1,2,0:T(8,128)(2,1)S(1)}, u32[]{:S(2)}, u32[]{:S(2)}) collective-permute-start(bf16[8,8,8,144]{3,1,2,0:T(8,128)(2,1)S(1)} %pad_maximum_fusion.4), channel_id=1, source_target_pairs={{1,0},{2,1},{3,2},{4,3},{5,4},{6,5},{7,6},{9,8},{10,9},{11,10},{12... | collective-permute-start | bytes 442376 | tf_op jit(solution)/shard_map/ppermute | solution.py:22
  72.8 0.9 %copy-start.3 = (bf16[8,8,1024]{2,1,0:T(8,128)(2,1)S(1)}, bf16[8,8,1024]{2,1,0:T(8,128)(2,1)}, u32[]{:S(2)}) copy-start(bf16[8,8,1024]{2,1,0:T(8,128)(2,1)} %shard_map.118) | copy-start | bytes 393220

commit v5 on v4

--- a/solution.py
+++ b/solution.py
@@ -54,9 +54,20 @@
 def attention_kernel(
     hs_ref, x_ref, w1_ref, gain_ref, pw_ref, ow_ref, rw_ref, out_ref, *, chunk, heads
 ):
+    lax.fori_loop(
+        0,
+        x_ref.shape[1],
+        lambda r, carry: attention_row(
+            r, hs_ref, x_ref, w1_ref, gain_ref, pw_ref, ow_ref, rw_ref, out_ref, chunk, heads
+        ),
+        0,
+    )
+
+
+def attention_row(r, hs_ref, x_ref, w1_ref, gain_ref, pw_ref, ow_ref, rw_ref, out_ref, chunk, heads):
     width = w1_ref.shape[0]
     sources = x_ref.shape[0]
-    layers = jnp.concatenate([x_ref[s, 0] for s in range(sources)], axis=1)
+    layers = jnp.concatenate([x_ref[s, r] for s in range(sources)], axis=1)
     lanes = layers.shape[1]
     members = lanes // chunk
     embedded = jnp.dot(w1_ref[...], layers, preferred_element_type=jnp.float32)
@@ -90,7 +101,8 @@
     attended = jnp.dot(ow_ref[...], mixed, preferred_element_type=jnp.float32)
     residual = (embedded + attended).astype(jnp.bfloat16)
     features = jnp.dot(rw_ref[...], residual, preferred_element_type=jnp.float32)
-    out_ref[0] = features.astype(out_ref.dtype)
+    out_ref[r] = features.astype(out_ref.dtype)
+    return 0
 
 
 def post_block(
@@ -114,20 +126,8 @@
     project_t = project_weight.T.reshape(3, width, width)[:, order].reshape(3 * width, width)
     output_t = output_weight.T[:, order]
     scale = jnp.tile(head_scale, sub // heads).reshape(sub, 1)
-    full = lambda r: (0, 0)
     return pl.pallas_call(
         functools.partial(attention_kernel, chunk=chunk, heads=heads),
-        grid=(row_count,),
-        in_specs=[
-            pl.BlockSpec((sub, 1), full),
-            pl.BlockSpec((sources, 1, levels_count, source_lanes), lambda r: (0, r, 0, 0)),
-            pl.BlockSpec((width, levels_count), full),
-            pl.BlockSpec((width, 1), full),
-            pl.BlockSpec((3 * width, width), full),
-            pl.BlockSpec((width, width), full),
-            pl.BlockSpec((feat, width), full),
-        ],
-        out_specs=pl.BlockSpec((1, feat, lanes), lambda r: (r, 0, 0)),
         out_shape=jax.ShapeDtypeStruct((row_count, feat, lanes), jnp.bfloat16),
     )(
         scale,

time: 75.2 us -> 75.3 us (level)
  no operation moved by 1% of the time
where the time goes in v5:
time: 75.3 us; the launch traced here: 74.8 us
  waiting for transfers between devices  21.3 us (28%)
  starting transfers between devices  21 us (28%)
  local copies, waits for them, and re-layouts  13.5 us (18%)
  Pallas kernels  9.91 us (13%)
  matrix products  5.36 us (7%)
  other arithmetic  3.29 us (4%)
    ppermute x3, waiting for transfers between devices, padded(): lax.ppermute(lax.slice_in_dim(block, block.shape[dim] - width, None, axis...  10.1 us
    pallas_call x1, Pallas kernels, post_block(): pl.pallas_call(functools.partial(attention_kernel, chunk=chunk, heads=hea...  9.91 us
    ppermute x3, starting transfers between devices, padded(): lax.ppermute(lax.slice_in_dim(block, 0, width, axis=dim), axis, backward)  8.94 us
    ppermute x3, starting transfers between devices, padded(): lax.ppermute(lax.slice_in_dim(block, block.shape[dim] - width, None, axis...  8.25 us
    ppermute x3, waiting for transfers between devices, padded(): lax.ppermute(lax.slice_in_dim(block, 0, width, axis=dim), axis, backward)  7.55 us
    unnamed x41, local copies, waits for them, and re-layouts  7.15 us
    dot_general x18, matrix products, convolve(): jnp.einsum('oc,mcij->moij', kernel[row_stencil * 3 + column_stencil], shi...  5.36 us
    all_to_all x1, starting transfers between devices, on_device(): lax.all_to_all(by_chunk, 'mem', split_axis=0, concat_axis=0, tiled=True)  3.79 us
  transfers between devices with their start and end apart: 7, of which 6 were waited for; matrix products, arithmetic and copies ran while one was open for 10% of the time, Pallas kernels for 0%

profile of v5, /device:TPU:9, one launch (start us, length us, event | category | flops | bytes accessed | tf_op | source)
XLA Modules:
  0.0 74.8 jit_solution(12947191525235839565)
XLA Ops:
  0.0 1.0 %copy.147 = f32[8,8,512]{2,0,1:T(8,128)S(1)} copy(f32[8,8,512]{2,1,0:T(8,128)} %param.15) | data formatting | bytes 262144 | tf_op args[3]
  1.0 1.1 %copy.69 = f32[2,8,8,512]{3,1,2,0:T(8,128)S(1)} copy(f32[2,8,8,512]{3,2,1,0:T(8,128)} %param.12) | data formatting | bytes 524288 | tf_op args[0]
  2.1 1.1 %fusion.60 = (f32[8,8,512]{2,0,1:T(8,128)S(1)}, f32[1,8,8,512]{3,1,2,0:T(8,128)S(1)}, f32[1,8,8,512]{3,1,2,0:T(8,128)S(1)}, f32[8,8,512]{2,0,1:T(8,128)S(1)}) fusion(f32[8,8,512]{2,1,0:T(8,128)} %param.13, f32[8,8,512]{2,1,0:T(8,128)} %param.14), kind=kLoop, calls=%fused_computation.114 | loop fusion | bytes 786432 | tf_op args[1]
  3.4 3.1 %collective-permute-start = (f32[5,8,4,512]{3,1,2,0:T(8,128)S(1)}, f32[5,8,4,512]{3,1,2,0:T(8,128)S(1)}, u32[]{:S(2)}, u32[]{:S(2)}) collective-permute-start(f32[5,8,4,512]{3,1,2,0:T(8,128)S(1)} %get-tuple-element.14), channel_id=1, source_target_pairs={{0,1},{1,2},{2,3},{3,4},{4,5},{5,6},{6,7},{8,9},{9,10},{10,11},{11... | collective-permute-start | bytes 983048 | tf_op jit(solution)/shard_map/ppermute | solution.py:19
  6.6 3.1 %collective-permute-start.1 = (f32[5,8,4,512]{3,1,2,0:T(8,128)S(1)}, f32[5,8,4,512]{3,1,2,0:T(8,128)S(1)}, u32[]{:S(2)}, u32[]{:S(2)}) collective-permute-start(f32[5,8,4,512]{3,1,2,0:T(8,128)S(1)} %get-tuple-element.15), channel_id=1, source_target_pairs={{1,0},{2,1},{3,2},{4,3},{5,4},{6,5},{7,6},{9,8},{10,9},{11,10},{12... | collective-permute-start | bytes 983048 | tf_op jit(solution)/shard_map/ppermute | solution.py:22
  10.0 0.7 gather_fusion
  10.6 0.6 copy.77
  11.3 0.6 gather_fusion.1
  11.9 0.7 copy.78
  12.6 0.7 copy.80.gain_ref
  13.3 0.7 copy.74
  14.0 0.7 reshape_tile.4.hs_ref
  14.9 5.0 %collective-permute-done = f32[5,8,4,512]{3,1,2,0:T(8,128)S(1)} collective-permute-done((f32[5,8,4,512]{3,1,2,0:T(8,128)S(1)}, f32[5,8,4,512]{3,1,2,0:T(8,128)S(1)}, u32[]{:S(2)}, u32[]{:S(2)}) %collective-permute-start) | collective-permute-done | bytes 327712 | tf_op jit(solution)/shard_map/ppermute | solution.py:19
  19.9 2.9 %collective-permute-done.1 = f32[5,8,4,512]{3,1,2,0:T(8,128)S(1)} collective-permute-done((f32[5,8,4,512]{3,1,2,0:T(8,128)S(1)}, f32[5,8,4,512]{3,1,2,0:T(8,128)S(1)}, u32[]{:S(2)}, u32[]{:S(2)}) %collective-permute-start.1) | collective-permute-done | bytes 327712 | tf_op jit(solution)/shard_map/ppermute | solution.py:22
  23.2 0.5 add_select_fusion
  23.7 0.4 add_select_fusion.1
  24.1 0.4 add_select_fusion.2
  24.5 0.9 %copy_bitcast_fusion.1 = bf16[4,8,8,256]{3,2,1,0:T(8,128)(2,1)} fusion(f32[2,8,8,512]{3,1,2,0:T(8,128)S(1)} %slice.337, f32[8,8,512]{2,0,1:T(8,128)S(1)} %copy.147, f32[2,8,10,512]{3,1,2,0:T(8,128)S(1)} %add_select_fusion.2, f32[8,8,512]{2,0,1:T(8,128)S(1)} %get-tuple-element.45, f32[8,8,512]{2,0,1:T(8,128)S(1)} %get-tuple-element.20, ...), kind=kLoop, calls=%fused_computation.78 | loop fusion | flops 1310720 | bytes 1311232 | tf_op jit(solution)/shard_map/reshape | solution.py:202
  25.5 3.8 %all-to-all-start = ((bf16[4,8,8,256]{3,2,1,0:T(8,128)(2,1)}), bf16[4,8,8,256]{3,2,1,0:T(8,128)(2,1)S(1)}, u32[]{:S(2)}, u32[]{:S(2)}) async-start(bf16[4,8,8,256]{3,2,1,0:T(8,128)(2,1)} %copy_bitcast_fusion.1), calls=%async_computation | async-start | bytes 262144 | tf_op jit(solution)/shard_map/all_to_all | solution.py:205
  29.3 3.6 %all-to-all-done.x_ref = bf16[4,8,8,256]{3,2,1,0:T(8,128)(2,1)S(1)} async-done(((bf16[4,8,8,256]{3,2,1,0:T(8,128)(2,1)}), bf16[4,8,8,256]{3,2,1,0:T(8,128)(2,1)S(1)}, u32[]{:S(2)}, u32[]{:S(2)}) %all-to-all-start) | async-done | bytes 131104 | tf_op jit(solution)/shard_map/all_to_all | solution.py:205
  32.9 0.7 copy-done.4
  33.5 9.9 %shard_map.118 = bf16[8,8,1024]{2,1,0:T(8,128)(2,1)} custom-call(f32[8,1]{1,0:T(8,128)} %reshape_tile.4.hs_ref, bf16[4,8,8,256]{3,2,1,0:T(8,128)(2,1)} %copy-done.4, bf16[64,8]{1,0:T(8,128)(2,1)} %bitcast.195, f32[64,1]{1,0:T(8,128)} %copy.80.gain_ref, bf16[192,64]{1,0:T(8,128)(2,1)} %bitcast.192, bf16[64,64]{1,0:T(8,128)(2,1)} %bitcast.194, ...), custom_call_target="tpu_custom_call" | custom-call | tf_op jit(solution)/shard_map/pallas_call | solution.py:129
  43.4 0.9 %copy_bitcast_fusion = bf16[8,8,8,128]{3,1,2,0:T(8,128)(2,1)S(1)} fusion(bf16[8,8,1024]{2,1,0:T(8,128)(2,1)} %shard_map.118), kind=kLoop, calls=%fused_computation.77 | loop fusion | bytes 262144 | tf_op jit(solution)/shard_map/transpose | solution.py:219
  44.5 2.9 %collective-permute-start.2 = (bf16[8,8,8,8]{3,1,2,0:T(8,128)(2,1)S(1)}, bf16[8,8,8,8]{3,1,2,0:T(8,128)(2,1)S(1)}, u32[]{:S(2)}, u32[]{:S(2)}) collective-permute-start(bf16[8,8,8,8]{3,1,2,0:T(8,128)(2,1)S(1)} %get-tuple-element.18), channel_id=1, source_target_pairs={{0,8},{8,16},{16,24},{1,9},{9,17},{17,25},{2,10},{10,18},{18,26},{... | collective-permute-start | bytes 24584 | tf_op jit(solution)/shard_map/ppermute | solution.py:19
  47.4 1.9 %collective-permute-start.3 = (bf16[8,8,8,8]{3,1,2,0:T(8,128)(2,1)S(1)}, bf16[8,8,8,8]{3,1,2,0:T(8,128)(2,1)S(1)}, u32[]{:S(2)}, u32[]{:S(2)}) collective-permute-start(bf16[8,8,8,8]{3,1,2,0:T(8,128)(2,1)S(1)} %get-tuple-element.19), channel_id=1, source_target_pairs={{8,0},{16,8},{24,16},{9,1},{17,9},{25,17},{10,2},{18,10},{26,18},{... | collective-permute-start | bytes 24584 | tf_op jit(solution)/shard_map/ppermute | solution.py:22
  50.0 0.1 copy.125
  50.1 0.1 copy.121
  50.3 0.1 copy.120
  50.4 0.1 copy.119
  50.5 0.1 copy.128
  50.7 0.1 copy.129
  50.8 0.1 copy.130
  50.9 0.1 copy.131
  51.1 0.1 copy.132
  51.2 0.1 copy.133
  51.3 0.1 copy.134
  51.5 0.1 copy.135
  51.8 1.9 %collective-permute-done.3 = bf16[8,8,8,8]{3,1,2,0:T(8,128)(2,1)S(1)} collective-permute-done((bf16[8,8,8,8]{3,1,2,0:T(8,128)(2,1)S(1)}, bf16[8,8,8,8]{3,1,2,0:T(8,128)(2,1)S(1)}, u32[]{:S(2)}, u32[]{:S(2)}) %collective-permute-start.3) | collective-permute-done | bytes 8224 | tf_op jit(solution)/shard_map/ppermute | solution.py:22
  53.7 0.2 pad_maximum_fusion.4
  53.9 2.2 %collective-permute-start.4 = (bf16[8,8,8,144]{3,1,2,0:T(8,128)(2,1)S(1)}, bf16[8,8,8,144]{3,1,2,0:T(8,128)(2,1)S(1)}, u32[]{:S(2)}, u32[]{:S(2)}) collective-permute-start(bf16[8,8,8,144]{3,1,2,0:T(8,128)(2,1)S(1)} %pad_maximum_fusion.4), channel_id=1, source_target_pairs={{0,1},{1,2},{2,3},{3,4},{4,5},{5,6},{6,7},{8,9},{9,10},{10,11},{11... | collective-permute-start | bytes 442376 | tf_op jit(solution)/shard_map/ppermute | solution.py:19
  56.1 4.0 %collective-permute-start.5 = (bf16[8,8,8,144]{3,1,2,0:T(8,128)(2,1)S(1)}, bf16[8,8,8,144]{3,1,2,0:T(8,128)(2,1)S(1)}, u32[]{:S(2)}, u32[]{:S(2)}) collective-permute-start(bf16[8,8,8,144]{3,1,2,0:T(8,128)(2,1)S(1)} %pad_maximum_fusion.4), channel_id=1, source_target_pairs={{1,0},{2,1},{3,2},{4,3},{5,4},{6,5},{7,6},{9,8},{10,9},{11,10},{12... | collective-permute-start | bytes 442376 | tf_op jit(solution)/shard_map/ppermute | solution.py:22
  60.1 5.1 %collective-permute-done.4 = bf16[8,8,8,144]{3,1,2,0:T(8,128)(2,1)S(1)} collective-permute-done((bf16[8,8,8,144]{3,1,2,0:T(8,128)(2,1)S(1)}, bf16[8,8,8,144]{3,1,2,0:T(8,128)(2,1)S(1)}, u32[]{:S(2)}, u32[]{:S(2)}) %collective-permute-start.4) | collective-permute-done | bytes 147488 | tf_op jit(solution)/shard_map/ppermute | solution.py:19
  65.3 2.7 %collective-permute-done.5 = bf16[8,8,8,144]{3,1,2,0:T(8,128)(2,1)S(1)} collective-permute-done((bf16[8,8,8,144]{3,1,2,0:T(8,128)(2,1)S(1)}, bf16[8,8,8,144]{3,1,2,0:T(8,128)(2,1)S(1)}, u32[]{:S(2)}, u32[]{:S(2)}) %collective-permute-start.5) | collective-permute-done | bytes 147488 | tf_op jit(solution)/shard_map/ppermute | solution.py:22
  68.0 0.2 pad_maximum_fusion.1
  68.2 0.4 fusion.19
  68.6 0.3 fusion.21
  68.8 0.3 fusion.17
  69.2 0.4 maximum_maximum_fusion
  69.6 0.3 fusion.11
  69.9 0.3 fusion.13
  70.3 0.3 fusion.15
  70.6 0.4 fusion.23
  70.9 0.4 fusion.25
  71.3 0.8 %select_convert_fusion = bf16[8,8,16,136]{3,1,2,0:T(8,128)(2,1)S(1)} fusion(f32[8,16,136,8]{2,3,1,0:T(8,128)S(1)} %fusion.11, f32[8,16,136,8]{2,3,1,0:T(8,128)S(1)} %fusion.13, f32[8,16,136,8]{2,3,1,0:T(8,128)S(1)} %fusion.15, f32[8,16,136,8]{2,3,1,0:T(8,128)S(1)} %fusion.17, f32[8,16,136,8]{2,3,1,0:T(8,128)S(1)} %fusion.19, ...), kind=kOutput, calls=%fused_computation.23 | convolution fusion | flops 4177920 | bytes 5032192 | tf_op jit(solution)/shard_map/oc,mcij->moij/dot_general | solution.py:157
  72.1 0.2 fusion.36
  72.3 0.2 convolution_add_fusion.8
  72.5 0.2 convolution_add_fusion.7
  72.8 0.2 convolution_add_fusion.6
  72.9 0.2 convolution_add_fusion.5
  73.2 0.2 convolution_add_fusion.4
  73.4 0.2 convolution_add_fusion.3
  73.6 0.2 convolution_add_fusion.2
  73.8 0.2 fusion.10
  74.1 0.7 copy.100
  (51 shorter events, 2.0 us)
Async XLA Ops:
  0.0 11.3 %copy-start = (bf16[64,64]{1,0:T(8,128)(2,1)S(1)}, bf16[64,64]{1,0:T(8,128)(2,1)}, u32[]{:S(2)}) copy-start(bf16[64,64]{1,0:T(8,128)(2,1)} %param.20) | copy-start | bytes 24580
  3.2 6.6 %copy-start.5 = (bf16[64,192]{1,0:T(8,128)(2,1)S(1)}, bf16[64,192]{1,0:T(8,128)(2,1)}, u32[]{:S(2)}) copy-start(bf16[64,192]{1,0:T(8,128)(2,1)} %param.18) | copy-start | bytes 73732
  3.3 9.4 %copy-start.7 = (f32[64]{0:T(128)S(1)}, f32[64]{0:T(128)}, u32[]{:S(2)}) copy-start(f32[64]{0:T(128)} %param.17) | copy-start | bytes 772
  3.3 10.0 %copy-start.6 = (bf16[8,64]{1,0:T(8,128)(2,1)S(1)}, bf16[8,64]{1,0:T(8,128)(2,1)}, u32[]{:S(2)}) copy-start(bf16[8,64]{1,0:T(8,128)(2,1)} %param.16) | copy-start | bytes 3076
  3.3 10.7 %copy-start.8 = (f32[4]{0:T(128)S(1)}, f32[4]{0:T(128)}, u32[]{:S(2)}) copy-start(f32[4]{0:T(128)} %param.19) | copy-start | bytes 52
  3.4 11.3 %copy-start.1 = (bf16[9,8,8]{0,2,1:T(8,128)(2,1)S(1)}, bf16[9,8,8]{0,2,1:T(8,128)(2,1)}, u32[]{:S(2)}) copy-start(bf16[9,8,8]{0,2,1:T(8,128)(2,1)} %param.22) | copy-start | bytes 3460
  3.4 11.5 %copy-start.2 = (bf16[9,8,8]{0,2,1:T(8,128)(2,1)S(1)}, bf16[9,8,8]{0,2,1:T(8,128)(2,1)}, u32[]{:S(2)}) copy-start(bf16[9,8,8]{0,2,1:T(8,128)(2,1)} %param.23) | copy-start | bytes 3460
  3.4 16.5 %collective-permute-start = (f32[5,8,4,512]{3,1,2,0:T(8,128)S(1)}, f32[5,8,4,512]{3,1,2,0:T(8,128)S(1)}, u32[]{:S(2)}, u32[]{:S(2)}) collective-permute-start(f32[5,8,4,512]{3,1,2,0:T(8,128)S(1)} %get-tuple-element.14), channel_id=1, source_target_pairs={{0,1},{1,2},{2,3},{3,4},{4,5},{5,6},{6,7},{8,9},{9,10},{10,11},{11... | collective-permute-start | bytes 983048 | tf_op jit(solution)/shard_map/ppermute | solution.py:19
  6.6 16.3 %collective-permute-start.1 = (f32[5,8,4,512]{3,1,2,0:T(8,128)S(1)}, f32[5,8,4,512]{3,1,2,0:T(8,128)S(1)}, u32[]{:S(2)}, u32[]{:S(2)}) collective-permute-start(f32[5,8,4,512]{3,1,2,0:T(8,128)S(1)} %get-tuple-element.15), channel_id=1, source_target_pairs={{1,0},{2,1},{3,2},{4,3},{5,4},{6,5},{7,6},{9,8},{10,9},{11,10},{12... | collective-permute-start | bytes 983048 | tf_op jit(solution)/shard_map/ppermute | solution.py:22
  25.5 7.4 %all-to-all-start = ((bf16[4,8,8,256]{3,2,1,0:T(8,128)(2,1)}), bf16[4,8,8,256]{3,2,1,0:T(8,128)(2,1)S(1)}, u32[]{:S(2)}, u32[]{:S(2)}) async-start(bf16[4,8,8,256]{3,2,1,0:T(8,128)(2,1)} %copy_bitcast_fusion.1), calls=%async_computation | async-start | bytes 262144 | tf_op jit(solution)/shard_map/all_to_all | solution.py:205
  32.9 0.7 copy-start.4
  44.5 7.3 %collective-permute-start.2 = (bf16[8,8,8,8]{3,1,2,0:T(8,128)(2,1)S(1)}, bf16[8,8,8,8]{3,1,2,0:T(8,128)(2,1)S(1)}, u32[]{:S(2)}, u32[]{:S(2)}) collective-permute-start(bf16[8,8,8,8]{3,1,2,0:T(8,128)(2,1)S(1)} %get-tuple-element.18), channel_id=1, source_target_pairs={{0,8},{8,16},{16,24},{1,9},{9,17},{17,25},{2,10},{10,18},{18,26},{... | collective-permute-start | bytes 24584 | tf_op jit(solution)/shard_map/ppermute | solution.py:19
  47.4 6.3 %collective-permute-start.3 = (bf16[8,8,8,8]{3,1,2,0:T(8,128)(2,1)S(1)}, bf16[8,8,8,8]{3,1,2,0:T(8,128)(2,1)S(1)}, u32[]{:S(2)}, u32[]{:S(2)}) collective-permute-start(bf16[8,8,8,8]{3,1,2,0:T(8,128)(2,1)S(1)} %get-tuple-element.19), channel_id=1, source_target_pairs={{8,0},{16,8},{24,16},{9,1},{17,9},{25,17},{10,2},{18,10},{26,18},{... | collective-permute-start | bytes 24584 | tf_op jit(solution)/shard_map/ppermute | solution.py:22
  53.9 11.4 %collective-permute-start.4 = (bf16[8,8,8,144]{3,1,2,0:T(8,128)(2,1)S(1)}, bf16[8,8,8,144]{3,1,2,0:T(8,128)(2,1)S(1)}, u32[]{:S(2)}, u32[]{:S(2)}) collective-permute-start(bf16[8,8,8,144]{3,1,2,0:T(8,128)(2,1)S(1)} %pad_maximum_fusion.4), channel_id=1, source_target_pairs={{0,1},{1,2},{2,3},{3,4},{4,5},{5,6},{6,7},{8,9},{9,10},{10,11},{11... | collective-permute-start | bytes 442376 | tf_op jit(solution)/shard_map/ppermute | solution.py:19
  56.1 11.9 %collective-permute-start.5 = (bf16[8,8,8,144]{3,1,2,0:T(8,128)(2,1)S(1)}, bf16[8,8,8,144]{3,1,2,0:T(8,128)(2,1)S(1)}, u32[]{:S(2)}, u32[]{:S(2)}) collective-permute-start(bf16[8,8,8,144]{3,1,2,0:T(8,128)(2,1)S(1)} %pad_maximum_fusion.4), channel_id=1, source_target_pairs={{1,0},{2,1},{3,2},{4,3},{5,4},{6,5},{7,6},{9,8},{10,9},{11,10},{12... | collective-permute-start | bytes 442376 | tf_op jit(solution)/shard_map/ppermute | solution.py:22
  72.9 0.9 %copy-start.3 = (bf16[8,8,1024]{2,1,0:T(8,128)(2,1)S(1)}, bf16[8,8,1024]{2,1,0:T(8,128)(2,1)}, u32[]{:S(2)}) copy-start(bf16[8,8,1024]{2,1,0:T(8,128)(2,1)} %shard_map.118) | copy-start | bytes 393220

commit v6 on v5

--- a/solution.py
+++ b/solution.py
@@ -52,19 +52,17 @@
 
 
 def attention_kernel(
-    hs_ref, x_ref, w1_ref, gain_ref, pw_ref, ow_ref, rw_ref, out_ref, *, chunk, heads
-):
-    lax.fori_loop(
-        0,
-        x_ref.shape[1],
-        lambda r, carry: attention_row(
-            r, hs_ref, x_ref, w1_ref, gain_ref, pw_ref, ow_ref, rw_ref, out_ref, chunk, heads
-        ),
-        0,
-    )
-
-
-def attention_row(r, hs_ref, x_ref, w1_ref, gain_ref, pw_ref, ow_ref, rw_ref, out_ref, chunk, heads):
+    hs_ref, x_ref, w1_ref, gain_ref, pw_ref, ow_ref, rw_ref, out_ref, q_s, k_s, v_s, mix_s, *,
+    chunk, heads
+):
+    refs = (hs_ref, x_ref, w1_ref, gain_ref, pw_ref, ow_ref, rw_ref, out_ref, q_s, k_s, v_s, mix_s)
+    lax.fori_loop(0, x_ref.shape[1], lambda r, c: attention_row(r, *refs, chunk, heads), 0)
+
+
+def attention_row(
+    r, hs_ref, x_ref, w1_ref, gain_ref, pw_ref, ow_ref, rw_ref, out_ref, q_s, k_s, v_s, mix_s,
+    chunk, heads
+):
     width = w1_ref.shape[0]
     sources = x_ref.shape[0]
     layers = jnp.concatenate([x_ref[s, r] for s in range(sources)], axis=1)
@@ -79,25 +77,31 @@
     q = projected[:width].reshape(tiles, sub, lanes)
     k = projected[width : 2 * width].reshape(tiles, sub, lanes)
     v = projected[2 * width :].astype(jnp.bfloat16).astype(jnp.float32).reshape(tiles, sub, lanes)
-    q = (q * lax.rsqrt(head_sums(q * q, heads) + 1.0)).astype(jnp.bfloat16).astype(jnp.float32)
-    k = (k * lax.rsqrt(head_sums(k * k, heads) + 1.0)).astype(jnp.bfloat16).astype(jnp.float32)
+    q_s[...] = (q * lax.rsqrt(head_sums(q * q, heads) + 1.0)).astype(jnp.bfloat16).astype(jnp.float32)
+    k_s[...] = (k * lax.rsqrt(head_sums(k * k, heads) + 1.0)).astype(jnp.bfloat16).astype(jnp.float32)
+    v_s[...] = v
     scale = hs_ref[...]
-    weights = []
-    for n in range(members):
-        k_n = k[:, :, n * chunk : (n + 1) * chunk]
-        k_wide = jnp.concatenate([k_n] * members, axis=2)
-        weights.append(jnp.exp(head_sums(q * k_wide, heads) * scale))
-    total = weights[0]
-    for n in range(1, members):
-        total = total + weights[n]
-    inverse = 1.0 / total
-    mixed = jnp.zeros(q.shape, jnp.float32)
-    for n in range(members):
-        prob = (weights[n] * inverse).astype(jnp.bfloat16).astype(jnp.float32)
-        v_n = v[:, :, n * chunk : (n + 1) * chunk]
-        v_wide = jnp.concatenate([v_n] * members, axis=2)
-        mixed = mixed + prob[None] * v_wide
-    mixed = mixed.reshape(width, lanes).astype(jnp.bfloat16)
+
+    def one_member(m, carry):
+        start = pl.multiple_of(m * chunk, chunk)
+        q_m = q_s[:, :, pl.ds(start, chunk)]
+        weights = []
+        for n in range(members):
+            k_n = k_s[:, :, n * chunk : (n + 1) * chunk]
+            weights.append(jnp.exp(head_sums(q_m * k_n, heads) * scale))
+        total = weights[0]
+        for n in range(1, members):
+            total = total + weights[n]
+        inverse = 1.0 / total
+        mixed = jnp.zeros(q_m.shape, jnp.float32)
+        for n in range(members):
+            prob = (weights[n] * inverse).astype(jnp.bfloat16).astype(jnp.float32)
+            mixed = mixed + prob[None] * v_s[:, :, n * chunk : (n + 1) * chunk]
+        mix_s[:, :, pl.ds(start, chunk)] = mixed
+        return carry
+
+    lax.fori_loop(0, members, one_member, 0)
+    mixed = mix_s[...].reshape(width, lanes).astype(jnp.bfloat16)
     attended = jnp.dot(ow_ref[...], mixed, preferred_element_type=jnp.float32)
     residual = (embedded + attended).astype(jnp.bfloat16)
     features = jnp.dot(rw_ref[...], residual, preferred_element_type=jnp.float32)
@@ -129,6 +133,7 @@
     return pl.pallas_call(
         functools.partial(attention_kernel, chunk=chunk, heads=heads),
         out_shape=jax.ShapeDtypeStruct((row_count, feat, lanes), jnp.bfloat16),
+        scratch_shapes=[pltpu.VMEM((width // sub, sub, lanes), jnp.float32)] * 4,
     )(
         scale,
         by_source,

time: 75.3 us -> 79.8 us (1.060)
  Pallas kernels: 9.91 us -> 14.4 us
    pallas_call x1, Pallas kernels: 9.91 us -> 14.4 us  [post_block(): pl.pallas_call(functools.partial(attention_kernel, chunk=chunk, heads=hea...]
where the time goes in v6:
time: 79.8 us; the launch traced here: 79.3 us
  waiting for transfers between devices  21.3 us (27%)
  starting transfers between devices  21 us (26%)
  Pallas kernels  14.4 us (18%)
  local copies, waits for them, and re-layouts  13.5 us (17%)
  matrix products  5.36 us (7%)
  other arithmetic  3.29 us (4%)
    pallas_call x1, Pallas kernels, post_block(): pl.pallas_call(functools.partial(attention_kernel, chunk=chunk, heads=hea...  14.4 us
    ppermute x3, waiting for transfers between devices, padded(): lax.ppermute(lax.slice_in_dim(block, block.shape[dim] - width, None, axis...  10.1 us
    ppermute x3, starting transfers between devices, padded(): lax.ppermute(lax.slice_in_dim(block, 0, width, axis=dim), axis, backward)  8.94 us
    ppermute x3, starting transfers between devices, padded(): lax.ppermute(lax.slice_in_dim(block, block.shape[dim] - width, None, axis...  8.25 us
    ppermute x3, waiting for transfers between devices, padded(): lax.ppermute(lax.slice_in_dim(block, 0, width, axis=dim), axis, backward)  7.54 us
    unnamed x41, local copies, waits for them, and re-layouts  7.15 us
    dot_general x18, matrix products, convolve(): jnp.einsum('oc,mcij->moij', kernel[row_stencil * 3 + column_stencil], shi...  5.36 us
    all_to_all x1, starting transfers between devices, on_device(): lax.all_to_all(by_chunk, 'mem', split_axis=0, concat_axis=0, tiled=True)  3.79 us
  transfers between devices with their start and end apart: 7, of which 6 were waited for; matrix products, arithmetic and copies ran while one was open for 10% of the time, Pallas kernels for 0%

profile of v6, /device:TPU:9, one launch (start us, length us, event | category | flops | bytes accessed | tf_op | source)
XLA Modules:
  0.0 79.3 jit_solution(13729932046343551080)
XLA Ops:
  0.0 1.0 %copy.147 = f32[8,8,512]{2,0,1:T(8,128)S(1)} copy(f32[8,8,512]{2,1,0:T(8,128)} %param.15) | data formatting | bytes 262144 | tf_op args[3]
  1.0 1.1 %copy.69 = f32[2,8,8,512]{3,1,2,0:T(8,128)S(1)} copy(f32[2,8,8,512]{3,2,1,0:T(8,128)} %param.12) | data formatting | bytes 524288 | tf_op args[0]
  2.1 1.1 %fusion.60 = (f32[8,8,512]{2,0,1:T(8,128)S(1)}, f32[1,8,8,512]{3,1,2,0:T(8,128)S(1)}, f32[1,8,8,512]{3,1,2,0:T(8,128)S(1)}, f32[8,8,512]{2,0,1:T(8,128)S(1)}) fusion(f32[8,8,512]{2,1,0:T(8,128)} %param.13, f32[8,8,512]{2,1,0:T(8,128)} %param.14), kind=kLoop, calls=%fused_computation.114 | loop fusion | bytes 786432 | tf_op args[1]
  3.4 3.1 %collective-permute-start = (f32[5,8,4,512]{3,1,2,0:T(8,128)S(1)}, f32[5,8,4,512]{3,1,2,0:T(8,128)S(1)}, u32[]{:S(2)}, u32[]{:S(2)}) collective-permute-start(f32[5,8,4,512]{3,1,2,0:T(8,128)S(1)} %get-tuple-element.14), channel_id=1, source_target_pairs={{0,1},{1,2},{2,3},{3,4},{4,5},{5,6},{6,7},{8,9},{9,10},{10,11},{11... | collective-permute-start | bytes 983048 | tf_op jit(solution)/shard_map/ppermute | solution.py:19
  6.6 3.1 %collective-permute-start.1 = (f32[5,8,4,512]{3,1,2,0:T(8,128)S(1)}, f32[5,8,4,512]{3,1,2,0:T(8,128)S(1)}, u32[]{:S(2)}, u32[]{:S(2)}) collective-permute-start(f32[5,8,4,512]{3,1,2,0:T(8,128)S(1)} %get-tuple-element.15), channel_id=1, source_target_pairs={{1,0},{2,1},{3,2},{4,3},{5,4},{6,5},{7,6},{9,8},{10,9},{11,10},{12... | collective-permute-start | bytes 983048 | tf_op jit(solution)/shard_map/ppermute | solution.py:22
  10.0 0.7 gather_fusion
  10.6 0.6 copy.77
  11.3 0.6 gather_fusion.1
  11.9 0.7 copy.78
  12.6 0.7 copy.80.gain_ref
  13.3 0.7 copy.74
  14.0 0.7 reshape_tile.4.hs_ref
  14.9 5.0 %collective-permute-done = f32[5,8,4,512]{3,1,2,0:T(8,128)S(1)} collective-permute-done((f32[5,8,4,512]{3,1,2,0:T(8,128)S(1)}, f32[5,8,4,512]{3,1,2,0:T(8,128)S(1)}, u32[]{:S(2)}, u32[]{:S(2)}) %collective-permute-start) | collective-permute-done | bytes 327712 | tf_op jit(solution)/shard_map/ppermute | solution.py:19
  19.9 2.9 %collective-permute-done.1 = f32[5,8,4,512]{3,1,2,0:T(8,128)S(1)} collective-permute-done((f32[5,8,4,512]{3,1,2,0:T(8,128)S(1)}, f32[5,8,4,512]{3,1,2,0:T(8,128)S(1)}, u32[]{:S(2)}, u32[]{:S(2)}) %collective-permute-start.1) | collective-permute-done | bytes 327712 | tf_op jit(solution)/shard_map/ppermute | solution.py:22
  23.2 0.5 add_select_fusion
  23.7 0.4 add_select_fusion.1
  24.1 0.4 add_select_fusion.2
  24.5 0.9 %copy_bitcast_fusion.1 = bf16[4,8,8,256]{3,2,1,0:T(8,128)(2,1)} fusion(f32[2,8,8,512]{3,1,2,0:T(8,128)S(1)} %slice.337, f32[8,8,512]{2,0,1:T(8,128)S(1)} %copy.147, f32[2,8,10,512]{3,1,2,0:T(8,128)S(1)} %add_select_fusion.2, f32[8,8,512]{2,0,1:T(8,128)S(1)} %get-tuple-element.45, f32[8,8,512]{2,0,1:T(8,128)S(1)} %get-tuple-element.20, ...), kind=kLoop, calls=%fused_computation.78 | loop fusion | flops 1310720 | bytes 1311232 | tf_op jit(solution)/shard_map/reshape | solution.py:207
  25.5 3.8 %all-to-all-start = ((bf16[4,8,8,256]{3,2,1,0:T(8,128)(2,1)}), bf16[4,8,8,256]{3,2,1,0:T(8,128)(2,1)S(1)}, u32[]{:S(2)}, u32[]{:S(2)}) async-start(bf16[4,8,8,256]{3,2,1,0:T(8,128)(2,1)} %copy_bitcast_fusion.1), calls=%async_computation | async-start | bytes 262144 | tf_op jit(solution)/shard_map/all_to_all | solution.py:210
  29.3 3.6 %all-to-all-done.x_ref = bf16[4,8,8,256]{3,2,1,0:T(8,128)(2,1)S(1)} async-done(((bf16[4,8,8,256]{3,2,1,0:T(8,128)(2,1)}), bf16[4,8,8,256]{3,2,1,0:T(8,128)(2,1)S(1)}, u32[]{:S(2)}, u32[]{:S(2)}) %all-to-all-start) | async-done | bytes 131104 | tf_op jit(solution)/shard_map/all_to_all | solution.py:210
  32.9 0.7 copy-done.4
  33.5 14.4 %shard_map.118 = bf16[8,8,1024]{2,1,0:T(8,128)(2,1)} custom-call(f32[8,1]{1,0:T(8,128)} %reshape_tile.4.hs_ref, bf16[4,8,8,256]{3,2,1,0:T(8,128)(2,1)} %copy-done.4, bf16[64,8]{1,0:T(8,128)(2,1)} %bitcast.195, f32[64,1]{1,0:T(8,128)} %copy.80.gain_ref, bf16[192,64]{1,0:T(8,128)(2,1)} %bitcast.192, bf16[64,64]{1,0:T(8,128)(2,1)} %bitcast.194, ...), custom_call_target="tpu_custom_call" | custom-call | tf_op jit(solution)/shard_map/pallas_call | solution.py:133
  47.9 0.9 %copy_bitcast_fusion = bf16[8,8,8,128]{3,1,2,0:T(8,128)(2,1)S(1)} fusion(bf16[8,8,1024]{2,1,0:T(8,128)(2,1)} %shard_map.118), kind=kLoop, calls=%fused_computation.77 | loop fusion | bytes 262144 | tf_op jit(solution)/shard_map/transpose | solution.py:224
  49.0 2.9 %collective-permute-start.2 = (bf16[8,8,8,8]{3,1,2,0:T(8,128)(2,1)S(1)}, bf16[8,8,8,8]{3,1,2,0:T(8,128)(2,1)S(1)}, u32[]{:S(2)}, u32[]{:S(2)}) collective-permute-start(bf16[8,8,8,8]{3,1,2,0:T(8,128)(2,1)S(1)} %get-tuple-element.18), channel_id=1, source_target_pairs={{0,8},{8,16},{16,24},{1,9},{9,17},{17,25},{2,10},{10,18},{18,26},{... | collective-permute-start | bytes 24584 | tf_op jit(solution)/shard_map/ppermute | solution.py:19
  51.9 1.9 %collective-permute-start.3 = (bf16[8,8,8,8]{3,1,2,0:T(8,128)(2,1)S(1)}, bf16[8,8,8,8]{3,1,2,0:T(8,128)(2,1)S(1)}, u32[]{:S(2)}, u32[]{:S(2)}) collective-permute-start(bf16[8,8,8,8]{3,1,2,0:T(8,128)(2,1)S(1)} %get-tuple-element.19), channel_id=1, source_target_pairs={{8,0},{16,8},{24,16},{9,1},{17,9},{25,17},{10,2},{18,10},{26,18},{... | collective-permute-start | bytes 24584 | tf_op jit(solution)/shard_map/ppermute | solution.py:22
  54.5 0.1 copy.125
  54.6 0.1 copy.121
  54.8 0.1 copy.120
  54.9 0.1 copy.119
  55.0 0.1 copy.128
  55.2 0.1 copy.129
  55.3 0.1 copy.130
  55.4 0.1 copy.131
  55.6 0.1 copy.132
  55.7 0.1 copy.133
  55.9 0.1 copy.134
  56.0 0.1 copy.135
  56.3 1.9 %collective-permute-done.3 = bf16[8,8,8,8]{3,1,2,0:T(8,128)(2,1)S(1)} collective-permute-done((bf16[8,8,8,8]{3,1,2,0:T(8,128)(2,1)S(1)}, bf16[8,8,8,8]{3,1,2,0:T(8,128)(2,1)S(1)}, u32[]{:S(2)}, u32[]{:S(2)}) %collective-permute-start.3) | collective-permute-done | bytes 8224 | tf_op jit(solution)/shard_map/ppermute | solution.py:22
  58.2 0.2 pad_maximum_fusion.4
  58.4 2.2 %collective-permute-start.4 = (bf16[8,8,8,144]{3,1,2,0:T(8,128)(2,1)S(1)}, bf16[8,8,8,144]{3,1,2,0:T(8,128)(2,1)S(1)}, u32[]{:S(2)}, u32[]{:S(2)}) collective-permute-start(bf16[8,8,8,144]{3,1,2,0:T(8,128)(2,1)S(1)} %pad_maximum_fusion.4), channel_id=1, source_target_pairs={{0,1},{1,2},{2,3},{3,4},{4,5},{5,6},{6,7},{8,9},{9,10},{10,11},{11... | collective-permute-start | bytes 442376 | tf_op jit(solution)/shard_map/ppermute | solution.py:19
  60.6 4.0 %collective-permute-start.5 = (bf16[8,8,8,144]{3,1,2,0:T(8,128)(2,1)S(1)}, bf16[8,8,8,144]{3,1,2,0:T(8,128)(2,1)S(1)}, u32[]{:S(2)}, u32[]{:S(2)}) collective-permute-start(bf16[8,8,8,144]{3,1,2,0:T(8,128)(2,1)S(1)} %pad_maximum_fusion.4), channel_id=1, source_target_pairs={{1,0},{2,1},{3,2},{4,3},{5,4},{6,5},{7,6},{9,8},{10,9},{11,10},{12... | collective-permute-start | bytes 442376 | tf_op jit(solution)/shard_map/ppermute | solution.py:22
  64.6 5.1 %collective-permute-done.4 = bf16[8,8,8,144]{3,1,2,0:T(8,128)(2,1)S(1)} collective-permute-done((bf16[8,8,8,144]{3,1,2,0:T(8,128)(2,1)S(1)}, bf16[8,8,8,144]{3,1,2,0:T(8,128)(2,1)S(1)}, u32[]{:S(2)}, u32[]{:S(2)}) %collective-permute-start.4) | collective-permute-done | bytes 147488 | tf_op jit(solution)/shard_map/ppermute | solution.py:19
  69.8 2.7 %collective-permute-done.5 = bf16[8,8,8,144]{3,1,2,0:T(8,128)(2,1)S(1)} collective-permute-done((bf16[8,8,8,144]{3,1,2,0:T(8,128)(2,1)S(1)}, bf16[8,8,8,144]{3,1,2,0:T(8,128)(2,1)S(1)}, u32[]{:S(2)}, u32[]{:S(2)}) %collective-permute-start.5) | collective-permute-done | bytes 147488 | tf_op jit(solution)/shard_map/ppermute | solution.py:22
  72.5 0.2 pad_maximum_fusion.1
  72.7 0.4 fusion.19
  73.1 0.3 fusion.21
  73.4 0.3 fusion.17
  73.7 0.4 maximum_maximum_fusion
  74.1 0.3 fusion.11
  74.4 0.3 fusion.13
  74.8 0.3 fusion.15
  75.1 0.4 fusion.23
  75.4 0.4 fusion.25
  75.8 0.8 %select_convert_fusion = bf16[8,8,16,136]{3,1,2,0:T(8,128)(2,1)S(1)} fusion(f32[8,16,136,8]{2,3,1,0:T(8,128)S(1)} %fusion.11, f32[8,16,136,8]{2,3,1,0:T(8,128)S(1)} %fusion.13, f32[8,16,136,8]{2,3,1,0:T(8,128)S(1)} %fusion.15, f32[8,16,136,8]{2,3,1,0:T(8,128)S(1)} %fusion.17, f32[8,16,136,8]{2,3,1,0:T(8,128)S(1)} %fusion.19, ...), kind=kOutput, calls=%fused_computation.23 | convolution fusion | flops 4177920 | bytes 5032192 | tf_op jit(solution)/shard_map/oc,mcij->moij/dot_general | solution.py:162
  76.6 0.2 fusion.36
  76.8 0.2 convolution_add_fusion.8
  77.0 0.2 convolution_add_fusion.7
  77.3 0.2 convolution_add_fusion.6
  77.5 0.2 convolution_add_fusion.5
  77.7 0.2 convolution_add_fusion.4
  77.9 0.2 convolution_add_fusion.3
  78.1 0.2 convolution_add_fusion.2
  78.3 0.2 fusion.10
  78.6 0.7 copy.100
  (51 shorter events, 2.0 us)
Async XLA Ops:
  0.0 11.3 %copy-start = (bf16[64,64]{1,0:T(8,128)(2,1)S(1)}, bf16[64,64]{1,0:T(8,128)(2,1)}, u32[]{:S(2)}) copy-start(bf16[64,64]{1,0:T(8,128)(2,1)} %param.20) | copy-start | bytes 24580
  3.2 6.6 %copy-start.5 = (bf16[64,192]{1,0:T(8,128)(2,1)S(1)}, bf16[64,192]{1,0:T(8,128)(2,1)}, u32[]{:S(2)}) copy-start(bf16[64,192]{1,0:T(8,128)(2,1)} %param.18) | copy-start | bytes 73732
  3.3 9.4 %copy-start.7 = (f32[64]{0:T(128)S(1)}, f32[64]{0:T(128)}, u32[]{:S(2)}) copy-start(f32[64]{0:T(128)} %param.17) | copy-start | bytes 772
  3.3 10.0 %copy-start.6 = (bf16[8,64]{1,0:T(8,128)(2,1)S(1)}, bf16[8,64]{1,0:T(8,128)(2,1)}, u32[]{:S(2)}) copy-start(bf16[8,64]{1,0:T(8,128)(2,1)} %param.16) | copy-start | bytes 3076
  3.3 10.7 %copy-start.8 = (f32[4]{0:T(128)S(1)}, f32[4]{0:T(128)}, u32[]{:S(2)}) copy-start(f32[4]{0:T(128)} %param.19) | copy-start | bytes 52
  3.4 11.3 %copy-start.1 = (bf16[9,8,8]{0,2,1:T(8,128)(2,1)S(1)}, bf16[9,8,8]{0,2,1:T(8,128)(2,1)}, u32[]{:S(2)}) copy-start(bf16[9,8,8]{0,2,1:T(8,128)(2,1)} %param.22) | copy-start | bytes 3460
  3.4 11.5 %copy-start.2 = (bf16[9,8,8]{0,2,1:T(8,128)(2,1)S(1)}, bf16[9,8,8]{0,2,1:T(8,128)(2,1)}, u32[]{:S(2)}) copy-start(bf16[9,8,8]{0,2,1:T(8,128)(2,1)} %param.23) | copy-start | bytes 3460
  3.4 16.5 %collective-permute-start = (f32[5,8,4,512]{3,1,2,0:T(8,128)S(1)}, f32[5,8,4,512]{3,1,2,0:T(8,128)S(1)}, u32[]{:S(2)}, u32[]{:S(2)}) collective-permute-start(f32[5,8,4,512]{3,1,2,0:T(8,128)S(1)} %get-tuple-element.14), channel_id=1, source_target_pairs={{0,1},{1,2},{2,3},{3,4},{4,5},{5,6},{6,7},{8,9},{9,10},{10,11},{11... | collective-permute-start | bytes 983048 | tf_op jit(solution)/shard_map/ppermute | solution.py:19
  6.6 16.3 %collective-permute-start.1 = (f32[5,8,4,512]{3,1,2,0:T(8,128)S(1)}, f32[5,8,4,512]{3,1,2,0:T(8,128)S(1)}, u32[]{:S(2)}, u32[]{:S(2)}) collective-permute-start(f32[5,8,4,512]{3,1,2,0:T(8,128)S(1)} %get-tuple-element.15), channel_id=1, source_target_pairs={{1,0},{2,1},{3,2},{4,3},{5,4},{6,5},{7,6},{9,8},{10,9},{11,10},{12... | collective-permute-start | bytes 983048 | tf_op jit(solution)/shard_map/ppermute | solution.py:22
  25.5 7.4 %all-to-all-start = ((bf16[4,8,8,256]{3,2,1,0:T(8,128)(2,1)}), bf16[4,8,8,256]{3,2,1,0:T(8,128)(2,1)S(1)}, u32[]{:S(2)}, u32[]{:S(2)}) async-start(bf16[4,8,8,256]{3,2,1,0:T(8,128)(2,1)} %copy_bitcast_fusion.1), calls=%async_computation | async-start | bytes 262144 | tf_op jit(solution)/shard_map/all_to_all | solution.py:210
  32.9 0.7 copy-start.4
  49.0 7.3 %collective-permute-start.2 = (bf16[8,8,8,8]{3,1,2,0:T(8,128)(2,1)S(1)}, bf16[8,8,8,8]{3,1,2,0:T(8,128)(2,1)S(1)}, u32[]{:S(2)}, u32[]{:S(2)}) collective-permute-start(bf16[8,8,8,8]{3,1,2,0:T(8,128)(2,1)S(1)} %get-tuple-element.18), channel_id=1, source_target_pairs={{0,8},{8,16},{16,24},{1,9},{9,17},{17,25},{2,10},{10,18},{18,26},{... | collective-permute-start | bytes 24584 | tf_op jit(solution)/shard_map/ppermute | solution.py:19
  51.9 6.3 %collective-permute-start.3 = (bf16[8,8,8,8]{3,1,2,0:T(8,128)(2,1)S(1)}, bf16[8,8,8,8]{3,1,2,0:T(8,128)(2,1)S(1)}, u32[]{:S(2)}, u32[]{:S(2)}) collective-permute-start(bf16[8,8,8,8]{3,1,2,0:T(8,128)(2,1)S(1)} %get-tuple-element.19), channel_id=1, source_target_pairs={{8,0},{16,8},{24,16},{9,1},{17,9},{25,17},{10,2},{18,10},{26,18},{... | collective-permute-start | bytes 24584 | tf_op jit(solution)/shard_map/ppermute | solution.py:22
  58.4 11.4 %collective-permute-start.4 = (bf16[8,8,8,144]{3,1,2,0:T(8,128)(2,1)S(1)}, bf16[8,8,8,144]{3,1,2,0:T(8,128)(2,1)S(1)}, u32[]{:S(2)}, u32[]{:S(2)}) collective-permute-start(bf16[8,8,8,144]{3,1,2,0:T(8,128)(2,1)S(1)} %pad_maximum_fusion.4), channel_id=1, source_target_pairs={{0,1},{1,2},{2,3},{3,4},{4,5},{5,6},{6,7},{8,9},{9,10},{10,11},{11... | collective-permute-start | bytes 442376 | tf_op jit(solution)/shard_map/ppermute | solution.py:19
  60.6 11.9 %collective-permute-start.5 = (bf16[8,8,8,144]{3,1,2,0:T(8,128)(2,1)S(1)}, bf16[8,8,8,144]{3,1,2,0:T(8,128)(2,1)S(1)}, u32[]{:S(2)}, u32[]{:S(2)}) collective-permute-start(bf16[8,8,8,144]{3,1,2,0:T(8,128)(2,1)S(1)} %pad_maximum_fusion.4), channel_id=1, source_target_pairs={{1,0},{2,1},{3,2},{4,3},{5,4},{6,5},{7,6},{9,8},{10,9},{11,10},{12... | collective-permute-start | bytes 442376 | tf_op jit(solution)/shard_map/ppermute | solution.py:22
  77.4 0.9 %copy-start.3 = (bf16[8,8,1024]{2,1,0:T(8,128)(2,1)S(1)}, bf16[8,8,1024]{2,1,0:T(8,128)(2,1)}, u32[]{:S(2)}) copy-start(bf16[8,8,1024]{2,1,0:T(8,128)(2,1)} %shard_map.118) | copy-start | bytes 393220

commit v7 on v5

--- a/solution.py
+++ b/solution.py
@@ -22,6 +22,17 @@
         high = lax.ppermute(lax.slice_in_dim(block, 0, width, axis=dim), axis, backward)
         block = jnp.concatenate([low, block, high], axis=dim)
     return block
+
+
+def strips_padded(block, axis, width):
+    count = lax.axis_size(axis)
+    forward = [(i, i + 1) for i in range(count - 1)]
+    backward = [(target, source) for source, target in forward]
+    shape = block.shape[:-1] + (width,)
+    flat = block.shape[:-2] + (block.shape[-2] * width,)
+    low = lax.ppermute(block[..., block.shape[-1] - width :].reshape(flat), axis, forward)
+    high = lax.ppermute(block[..., :width].reshape(flat), axis, backward)
+    return jnp.concatenate([low.reshape(shape), block, high.reshape(shape)], axis=-1)
 
 
 def advance(padded_field, wind_east, wind_north, diffusivity):
@@ -219,7 +230,7 @@
     features = jnp.transpose(step_result, (2, 1, 0, 3))
     tile_cols = features.shape[3]
     span = DILATION_SPAN
-    padded_feature = padded(features, (("mem", 3), ("row", 2)), 2 * span)
+    padded_feature = strips_padded(padded(features, (("row", 2),), 2 * span), "mem", 2 * span)
     first = jax.nn.silu(convolve(padded_feature, first_kernel))
     row_ids = lax.axis_index("row") * tile_rows - span + jnp.arange(tile_rows + 2 * span)
     col_ids = lax.axis_index("mem") * tile_cols - span + jnp.arange(tile_cols + 2 * span)

time: 75.3 us -> 73.7 us (0.979)
  waiting for transfers between devices: 21.3 us -> 17.5 us
  local copies, waits for them, and re-layouts: 13.5 us -> 14.9 us
    ppermute x0 -> x2, starting transfers between devices: none -> 5.56 us  [the longest x1 3.21 us: strips_padded(): lax.ppermute(block[..., block.shape[-1] - width:].reshape(flat), axis, fo...]
    all_to_all x1, waiting for transfers between devices: 3.59 us -> 0.01 us  [on_device(): lax.all_to_all(by_chunk, 'mem', split_axis=0, concat_axis=0, tiled=True)]
    ppermute x3 -> x2, starting transfers between devices: 8.25 us -> 5.34 us  [padded(): lax.ppermute(lax.slice_in_dim(block, block.shape[dim] - width, None, axis...]
    ppermute x3 -> x2, starting transfers between devices: 8.94 us -> 7.02 us  [padded(): lax.ppermute(lax.slice_in_dim(block, 0, width, axis=dim), axis, backward)]
    ppermute x3 -> x2, waiting for transfers between devices: 7.55 us -> 6.14 us  [padded(): lax.ppermute(lax.slice_in_dim(block, 0, width, axis=dim), axis, backward)]
    reshape x0 -> x6, local copies, waits for them, and re-layouts: none -> 1.3 us  [the longest x2 0.39 us: strips_padded(): high.reshape(shape)]
    ppermute x3 -> x2, waiting for transfers between devices: 10.1 us -> 11.3 us  [padded(): lax.ppermute(lax.slice_in_dim(block, block.shape[dim] - width, None, axis...]
    concatenate x4 -> x2, other arithmetic: 0.89 us -> 0.14 us  [padded(): block = jnp.concatenate([low, block, high], axis=dim)]
  transfers between devices with their start and end apart: 7 -> 7, of which waited for: 6 -> 4; matrix products, arithmetic and copies ran while one was open for 10% -> 11% of each run, Pallas kernels for 0% -> 0%
where the time goes in v7:
time: 73.7 us; the launch traced here: 72.9 us
  starting transfers between devices  21.7 us (29%)
  waiting for transfers between devices  17.5 us (24%)
  local copies, waits for them, and re-layouts  14.9 us (20%)
  Pallas kernels  9.91 us (13%)
  matrix products  5.26 us (7%)
  other arithmetic  3.01 us (4%)
    ppermute x2, waiting for transfers between devices, padded(): lax.ppermute(lax.slice_in_dim(block, block.shape[dim] - width, None, axis...  11.3 us
    pallas_call x1, Pallas kernels, post_block(): pl.pallas_call(functools.partial(attention_kernel, chunk=chunk, heads=hea...  9.91 us
    unnamed x41, local copies, waits for them, and re-layouts  7.15 us
    ppermute x2, starting transfers between devices, padded(): lax.ppermute(lax.slice_in_dim(block, 0, width, axis=dim), axis, backward)  7.02 us
    ppermute x2, waiting for transfers between devices, padded(): lax.ppermute(lax.slice_in_dim(block, 0, width, axis=dim), axis, backward)  6.14 us
    ppermute x2, starting transfers between devices, padded(): lax.ppermute(lax.slice_in_dim(block, block.shape[dim] - width, None, axis...  5.34 us
    dot_general x18, matrix products, convolve(): jnp.einsum('oc,mcij->moij', kernel[row_stencil * 3 + column_stencil], shi...  5.26 us
    all_to_all x1, starting transfers between devices, on_device(): lax.all_to_all(by_chunk, 'mem', split_axis=0, concat_axis=0, tiled=True)  3.79 us
  transfers between devices with their start and end apart: 7, of which 4 were waited for; matrix products, arithmetic and copies ran while one was open for 11% of the time, Pallas kernels for 0%

profile of v7, /device:TPU:9, one launch (start us, length us, event | category | flops | bytes accessed | tf_op | source)
XLA Modules:
  0.0 72.9 jit_solution(8051230533770584011)
XLA Ops:
  0.0 1.0 %copy.159 = f32[8,8,512]{2,0,1:T(8,128)S(1)} copy(f32[8,8,512]{2,1,0:T(8,128)} %param.15) | data formatting | bytes 262144 | tf_op args[3]
  1.0 1.1 %copy.75 = f32[2,8,8,512]{3,1,2,0:T(8,128)S(1)} copy(f32[2,8,8,512]{3,2,1,0:T(8,128)} %param.12) | data formatting | bytes 524288 | tf_op args[0]
  2.1 1.1 %fusion.50 = (f32[8,8,512]{2,0,1:T(8,128)S(1)}, f32[1,8,8,512]{3,1,2,0:T(8,128)S(1)}, f32[1,8,8,512]{3,1,2,0:T(8,128)S(1)}, f32[8,8,512]{2,0,1:T(8,128)S(1)}) fusion(f32[8,8,512]{2,1,0:T(8,128)} %param.13, f32[8,8,512]{2,1,0:T(8,128)} %param.14), kind=kLoop, calls=%fused_computation.106 | loop fusion | bytes 786432 | tf_op args[1]
  3.4 3.1 %collective-permute-start = (f32[5,8,4,512]{3,1,2,0:T(8,128)S(1)}, f32[5,8,4,512]{3,1,2,0:T(8,128)S(1)}, u32[]{:S(2)}, u32[]{:S(2)}) collective-permute-start(f32[5,8,4,512]{3,1,2,0:T(8,128)S(1)} %get-tuple-element.14), channel_id=1, source_target_pairs={{0,1},{1,2},{2,3},{3,4},{4,5},{5,6},{6,7},{8,9},{9,10},{10,11},{11... | collective-permute-start | bytes 983048 | tf_op jit(solution)/shard_map/ppermute | solution.py:19
  6.5 3.1 %collective-permute-start.1 = (f32[5,8,4,512]{3,1,2,0:T(8,128)S(1)}, f32[5,8,4,512]{3,1,2,0:T(8,128)S(1)}, u32[]{:S(2)}, u32[]{:S(2)}) collective-permute-start(f32[5,8,4,512]{3,1,2,0:T(8,128)S(1)} %get-tuple-element.15), channel_id=1, source_target_pairs={{1,0},{2,1},{3,2},{4,3},{5,4},{6,5},{7,6},{9,8},{10,9},{11,10},{12... | collective-permute-start | bytes 983048 | tf_op jit(solution)/shard_map/ppermute | solution.py:22
  10.2 9.7 %collective-permute-done = f32[5,8,4,512]{3,1,2,0:T(8,128)S(1)} collective-permute-done((f32[5,8,4,512]{3,1,2,0:T(8,128)S(1)}, f32[5,8,4,512]{3,1,2,0:T(8,128)S(1)}, u32[]{:S(2)}, u32[]{:S(2)}) %collective-permute-start) | collective-permute-done | bytes 327712 | tf_op jit(solution)/shard_map/ppermute | solution.py:19
  19.9 2.9 %collective-permute-done.1 = f32[5,8,4,512]{3,1,2,0:T(8,128)S(1)} collective-permute-done((f32[5,8,4,512]{3,1,2,0:T(8,128)S(1)}, f32[5,8,4,512]{3,1,2,0:T(8,128)S(1)}, u32[]{:S(2)}, u32[]{:S(2)}) %collective-permute-start.1) | collective-permute-done | bytes 327712 | tf_op jit(solution)/shard_map/ppermute | solution.py:22
  23.1 0.5 add_select_fusion
  23.6 0.4 add_select_fusion.1
  24.1 0.4 add_select_fusion.2
  24.5 0.9 %copy_bitcast_fusion.1 = bf16[4,8,8,256]{3,2,1,0:T(8,128)(2,1)} fusion(f32[2,8,8,512]{3,1,2,0:T(8,128)S(1)} %slice.337, f32[8,8,512]{2,0,1:T(8,128)S(1)} %copy.159, f32[2,8,10,512]{3,1,2,0:T(8,128)S(1)} %add_select_fusion.2, f32[8,8,512]{2,0,1:T(8,128)S(1)} %get-tuple-element.43, f32[8,8,512]{2,0,1:T(8,128)S(1)} %get-tuple-element.18, ...), kind=kLoop, calls=%fused_computation.67 | loop fusion | flops 1310720 | bytes 1311232 | tf_op jit(solution)/shard_map/reshape | solution.py:213
  25.5 3.8 %all-to-all-start = ((bf16[4,8,8,256]{3,2,1,0:T(8,128)(2,1)}), bf16[4,8,8,256]{3,2,1,0:T(8,128)(2,1)S(1)}, u32[]{:S(2)}, u32[]{:S(2)}) async-start(bf16[4,8,8,256]{3,2,1,0:T(8,128)(2,1)} %copy_bitcast_fusion.1), calls=%async_computation | async-start | bytes 262144 | tf_op jit(solution)/shard_map/all_to_all | solution.py:216
  29.3 0.7 gather_fusion
  29.9 0.6 copy.83
  30.5 0.6 gather_fusion.1
  31.2 0.7 copy.84
  31.9 0.7 copy.86.gain_ref
  32.6 0.7 copy.80
  33.3 0.7 reshape_tile.4.hs_ref
  33.9 0.7 copy-done.4
  34.6 9.9 %shard_map.118 = bf16[8,8,1024]{2,1,0:T(8,128)(2,1)} custom-call(f32[8,1]{1,0:T(8,128)} %reshape_tile.4.hs_ref, bf16[4,8,8,256]{3,2,1,0:T(8,128)(2,1)} %copy-done.4, bf16[64,8]{1,0:T(8,128)(2,1)} %bitcast.199, f32[64,1]{1,0:T(8,128)} %copy.86.gain_ref, bf16[192,64]{1,0:T(8,128)(2,1)} %bitcast.196, bf16[64,64]{1,0:T(8,128)(2,1)} %bitcast.198, ...), custom_call_target="tpu_custom_call" | custom-call | tf_op jit(solution)/shard_map/pallas_call | solution.py:140
  44.5 0.9 %copy_bitcast_fusion = bf16[8,8,8,128]{3,1,2,0:T(8,128)(2,1)S(1)} fusion(bf16[8,8,1024]{2,1,0:T(8,128)(2,1)} %shard_map.118), kind=kLoop, calls=%fused_computation.66 | loop fusion | bytes 262144 | tf_op jit(solution)/shard_map/transpose | solution.py:230
  45.4 2.2 %collective-permute-start.2 = (bf16[8,8,8,128]{3,1,2,0:T(8,128)(2,1)S(1)}, bf16[8,8,8,128]{3,1,2,0:T(8,128)(2,1)S(1)}, u32[]{:S(2)}, u32[]{:S(2)}) collective-permute-start(bf16[8,8,8,128]{3,1,2,0:T(8,128)(2,1)S(1)} %copy_bitcast_fusion), channel_id=1, source_target_pairs={{0,1},{1,2},{2,3},{3,4},{4,5},{5,6},{6,7},{8,9},{9,10},{10,11},{11... | collective-permute-start | bytes 393224 | tf_op jit(solution)/shard_map/ppermute | solution.py:19
  47.7 4.0 %collective-permute-start.3 = (bf16[8,8,8,128]{3,1,2,0:T(8,128)(2,1)S(1)}, bf16[8,8,8,128]{3,1,2,0:T(8,128)(2,1)S(1)}, u32[]{:S(2)}, u32[]{:S(2)}) collective-permute-start(bf16[8,8,8,128]{3,1,2,0:T(8,128)(2,1)S(1)} %copy_bitcast_fusion), channel_id=1, source_target_pairs={{1,0},{2,1},{3,2},{4,3},{5,4},{6,5},{7,6},{9,8},{10,9},{11,10},{12... | collective-permute-start | bytes 393224 | tf_op jit(solution)/shard_map/ppermute | solution.py:22
  51.7 1.6 %collective-permute-done.2 = bf16[8,8,8,128]{3,1,2,0:T(8,128)(2,1)S(1)} collective-permute-done((bf16[8,8,8,128]{3,1,2,0:T(8,128)(2,1)S(1)}, bf16[8,8,8,128]{3,1,2,0:T(8,128)(2,1)S(1)}, u32[]{:S(2)}, u32[]{:S(2)}) %collective-permute-start.2) | collective-permute-done | bytes 131104 | tf_op jit(solution)/shard_map/ppermute | solution.py:19
  53.3 3.2 %collective-permute-done.3 = bf16[8,8,8,128]{3,1,2,0:T(8,128)(2,1)S(1)} collective-permute-done((bf16[8,8,8,128]{3,1,2,0:T(8,128)(2,1)S(1)}, bf16[8,8,8,128]{3,1,2,0:T(8,128)(2,1)S(1)}, u32[]{:S(2)}, u32[]{:S(2)}) %collective-permute-start.3) | collective-permute-done | bytes 131104 | tf_op jit(solution)/shard_map/ppermute | solution.py:22
  56.5 0.2 fusion.49
  56.8 0.3 reshape.165
  57.1 2.4 %collective-permute-start.5 = (bf16[8,8,192]{2,1,0:T(8,128)(2,1)S(1)}, bf16[8,8,192]{2,1,0:T(8,128)(2,1)S(1)}, u32[]{:S(2)}, u32[]{:S(2)}) collective-permute-start(bf16[8,8,192]{2,1,0:T(8,128)(2,1)S(1)} %reshape.165), channel_id=1, source_target_pairs={{8,0},{16,8},{24,16},{9,1},{17,9},{25,17},{10,2},{18,10},{26,18},{... | collective-permute-start | bytes 73736 | tf_op jit(solution)/shard_map/ppermute | solution.py:34
  59.5 0.3 reshape.163
  59.8 3.2 %collective-permute-start.4 = (bf16[8,8,192]{2,1,0:T(8,128)(2,1)S(1)}, bf16[8,8,192]{2,1,0:T(8,128)(2,1)S(1)}, u32[]{:S(2)}, u32[]{:S(2)}) collective-permute-start(bf16[8,8,192]{2,1,0:T(8,128)(2,1)S(1)} %reshape.163), channel_id=1, source_target_pairs={{0,8},{8,16},{16,24},{1,9},{9,17},{17,25},{2,10},{10,18},{18,26},{... | collective-permute-start | bytes 73736 | tf_op jit(solution)/shard_map/ppermute | solution.py:33
  63.7 0.1 copy.137
  63.9 0.1 copy.138
  64.0 0.1 copy.136
  64.1 0.1 copy.139
  64.3 0.1 copy.140
  64.4 0.1 copy.141
  64.5 0.1 copy.142
  64.7 0.1 copy.143
  64.8 0.1 copy.144
  65.1 0.1 copy.146
  65.4 0.1 copy.148
  65.5 0.3 reshape.166
  65.9 0.3 reshape.164
  66.3 0.5 pad_maximum_fusion.1
  66.8 0.3 fusion.11
  67.1 0.3 fusion.13
  67.5 0.3 fusion.9
  67.8 0.3 fusion.43
  68.1 0.4 fusion.41
  68.5 0.4 fusion.37
  68.9 0.5 fusion.3
  69.3 0.3 fusion.5
  69.7 0.5 select_convert_fusion
  70.2 0.2 fusion.23
  70.4 0.2 convolution_add_fusion.10
  70.6 0.2 convolution_add_fusion.9
  70.9 0.2 convolution_add_fusion.8
  71.0 0.2 convolution_add_fusion.7
  71.3 0.2 convolution_add_fusion.6
  71.5 0.2 convolution_add_fusion.5
  71.7 0.2 convolution_add_fusion.4
  71.9 0.2 fusion.8
  72.2 0.7 copy.112
  (58 shorter events, 2.3 us)
Async XLA Ops:
  0.0 30.5 %copy-start = (bf16[64,64]{1,0:T(8,128)(2,1)S(1)}, bf16[64,64]{1,0:T(8,128)(2,1)}, u32[]{:S(2)}) copy-start(bf16[64,64]{1,0:T(8,128)(2,1)} %param.20) | copy-start | bytes 24580
  3.2 6.5 %copy-start.5 = (bf16[64,192]{1,0:T(8,128)(2,1)S(1)}, bf16[64,192]{1,0:T(8,128)(2,1)}, u32[]{:S(2)}) copy-start(bf16[64,192]{1,0:T(8,128)(2,1)} %param.18) | copy-start | bytes 73732
  3.3 6.7 %copy-start.1 = (bf16[9,8,8]{0,2,1:T(8,128)(2,1)S(1)}, bf16[9,8,8]{0,2,1:T(8,128)(2,1)}, u32[]{:S(2)}) copy-start(bf16[9,8,8]{0,2,1:T(8,128)(2,1)} %param.22) | copy-start | bytes 3460
  3.3 6.8 %copy-start.2 = (bf16[9,8,8]{0,2,1:T(8,128)(2,1)S(1)}, bf16[9,8,8]{0,2,1:T(8,128)(2,1)}, u32[]{:S(2)}) copy-start(bf16[9,8,8]{0,2,1:T(8,128)(2,1)} %param.23) | copy-start | bytes 3460
  3.4 16.5 %collective-permute-start = (f32[5,8,4,512]{3,1,2,0:T(8,128)S(1)}, f32[5,8,4,512]{3,1,2,0:T(8,128)S(1)}, u32[]{:S(2)}, u32[]{:S(2)}) collective-permute-start(f32[5,8,4,512]{3,1,2,0:T(8,128)S(1)} %get-tuple-element.14), channel_id=1, source_target_pairs={{0,1},{1,2},{2,3},{3,4},{4,5},{5,6},{6,7},{8,9},{9,10},{10,11},{11... | collective-permute-start | bytes 983048 | tf_op jit(solution)/shard_map/ppermute | solution.py:19
  6.5 16.3 %collective-permute-start.1 = (f32[5,8,4,512]{3,1,2,0:T(8,128)S(1)}, f32[5,8,4,512]{3,1,2,0:T(8,128)S(1)}, u32[]{:S(2)}, u32[]{:S(2)}) collective-permute-start(f32[5,8,4,512]{3,1,2,0:T(8,128)S(1)} %get-tuple-element.15), channel_id=1, source_target_pairs={{1,0},{2,1},{3,2},{4,3},{5,4},{6,5},{7,6},{9,8},{10,9},{11,10},{12... | collective-permute-start | bytes 983048 | tf_op jit(solution)/shard_map/ppermute | solution.py:22
  24.5 7.4 %copy-start.7 = (f32[64]{0:T(128)S(1)}, f32[64]{0:T(128)}, u32[]{:S(2)}) copy-start(f32[64]{0:T(128)} %param.17) | copy-start | bytes 772
  24.5 8.1 %copy-start.6 = (bf16[8,64]{1,0:T(8,128)(2,1)S(1)}, bf16[8,64]{1,0:T(8,128)(2,1)}, u32[]{:S(2)}) copy-start(bf16[8,64]{1,0:T(8,128)(2,1)} %param.16) | copy-start | bytes 3076
  24.5 8.8 %copy-start.8 = (f32[4]{0:T(128)S(1)}, f32[4]{0:T(128)}, u32[]{:S(2)}) copy-start(f32[4]{0:T(128)} %param.19) | copy-start | bytes 52
  25.5 8.5 %all-to-all-start = ((bf16[4,8,8,256]{3,2,1,0:T(8,128)(2,1)}), bf16[4,8,8,256]{3,2,1,0:T(8,128)(2,1)S(1)}, u32[]{:S(2)}, u32[]{:S(2)}) async-start(bf16[4,8,8,256]{3,2,1,0:T(8,128)(2,1)} %copy_bitcast_fusion.1), calls=%async_computation | async-start | bytes 262144 | tf_op jit(solution)/shard_map/all_to_all | solution.py:216
  33.9 0.7 copy-start.4
  45.4 7.9 %collective-permute-start.2 = (bf16[8,8,8,128]{3,1,2,0:T(8,128)(2,1)S(1)}, bf16[8,8,8,128]{3,1,2,0:T(8,128)(2,1)S(1)}, u32[]{:S(2)}, u32[]{:S(2)}) collective-permute-start(bf16[8,8,8,128]{3,1,2,0:T(8,128)(2,1)S(1)} %copy_bitcast_fusion), channel_id=1, source_target_pairs={{0,1},{1,2},{2,3},{3,4},{4,5},{5,6},{6,7},{8,9},{9,10},{10,11},{11... | collective-permute-start | bytes 393224 | tf_op jit(solution)/shard_map/ppermute | solution.py:19
  47.7 8.8 %collective-permute-start.3 = (bf16[8,8,8,128]{3,1,2,0:T(8,128)(2,1)S(1)}, bf16[8,8,8,128]{3,1,2,0:T(8,128)(2,1)S(1)}, u32[]{:S(2)}, u32[]{:S(2)}) collective-permute-start(bf16[8,8,8,128]{3,1,2,0:T(8,128)(2,1)S(1)} %copy_bitcast_fusion), channel_id=1, source_target_pairs={{1,0},{2,1},{3,2},{4,3},{5,4},{6,5},{7,6},{9,8},{10,9},{11,10},{12... | collective-permute-start | bytes 393224 | tf_op jit(solution)/shard_map/ppermute | solution.py:22
  57.1 8.4 %collective-permute-start.5 = (bf16[8,8,192]{2,1,0:T(8,128)(2,1)S(1)}, bf16[8,8,192]{2,1,0:T(8,128)(2,1)S(1)}, u32[]{:S(2)}, u32[]{:S(2)}) collective-permute-start(bf16[8,8,192]{2,1,0:T(8,128)(2,1)S(1)} %reshape.165), channel_id=1, source_target_pairs={{8,0},{16,8},{24,16},{9,1},{17,9},{25,17},{10,2},{18,10},{26,18},{... | collective-permute-start | bytes 73736 | tf_op jit(solution)/shard_map/ppermute | solution.py:34
  59.8 6.1 %collective-permute-start.4 = (bf16[8,8,192]{2,1,0:T(8,128)(2,1)S(1)}, bf16[8,8,192]{2,1,0:T(8,128)(2,1)S(1)}, u32[]{:S(2)}, u32[]{:S(2)}) collective-permute-start(bf16[8,8,192]{2,1,0:T(8,128)(2,1)S(1)} %reshape.163), channel_id=1, source_target_pairs={{0,8},{8,16},{16,24},{1,9},{9,17},{17,25},{2,10},{10,18},{18,26},{... | collective-permute-start | bytes 73736 | tf_op jit(solution)/shard_map/ppermute | solution.py:33
  71.0 0.9 %copy-start.3 = (bf16[8,8,1024]{2,1,0:T(8,128)(2,1)S(1)}, bf16[8,8,1024]{2,1,0:T(8,128)(2,1)}, u32[]{:S(2)}) copy-start(bf16[8,8,1024]{2,1,0:T(8,128)(2,1)} %shard_map.118) | copy-start | bytes 393220

commit v8 on v5

--- a/solution.py
+++ b/solution.py
@@ -22,6 +22,40 @@
         high = lax.ppermute(lax.slice_in_dim(block, 0, width, axis=dim), axis, backward)
         block = jnp.concatenate([low, block, high], axis=dim)
     return block
+
+
+def flat(x):
+    return x.reshape(x.shape[:-2] + (x.shape[-2] * x.shape[-1],))
+
+
+def shifted(x, axis, shape):
+    count = lax.axis_size(axis)
+    forward = [(i, i + 1) for i in range(count - 1)]
+    backward = [(target, source) for source, target in forward]
+    low, high = x
+    return (
+        lax.ppermute(flat(low), axis, forward).reshape(shape),
+        lax.ppermute(flat(high), axis, backward).reshape(shape),
+    )
+
+
+def halo_2d(block, width):
+    rows, cols = block.shape[-2:]
+    lead = block.shape[:-2]
+    up, down = shifted(
+        (block[..., rows - width :, :], block[..., :width, :]), "row", lead + (width, cols)
+    )
+    left, right = shifted(
+        (block[..., cols - width :], block[..., :width]), "mem", lead + (rows, width)
+    )
+    sides = jnp.concatenate([left, right], axis=-1)
+    up_corner, down_corner = shifted(
+        (sides[..., rows - width :, :], sides[..., :width, :]), "row", lead + (width, 2 * width)
+    )
+    top = jnp.concatenate([up_corner[..., :width], up, up_corner[..., width:]], axis=-1)
+    middle = jnp.concatenate([left, block, right], axis=-1)
+    bottom = jnp.concatenate([down_corner[..., :width], down, down_corner[..., width:]], axis=-1)
+    return jnp.concatenate([top, middle, bottom], axis=-2)
 
 
 def advance(padded_field, wind_east, wind_north, diffusivity):
@@ -219,7 +253,7 @@
     features = jnp.transpose(step_result, (2, 1, 0, 3))
     tile_cols = features.shape[3]
     span = DILATION_SPAN
-    padded_feature = padded(features, (("mem", 3), ("row", 2)), 2 * span)
+    padded_feature = halo_2d(features, 2 * span)
     first = jax.nn.silu(convolve(padded_feature, first_kernel))
     row_ids = lax.axis_index("row") * tile_rows - span + jnp.arange(tile_rows + 2 * span)
     col_ids = lax.axis_index("mem") * tile_cols - span + jnp.arange(tile_cols + 2 * span)

time: 75.3 us -> 77.6 us (1.031)
  the two profiles are of different devices: /device:TPU:9 before, /device:TPU:22 now
where the time goes in v8:
time: 77.6 us; the launch traced here: 77.1 us
  starting transfers between devices  27.8 us (36%)
  waiting for transfers between devices  15.2 us (20%)
  local copies, waits for them, and re-layouts  14.7 us (19%)
  Pallas kernels  9.92 us (13%)
  matrix products  5.01 us (6%)
  other arithmetic  3.71 us (5%)
    ppermute x3, starting transfers between devices, shifted(): lax.ppermute(flat(high), axis, backward).reshape(shape)  9.95 us
    pallas_call x1, Pallas kernels, post_block(): pl.pallas_call(functools.partial(attention_kernel, chunk=chunk, heads=hea...  9.92 us
    ppermute x3, starting transfers between devices, shifted(): lax.ppermute(flat(low), axis, forward).reshape(shape)  8.2 us
    ppermute x1, waiting for transfers between devices, padded(): lax.ppermute(lax.slice_in_dim(block, block.shape[dim] - width, None, axis...  7.24 us
    unnamed x45, local copies, waits for them, and re-layouts  7.23 us
    ppermute x3, waiting for transfers between devices, shifted(): lax.ppermute(flat(high), axis, backward).reshape(shape)  5.02 us
    dot_general x18, matrix products, convolve(): jnp.einsum('oc,mcij->moij', kernel[row_stencil * 3 + column_stencil], shi...  5.01 us
    all_to_all x1, starting transfers between devices, on_device(): lax.all_to_all(by_chunk, 'mem', split_axis=0, concat_axis=0, tiled=True)  3.8 us
  transfers between devices with their start and end apart: 9, of which 4 were waited for; matrix products, arithmetic and copies ran while one was open for 11% of the time, Pallas kernels for 0%

profile of v8, /device:TPU:22, one launch (start us, length us, event | category | flops | bytes accessed | tf_op | source)
XLA Modules:
  0.0 77.1 jit_solution(12281749429553281998)
XLA Ops:
  0.0 1.0 %copy.168 = f32[8,8,512]{2,0,1:T(8,128)S(1)} copy(f32[8,8,512]{2,1,0:T(8,128)} %param.15) | data formatting | bytes 262144 | tf_op args[3]
  1.0 1.1 %copy.77 = f32[2,8,8,512]{3,1,2,0:T(8,128)S(1)} copy(f32[2,8,8,512]{3,2,1,0:T(8,128)} %param.12) | data formatting | bytes 524288 | tf_op args[0]
  2.1 1.1 %fusion.48 = (f32[8,8,512]{2,0,1:T(8,128)S(1)}, f32[1,8,8,512]{3,1,2,0:T(8,128)S(1)}, f32[1,8,8,512]{3,1,2,0:T(8,128)S(1)}, f32[8,8,512]{2,0,1:T(8,128)S(1)}) fusion(f32[8,8,512]{2,1,0:T(8,128)} %param.13, f32[8,8,512]{2,1,0:T(8,128)} %param.14), kind=kLoop, calls=%fused_computation.110 | loop fusion | bytes 786432 | tf_op args[1]
  3.4 3.5 %collective-permute-start = (f32[5,8,4,512]{3,1,2,0:T(8,128)S(1)}, f32[5,8,4,512]{3,1,2,0:T(8,128)S(1)}, u32[]{:S(2)}, u32[]{:S(2)}) collective-permute-start(f32[5,8,4,512]{3,1,2,0:T(8,128)S(1)} %get-tuple-element.14), channel_id=1, source_target_pairs={{0,1},{1,2},{2,3},{3,4},{4,5},{5,6},{6,7},{8,9},{9,10},{10,11},{11... | collective-permute-start | bytes 983048 | tf_op jit(solution)/shard_map/ppermute | solution.py:19
  6.9 2.4 %collective-permute-start.1 = (f32[5,8,4,512]{3,1,2,0:T(8,128)S(1)}, f32[5,8,4,512]{3,1,2,0:T(8,128)S(1)}, u32[]{:S(2)}, u32[]{:S(2)}) collective-permute-start(f32[5,8,4,512]{3,1,2,0:T(8,128)S(1)} %get-tuple-element.15), channel_id=1, source_target_pairs={{1,0},{2,1},{3,2},{4,3},{5,4},{6,5},{7,6},{9,8},{10,9},{11,10},{12... | collective-permute-start | bytes 983048 | tf_op jit(solution)/shard_map/ppermute | solution.py:22
  9.7 0.7 gather_fusion
  10.3 0.6 copy.85
  10.9 0.6 gather_fusion.1
  11.6 0.7 copy.86
  12.3 0.7 copy.88.gain_ref
  13.0 0.7 copy.82
  13.7 0.7 reshape_tile.4.hs_ref
  14.6 7.2 %collective-permute-done = f32[5,8,4,512]{3,1,2,0:T(8,128)S(1)} collective-permute-done((f32[5,8,4,512]{3,1,2,0:T(8,128)S(1)}, f32[5,8,4,512]{3,1,2,0:T(8,128)S(1)}, u32[]{:S(2)}, u32[]{:S(2)}) %collective-permute-start) | collective-permute-done | bytes 327712 | tf_op jit(solution)/shard_map/ppermute | solution.py:19
  22.1 0.5 add_select_fusion
  22.6 0.4 add_select_fusion.1
  23.1 0.4 add_select_fusion.2
  23.5 0.9 %copy_bitcast_fusion = bf16[4,8,8,256]{3,2,1,0:T(8,128)(2,1)} fusion(f32[2,8,8,512]{3,1,2,0:T(8,128)S(1)} %slice.353, f32[8,8,512]{2,0,1:T(8,128)S(1)} %copy.168, f32[2,8,10,512]{3,1,2,0:T(8,128)S(1)} %add_select_fusion.2, f32[8,8,512]{2,0,1:T(8,128)S(1)} %get-tuple-element.51, f32[8,8,512]{2,0,1:T(8,128)S(1)} %get-tuple-element.26, ...), kind=kLoop, calls=%fused_computation.70 | loop fusion | flops 1310720 | bytes 1311232 | tf_op jit(solution)/shard_map/reshape | solution.py:236
  24.4 3.8 %all-to-all-start = ((bf16[4,8,8,256]{3,2,1,0:T(8,128)(2,1)}), bf16[4,8,8,256]{3,2,1,0:T(8,128)(2,1)S(1)}, u32[]{:S(2)}, u32[]{:S(2)}) async-start(bf16[4,8,8,256]{3,2,1,0:T(8,128)(2,1)} %copy_bitcast_fusion), calls=%async_computation | async-start | bytes 262144 | tf_op jit(solution)/shard_map/all_to_all | solution.py:239
  28.2 3.0 %all-to-all-done.x_ref = bf16[4,8,8,256]{3,2,1,0:T(8,128)(2,1)S(1)} async-done(((bf16[4,8,8,256]{3,2,1,0:T(8,128)(2,1)}), bf16[4,8,8,256]{3,2,1,0:T(8,128)(2,1)S(1)}, u32[]{:S(2)}, u32[]{:S(2)}) %all-to-all-start) | async-done | bytes 131104 | tf_op jit(solution)/shard_map/all_to_all | solution.py:239
  31.2 0.7 copy-done.4
  31.8 9.9 %shard_map.118 = bf16[8,8,1024]{2,1,0:T(8,128)(2,1)} custom-call(f32[8,1]{1,0:T(8,128)} %reshape_tile.4.hs_ref, bf16[4,8,8,256]{3,2,1,0:T(8,128)(2,1)} %copy-done.4, bf16[64,8]{1,0:T(8,128)(2,1)} %bitcast.210, f32[64,1]{1,0:T(8,128)} %copy.88.gain_ref, bf16[192,64]{1,0:T(8,128)(2,1)} %bitcast.207, bf16[64,64]{1,0:T(8,128)(2,1)} %bitcast.209, ...), custom_call_target="tpu_custom_call" | custom-call | tf_op jit(solution)/shard_map/pallas_call | solution.py:163
  41.7 0.9 %copy_bitcast_fusion.1 = (bf16[8,8,1024]{2,1,0:T(8,128)(2,1)S(1)}, bf16[8,8,8,128]{3,1,2,0:T(8,128)(2,1)S(1)}) fusion(bf16[8,8,1024]{2,1,0:T(8,128)(2,1)} %shard_map.118), kind=kLoop, calls=%fused_computation.72 | loop fusion | bytes 393216 | tf_op jit(solution)/shard_map/reshape | solution.py:28
  43.0 1.9 %collective-permute-start.2 = (bf16[8,8,64]{2,1,0:T(8,128)(2,1)S(1)}, bf16[8,8,64]{2,1,0:T(8,128)(2,1)S(1)}, u32[]{:S(2)}, u32[]{:S(2)}) collective-permute-start(bf16[8,8,64]{2,1,0:T(8,128)(2,1)S(1)} %reshape.183), channel_id=1, source_target_pairs={{0,8},{8,16},{16,24},{1,9},{9,17},{17,25},{2,10},{10,18},{18,26},{... | collective-permute-start | bytes 24584 | tf_op jit(solution)/shard_map/ppermute | solution.py:37
  45.0 3.6 %collective-permute-start.3 = (bf16[8,8,64]{2,1,0:T(8,128)(2,1)S(1)}, bf16[8,8,64]{2,1,0:T(8,128)(2,1)S(1)}, u32[]{:S(2)}, u32[]{:S(2)}) collective-permute-start(bf16[8,8,64]{2,1,0:T(8,128)(2,1)S(1)} %reshape.185), channel_id=1, source_target_pairs={{8,0},{16,8},{24,16},{9,1},{17,9},{25,17},{10,2},{18,10},{26,18},{... | collective-permute-start | bytes 24584 | tf_op jit(solution)/shard_map/ppermute | solution.py:38
  48.9 1.3 %collective-permute-done.3 = bf16[8,8,64]{2,1,0:T(8,128)(2,1)S(1)} collective-permute-done((bf16[8,8,64]{2,1,0:T(8,128)(2,1)S(1)}, bf16[8,8,64]{2,1,0:T(8,128)(2,1)S(1)}, u32[]{:S(2)}, u32[]{:S(2)}) %collective-permute-start.3) | collective-permute-done | bytes 8224 | tf_op jit(solution)/shard_map/ppermute | solution.py:38
  50.5 4.4 %collective-permute-start.4 = (bf16[8,8,128]{2,1,0:T(8,128)(2,1)S(1)}, bf16[8,8,128]{2,1,0:T(8,128)(2,1)S(1)}, u32[]{:S(2)}, u32[]{:S(2)}) collective-permute-start(bf16[8,8,128]{2,1,0:T(8,128)(2,1)S(1)} %reshape.187), channel_id=1, source_target_pairs={{0,1},{1,2},{2,3},{3,4},{4,5},{5,6},{6,7},{8,9},{9,10},{10,11},{11... | collective-permute-start | bytes 49160 | tf_op jit(solution)/shard_map/ppermute | solution.py:37
  55.6 0.1 copy.144
  55.7 0.1 copy.145
  55.9 0.1 copy.146
  56.0 0.1 copy.147
  56.1 0.1 copy.148
  56.3 0.1 copy.149
  56.4 0.1 copy.150
  56.5 0.1 copy.151
  56.7 0.1 copy.152
  56.8 0.1 copy.153
  57.0 0.1 copy.154
  57.1 0.1 copy.155
  57.2 0.1 copy.156
  57.4 1.9 %collective-permute-start.5 = (bf16[8,8,1024]{2,1,0:T(8,128)(2,1)S(1)}, bf16[8,8,1024]{2,1,0:T(8,128)(2,1)S(1)}, u32[]{:S(2)}, u32[]{:S(2)}) collective-permute-start(bf16[8,8,1024]{2,1,0:T(8,128)(2,1)S(1)} %get-tuple-element.22), channel_id=1, source_target_pairs={{0,1},{1,2},{2,3},{3,4},{4,5},{5,6},{6,7},{8,9},{9,10},{10,11},{11... | collective-permute-start | bytes 393224 | tf_op jit(solution)/shard_map/ppermute | solution.py:37
  59.3 3.9 %collective-permute-start.7 = (bf16[8,8,1024]{2,1,0:T(8,128)(2,1)S(1)}, bf16[8,8,1024]{2,1,0:T(8,128)(2,1)S(1)}, u32[]{:S(2)}, u32[]{:S(2)}) collective-permute-start(bf16[8,8,1024]{2,1,0:T(8,128)(2,1)S(1)} %get-tuple-element.22), channel_id=1, source_target_pairs={{1,0},{2,1},{3,2},{4,3},{5,4},{6,5},{7,6},{9,8},{10,9},{11,10},{12... | collective-permute-start | bytes 393224 | tf_op jit(solution)/shard_map/ppermute | solution.py:38
  63.2 2.4 %collective-permute-start.6 = (bf16[8,8,128]{2,1,0:T(8,128)(2,1)S(1)}, bf16[8,8,128]{2,1,0:T(8,128)(2,1)S(1)}, u32[]{:S(2)}, u32[]{:S(2)}) collective-permute-start(bf16[8,8,128]{2,1,0:T(8,128)(2,1)S(1)} %reshape.187), channel_id=1, source_target_pairs={{1,0},{2,1},{3,2},{4,3},{5,4},{6,5},{7,6},{9,8},{10,9},{11,10},{12... | collective-permute-start | bytes 49160 | tf_op jit(solution)/shard_map/ppermute | solution.py:38
  66.0 3.8 %collective-permute-done.6 = bf16[8,8,128]{2,1,0:T(8,128)(2,1)S(1)} collective-permute-done((bf16[8,8,128]{2,1,0:T(8,128)(2,1)S(1)}, bf16[8,8,128]{2,1,0:T(8,128)(2,1)S(1)}, u32[]{:S(2)}, u32[]{:S(2)}) %collective-permute-start.6) | collective-permute-done | bytes 16416 | tf_op jit(solution)/shard_map/ppermute | solution.py:38
  70.1 0.5 maximum_maximum_fusion
  70.6 0.6 maximum_maximum_fusion.2
  71.2 0.3 fusion.12
  71.5 0.4 convolution_add_fusion.7
  71.9 0.4 convolution_add_fusion.6
  72.2 0.3 convolution_add_fusion.5
  72.5 0.3 convolution_add_fusion.4
  72.9 0.4 convolution_add_fusion.3
  73.2 0.3 convolution_add_fusion.2
  73.5 0.4 convolution_add_fusion.1
  73.9 0.5 select_convert_fusion
  74.4 0.2 fusion.22
  74.6 0.2 convolution_add_fusion.15
  74.8 0.2 convolution_add_fusion.14
  75.1 0.2 convolution_add_fusion.13
  75.2 0.2 convolution_add_fusion.12
  75.5 0.2 convolution_add_fusion.11
  75.7 0.2 convolution_add_fusion.10
  75.9 0.2 convolution_add_fusion.9
  76.1 0.2 fusion.3
  76.4 0.7 copy.116
  (72 shorter events, 3.3 us)
Async XLA Ops:
  0.0 10.9 %copy-start = (bf16[64,64]{1,0:T(8,128)(2,1)S(1)}, bf16[64,64]{1,0:T(8,128)(2,1)}, u32[]{:S(2)}) copy-start(bf16[64,64]{1,0:T(8,128)(2,1)} %param.20) | copy-start | bytes 24580
  3.2 6.2 %copy-start.5 = (bf16[64,192]{1,0:T(8,128)(2,1)S(1)}, bf16[64,192]{1,0:T(8,128)(2,1)}, u32[]{:S(2)}) copy-start(bf16[64,192]{1,0:T(8,128)(2,1)} %param.18) | copy-start | bytes 73732
  3.3 9.0 %copy-start.7 = (f32[64]{0:T(128)S(1)}, f32[64]{0:T(128)}, u32[]{:S(2)}) copy-start(f32[64]{0:T(128)} %param.17) | copy-start | bytes 772
  3.3 9.6 %copy-start.6 = (bf16[8,64]{1,0:T(8,128)(2,1)S(1)}, bf16[8,64]{1,0:T(8,128)(2,1)}, u32[]{:S(2)}) copy-start(bf16[8,64]{1,0:T(8,128)(2,1)} %param.16) | copy-start | bytes 3076
  3.3 10.3 %copy-start.8 = (f32[4]{0:T(128)S(1)}, f32[4]{0:T(128)}, u32[]{:S(2)}) copy-start(f32[4]{0:T(128)} %param.19) | copy-start | bytes 52
  3.4 11.0 %copy-start.1 = (bf16[9,8,8]{0,2,1:T(8,128)(2,1)S(1)}, bf16[9,8,8]{0,2,1:T(8,128)(2,1)}, u32[]{:S(2)}) copy-start(bf16[9,8,8]{0,2,1:T(8,128)(2,1)} %param.22) | copy-start | bytes 3460
  3.4 11.1 %copy-start.2 = (bf16[9,8,8]{0,2,1:T(8,128)(2,1)S(1)}, bf16[9,8,8]{0,2,1:T(8,128)(2,1)}, u32[]{:S(2)}) copy-start(bf16[9,8,8]{0,2,1:T(8,128)(2,1)} %param.23) | copy-start | bytes 3460
  3.4 18.4 %collective-permute-start = (f32[5,8,4,512]{3,1,2,0:T(8,128)S(1)}, f32[5,8,4,512]{3,1,2,0:T(8,128)S(1)}, u32[]{:S(2)}, u32[]{:S(2)}) collective-permute-start(f32[5,8,4,512]{3,1,2,0:T(8,128)S(1)} %get-tuple-element.14), channel_id=1, source_target_pairs={{0,1},{1,2},{2,3},{3,4},{4,5},{5,6},{6,7},{8,9},{9,10},{10,11},{11... | collective-permute-start | bytes 983048 | tf_op jit(solution)/shard_map/ppermute | solution.py:19
  6.9 14.9 %collective-permute-start.1 = (f32[5,8,4,512]{3,1,2,0:T(8,128)S(1)}, f32[5,8,4,512]{3,1,2,0:T(8,128)S(1)}, u32[]{:S(2)}, u32[]{:S(2)}) collective-permute-start(f32[5,8,4,512]{3,1,2,0:T(8,128)S(1)} %get-tuple-element.15), channel_id=1, source_target_pairs={{1,0},{2,1},{3,2},{4,3},{5,4},{6,5},{7,6},{9,8},{10,9},{11,10},{12... | collective-permute-start | bytes 983048 | tf_op jit(solution)/shard_map/ppermute | solution.py:22
  24.4 6.8 %all-to-all-start = ((bf16[4,8,8,256]{3,2,1,0:T(8,128)(2,1)}), bf16[4,8,8,256]{3,2,1,0:T(8,128)(2,1)S(1)}, u32[]{:S(2)}, u32[]{:S(2)}) async-start(bf16[4,8,8,256]{3,2,1,0:T(8,128)(2,1)} %copy_bitcast_fusion), calls=%async_computation | async-start | bytes 262144 | tf_op jit(solution)/shard_map/all_to_all | solution.py:239
  31.2 0.7 copy-start.4
  43.0 5.8 %collective-permute-start.2 = (bf16[8,8,64]{2,1,0:T(8,128)(2,1)S(1)}, bf16[8,8,64]{2,1,0:T(8,128)(2,1)S(1)}, u32[]{:S(2)}, u32[]{:S(2)}) collective-permute-start(bf16[8,8,64]{2,1,0:T(8,128)(2,1)S(1)} %reshape.183), channel_id=1, source_target_pairs={{0,8},{8,16},{16,24},{1,9},{9,17},{17,25},{2,10},{10,18},{18,26},{... | collective-permute-start | bytes 24584 | tf_op jit(solution)/shard_map/ppermute | solution.py:37
  45.0 5.1 %collective-permute-start.3 = (bf16[8,8,64]{2,1,0:T(8,128)(2,1)S(1)}, bf16[8,8,64]{2,1,0:T(8,128)(2,1)S(1)}, u32[]{:S(2)}, u32[]{:S(2)}) collective-permute-start(bf16[8,8,64]{2,1,0:T(8,128)(2,1)S(1)} %reshape.185), channel_id=1, source_target_pairs={{8,0},{16,8},{24,16},{9,1},{17,9},{25,17},{10,2},{18,10},{26,18},{... | collective-permute-start | bytes 24584 | tf_op jit(solution)/shard_map/ppermute | solution.py:38
  50.5 15.2 %collective-permute-start.4 = (bf16[8,8,128]{2,1,0:T(8,128)(2,1)S(1)}, bf16[8,8,128]{2,1,0:T(8,128)(2,1)S(1)}, u32[]{:S(2)}, u32[]{:S(2)}) collective-permute-start(bf16[8,8,128]{2,1,0:T(8,128)(2,1)S(1)} %reshape.187), channel_id=1, source_target_pairs={{0,1},{1,2},{2,3},{3,4},{4,5},{5,6},{6,7},{8,9},{9,10},{10,11},{11... | collective-permute-start | bytes 49160 | tf_op jit(solution)/shard_map/ppermute | solution.py:37
  57.4 12.7 %collective-permute-start.5 = (bf16[8,8,1024]{2,1,0:T(8,128)(2,1)S(1)}, bf16[8,8,1024]{2,1,0:T(8,128)(2,1)S(1)}, u32[]{:S(2)}, u32[]{:S(2)}) collective-permute-start(bf16[8,8,1024]{2,1,0:T(8,128)(2,1)S(1)} %get-tuple-element.22), channel_id=1, source_target_pairs={{0,1},{1,2},{2,3},{3,4},{4,5},{5,6},{6,7},{8,9},{9,10},{10,11},{11... | collective-permute-start | bytes 393224 | tf_op jit(solution)/shard_map/ppermute | solution.py:37
  59.3 10.8 %collective-permute-start.7 = (bf16[8,8,1024]{2,1,0:T(8,128)(2,1)S(1)}, bf16[8,8,1024]{2,1,0:T(8,128)(2,1)S(1)}, u32[]{:S(2)}, u32[]{:S(2)}) collective-permute-start(bf16[8,8,1024]{2,1,0:T(8,128)(2,1)S(1)} %get-tuple-element.22), channel_id=1, source_target_pairs={{1,0},{2,1},{3,2},{4,3},{5,4},{6,5},{7,6},{9,8},{10,9},{11,10},{12... | collective-permute-start | bytes 393224 | tf_op jit(solution)/shard_map/ppermute | solution.py:38
  63.2 6.5 %collective-permute-start.6 = (bf16[8,8,128]{2,1,0:T(8,128)(2,1)S(1)}, bf16[8,8,128]{2,1,0:T(8,128)(2,1)S(1)}, u32[]{:S(2)}, u32[]{:S(2)}) collective-permute-start(bf16[8,8,128]{2,1,0:T(8,128)(2,1)S(1)} %reshape.187), channel_id=1, source_target_pairs={{1,0},{2,1},{3,2},{4,3},{5,4},{6,5},{7,6},{9,8},{10,9},{11,10},{12... | collective-permute-start | bytes 49160 | tf_op jit(solution)/shard_map/ppermute | solution.py:38
  75.2 0.9 %copy-start.3 = (bf16[8,8,1024]{2,1,0:T(8,128)(2,1)S(1)}, bf16[8,8,1024]{2,1,0:T(8,128)(2,1)}, u32[]{:S(2)}) copy-start(bf16[8,8,1024]{2,1,0:T(8,128)(2,1)} %shard_map.118) | copy-start | bytes 393220

commit v9 on v5

--- a/solution.py
+++ b/solution.py
@@ -22,6 +22,18 @@
         high = lax.ppermute(lax.slice_in_dim(block, 0, width, axis=dim), axis, backward)
         block = jnp.concatenate([low, block, high], axis=dim)
     return block
+
+
+def row_padded(block, width):
+    count = lax.axis_size("row")
+    forward = [(i, i + 1) for i in range(count - 1)]
+    backward = [(target, source) for source, target in forward]
+    rows, cols = block.shape[-2:]
+    shape = block.shape[:-2] + (width, cols)
+    flat = block.shape[:-2] + (width * cols,)
+    low = lax.ppermute(block[..., rows - width :, :].reshape(flat), "row", forward)
+    high = lax.ppermute(block[..., :width, :].reshape(flat), "row", backward)
+    return jnp.concatenate([low.reshape(shape), block, high.reshape(shape)], axis=-2)
 
 
 def advance(padded_field, wind_east, wind_north, diffusivity):
@@ -198,10 +210,19 @@
     chunks = lax.axis_size("mem")
     _, levels_count, tile_rows, cols_all = predicted_states.shape
     tile_cols = cols_all // chunks
+    halo = 2 * DILATION_SPAN
     by_chunk = predicted_states.reshape(members_here, levels_count, tile_rows, chunks, tile_cols)
     by_chunk = jnp.transpose(by_chunk, (3, 2, 1, 0, 4)).reshape(
         chunks, tile_rows, levels_count, members_here * tile_cols
     )
+    wide = jnp.pad(predicted_states, ((0, 0), (0, 0), (0, 0), (halo, halo)))
+    lefts = wide[..., :cols_all].reshape(members_here, levels_count, tile_rows, chunks, tile_cols)
+    rights = wide[..., 2 * halo :].reshape(members_here, levels_count, tile_rows, chunks, tile_cols)
+    edges = jnp.concatenate([lefts[..., :halo], rights[..., tile_cols - halo :]], axis=-1)
+    edges = jnp.transpose(edges, (3, 1, 0, 2, 4)).reshape(
+        chunks, 1, levels_count, members_here * tile_rows * 2 * halo
+    )
+    by_chunk = jnp.concatenate([by_chunk, edges], axis=1)
     by_source = lax.all_to_all(by_chunk, "mem", split_axis=0, concat_axis=0, tiled=True)
     members = chunks * members_here
     step_result = post_block(
@@ -215,19 +236,24 @@
         readout_weight,
     )
     feat = readout_weight.shape[1]
-    step_result = step_result.reshape(tile_rows, feat, members, tile_cols)
-    features = jnp.transpose(step_result, (2, 1, 0, 3))
-    tile_cols = features.shape[3]
+    inner = step_result[:tile_rows].reshape(tile_rows, feat, members, tile_cols)
+    inner = jnp.transpose(inner, (2, 1, 0, 3))
+    outer = step_result[tile_rows].reshape(feat, members, tile_rows, 2 * halo)
+    outer = jnp.transpose(outer, (1, 0, 2, 3))
+    mem_index = lax.axis_index("mem")
+    left = jnp.where(mem_index > 0, outer[..., :halo], 0)
+    right = jnp.where(mem_index < chunks - 1, outer[..., halo:], 0)
+    features_wide = jnp.concatenate([left, inner, right], axis=-1)
     span = DILATION_SPAN
-    padded_feature = padded(features, (("mem", 3), ("row", 2)), 2 * span)
+    padded_feature = row_padded(features_wide, halo)
     first = jax.nn.silu(convolve(padded_feature, first_kernel))
     row_ids = lax.axis_index("row") * tile_rows - span + jnp.arange(tile_rows + 2 * span)
-    col_ids = lax.axis_index("mem") * tile_cols - span + jnp.arange(tile_cols + 2 * span)
+    col_ids = mem_index * tile_cols - span + jnp.arange(tile_cols + 2 * span)
     row_in = (row_ids >= 0) & (row_ids < lax.axis_size("row") * tile_rows)
-    col_in = (col_ids >= 0) & (col_ids < lax.axis_size("mem") * tile_cols)
+    col_in = (col_ids >= 0) & (col_ids < chunks * tile_cols)
     inside = row_in[:, None] & col_in[None, :]
     activated_output = jnp.where(inside[None, None], first, 0.0).astype(jnp.bfloat16)
-    return (features.astype(jnp.float32) + convolve(activated_output, second_kernel)).astype(
+    return (inner.astype(jnp.float32) + convolve(activated_output, second_kernel)).astype(
         jnp.bfloat16
     )
 

time: 75.3 us -> 66.4 us (0.88)
  the two profiles are of different devices: /device:TPU:9 before, /device:TPU:0 now
where the time goes in v9:
time: 66.4 us; the launch traced here: 65.8 us
  local copies, waits for them, and re-layouts  15.9 us (24%)
  starting transfers between devices  15.8 us (24%)
  waiting for transfers between devices  14 us (21%)
  Pallas kernels  11 us (17%)
  matrix products  5 us (8%)
  other arithmetic  3.55 us (5%)
    pallas_call x1, Pallas kernels, post_block(): pl.pallas_call(functools.partial(attention_kernel, chunk=chunk, heads=hea...  11 us
    unnamed x43, local copies, waits for them, and re-layouts  7.23 us
    ppermute x1, starting transfers between devices, row_padded(): lax.ppermute(block[..., rows - width:, :].reshape(flat), 'row', forward)  5.02 us
    dot_general x18, matrix products, convolve(): jnp.einsum('oc,mcij->moij', kernel[row_stencil * 3 + column_stencil], shi...  5 us
    ppermute x1, waiting for transfers between devices, padded(): lax.ppermute(lax.slice_in_dim(block, block.shape[dim] - width, None, axis...  4.93 us
    ppermute x1, starting transfers between devices, padded(): lax.ppermute(lax.slice_in_dim(block, block.shape[dim] - width, None, axis...  4.86 us
    all_to_all x1, waiting for transfers between devices, on_device(): lax.all_to_all(by_chunk, 'mem', split_axis=0, concat_axis=0, tiled=True)  4.76 us
    all_to_all x1, starting transfers between devices, on_device(): lax.all_to_all(by_chunk, 'mem', split_axis=0, concat_axis=0, tiled=True)  3.33 us
  transfers between devices with their start and end apart: 5, of which 4 were waited for; matrix products, arithmetic and copies ran while one was open for 12% of the time, Pallas kernels for 0%

profile of v9, /device:TPU:0, one launch (start us, length us, event | category | flops | bytes accessed | tf_op | source)
XLA Modules:
  0.0 65.8 jit_solution(4358480199874600582)
XLA Ops:
  0.0 1.0 %copy.170 = f32[8,8,512]{2,0,1:T(8,128)S(1)} copy(f32[8,8,512]{2,1,0:T(8,128)} %param.15) | data formatting | bytes 262144 | tf_op args[3]
  1.0 1.1 %copy.80 = f32[2,8,8,512]{3,1,2,0:T(8,128)S(1)} copy(f32[2,8,8,512]{3,2,1,0:T(8,128)} %param.12) | data formatting | bytes 524288 | tf_op args[0]
  2.1 1.1 %fusion.46 = (f32[8,8,512]{2,0,1:T(8,128)S(1)}, f32[1,8,8,512]{3,1,2,0:T(8,128)S(1)}, f32[1,8,8,512]{3,1,2,0:T(8,128)S(1)}, f32[8,8,512]{2,0,1:T(8,128)S(1)}) fusion(f32[8,8,512]{2,1,0:T(8,128)} %param.13, f32[8,8,512]{2,1,0:T(8,128)} %param.14), kind=kLoop, calls=%fused_computation.115 | loop fusion | bytes 786432 | tf_op args[1]
  3.4 4.9 %collective-permute-start = (f32[5,8,4,512]{3,1,2,0:T(8,128)S(1)}, f32[5,8,4,512]{3,1,2,0:T(8,128)S(1)}, u32[]{:S(2)}, u32[]{:S(2)}) collective-permute-start(f32[5,8,4,512]{3,1,2,0:T(8,128)S(1)} %get-tuple-element.14), channel_id=1, source_target_pairs={{0,1},{1,2},{2,3},{3,4},{4,5},{5,6},{6,7},{8,9},{9,10},{10,11},{11... | collective-permute-start | bytes 983048 | tf_op jit(solution)/shard_map/ppermute | solution.py:19
  8.3 1.3 %collective-permute-start.1 = (f32[5,8,4,512]{3,1,2,0:T(8,128)S(1)}, f32[5,8,4,512]{3,1,2,0:T(8,128)S(1)}, u32[]{:S(2)}, u32[]{:S(2)}) collective-permute-start(f32[5,8,4,512]{3,1,2,0:T(8,128)S(1)} %get-tuple-element.15), channel_id=1, source_target_pairs={{1,0},{2,1},{3,2},{4,3},{5,4},{6,5},{7,6},{9,8},{10,9},{11,10},{12... | collective-permute-start | bytes 983048 | tf_op jit(solution)/shard_map/ppermute | solution.py:22
  9.9 0.7 gather_fusion
  10.6 0.6 copy.90
  11.2 0.6 gather_fusion.1
  11.9 0.7 %copy.91 = bf16[64,64]{0,1:T(8,128)(2,1)} copy(bf16[64,64]{1,0:T(8,128)(2,1)S(1)} %gather_fusion.1) | data formatting | bytes 16384 | tf_op jit(solution)/shard_map/gather | solution.py:139
  12.6 0.7 %copy.93.gain_ref = f32[64,1]{1,0:T(8,128)} copy(f32[64,1]{0,1:T(1,128)S(1)} %bitcast.212) | data formatting | bytes 512 | tf_op jit(solution)/shard_map/reshape | solution.py:148
  13.3 0.7 %copy.87 = bf16[8,64]{0,1:T(8,128)(2,1)} copy(bf16[8,64]{1,0:T(8,128)(2,1)S(1)} %copy-done.6) | data formatting | bytes 2048 | tf_op args[4]
  14.0 0.7 %reshape_tile.4.hs_ref = f32[8,1]{1,0:T(8,128)} reshape(f32[2,4]{1,0:T(2,128)S(1)} %tile.2) | data formatting | bytes 64 | tf_op jit(solution)/shard_map/reshape;tile | solution.py:140
  15.4 0.1 copy.145
  15.5 0.1 copy.146
  15.7 0.1 copy.147
  15.8 0.1 copy.148
  16.7 0.1 copy.154
  16.9 0.1 copy.155
  17.0 0.1 copy.156
  17.1 0.1 copy.157
  17.3 4.9 %collective-permute-done = f32[5,8,4,512]{3,1,2,0:T(8,128)S(1)} collective-permute-done((f32[5,8,4,512]{3,1,2,0:T(8,128)S(1)}, f32[5,8,4,512]{3,1,2,0:T(8,128)S(1)}, u32[]{:S(2)}, u32[]{:S(2)}) %collective-permute-start) | collective-permute-done | bytes 327712 | tf_op jit(solution)/shard_map/ppermute | solution.py:19
  22.5 0.5 add_select_fusion
  23.1 0.4 add_select_fusion.1
  23.5 0.4 add_select_fusion.2
  23.9 0.3 select_convert_fusion.1
  24.2 0.1 fusion.14
  24.7 0.2 reshape.164
  24.9 0.7 %pad_maximum_fusion.5 = bf16[4,9,8,256]{3,2,1,0:T(8,128)(2,1)} fusion(bf16[4,1,8,256]{3,2,1,0:T(8,128)(2,1)S(1)} %reshape.164, bf16[4,8,8,256]{3,2,1,0:T(8,128)(2,1)S(1)} %copy_bitcast_fusion.2), kind=kLoop, calls=%fused_computation.62 | loop fusion | flops 73728 | bytes 294912 | tf_op jit(solution)/shard_map/concatenate | solution.py:225
  25.6 3.3 %all-to-all-start = ((bf16[4,9,8,256]{3,2,1,0:T(8,128)(2,1)}), bf16[4,9,8,256]{3,2,1,0:T(8,128)(2,1)S(1)}, u32[]{:S(2)}, u32[]{:S(2)}) async-start(bf16[4,9,8,256]{3,2,1,0:T(8,128)(2,1)} %pad_maximum_fusion.5), calls=%async_computation | async-start | bytes 294912 | tf_op jit(solution)/shard_map/all_to_all | solution.py:226
  28.9 4.8 %all-to-all-done.x_ref = bf16[4,9,8,256]{3,2,1,0:T(8,128)(2,1)S(1)} async-done(((bf16[4,9,8,256]{3,2,1,0:T(8,128)(2,1)}), bf16[4,9,8,256]{3,2,1,0:T(8,128)(2,1)S(1)}, u32[]{:S(2)}, u32[]{:S(2)}) %all-to-all-start) | async-done | bytes 147488 | tf_op jit(solution)/shard_map/all_to_all | solution.py:226
  33.7 0.6 copy-done.4
  34.3 11.0 %shard_map.118 = bf16[9,8,1024]{2,1,0:T(8,128)(2,1)} custom-call(f32[8,1]{1,0:T(8,128)} %reshape_tile.4.hs_ref, bf16[4,9,8,256]{3,2,1,0:T(8,128)(2,1)} %copy-done.4, bf16[64,8]{1,0:T(8,128)(2,1)} %bitcast.210, f32[64,1]{1,0:T(8,128)} %copy.93.gain_ref, bf16[192,64]{1,0:T(8,128)(2,1)} %bitcast.207, bf16[64,64]{1,0:T(8,128)(2,1)} %bitcast.209, ...), custom_call_target="tpu_custom_call" | custom-call | tf_op jit(solution)/shard_map/pallas_call | solution.py:141
  45.3 0.7 %slice.367 = bf16[1,8,1024]{2,1,0:T(8,128)(2,1)S(1)} slice(bf16[9,8,1024]{2,1,0:T(8,128)(2,1)} %shard_map.118), slice={[8:9], [0:8], [0:1024]} | slice | bytes 32768 | tf_op jit(solution)/shard_map/slice | solution.py:241
  46.0 0.9 %copy_bitcast_fusion.1 = bf16[8,8,8,128]{3,1,2,0:T(8,128)(2,1)S(1)} fusion(bf16[9,8,1024]{2,1,0:T(8,128)(2,1)} %shard_map.118), kind=kLoop, calls=%fused_computation.80 | loop fusion | bytes 262144 | tf_op jit(solution)/shard_map/transpose | solution.py:240
  46.9 0.1 reshape_squeeze.3
  47.3 0.2 pad_maximum_fusion.4
  47.6 0.3 reshape.173
  47.8 1.3 %collective-permute-start.3 = (bf16[8,8,1152]{2,1,0:T(8,128)(2,1)S(1)}, bf16[8,8,1152]{2,1,0:T(8,128)(2,1)S(1)}, u32[]{:S(2)}, u32[]{:S(2)}) collective-permute-start(bf16[8,8,1152]{2,1,0:T(8,128)(2,1)S(1)} %reshape.173), channel_id=1, source_target_pairs={{1,0},{2,1},{3,2},{4,3},{5,4},{6,5},{7,6},{9,8},{10,9},{11,10},{12... | collective-permute-start | bytes 442376 | tf_op jit(solution)/shard_map/ppermute | solution.py:35
  49.1 5.0 %collective-permute-start.2 = (bf16[8,8,1152]{2,1,0:T(8,128)(2,1)S(1)}, bf16[8,8,1152]{2,1,0:T(8,128)(2,1)S(1)}, u32[]{:S(2)}, u32[]{:S(2)}) collective-permute-start(bf16[8,8,1152]{2,1,0:T(8,128)(2,1)S(1)} %reshape.173), channel_id=1, source_target_pairs={{0,1},{1,2},{2,3},{3,4},{4,5},{5,6},{6,7},{8,9},{9,10},{10,11},{11... | collective-permute-start | bytes 442376 | tf_op jit(solution)/shard_map/ppermute | solution.py:34
  54.2 1.4 %collective-permute-done.3 = bf16[8,8,1152]{2,1,0:T(8,128)(2,1)S(1)} collective-permute-done((bf16[8,8,1152]{2,1,0:T(8,128)(2,1)S(1)}, bf16[8,8,1152]{2,1,0:T(8,128)(2,1)S(1)}, u32[]{:S(2)}, u32[]{:S(2)}) %collective-permute-start.3) | collective-permute-done | bytes 147488 | tf_op jit(solution)/shard_map/ppermute | solution.py:35
  55.6 0.4 reshape.175
  56.1 2.9 %collective-permute-done.2 = bf16[8,8,1152]{2,1,0:T(8,128)(2,1)S(1)} collective-permute-done((bf16[8,8,1152]{2,1,0:T(8,128)(2,1)S(1)}, bf16[8,8,1152]{2,1,0:T(8,128)(2,1)S(1)}, u32[]{:S(2)}, u32[]{:S(2)}) %collective-permute-start.2) | collective-permute-done | bytes 147488 | tf_op jit(solution)/shard_map/ppermute | solution.py:34
  59.0 0.4 reshape.174
  59.4 0.2 pad_maximum_fusion.1
  59.6 0.4 pad_maximum_fusion.3
  60.0 0.3 fusion.12
  60.3 0.3 convolution_add_fusion.7
  60.6 0.4 convolution_add_fusion.6
  61.0 0.3 convolution_add_fusion.5
  61.3 0.4 convolution_add_fusion.4
  61.7 0.4 convolution_add_fusion.3
  62.0 0.3 convolution_add_fusion.2
  62.3 0.4 convolution_add_fusion.1
  62.7 0.5 select_convert_fusion
  63.2 0.2 fusion.24
  63.4 0.2 convolution_add_fusion.15
  63.6 0.2 convolution_add_fusion.14
  63.9 0.2 convolution_add_fusion.13
  64.0 0.2 convolution_add_fusion.12
  64.3 0.2 convolution_add_fusion.11
  64.5 0.2 convolution_add_fusion.10
  64.7 0.2 convolution_add_fusion.9
  64.9 0.2 fusion.3
  65.2 0.7 %copy.119 = bf16[8,8,8,128]{3,2,1,0:T(8,128)(2,1)} copy(bf16[8,8,8,128]{3,1,2,0:T(8,128)(2,1)S(1)} %fusion.3) | data formatting | bytes 262144 | tf_op jit(solution)/shard_map/convert_element_type | solution.py:256
  (64 shorter events, 3.1 us)
Async XLA Ops:
  0.0 11.2 %copy-start = (bf16[64,64]{1,0:T(8,128)(2,1)S(1)}, bf16[64,64]{1,0:T(8,128)(2,1)}, u32[]{:S(2)}) copy-start(bf16[64,64]{1,0:T(8,128)(2,1)} %param.20) | copy-start | bytes 24580
  3.2 6.5 %copy-start.5 = (bf16[64,192]{1,0:T(8,128)(2,1)S(1)}, bf16[64,192]{1,0:T(8,128)(2,1)}, u32[]{:S(2)}) copy-start(bf16[64,192]{1,0:T(8,128)(2,1)} %param.18) | copy-start | bytes 73732
  3.3 9.3 %copy-start.7 = (f32[64]{0:T(128)S(1)}, f32[64]{0:T(128)}, u32[]{:S(2)}) copy-start(f32[64]{0:T(128)} %param.17) | copy-start | bytes 772
  3.3 9.9 %copy-start.6 = (bf16[8,64]{1,0:T(8,128)(2,1)S(1)}, bf16[8,64]{1,0:T(8,128)(2,1)}, u32[]{:S(2)}) copy-start(bf16[8,64]{1,0:T(8,128)(2,1)} %param.16) | copy-start | bytes 3076
  3.3 10.6 %copy-start.8 = (f32[4]{0:T(128)S(1)}, f32[4]{0:T(128)}, u32[]{:S(2)}) copy-start(f32[4]{0:T(128)} %param.19) | copy-start | bytes 52
  3.4 11.3 %copy-start.1 = (bf16[9,8,8]{0,2,1:T(8,128)(2,1)S(1)}, bf16[9,8,8]{0,2,1:T(8,128)(2,1)}, u32[]{:S(2)}) copy-start(bf16[9,8,8]{0,2,1:T(8,128)(2,1)} %param.22) | copy-start | bytes 3460
  3.4 12.6 %copy-start.2 = (bf16[9,8,8]{0,2,1:T(8,128)(2,1)S(1)}, bf16[9,8,8]{0,2,1:T(8,128)(2,1)}, u32[]{:S(2)}) copy-start(bf16[9,8,8]{0,2,1:T(8,128)(2,1)} %param.23) | copy-start | bytes 3460
  3.4 18.8 %collective-permute-start = (f32[5,8,4,512]{3,1,2,0:T(8,128)S(1)}, f32[5,8,4,512]{3,1,2,0:T(8,128)S(1)}, u32[]{:S(2)}, u32[]{:S(2)}) collective-permute-start(f32[5,8,4,512]{3,1,2,0:T(8,128)S(1)} %get-tuple-element.14), channel_id=1, source_target_pairs={{0,1},{1,2},{2,3},{3,4},{4,5},{5,6},{6,7},{8,9},{9,10},{10,11},{11... | collective-permute-start | bytes 983048 | tf_op jit(solution)/shard_map/ppermute | solution.py:19
  8.3 14.0 %collective-permute-start.1 = (f32[5,8,4,512]{3,1,2,0:T(8,128)S(1)}, f32[5,8,4,512]{3,1,2,0:T(8,128)S(1)}, u32[]{:S(2)}, u32[]{:S(2)}) collective-permute-start(f32[5,8,4,512]{3,1,2,0:T(8,128)S(1)} %get-tuple-element.15), channel_id=1, source_target_pairs={{1,0},{2,1},{3,2},{4,3},{5,4},{6,5},{7,6},{9,8},{10,9},{11,10},{12... | collective-permute-start | bytes 983048 | tf_op jit(solution)/shard_map/ppermute | solution.py:22
  25.6 8.1 %all-to-all-start = ((bf16[4,9,8,256]{3,2,1,0:T(8,128)(2,1)}), bf16[4,9,8,256]{3,2,1,0:T(8,128)(2,1)S(1)}, u32[]{:S(2)}, u32[]{:S(2)}) async-start(bf16[4,9,8,256]{3,2,1,0:T(8,128)(2,1)} %pad_maximum_fusion.5), calls=%async_computation | async-start | bytes 294912 | tf_op jit(solution)/shard_map/all_to_all | solution.py:226
  33.7 0.6 copy-start.4
  47.8 7.8 %collective-permute-start.3 = (bf16[8,8,1152]{2,1,0:T(8,128)(2,1)S(1)}, bf16[8,8,1152]{2,1,0:T(8,128)(2,1)S(1)}, u32[]{:S(2)}, u32[]{:S(2)}) collective-permute-start(bf16[8,8,1152]{2,1,0:T(8,128)(2,1)S(1)} %reshape.173), channel_id=1, source_target_pairs={{1,0},{2,1},{3,2},{4,3},{5,4},{6,5},{7,6},{9,8},{10,9},{11,10},{12... | collective-permute-start | bytes 442376 | tf_op jit(solution)/shard_map/ppermute | solution.py:35
  49.1 9.8 %collective-permute-start.2 = (bf16[8,8,1152]{2,1,0:T(8,128)(2,1)S(1)}, bf16[8,8,1152]{2,1,0:T(8,128)(2,1)S(1)}, u32[]{:S(2)}, u32[]{:S(2)}) collective-permute-start(bf16[8,8,1152]{2,1,0:T(8,128)(2,1)S(1)} %reshape.173), channel_id=1, source_target_pairs={{0,1},{1,2},{2,3},{3,4},{4,5},{5,6},{6,7},{8,9},{9,10},{10,11},{11... | collective-permute-start | bytes 442376 | tf_op jit(solution)/shard_map/ppermute | solution.py:34
  64.0 0.9 %copy-start.3 = (bf16[9,8,1024]{2,1,0:T(8,128)(2,1)S(1)}, bf16[9,8,1024]{2,1,0:T(8,128)(2,1)}, u32[]{:S(2)}) copy-start(bf16[9,8,1024]{2,1,0:T(8,128)(2,1)} %shard_map.118) | copy-start | bytes 442372

commit v10 on v9

--- a/solution.py
+++ b/solution.py
@@ -192,16 +192,45 @@
     members_here = starting_states.shape[0]
     row_total = starting_states.shape[2]
     coefficients = jnp.stack([wind_east, wind_north, diffusivity])
-    joined = jnp.concatenate([starting_states, coefficients], 0)
-    widened = padded(joined, (("row", 2),), STEPS)
-    gridded_quantity_list = widened[:members_here]
-    coef_rows = widened[members_here:]
+    state_halo = STEPS
+    coef_halo = STEPS - 1
+    count = lax.axis_size("row")
+    forward = [(i, i + 1) for i in range(count - 1)]
+    backward = [(target, source) for source, target in forward]
+    cols = starting_states.shape[3]
+
+    def pack(states_part, coef_part):
+        return jnp.concatenate(
+            [states_part.reshape(-1, cols), coef_part.reshape(-1, cols)], axis=0
+        )
+
+    low = lax.ppermute(
+        pack(
+            starting_states[:, :, row_total - state_halo :],
+            coefficients[:, :, row_total - coef_halo :],
+        ),
+        "row",
+        forward,
+    )
+    high = lax.ppermute(
+        pack(starting_states[:, :, :state_halo], coefficients[:, :, :coef_halo]), "row", backward
+    )
+    split = members_here * starting_states.shape[1] * state_halo
+    state_shape = starting_states.shape[:2] + (state_halo, cols)
+    coef_shape = coefficients.shape[:2] + (coef_halo, cols)
+    gridded_quantity_list = jnp.concatenate(
+        [low[:split].reshape(state_shape), starting_states, high[:split].reshape(state_shape)],
+        axis=2,
+    )
+    coef_rows = jnp.concatenate(
+        [low[split:].reshape(coef_shape), coefficients, high[split:].reshape(coef_shape)], axis=2
+    )
     first_row = lax.axis_index("row") * row_total - STEPS
     all_rows = lax.axis_size("row") * row_total
     for section in range(STEPS):
         out_rows = row_total + 2 * (STEPS - section - 1)
         offset = section + 1
-        window = coef_rows[:, :, offset : offset + out_rows]
+        window = coef_rows[:, :, section : section + out_rows]
         gridded_quantity_list = advance(gridded_quantity_list, window[0], window[1], window[2])
         row_ids = first_row + offset + jnp.arange(out_rows)
         inside = (row_ids >= 0) & (row_ids < all_rows)

time: 66.4 us -> 65.5 us (0.986)
  the two profiles are of different devices: /device:TPU:0 before, /device:TPU:9 now
where the time goes in v10:
time: 65.5 us; the launch traced here: 64.5 us
  starting transfers between devices  16.3 us (25%)
  local copies, waits for them, and re-layouts  15 us (23%)
  waiting for transfers between devices  11.3 us (17%)
  Pallas kernels  11 us (17%)
  other arithmetic  5.14 us (8%)
  matrix products  5.01 us (8%)
  between operations  0.72 us (1%)
    pallas_call x1, Pallas kernels, post_block(): pl.pallas_call(functools.partial(attention_kernel, chunk=chunk, heads=hea...  11 us
    dot_general x18, matrix products, convolve(): jnp.einsum('oc,mcij->moij', kernel[row_stencil * 3 + column_stencil], shi...  5.01 us
    unnamed x48, local copies, waits for them, and re-layouts  4.65 us
    ppermute x1, waiting for transfers between devices, row_padded(): high = lax.ppermute(block[..., :width, :].reshape(flat), 'row', backward)  4.13 us
    ppermute x1, starting transfers between devices, row_padded(): high = lax.ppermute(block[..., :width, :].reshape(flat), 'row', backward)  4.05 us
    all_to_all x1, starting transfers between devices, on_device(): lax.all_to_all(by_chunk, 'mem', split_axis=0, concat_axis=0, tiled=True)  3.79 us
    all_to_all x1, waiting for transfers between devices, on_device(): lax.all_to_all(by_chunk, 'mem', split_axis=0, concat_axis=0, tiled=True)  3.72 us
    ppermute x1, starting transfers between devices, on_device(): lax.ppermute(pack(starting_states[:, :, row_total - state_halo:], coeffic...  3.12 us
  transfers between devices with their start and end apart: 5, of which 5 were waited for; matrix products, arithmetic and copies ran while one was open for 13% of the time, Pallas kernels for 0%

profile of v10, /device:TPU:9, one launch (start us, length us, event | category | flops | bytes accessed | tf_op | source)
XLA Modules:
  0.0 64.5 jit_solution(8215075573160330271)
XLA Ops:
  0.0 1.1 %pad_maximum_fusion.4 = f32[3,8,8,512]{3,2,1,0:T(8,128)S(1)} fusion(f32[1,8,8,512]{3,2,1,0:T(8,128)} %bitcast.199, f32[1,8,8,512]{3,2,1,0:T(8,128)} %bitcast.201, f32[1,8,8,512]{3,2,1,0:T(8,128)} %bitcast.203), kind=kLoop, calls=%fused_computation.47 | loop fusion | flops 196608 | bytes 786432 | tf_op jit(solution)/shard_map/stack | solution.py:194
  1.4 3.1 %collective-permute-start = (f32[136,512]{1,0:T(8,128)S(1)}, f32[136,512]{1,0:T(8,128)S(1)}, u32[]{:S(2)}, u32[]{:S(2)}) collective-permute-start(f32[136,512]{1,0:T(8,128)S(1)} %pad_maximum_fusion.5), channel_id=1, source_target_pairs={{0,1},{1,2},{2,3},{3,4},{4,5},{5,6},{6,7},{8,9},{9,10},{10,11},{11... | collective-permute-start | bytes 835592 | tf_op jit(solution)/shard_map/ppermute | solution.py:207
  4.8 3.1 %collective-permute-start.1 = (f32[136,512]{1,0:T(8,128)S(1)}, f32[136,512]{1,0:T(8,128)S(1)}, u32[]{:S(2)}, u32[]{:S(2)}) collective-permute-start(f32[136,512]{1,0:T(8,128)S(1)} %pad_maximum_fusion.6), channel_id=1, source_target_pairs={{1,0},{2,1},{3,2},{4,3},{5,4},{6,5},{7,6},{9,8},{10,9},{11,10},{12... | collective-permute-start | bytes 835592 | tf_op jit(solution)/shard_map/ppermute | solution.py:215
  8.5 0.7 %gather_fusion = bf16[64,3,64]{2,1,0:T(4,128)(2,1)S(1)} fusion(bf16[3,64,64]{2,0,1:T(4,128)(2,1)S(1)} %copy.46, s32[1024]{0:T(1024)S(1)} %pad_clamp_fusion), kind=kCustom, calls=%fused_computation | custom fusion | bytes 49408 | tf_op jit(solution)/shard_map/gather | solution.py:138
  9.1 0.6 copy.47
  9.8 0.6 gather_fusion.1
  10.4 0.7 %copy.48 = bf16[64,64]{0,1:T(8,128)(2,1)} copy(bf16[64,64]{1,0:T(8,128)(2,1)S(1)} %gather_fusion.1) | data formatting | bytes 16384 | tf_op jit(solution)/shard_map/gather | solution.py:139
  11.1 0.7 %copy.50.gain_ref = f32[64,1]{1,0:T(8,128)} copy(f32[64,1]{0,1:T(1,128)S(1)} %bitcast.214) | data formatting | bytes 512 | tf_op jit(solution)/shard_map/reshape | solution.py:148
  11.8 0.7 %copy.44 = bf16[8,64]{0,1:T(8,128)(2,1)} copy(bf16[8,64]{1,0:T(8,128)(2,1)S(1)} %copy-done.11) | data formatting | bytes 2048 | tf_op args[4]
  12.5 0.7 %reshape_tile.4.hs_ref = f32[8,1]{1,0:T(8,128)} reshape(f32[2,4]{1,0:T(2,128)S(1)} %tile.2) | data formatting | bytes 64 | tf_op jit(solution)/shard_map/reshape;tile | solution.py:140
  13.8 0.1 copy.102
  13.9 0.1 copy.103
  14.1 0.1 copy.104
  14.2 0.1 copy.105
  14.3 0.1 copy.106
  14.6 0.1 copy.108
  14.9 0.1 copy.110
  15.8 3.0 %collective-permute-done.1 = f32[136,512]{1,0:T(8,128)S(1)} collective-permute-done((f32[136,512]{1,0:T(8,128)S(1)}, f32[136,512]{1,0:T(8,128)S(1)}, u32[]{:S(2)}, u32[]{:S(2)}) %collective-permute-start.1) | collective-permute-done | bytes 278560 | tf_op jit(solution)/shard_map/ppermute | solution.py:215
  18.9 0.1 pad_maximum_fusion
  19.0 0.5 copy-done.9
  19.8 0.9 %slice.345 = f32[64,512]{1,0:T(8,128)S(1)} slice(f32[136,512]{1,0:T(8,128)} %copy-done.9), slice={[0:64], [0:512]} | slice | bytes 262144 | tf_op jit(solution)/shard_map/slice | solution.py:222
  21.0 0.5 add_select_fusion.2
  21.6 0.5 add_select_fusion.1
  22.2 0.5 add_select_fusion
  22.7 0.3 select_convert_fusion.1
  23.4 0.2 reshape.196
  23.6 0.7 %pad_maximum_fusion.8 = bf16[4,9,8,256]{3,2,1,0:T(8,128)(2,1)} fusion(bf16[4,1,8,256]{3,2,1,0:T(8,128)(2,1)S(1)} %reshape.196, bf16[4,8,8,256]{3,2,1,0:T(8,128)(2,1)S(1)} %bitcast.207), kind=kLoop, calls=%fused_computation.65 | loop fusion | flops 73728 | bytes 294912 | tf_op jit(solution)/shard_map/concatenate | solution.py:254
  24.3 3.8 %all-to-all-start = ((bf16[4,9,8,256]{3,2,1,0:T(8,128)(2,1)}), bf16[4,9,8,256]{3,2,1,0:T(8,128)(2,1)S(1)}, u32[]{:S(2)}, u32[]{:S(2)}) async-start(bf16[4,9,8,256]{3,2,1,0:T(8,128)(2,1)} %pad_maximum_fusion.8), calls=%async_computation | async-start | bytes 294912 | tf_op jit(solution)/shard_map/all_to_all | solution.py:255
  28.1 3.7 %all-to-all-done.x_ref = bf16[4,9,8,256]{3,2,1,0:T(8,128)(2,1)S(1)} async-done(((bf16[4,9,8,256]{3,2,1,0:T(8,128)(2,1)}), bf16[4,9,8,256]{3,2,1,0:T(8,128)(2,1)S(1)}, u32[]{:S(2)}, u32[]{:S(2)}) %all-to-all-start) | async-done | bytes 147488 | tf_op jit(solution)/shard_map/all_to_all | solution.py:255
  31.8 0.7 %copy-done.8 = bf16[4,9,8,256]{3,2,1,0:T(8,128)(2,1)} copy-done((bf16[4,9,8,256]{3,2,1,0:T(8,128)(2,1)}, bf16[4,9,8,256]{3,2,1,0:T(8,128)(2,1)S(1)}, u32[]{:S(2)}) %copy-start.8) | copy-done | bytes 147480
  32.5 11.0 %shard_map.118 = bf16[9,8,1024]{2,1,0:T(8,128)(2,1)} custom-call(f32[8,1]{1,0:T(8,128)} %reshape_tile.4.hs_ref, bf16[4,9,8,256]{3,2,1,0:T(8,128)(2,1)} %copy-done.8, bf16[64,8]{1,0:T(8,128)(2,1)} %bitcast.212, f32[64,1]{1,0:T(8,128)} %copy.50.gain_ref, bf16[192,64]{1,0:T(8,128)(2,1)} %bitcast.209, bf16[64,64]{1,0:T(8,128)(2,1)} %bitcast.211, ...), custom_call_target="tpu_custom_call" | custom-call | tf_op jit(solution)/shard_map/pallas_call | solution.py:141
  43.5 0.7 %slice.372 = bf16[1,8,1024]{2,1,0:T(8,128)(2,1)S(1)} slice(bf16[9,8,1024]{2,1,0:T(8,128)(2,1)} %shard_map.118), slice={[8:9], [0:8], [0:1024]} | slice | bytes 32768 | tf_op jit(solution)/shard_map/slice | solution.py:270
  44.2 0.9 %copy_bitcast_fusion.2 = bf16[8,8,8,128]{3,1,2,0:T(8,128)(2,1)S(1)} fusion(bf16[9,8,1024]{2,1,0:T(8,128)(2,1)} %shard_map.118), kind=kLoop, calls=%fused_computation.84 | loop fusion | bytes 262144 | tf_op jit(solution)/shard_map/transpose | solution.py:269
  45.1 0.1 reshape_squeeze.3
  45.5 0.2 pad_maximum_fusion.7
  45.7 0.3 reshape.205
  46.0 2.3 %collective-permute-start.2 = (bf16[8,8,1152]{2,1,0:T(8,128)(2,1)S(1)}, bf16[8,8,1152]{2,1,0:T(8,128)(2,1)S(1)}, u32[]{:S(2)}, u32[]{:S(2)}) collective-permute-start(bf16[8,8,1152]{2,1,0:T(8,128)(2,1)S(1)} %reshape.205), channel_id=1, source_target_pairs={{0,1},{1,2},{2,3},{3,4},{4,5},{5,6},{6,7},{8,9},{9,10},{10,11},{11... | collective-permute-start | bytes 442376 | tf_op jit(solution)/shard_map/ppermute | solution.py:34
  48.3 4.1 %collective-permute-start.3 = (bf16[8,8,1152]{2,1,0:T(8,128)(2,1)S(1)}, bf16[8,8,1152]{2,1,0:T(8,128)(2,1)S(1)}, u32[]{:S(2)}, u32[]{:S(2)}) collective-permute-start(bf16[8,8,1152]{2,1,0:T(8,128)(2,1)S(1)} %reshape.205), channel_id=1, source_target_pairs={{1,0},{2,1},{3,2},{4,3},{5,4},{6,5},{7,6},{9,8},{10,9},{11,10},{12... | collective-permute-start | bytes 442376 | tf_op jit(solution)/shard_map/ppermute | solution.py:35
  52.5 0.3 collective-permute-done.2
  52.8 0.4 reshape.206
  53.2 4.1 %collective-permute-done.3 = bf16[8,8,1152]{2,1,0:T(8,128)(2,1)S(1)} collective-permute-done((bf16[8,8,1152]{2,1,0:T(8,128)(2,1)S(1)}, bf16[8,8,1152]{2,1,0:T(8,128)(2,1)S(1)}, u32[]{:S(2)}, u32[]{:S(2)}) %collective-permute-start.3) | collective-permute-done | bytes 147488 | tf_op jit(solution)/shard_map/ppermute | solution.py:35
  57.3 0.4 reshape.207
  57.8 0.2 pad_maximum_fusion.1
  58.0 0.4 pad_maximum_fusion.3
  58.4 0.3 fusion.12
  58.7 0.4 convolution_add_fusion.7
  59.0 0.4 convolution_add_fusion.6
  59.4 0.3 convolution_add_fusion.5
  59.7 0.4 convolution_add_fusion.4
  60.0 0.4 convolution_add_fusion.3
  60.4 0.3 convolution_add_fusion.2
  60.7 0.3 convolution_add_fusion.1
  61.1 0.5 select_convert_fusion
  61.6 0.2 fusion.24
  61.8 0.2 convolution_add_fusion.15
  62.0 0.2 convolution_add_fusion.14
  62.2 0.2 convolution_add_fusion.13
  62.4 0.2 convolution_add_fusion.12
  62.7 0.2 convolution_add_fusion.11
  62.9 0.2 convolution_add_fusion.10
  63.1 0.2 convolution_add_fusion.9
  63.3 0.3 copy-done.3
  63.6 0.2 fusion.3
  63.8 0.7 %copy.76 = bf16[8,8,8,128]{3,2,1,0:T(8,128)(2,1)} copy(bf16[8,8,8,128]{3,1,2,0:T(8,128)(2,1)S(1)} %fusion.3) | data formatting | bytes 262144 | tf_op jit(solution)/shard_map/convert_element_type | solution.py:285
  (85 shorter events, 4.1 us)
Async XLA Ops:
  0.0 9.8 %copy-start = (bf16[64,64]{1,0:T(8,128)(2,1)S(1)}, bf16[64,64]{1,0:T(8,128)(2,1)}, u32[]{:S(2)}) copy-start(bf16[64,64]{1,0:T(8,128)(2,1)} %param.20) | copy-start | bytes 24580
  0.0 1.3 %copy-start.7 = (f32[2,8,8,512]{3,2,1,0:T(8,128)S(1)}, f32[2,8,8,512]{3,2,1,0:T(8,128)}, u32[]{:S(2)}) copy-start(f32[2,8,8,512]{3,2,1,0:T(8,128)} %param.12) | copy-start | bytes 786436
  1.3 6.7 %copy-start.1 = (bf16[9,8,8]{0,2,1:T(8,128)(2,1)S(1)}, bf16[9,8,8]{0,2,1:T(8,128)(2,1)}, u32[]{:S(2)}) copy-start(bf16[9,8,8]{0,2,1:T(8,128)(2,1)} %param.22) | copy-start | bytes 3460
  1.4 6.7 %copy-start.2 = (bf16[9,8,8]{0,2,1:T(8,128)(2,1)S(1)}, bf16[9,8,8]{0,2,1:T(8,128)(2,1)}, u32[]{:S(2)}) copy-start(bf16[9,8,8]{0,2,1:T(8,128)(2,1)} %param.23) | copy-start | bytes 3460
  1.4 6.9 %copy-start.10 = (bf16[64,192]{1,0:T(8,128)(2,1)S(1)}, bf16[64,192]{1,0:T(8,128)(2,1)}, u32[]{:S(2)}) copy-start(bf16[64,192]{1,0:T(8,128)(2,1)} %param.18) | copy-start | bytes 73732
  1.4 14.3 %collective-permute-start = (f32[136,512]{1,0:T(8,128)S(1)}, f32[136,512]{1,0:T(8,128)S(1)}, u32[]{:S(2)}, u32[]{:S(2)}) collective-permute-start(f32[136,512]{1,0:T(8,128)S(1)} %pad_maximum_fusion.5), channel_id=1, source_target_pairs={{0,1},{1,2},{2,3},{3,4},{4,5},{5,6},{6,7},{8,9},{9,10},{10,11},{11... | collective-permute-start | bytes 835592 | tf_op jit(solution)/shard_map/ppermute | solution.py:207
  4.7 6.4 %copy-start.12 = (f32[64]{0:T(128)S(1)}, f32[64]{0:T(128)}, u32[]{:S(2)}) copy-start(f32[64]{0:T(128)} %param.17) | copy-start | bytes 772
  4.7 7.1 %copy-start.11 = (bf16[8,64]{1,0:T(8,128)(2,1)S(1)}, bf16[8,64]{1,0:T(8,128)(2,1)}, u32[]{:S(2)}) copy-start(bf16[8,64]{1,0:T(8,128)(2,1)} %param.16) | copy-start | bytes 3076
  4.7 7.8 %copy-start.13 = (f32[4]{0:T(128)S(1)}, f32[4]{0:T(128)}, u32[]{:S(2)}) copy-start(f32[4]{0:T(128)} %param.19) | copy-start | bytes 52
  4.8 14.0 %collective-permute-start.1 = (f32[136,512]{1,0:T(8,128)S(1)}, f32[136,512]{1,0:T(8,128)S(1)}, u32[]{:S(2)}, u32[]{:S(2)}) collective-permute-start(f32[136,512]{1,0:T(8,128)S(1)} %pad_maximum_fusion.6), channel_id=1, source_target_pairs={{1,0},{2,1},{3,2},{4,3},{5,4},{6,5},{7,6},{9,8},{10,9},{11,10},{12... | collective-permute-start | bytes 835592 | tf_op jit(solution)/shard_map/ppermute | solution.py:215
  8.4 10.4 %copy-start.4 = (f32[8,8,512]{2,1,0:T(8,128)S(1)}, f32[8,8,512]{2,1,0:T(8,128)}, u32[]{:S(2)}) copy-start(f32[8,8,512]{2,1,0:T(8,128)} %param.15) | copy-start | bytes 393220
  8.5 10.4 %copy-start.5 = (f32[8,8,512]{2,1,0:T(8,128)S(1)}, f32[8,8,512]{2,1,0:T(8,128)}, u32[]{:S(2)}) copy-start(f32[8,8,512]{2,1,0:T(8,128)} %param.14) | copy-start | bytes 393220
  8.5 10.4 %copy-start.6 = (f32[8,8,512]{2,1,0:T(8,128)S(1)}, f32[8,8,512]{2,1,0:T(8,128)}, u32[]{:S(2)}) copy-start(f32[8,8,512]{2,1,0:T(8,128)} %param.13) | copy-start | bytes 393220
  18.8 0.7 %copy-start.9 = (f32[136,512]{1,0:T(8,128)}, f32[136,512]{1,0:T(8,128)S(1)}, u32[]{:S(2)}) copy-start(f32[136,512]{1,0:T(8,128)S(1)} %collective-permute-done.1) | copy-start | bytes 835588
  24.3 7.5 %all-to-all-start = ((bf16[4,9,8,256]{3,2,1,0:T(8,128)(2,1)}), bf16[4,9,8,256]{3,2,1,0:T(8,128)(2,1)S(1)}, u32[]{:S(2)}, u32[]{:S(2)}) async-start(bf16[4,9,8,256]{3,2,1,0:T(8,128)(2,1)} %pad_maximum_fusion.8), calls=%async_computation | async-start | bytes 294912 | tf_op jit(solution)/shard_map/all_to_all | solution.py:255
  31.8 0.7 %copy-start.8 = (bf16[4,9,8,256]{3,2,1,0:T(8,128)(2,1)}, bf16[4,9,8,256]{3,2,1,0:T(8,128)(2,1)S(1)}, u32[]{:S(2)}) copy-start(bf16[4,9,8,256]{3,2,1,0:T(8,128)(2,1)S(1)} %all-to-all-done.x_ref) | copy-start | bytes 442372
  46.0 6.8 %collective-permute-start.2 = (bf16[8,8,1152]{2,1,0:T(8,128)(2,1)S(1)}, bf16[8,8,1152]{2,1,0:T(8,128)(2,1)S(1)}, u32[]{:S(2)}, u32[]{:S(2)}) collective-permute-start(bf16[8,8,1152]{2,1,0:T(8,128)(2,1)S(1)} %reshape.205), channel_id=1, source_target_pairs={{0,1},{1,2},{2,3},{3,4},{4,5},{5,6},{6,7},{8,9},{9,10},{10,11},{11... | collective-permute-start | bytes 442376 | tf_op jit(solution)/shard_map/ppermute | solution.py:34
  48.3 9.0 %collective-permute-start.3 = (bf16[8,8,1152]{2,1,0:T(8,128)(2,1)S(1)}, bf16[8,8,1152]{2,1,0:T(8,128)(2,1)S(1)}, u32[]{:S(2)}, u32[]{:S(2)}) collective-permute-start(bf16[8,8,1152]{2,1,0:T(8,128)(2,1)S(1)} %reshape.205), channel_id=1, source_target_pairs={{1,0},{2,1},{3,2},{4,3},{5,4},{6,5},{7,6},{9,8},{10,9},{11,10},{12... | collective-permute-start | bytes 442376 | tf_op jit(solution)/shard_map/ppermute | solution.py:35
  62.6 0.9 %copy-start.3 = (bf16[9,8,1024]{2,1,0:T(8,128)(2,1)S(1)}, bf16[9,8,1024]{2,1,0:T(8,128)(2,1)}, u32[]{:S(2)}) copy-start(bf16[9,8,1024]{2,1,0:T(8,128)(2,1)} %shard_map.118) | copy-start | bytes 442372

commit v11 on v10

--- a/solution.py
+++ b/solution.py
@@ -202,7 +202,7 @@
     def pack(states_part, coef_part):
         return jnp.concatenate(
             [states_part.reshape(-1, cols), coef_part.reshape(-1, cols)], axis=0
-        )
+        ).astype(jnp.bfloat16)
 
     low = lax.ppermute(
         pack(
@@ -215,6 +215,8 @@
     high = lax.ppermute(
         pack(starting_states[:, :, :state_halo], coefficients[:, :, :coef_halo]), "row", backward
     )
+    low = low.astype(jnp.float32)
+    high = high.astype(jnp.float32)
     split = members_here * starting_states.shape[1] * state_halo
     state_shape = starting_states.shape[:2] + (state_halo, cols)
     coef_shape = coefficients.shape[:2] + (coef_halo, cols)

time: 65.5 us -> 61.8 us (0.944)
  waiting for transfers between devices: 11.3 us -> 8.18 us
  local copies, waits for them, and re-layouts: 15 us -> 13.6 us
  starting transfers between devices: 16.3 us -> 17.1 us
    ppermute x1, waiting for transfers between devices: 3 us -> 0.01 us  [on_device(): lax.ppermute(pack(starting_states[:, :, :state_halo], coefficients[:, :,...]
    slice x1, local copies, waits for them, and re-layouts: 0.91 us -> 0.01 us  [on_device(): high[:split].reshape(state_shape)]
    all_to_all x1, starting transfers between devices: 3.79 us -> 4.54 us  [on_device(): lax.all_to_all(by_chunk, 'mem', split_axis=0, concat_axis=0, tiled=True)]
    unnamed x48 -> x46, local copies, waits for them, and re-layouts: 4.65 us -> 4.2 us
  transfers between devices with their start and end apart: 5 -> 5, of which waited for: 5 -> 3; matrix products, arithmetic and copies ran while one was open for 13% -> 14% of each run, Pallas kernels for 0% -> 0%
where the time goes in v11:
time: 61.8 us; the launch traced here: 60.8 us
  starting transfers between devices  17.1 us (28%)
  local copies, waits for them, and re-layouts  13.6 us (22%)
  Pallas kernels  11 us (18%)
  waiting for transfers between devices  8.18 us (13%)
  other arithmetic  5.14 us (8%)
  matrix products  5 us (8%)
  between operations  0.74 us (1%)
    pallas_call x1, Pallas kernels, post_block(): pl.pallas_call(functools.partial(attention_kernel, chunk=chunk, heads=hea...  11 us
    dot_general x18, matrix products, convolve(): jnp.einsum('oc,mcij->moij', kernel[row_stencil * 3 + column_stencil], shi...  5 us
    all_to_all x1, starting transfers between devices, on_device(): lax.all_to_all(by_chunk, 'mem', split_axis=0, concat_axis=0, tiled=True)  4.54 us
    unnamed x46, local copies, waits for them, and re-layouts  4.2 us
    ppermute x1, starting transfers between devices, row_padded(): high = lax.ppermute(block[..., :width, :].reshape(flat), 'row', backward)  4.14 us
    ppermute x1, waiting for transfers between devices, row_padded(): high = lax.ppermute(block[..., :width, :].reshape(flat), 'row', backward)  4.11 us
    all_to_all x1, waiting for transfers between devices, on_device(): lax.all_to_all(by_chunk, 'mem', split_axis=0, concat_axis=0, tiled=True)  3.72 us
    ppermute x1, starting transfers between devices, on_device(): lax.ppermute(pack(starting_states[:, :, row_total - state_halo:], coeffic...  3.12 us
  transfers between devices with their start and end apart: 5, of which 3 were waited for; matrix products, arithmetic and copies ran while one was open for 14% of the time, Pallas kernels for 0%

profile of v11, /device:TPU:9, one launch (start us, length us, event | category | flops | bytes accessed | tf_op | source)
XLA Modules:
  0.0 60.8 jit_solution(5628881439674100067)
XLA Ops:
  0.0 1.1 %maximum_convert_fusion = bf16[3,8,8,512]{3,2,1,0:T(8,128)(2,1)S(1)} fusion(f32[1,8,8,512]{3,2,1,0:T(8,128)} %bitcast.199, f32[1,8,8,512]{3,2,1,0:T(8,128)} %bitcast.201, f32[1,8,8,512]{3,2,1,0:T(8,128)} %bitcast.203), kind=kLoop, calls=%fused_computation.47 | loop fusion | flops 196608 | bytes 589824 | tf_op jit(solution)/shard_map/convert.9
  1.5 3.1 %collective-permute-start = (bf16[136,512]{1,0:T(8,128)(2,1)S(1)}, bf16[136,512]{1,0:T(8,128)(2,1)S(1)}, u32[]{:S(2)}, u32[]{:S(2)}) collective-permute-start(bf16[136,512]{1,0:T(8,128)(2,1)S(1)} %pad_maximum_fusion.6), channel_id=1, source_target_pairs={{0,1},{1,2},{2,3},{3,4},{4,5},{5,6},{6,7},{8,9},{9,10},{10,11},{11... | collective-permute-start | bytes 417800 | tf_op jit(solution)/shard_map/ppermute | solution.py:207
  4.7 3.1 %collective-permute-start.1 = (bf16[136,512]{1,0:T(8,128)(2,1)S(1)}, bf16[136,512]{1,0:T(8,128)(2,1)S(1)}, u32[]{:S(2)}, u32[]{:S(2)}) collective-permute-start(bf16[136,512]{1,0:T(8,128)(2,1)S(1)} %pad_maximum_fusion.7), channel_id=1, source_target_pairs={{1,0},{2,1},{3,2},{4,3},{5,4},{6,5},{7,6},{9,8},{10,9},{11,10},{12... | collective-permute-start | bytes 417800 | tf_op jit(solution)/shard_map/ppermute | solution.py:215
  8.4 0.7 %gather_fusion = bf16[64,3,64]{2,1,0:T(4,128)(2,1)S(1)} fusion(bf16[3,64,64]{2,0,1:T(4,128)(2,1)S(1)} %copy.46, s32[1024]{0:T(1024)S(1)} %pad_clamp_fusion), kind=kCustom, calls=%fused_computation | custom fusion | bytes 49408 | tf_op jit(solution)/shard_map/gather | solution.py:138
  9.1 0.6 %copy.47 = bf16[3,64,64]{2,1,0:T(8,128)(2,1)} copy(bf16[3,64,64]{2,0,1:T(4,128)(2,1)S(1)} %bitcast.208) | data formatting | bytes 49152 | tf_op jit(solution)/shard_map/gather | solution.py:138
  9.7 0.6 %gather_fusion.1 = bf16[64,64]{1,0:T(8,128)(2,1)S(1)} fusion(bf16[64,64]{0,1:T(8,128)(2,1)S(1)} %bitcast.197, s32[1024]{0:T(1024)S(1)} %pad_clamp_fusion), kind=kCustom, calls=%fused_computation.1 | custom fusion | bytes 16640 | tf_op jit(solution)/shard_map/gather | solution.py:139
  10.4 0.7 %copy.48 = bf16[64,64]{0,1:T(8,128)(2,1)} copy(bf16[64,64]{1,0:T(8,128)(2,1)S(1)} %gather_fusion.1) | data formatting | bytes 16384 | tf_op jit(solution)/shard_map/gather | solution.py:139
  11.0 0.7 %copy.50.gain_ref = f32[64,1]{1,0:T(8,128)} copy(f32[64,1]{0,1:T(1,128)S(1)} %bitcast.214) | data formatting | bytes 512 | tf_op jit(solution)/shard_map/reshape | solution.py:148
  11.7 0.7 %copy.44 = bf16[8,64]{0,1:T(8,128)(2,1)} copy(bf16[8,64]{1,0:T(8,128)(2,1)S(1)} %copy-done.10) | data formatting | bytes 2048 | tf_op args[4]
  12.4 0.7 %reshape_tile.4.hs_ref = f32[8,1]{1,0:T(8,128)} reshape(f32[2,4]{1,0:T(2,128)S(1)} %tile.2) | data formatting | bytes 64 | tf_op jit(solution)/shard_map/reshape;tile | solution.py:140
  13.8 0.1 copy.102
  13.9 0.1 copy.103
  14.0 0.1 copy.104
  14.2 0.1 copy.105
  14.3 0.1 copy.106
  14.4 0.1 copy.107
  14.6 0.1 copy.108
  14.7 0.1 copy.109
  14.8 0.1 copy.110
  15.0 0.1 copy.111
  15.8 0.1 pad_maximum_fusion
  16.5 0.5 add_select_fusion.2
  17.1 0.5 add_select_fusion.1
  17.7 0.5 add_select_fusion
  18.3 0.3 select_convert_fusion.1
  19.0 0.2 reshape.200
  19.2 0.7 %pad_maximum_fusion.5 = bf16[4,9,8,256]{3,2,1,0:T(8,128)(2,1)} fusion(bf16[4,1,8,256]{3,2,1,0:T(8,128)(2,1)S(1)} %reshape.200, bf16[4,8,8,256]{3,2,1,0:T(8,128)(2,1)S(1)} %bitcast.207), kind=kLoop, calls=%fused_computation.63 | loop fusion | flops 73728 | bytes 294912 | tf_op jit(solution)/shard_map/concatenate | solution.py:256
  19.9 4.5 %all-to-all-start = ((bf16[4,9,8,256]{3,2,1,0:T(8,128)(2,1)}), bf16[4,9,8,256]{3,2,1,0:T(8,128)(2,1)S(1)}, u32[]{:S(2)}, u32[]{:S(2)}) async-start(bf16[4,9,8,256]{3,2,1,0:T(8,128)(2,1)} %pad_maximum_fusion.5), calls=%async_computation | async-start | bytes 294912 | tf_op jit(solution)/shard_map/all_to_all | solution.py:257
  24.4 3.7 %all-to-all-done.x_ref = bf16[4,9,8,256]{3,2,1,0:T(8,128)(2,1)S(1)} async-done(((bf16[4,9,8,256]{3,2,1,0:T(8,128)(2,1)}), bf16[4,9,8,256]{3,2,1,0:T(8,128)(2,1)S(1)}, u32[]{:S(2)}, u32[]{:S(2)}) %all-to-all-start) | async-done | bytes 147488 | tf_op jit(solution)/shard_map/all_to_all | solution.py:257
  28.1 0.7 %copy-done.8 = bf16[4,9,8,256]{3,2,1,0:T(8,128)(2,1)} copy-done((bf16[4,9,8,256]{3,2,1,0:T(8,128)(2,1)}, bf16[4,9,8,256]{3,2,1,0:T(8,128)(2,1)S(1)}, u32[]{:S(2)}) %copy-start.8) | copy-done | bytes 147480
  28.8 11.0 %shard_map.118 = bf16[9,8,1024]{2,1,0:T(8,128)(2,1)} custom-call(f32[8,1]{1,0:T(8,128)} %reshape_tile.4.hs_ref, bf16[4,9,8,256]{3,2,1,0:T(8,128)(2,1)} %copy-done.8, bf16[64,8]{1,0:T(8,128)(2,1)} %bitcast.212, f32[64,1]{1,0:T(8,128)} %copy.50.gain_ref, bf16[192,64]{1,0:T(8,128)(2,1)} %bitcast.209, bf16[64,64]{1,0:T(8,128)(2,1)} %bitcast.211, ...), custom_call_target="tpu_custom_call" | custom-call | tf_op jit(solution)/shard_map/pallas_call | solution.py:141
  39.8 0.7 %slice.378 = bf16[1,8,1024]{2,1,0:T(8,128)(2,1)S(1)} slice(bf16[9,8,1024]{2,1,0:T(8,128)(2,1)} %shard_map.118), slice={[8:9], [0:8], [0:1024]} | slice | bytes 32768 | tf_op jit(solution)/shard_map/slice | solution.py:272
  40.5 0.9 %copy_bitcast_fusion.2 = bf16[8,8,8,128]{3,1,2,0:T(8,128)(2,1)S(1)} fusion(bf16[9,8,1024]{2,1,0:T(8,128)(2,1)} %shard_map.118), kind=kLoop, calls=%fused_computation.84 | loop fusion | bytes 262144 | tf_op jit(solution)/shard_map/transpose | solution.py:271
  41.4 0.1 reshape_squeeze.3
  41.8 0.2 pad_maximum_fusion.4
  42.0 0.3 reshape.209
  42.3 2.2 %collective-permute-start.2 = (bf16[8,8,1152]{2,1,0:T(8,128)(2,1)S(1)}, bf16[8,8,1152]{2,1,0:T(8,128)(2,1)S(1)}, u32[]{:S(2)}, u32[]{:S(2)}) collective-permute-start(bf16[8,8,1152]{2,1,0:T(8,128)(2,1)S(1)} %reshape.209), channel_id=1, source_target_pairs={{0,1},{1,2},{2,3},{3,4},{4,5},{5,6},{6,7},{8,9},{9,10},{10,11},{11... | collective-permute-start | bytes 442376 | tf_op jit(solution)/shard_map/ppermute | solution.py:34
  44.5 4.1 %collective-permute-start.3 = (bf16[8,8,1152]{2,1,0:T(8,128)(2,1)S(1)}, bf16[8,8,1152]{2,1,0:T(8,128)(2,1)S(1)}, u32[]{:S(2)}, u32[]{:S(2)}) collective-permute-start(bf16[8,8,1152]{2,1,0:T(8,128)(2,1)S(1)} %reshape.209), channel_id=1, source_target_pairs={{1,0},{2,1},{3,2},{4,3},{5,4},{6,5},{7,6},{9,8},{10,9},{11,10},{12... | collective-permute-start | bytes 442376 | tf_op jit(solution)/shard_map/ppermute | solution.py:35
  48.8 0.3 collective-permute-done.2
  49.1 0.4 reshape.210
  49.5 4.1 %collective-permute-done.3 = bf16[8,8,1152]{2,1,0:T(8,128)(2,1)S(1)} collective-permute-done((bf16[8,8,1152]{2,1,0:T(8,128)(2,1)S(1)}, bf16[8,8,1152]{2,1,0:T(8,128)(2,1)S(1)}, u32[]{:S(2)}, u32[]{:S(2)}) %collective-permute-start.3) | collective-permute-done | bytes 147488 | tf_op jit(solution)/shard_map/ppermute | solution.py:35
  53.6 0.4 reshape.211
  54.0 0.2 pad_maximum_fusion.1
  54.3 0.4 pad_maximum_fusion.3
  54.7 0.3 fusion.12
  55.0 0.4 convolution_add_fusion.7
  55.3 0.3 convolution_add_fusion.6
  55.7 0.3 convolution_add_fusion.5
  56.0 0.3 convolution_add_fusion.4
  56.3 0.4 convolution_add_fusion.3
  56.7 0.3 convolution_add_fusion.2
  57.0 0.4 convolution_add_fusion.1
  57.3 0.5 select_convert_fusion
  57.9 0.2 fusion.24
  58.0 0.2 convolution_add_fusion.15
  58.3 0.2 convolution_add_fusion.14
  58.5 0.2 convolution_add_fusion.13
  58.7 0.2 convolution_add_fusion.12
  58.9 0.2 convolution_add_fusion.11
  59.2 0.2 convolution_add_fusion.10
  59.3 0.2 convolution_add_fusion.9
  59.6 0.3 copy-done.3
  59.8 0.2 fusion.3
  60.1 0.7 %copy.76 = bf16[8,8,8,128]{3,2,1,0:T(8,128)(2,1)} copy(bf16[8,8,8,128]{3,1,2,0:T(8,128)(2,1)S(1)} %fusion.3) | data formatting | bytes 262144 | tf_op jit(solution)/shard_map/convert_element_type | solution.py:287
  (84 shorter events, 3.6 us)
Async XLA Ops:
  0.0 9.7 %copy-start = (bf16[64,64]{1,0:T(8,128)(2,1)S(1)}, bf16[64,64]{1,0:T(8,128)(2,1)}, u32[]{:S(2)}) copy-start(bf16[64,64]{1,0:T(8,128)(2,1)} %param.20) | copy-start | bytes 24580
  0.0 1.3 %copy-start.7 = (f32[2,8,8,512]{3,2,1,0:T(8,128)S(1)}, f32[2,8,8,512]{3,2,1,0:T(8,128)}, u32[]{:S(2)}) copy-start(f32[2,8,8,512]{3,2,1,0:T(8,128)} %param.12) | copy-start | bytes 786436
  1.1 6.9 %copy-start.1 = (bf16[9,8,8]{0,2,1:T(8,128)(2,1)S(1)}, bf16[9,8,8]{0,2,1:T(8,128)(2,1)}, u32[]{:S(2)}) copy-start(bf16[9,8,8]{0,2,1:T(8,128)(2,1)} %param.22) | copy-start | bytes 3460
  1.2 6.9 %copy-start.2 = (bf16[9,8,8]{0,2,1:T(8,128)(2,1)S(1)}, bf16[9,8,8]{0,2,1:T(8,128)(2,1)}, u32[]{:S(2)}) copy-start(bf16[9,8,8]{0,2,1:T(8,128)(2,1)} %param.23) | copy-start | bytes 3460
  1.3 6.9 %copy-start.9 = (bf16[64,192]{1,0:T(8,128)(2,1)S(1)}, bf16[64,192]{1,0:T(8,128)(2,1)}, u32[]{:S(2)}) copy-start(bf16[64,192]{1,0:T(8,128)(2,1)} %param.18) | copy-start | bytes 73732
  1.4 9.6 %copy-start.11 = (f32[64]{0:T(128)S(1)}, f32[64]{0:T(128)}, u32[]{:S(2)}) copy-start(f32[64]{0:T(128)} %param.17) | copy-start | bytes 772
  1.4 10.3 %copy-start.10 = (bf16[8,64]{1,0:T(8,128)(2,1)S(1)}, bf16[8,64]{1,0:T(8,128)(2,1)}, u32[]{:S(2)}) copy-start(bf16[8,64]{1,0:T(8,128)(2,1)} %param.16) | copy-start | bytes 3076
  1.4 11.0 %copy-start.12 = (f32[4]{0:T(128)S(1)}, f32[4]{0:T(128)}, u32[]{:S(2)}) copy-start(f32[4]{0:T(128)} %param.19) | copy-start | bytes 52
  1.5 14.1 %collective-permute-start = (bf16[136,512]{1,0:T(8,128)(2,1)S(1)}, bf16[136,512]{1,0:T(8,128)(2,1)S(1)}, u32[]{:S(2)}, u32[]{:S(2)}) collective-permute-start(bf16[136,512]{1,0:T(8,128)(2,1)S(1)} %pad_maximum_fusion.6), channel_id=1, source_target_pairs={{0,1},{1,2},{2,3},{3,4},{4,5},{5,6},{6,7},{8,9},{9,10},{10,11},{11... | collective-permute-start | bytes 417800 | tf_op jit(solution)/shard_map/ppermute | solution.py:207
  4.7 10.9 %collective-permute-start.1 = (bf16[136,512]{1,0:T(8,128)(2,1)S(1)}, bf16[136,512]{1,0:T(8,128)(2,1)S(1)}, u32[]{:S(2)}, u32[]{:S(2)}) collective-permute-start(bf16[136,512]{1,0:T(8,128)(2,1)S(1)} %pad_maximum_fusion.7), channel_id=1, source_target_pairs={{1,0},{2,1},{3,2},{4,3},{5,4},{6,5},{7,6},{9,8},{10,9},{11,10},{12... | collective-permute-start | bytes 417800 | tf_op jit(solution)/shard_map/ppermute | solution.py:215
  8.4 7.4 %copy-start.4 = (f32[8,8,512]{2,1,0:T(8,128)S(1)}, f32[8,8,512]{2,1,0:T(8,128)}, u32[]{:S(2)}) copy-start(f32[8,8,512]{2,1,0:T(8,128)} %param.15) | copy-start | bytes 393220
  8.4 7.4 %copy-start.5 = (f32[8,8,512]{2,1,0:T(8,128)S(1)}, f32[8,8,512]{2,1,0:T(8,128)}, u32[]{:S(2)}) copy-start(f32[8,8,512]{2,1,0:T(8,128)} %param.14) | copy-start | bytes 393220
  8.4 7.4 %copy-start.6 = (f32[8,8,512]{2,1,0:T(8,128)S(1)}, f32[8,8,512]{2,1,0:T(8,128)}, u32[]{:S(2)}) copy-start(f32[8,8,512]{2,1,0:T(8,128)} %param.13) | copy-start | bytes 393220
  19.9 8.3 %all-to-all-start = ((bf16[4,9,8,256]{3,2,1,0:T(8,128)(2,1)}), bf16[4,9,8,256]{3,2,1,0:T(8,128)(2,1)S(1)}, u32[]{:S(2)}, u32[]{:S(2)}) async-start(bf16[4,9,8,256]{3,2,1,0:T(8,128)(2,1)} %pad_maximum_fusion.5), calls=%async_computation | async-start | bytes 294912 | tf_op jit(solution)/shard_map/all_to_all | solution.py:257
  28.1 0.7 %copy-start.8 = (bf16[4,9,8,256]{3,2,1,0:T(8,128)(2,1)}, bf16[4,9,8,256]{3,2,1,0:T(8,128)(2,1)S(1)}, u32[]{:S(2)}) copy-start(bf16[4,9,8,256]{3,2,1,0:T(8,128)(2,1)S(1)} %all-to-all-done.x_ref) | copy-start | bytes 442372
  42.3 6.8 %collective-permute-start.2 = (bf16[8,8,1152]{2,1,0:T(8,128)(2,1)S(1)}, bf16[8,8,1152]{2,1,0:T(8,128)(2,1)S(1)}, u32[]{:S(2)}, u32[]{:S(2)}) collective-permute-start(bf16[8,8,1152]{2,1,0:T(8,128)(2,1)S(1)} %reshape.209), channel_id=1, source_target_pairs={{0,1},{1,2},{2,3},{3,4},{4,5},{5,6},{6,7},{8,9},{9,10},{10,11},{11... | collective-permute-start | bytes 442376 | tf_op jit(solution)/shard_map/ppermute | solution.py:34
  44.5 9.1 %collective-permute-start.3 = (bf16[8,8,1152]{2,1,0:T(8,128)(2,1)S(1)}, bf16[8,8,1152]{2,1,0:T(8,128)(2,1)S(1)}, u32[]{:S(2)}, u32[]{:S(2)}) collective-permute-start(bf16[8,8,1152]{2,1,0:T(8,128)(2,1)S(1)} %reshape.209), channel_id=1, source_target_pairs={{1,0},{2,1},{3,2},{4,3},{5,4},{6,5},{7,6},{9,8},{10,9},{11,10},{12... | collective-permute-start | bytes 442376 | tf_op jit(solution)/shard_map/ppermute | solution.py:35
  58.9 0.9 %copy-start.3 = (bf16[9,8,1024]{2,1,0:T(8,128)(2,1)S(1)}, bf16[9,8,1024]{2,1,0:T(8,128)(2,1)}, u32[]{:S(2)}) copy-start(bf16[9,8,1024]{2,1,0:T(8,128)(2,1)} %shard_map.118) | copy-start | bytes 442372

commit v12 on v10

--- a/solution.py
+++ b/solution.py
@@ -200,8 +200,11 @@
     cols = starting_states.shape[3]
 
     def pack(states_part, coef_part):
+        states_flat = states_part.reshape(-1, cols)
+        states_high = states_flat.astype(jnp.bfloat16)
+        states_low = (states_flat - states_high.astype(jnp.float32)).astype(jnp.bfloat16)
         return jnp.concatenate(
-            [states_part.reshape(-1, cols), coef_part.reshape(-1, cols)], axis=0
+            [states_high, states_low, coef_part.reshape(-1, cols).astype(jnp.bfloat16)], axis=0
         )
 
     low = lax.ppermute(
@@ -216,14 +219,22 @@
         pack(starting_states[:, :, :state_halo], coefficients[:, :, :coef_halo]), "row", backward
     )
     split = members_here * starting_states.shape[1] * state_halo
+
+    def unpack(received):
+        received = received.astype(jnp.float32)
+        states_part = received[:split] + received[split : 2 * split]
+        return states_part, received[2 * split :]
+
+    low_states, low_coefs = unpack(low)
+    high_states, high_coefs = unpack(high)
     state_shape = starting_states.shape[:2] + (state_halo, cols)
     coef_shape = coefficients.shape[:2] + (coef_halo, cols)
     gridded_quantity_list = jnp.concatenate(
-        [low[:split].reshape(state_shape), starting_states, high[:split].reshape(state_shape)],
+        [low_states.reshape(state_shape), starting_states, high_states.reshape(state_shape)],
         axis=2,
     )
     coef_rows = jnp.concatenate(
-        [low[split:].reshape(coef_shape), coefficients, high[split:].reshape(coef_shape)], axis=2
+        [low_coefs.reshape(coef_shape), coefficients, high_coefs.reshape(coef_shape)], axis=2
     )
     first_row = lax.axis_index("row") * row_total - STEPS
     all_rows = lax.axis_size("row") * row_total

time: 65.5 us -> 63.5 us (0.969)
  waiting for transfers between devices: 11.3 us -> 8.18 us
  other arithmetic: 5.14 us -> 6.15 us
  starting transfers between devices: 16.3 us -> 17.1 us
  local copies, waits for them, and re-layouts: 15 us -> 14.3 us
    ppermute x1, waiting for transfers between devices: 3 us -> 0.01 us  [on_device(): lax.ppermute(pack(starting_states[:, :, :state_halo], coefficients[:, :,...]
    slice x4 -> x2, local copies, waits for them, and re-layouts: 0.95 us -> 0.03 us  [unpack(): return (states_part, received[2 * split:])]
    concatenate x4, other arithmetic: 0.27 us -> 1.17 us  [the longest x1 1 us: on_device(): jnp.concatenate([low_states.reshape(state_shape), starting_states, high_s...]
    all_to_all x1, starting transfers between devices: 3.79 us -> 4.54 us  [on_device(): lax.all_to_all(by_chunk, 'mem', split_axis=0, concat_axis=0, tiled=True)]
    unnamed x48 -> x46, local copies, waits for them, and re-layouts: 4.65 us -> 4.16 us
  transfers between devices with their start and end apart: 5 -> 5, of which waited for: 5 -> 3; matrix products, arithmetic and copies ran while one was open for 13% -> 13% of each run, Pallas kernels for 0% -> 0%
where the time goes in v12:
time: 63.5 us; the launch traced here: 62.4 us
  starting transfers between devices  17.1 us (27%)
  local copies, waits for them, and re-layouts  14.3 us (23%)
  Pallas kernels  11 us (17%)
  waiting for transfers between devices  8.18 us (13%)
  other arithmetic  6.15 us (10%)
  matrix products  5.01 us (8%)
  between operations  0.73 us (1%)
    pallas_call x1, Pallas kernels, post_block(): pl.pallas_call(functools.partial(attention_kernel, chunk=chunk, heads=hea...  11 us
    dot_general x18, matrix products, convolve(): jnp.einsum('oc,mcij->moij', kernel[row_stencil * 3 + column_stencil], shi...  5.01 us
    all_to_all x1, starting transfers between devices, on_device(): lax.all_to_all(by_chunk, 'mem', split_axis=0, concat_axis=0, tiled=True)  4.54 us
    unnamed x46, local copies, waits for them, and re-layouts  4.16 us
    ppermute x1, starting transfers between devices, row_padded(): high = lax.ppermute(block[..., :width, :].reshape(flat), 'row', backward)  4.15 us
    ppermute x1, waiting for transfers between devices, row_padded(): high = lax.ppermute(block[..., :width, :].reshape(flat), 'row', backward)  4.13 us
    all_to_all x1, waiting for transfers between devices, on_device(): lax.all_to_all(by_chunk, 'mem', split_axis=0, concat_axis=0, tiled=True)  3.72 us
    ppermute x1, starting transfers between devices, on_device(): lax.ppermute(pack(starting_states[:, :, row_total - state_halo:], coeffic...  3.12 us
  transfers between devices with their start and end apart: 5, of which 3 were waited for; matrix products, arithmetic and copies ran while one was open for 13% of the time, Pallas kernels for 0%

profile of v12, /device:TPU:9, one launch (start us, length us, event | category | flops | bytes accessed | tf_op | source)
XLA Modules:
  0.0 62.4 jit_solution(18109862474412473034)
XLA Ops:
  0.0 1.1 %maximum_convert_fusion = bf16[3,8,8,512]{3,2,1,0:T(8,128)(2,1)S(1)} fusion(f32[1,8,8,512]{3,2,1,0:T(8,128)} %bitcast.199, f32[1,8,8,512]{3,2,1,0:T(8,128)} %bitcast.201, f32[1,8,8,512]{3,2,1,0:T(8,128)} %bitcast.203), kind=kLoop, calls=%fused_computation.47 | loop fusion | flops 196608 | bytes 589824 | tf_op jit(solution)/shard_map/convert.1
  1.5 3.1 %collective-permute-start = (bf16[200,512]{1,0:T(8,128)(2,1)S(1)}, bf16[200,512]{1,0:T(8,128)(2,1)S(1)}, u32[]{:S(2)}, u32[]{:S(2)}) collective-permute-start(bf16[200,512]{1,0:T(8,128)(2,1)S(1)} %pad_maximum_fusion.5), channel_id=1, source_target_pairs={{0,1},{1,2},{2,3},{3,4},{4,5},{5,6},{6,7},{8,9},{9,10},{10,11},{11... | collective-permute-start | bytes 614408 | tf_op jit(solution)/shard_map/ppermute | solution.py:210
  4.8 3.1 %collective-permute-start.1 = (bf16[200,512]{1,0:T(8,128)(2,1)S(1)}, bf16[200,512]{1,0:T(8,128)(2,1)S(1)}, u32[]{:S(2)}, u32[]{:S(2)}) collective-permute-start(bf16[200,512]{1,0:T(8,128)(2,1)S(1)} %pad_maximum_fusion.6), channel_id=1, source_target_pairs={{1,0},{2,1},{3,2},{4,3},{5,4},{6,5},{7,6},{9,8},{10,9},{11,10},{12... | collective-permute-start | bytes 614408 | tf_op jit(solution)/shard_map/ppermute | solution.py:218
  8.2 0.7 %gather_fusion = bf16[64,3,64]{2,1,0:T(4,128)(2,1)S(1)} fusion(bf16[3,64,64]{2,0,1:T(4,128)(2,1)S(1)} %copy.46, s32[1024]{0:T(1024)S(1)} %pad_clamp_fusion), kind=kCustom, calls=%fused_computation | custom fusion | bytes 49408 | tf_op jit(solution)/shard_map/gather | solution.py:138
  8.9 0.6 copy.47
  9.5 0.6 %gather_fusion.1 = bf16[64,64]{1,0:T(8,128)(2,1)S(1)} fusion(bf16[64,64]{0,1:T(8,128)(2,1)S(1)} %bitcast.197, s32[1024]{0:T(1024)S(1)} %pad_clamp_fusion), kind=kCustom, calls=%fused_computation.1 | custom fusion | bytes 16640 | tf_op jit(solution)/shard_map/gather | solution.py:139
  10.1 0.7 %copy.48 = bf16[64,64]{0,1:T(8,128)(2,1)} copy(bf16[64,64]{1,0:T(8,128)(2,1)S(1)} %gather_fusion.1) | data formatting | bytes 16384 | tf_op jit(solution)/shard_map/gather | solution.py:139
  10.8 0.7 %copy.50.gain_ref = f32[64,1]{1,0:T(8,128)} copy(f32[64,1]{0,1:T(1,128)S(1)} %bitcast.214) | data formatting | bytes 512 | tf_op jit(solution)/shard_map/reshape | solution.py:148
  11.5 0.7 %copy.44 = bf16[8,64]{0,1:T(8,128)(2,1)} copy(bf16[8,64]{1,0:T(8,128)(2,1)S(1)} %copy-done.10) | data formatting | bytes 2048 | tf_op args[4]
  12.2 0.7 %reshape_tile.4.hs_ref = f32[8,1]{1,0:T(8,128)} reshape(f32[2,4]{1,0:T(2,128)S(1)} %tile.2) | data formatting | bytes 64 | tf_op jit(solution)/shard_map/reshape;tile | solution.py:140
  13.7 0.1 copy.102
  13.8 0.1 copy.103
  13.9 0.1 copy.104
  14.1 0.1 copy.105
  15.0 0.1 copy.111
  15.1 0.1 copy.112
  15.3 0.1 copy.113
  15.4 0.1 copy.114
  15.8 0.1 pad_maximum_fusion
  16.3 0.7 %reshape.183 = f32[2,8,4,512]{3,2,1,0:T(4,128)} reshape(f32[64,512]{1,0:T(8,128)S(1)} %slice_add_fusion.1) | data formatting | bytes 262144 | tf_op jit(solution)/shard_map/reshape | solution.py:233
  17.1 1.0 %pad_maximum_fusion.2 = f32[2,8,16,512]{3,2,1,0:T(8,128)S(1)} fusion(f32[2,8,4,512]{3,2,1,0:T(4,128)S(1)} %reshape.185, f32[2,8,8,512]{3,2,1,0:T(8,128)S(1)} %copy-done.7, f32[2,8,4,512]{3,2,1,0:T(4,128)} %reshape.183), kind=kLoop, calls=%fused_computation.41 | loop fusion | flops 262144 | bytes 1048576 | tf_op jit(solution)/shard_map/concatenate | solution.py:232
  18.2 0.5 add_select_fusion.2
  18.8 0.5 add_select_fusion.1
  19.4 0.5 add_select_fusion
  20.0 0.3 select_convert_fusion.1
  20.6 0.2 reshape.192
  20.8 0.7 %pad_maximum_fusion.7 = bf16[4,9,8,256]{3,2,1,0:T(8,128)(2,1)} fusion(bf16[4,1,8,256]{3,2,1,0:T(8,128)(2,1)S(1)} %reshape.192, bf16[4,8,8,256]{3,2,1,0:T(8,128)(2,1)S(1)} %bitcast.207), kind=kLoop, calls=%fused_computation.65 | loop fusion | flops 73728 | bytes 294912 | tf_op jit(solution)/shard_map/concatenate | solution.py:265
  21.5 4.5 %all-to-all-start = ((bf16[4,9,8,256]{3,2,1,0:T(8,128)(2,1)}), bf16[4,9,8,256]{3,2,1,0:T(8,128)(2,1)S(1)}, u32[]{:S(2)}, u32[]{:S(2)}) async-start(bf16[4,9,8,256]{3,2,1,0:T(8,128)(2,1)} %pad_maximum_fusion.7), calls=%async_computation | async-start | bytes 294912 | tf_op jit(solution)/shard_map/all_to_all | solution.py:266
  26.1 3.7 %all-to-all-done.x_ref = bf16[4,9,8,256]{3,2,1,0:T(8,128)(2,1)S(1)} async-done(((bf16[4,9,8,256]{3,2,1,0:T(8,128)(2,1)}), bf16[4,9,8,256]{3,2,1,0:T(8,128)(2,1)S(1)}, u32[]{:S(2)}, u32[]{:S(2)}) %all-to-all-start) | async-done | bytes 147488 | tf_op jit(solution)/shard_map/all_to_all | solution.py:266
  29.8 0.7 %copy-done.8 = bf16[4,9,8,256]{3,2,1,0:T(8,128)(2,1)} copy-done((bf16[4,9,8,256]{3,2,1,0:T(8,128)(2,1)}, bf16[4,9,8,256]{3,2,1,0:T(8,128)(2,1)S(1)}, u32[]{:S(2)}) %copy-start.8) | copy-done | bytes 147480
  30.4 11.0 %shard_map.118 = bf16[9,8,1024]{2,1,0:T(8,128)(2,1)} custom-call(f32[8,1]{1,0:T(8,128)} %reshape_tile.4.hs_ref, bf16[4,9,8,256]{3,2,1,0:T(8,128)(2,1)} %copy-done.8, bf16[64,8]{1,0:T(8,128)(2,1)} %bitcast.212, f32[64,1]{1,0:T(8,128)} %copy.50.gain_ref, bf16[192,64]{1,0:T(8,128)(2,1)} %bitcast.209, bf16[64,64]{1,0:T(8,128)(2,1)} %bitcast.211, ...), custom_call_target="tpu_custom_call" | custom-call | tf_op jit(solution)/shard_map/pallas_call | solution.py:141
  41.4 0.7 %slice.384 = bf16[1,8,1024]{2,1,0:T(8,128)(2,1)S(1)} slice(bf16[9,8,1024]{2,1,0:T(8,128)(2,1)} %shard_map.118), slice={[8:9], [0:8], [0:1024]} | slice | bytes 32768 | tf_op jit(solution)/shard_map/slice | solution.py:281
  42.1 0.9 %copy_bitcast_fusion.2 = bf16[8,8,8,128]{3,1,2,0:T(8,128)(2,1)S(1)} fusion(bf16[9,8,1024]{2,1,0:T(8,128)(2,1)} %shard_map.118), kind=kLoop, calls=%fused_computation.86 | loop fusion | bytes 262144 | tf_op jit(solution)/shard_map/transpose | solution.py:280
  43.1 0.1 reshape_squeeze.3
  43.4 0.2 pad_maximum_fusion.4
  43.7 0.3 reshape.201
  43.9 2.2 %collective-permute-start.2 = (bf16[8,8,1152]{2,1,0:T(8,128)(2,1)S(1)}, bf16[8,8,1152]{2,1,0:T(8,128)(2,1)S(1)}, u32[]{:S(2)}, u32[]{:S(2)}) collective-permute-start(bf16[8,8,1152]{2,1,0:T(8,128)(2,1)S(1)} %reshape.201), channel_id=1, source_target_pairs={{0,1},{1,2},{2,3},{3,4},{4,5},{5,6},{6,7},{8,9},{9,10},{10,11},{11... | collective-permute-start | bytes 442376 | tf_op jit(solution)/shard_map/ppermute | solution.py:34
  46.2 4.1 %collective-permute-start.3 = (bf16[8,8,1152]{2,1,0:T(8,128)(2,1)S(1)}, bf16[8,8,1152]{2,1,0:T(8,128)(2,1)S(1)}, u32[]{:S(2)}, u32[]{:S(2)}) collective-permute-start(bf16[8,8,1152]{2,1,0:T(8,128)(2,1)S(1)} %reshape.201), channel_id=1, source_target_pairs={{1,0},{2,1},{3,2},{4,3},{5,4},{6,5},{7,6},{9,8},{10,9},{11,10},{12... | collective-permute-start | bytes 442376 | tf_op jit(solution)/shard_map/ppermute | solution.py:35
  50.4 0.3 collective-permute-done.2
  50.7 0.4 reshape.202
  51.1 4.1 %collective-permute-done.3 = bf16[8,8,1152]{2,1,0:T(8,128)(2,1)S(1)} collective-permute-done((bf16[8,8,1152]{2,1,0:T(8,128)(2,1)S(1)}, bf16[8,8,1152]{2,1,0:T(8,128)(2,1)S(1)}, u32[]{:S(2)}, u32[]{:S(2)}) %collective-permute-start.3) | collective-permute-done | bytes 147488 | tf_op jit(solution)/shard_map/ppermute | solution.py:35
  55.3 0.4 reshape.203
  55.7 0.2 pad_maximum_fusion.1
  55.9 0.4 pad_maximum_fusion.3
  56.3 0.3 fusion.12
  56.6 0.4 convolution_add_fusion.7
  57.0 0.4 convolution_add_fusion.6
  57.3 0.3 convolution_add_fusion.5
  57.6 0.4 convolution_add_fusion.4
  58.0 0.4 convolution_add_fusion.3
  58.3 0.3 convolution_add_fusion.2
  58.6 0.4 convolution_add_fusion.1
  59.0 0.5 select_convert_fusion
  59.5 0.2 fusion.24
  59.7 0.2 convolution_add_fusion.15
  59.9 0.2 convolution_add_fusion.14
  60.2 0.2 convolution_add_fusion.13
  60.3 0.2 convolution_add_fusion.12
  60.6 0.2 convolution_add_fusion.11
  60.8 0.2 convolution_add_fusion.10
  61.0 0.2 convolution_add_fusion.9
  61.2 0.3 copy-done.3
  61.5 0.2 fusion.3
  61.7 0.7 %copy.76 = bf16[8,8,8,128]{3,2,1,0:T(8,128)(2,1)} copy(bf16[8,8,8,128]{3,1,2,0:T(8,128)(2,1)S(1)} %fusion.3) | data formatting | bytes 262144 | tf_op jit(solution)/shard_map/convert_element_type | solution.py:296
  (87 shorter events, 3.9 us)
Async XLA Ops:
  0.0 9.5 %copy-start = (bf16[64,64]{1,0:T(8,128)(2,1)S(1)}, bf16[64,64]{1,0:T(8,128)(2,1)}, u32[]{:S(2)}) copy-start(bf16[64,64]{1,0:T(8,128)(2,1)} %param.20) | copy-start | bytes 24580
  0.0 1.3 %copy-start.7 = (f32[2,8,8,512]{3,2,1,0:T(8,128)S(1)}, f32[2,8,8,512]{3,2,1,0:T(8,128)}, u32[]{:S(2)}) copy-start(f32[2,8,8,512]{3,2,1,0:T(8,128)} %param.12) | copy-start | bytes 786436
  1.3 6.7 %copy-start.9 = (bf16[64,192]{1,0:T(8,128)(2,1)S(1)}, bf16[64,192]{1,0:T(8,128)(2,1)}, u32[]{:S(2)}) copy-start(bf16[64,192]{1,0:T(8,128)(2,1)} %param.18) | copy-start | bytes 73732
  1.4 9.4 %copy-start.11 = (f32[64]{0:T(128)S(1)}, f32[64]{0:T(128)}, u32[]{:S(2)}) copy-start(f32[64]{0:T(128)} %param.17) | copy-start | bytes 772
  1.4 10.1 %copy-start.10 = (bf16[8,64]{1,0:T(8,128)(2,1)S(1)}, bf16[8,64]{1,0:T(8,128)(2,1)}, u32[]{:S(2)}) copy-start(bf16[8,64]{1,0:T(8,128)(2,1)} %param.16) | copy-start | bytes 3076
  1.4 10.8 %copy-start.12 = (f32[4]{0:T(128)S(1)}, f32[4]{0:T(128)}, u32[]{:S(2)}) copy-start(f32[4]{0:T(128)} %param.19) | copy-start | bytes 52
  1.4 11.4 %copy-start.1 = (bf16[9,8,8]{0,2,1:T(8,128)(2,1)S(1)}, bf16[9,8,8]{0,2,1:T(8,128)(2,1)}, u32[]{:S(2)}) copy-start(bf16[9,8,8]{0,2,1:T(8,128)(2,1)} %param.22) | copy-start | bytes 3460
  1.5 14.1 %collective-permute-start = (bf16[200,512]{1,0:T(8,128)(2,1)S(1)}, bf16[200,512]{1,0:T(8,128)(2,1)S(1)}, u32[]{:S(2)}, u32[]{:S(2)}) collective-permute-start(bf16[200,512]{1,0:T(8,128)(2,1)S(1)} %pad_maximum_fusion.5), channel_id=1, source_target_pairs={{0,1},{1,2},{2,3},{3,4},{4,5},{5,6},{6,7},{8,9},{9,10},{10,11},{11... | collective-permute-start | bytes 614408 | tf_op jit(solution)/shard_map/ppermute | solution.py:210
  4.7 9.5 %copy-start.2 = (bf16[9,8,8]{0,2,1:T(8,128)(2,1)S(1)}, bf16[9,8,8]{0,2,1:T(8,128)(2,1)}, u32[]{:S(2)}) copy-start(bf16[9,8,8]{0,2,1:T(8,128)(2,1)} %param.23) | copy-start | bytes 3460
  4.8 10.9 %collective-permute-start.1 = (bf16[200,512]{1,0:T(8,128)(2,1)S(1)}, bf16[200,512]{1,0:T(8,128)(2,1)S(1)}, u32[]{:S(2)}, u32[]{:S(2)}) collective-permute-start(bf16[200,512]{1,0:T(8,128)(2,1)S(1)} %pad_maximum_fusion.6), channel_id=1, source_target_pairs={{1,0},{2,1},{3,2},{4,3},{5,4},{6,5},{7,6},{9,8},{10,9},{11,10},{12... | collective-permute-start | bytes 614408 | tf_op jit(solution)/shard_map/ppermute | solution.py:218
  12.9 2.9 %copy-start.4 = (f32[8,8,512]{2,1,0:T(8,128)S(1)}, f32[8,8,512]{2,1,0:T(8,128)}, u32[]{:S(2)}) copy-start(f32[8,8,512]{2,1,0:T(8,128)} %param.15) | copy-start | bytes 393220
  12.9 2.9 %copy-start.5 = (f32[8,8,512]{2,1,0:T(8,128)S(1)}, f32[8,8,512]{2,1,0:T(8,128)}, u32[]{:S(2)}) copy-start(f32[8,8,512]{2,1,0:T(8,128)} %param.14) | copy-start | bytes 393220
  12.9 2.9 %copy-start.6 = (f32[8,8,512]{2,1,0:T(8,128)S(1)}, f32[8,8,512]{2,1,0:T(8,128)}, u32[]{:S(2)}) copy-start(f32[8,8,512]{2,1,0:T(8,128)} %param.13) | copy-start | bytes 393220
  21.5 8.3 %all-to-all-start = ((bf16[4,9,8,256]{3,2,1,0:T(8,128)(2,1)}), bf16[4,9,8,256]{3,2,1,0:T(8,128)(2,1)S(1)}, u32[]{:S(2)}, u32[]{:S(2)}) async-start(bf16[4,9,8,256]{3,2,1,0:T(8,128)(2,1)} %pad_maximum_fusion.7), calls=%async_computation | async-start | bytes 294912 | tf_op jit(solution)/shard_map/all_to_all | solution.py:266
  29.8 0.7 %copy-start.8 = (bf16[4,9,8,256]{3,2,1,0:T(8,128)(2,1)}, bf16[4,9,8,256]{3,2,1,0:T(8,128)(2,1)S(1)}, u32[]{:S(2)}) copy-start(bf16[4,9,8,256]{3,2,1,0:T(8,128)(2,1)S(1)} %all-to-all-done.x_ref) | copy-start | bytes 442372
  43.9 6.8 %collective-permute-start.2 = (bf16[8,8,1152]{2,1,0:T(8,128)(2,1)S(1)}, bf16[8,8,1152]{2,1,0:T(8,128)(2,1)S(1)}, u32[]{:S(2)}, u32[]{:S(2)}) collective-permute-start(bf16[8,8,1152]{2,1,0:T(8,128)(2,1)S(1)} %reshape.201), channel_id=1, source_target_pairs={{0,1},{1,2},{2,3},{3,4},{4,5},{5,6},{6,7},{8,9},{9,10},{10,11},{11... | collective-permute-start | bytes 442376 | tf_op jit(solution)/shard_map/ppermute | solution.py:34
  46.2 9.1 %collective-permute-start.3 = (bf16[8,8,1152]{2,1,0:T(8,128)(2,1)S(1)}, bf16[8,8,1152]{2,1,0:T(8,128)(2,1)S(1)}, u32[]{:S(2)}, u32[]{:S(2)}) collective-permute-start(bf16[8,8,1152]{2,1,0:T(8,128)(2,1)S(1)} %reshape.201), channel_id=1, source_target_pairs={{1,0},{2,1},{3,2},{4,3},{5,4},{6,5},{7,6},{9,8},{10,9},{11,10},{12... | collective-permute-start | bytes 442376 | tf_op jit(solution)/shard_map/ppermute | solution.py:35
  60.6 0.9 %copy-start.3 = (bf16[9,8,1024]{2,1,0:T(8,128)(2,1)S(1)}, bf16[9,8,1024]{2,1,0:T(8,128)(2,1)}, u32[]{:S(2)}) copy-start(bf16[9,8,1024]{2,1,0:T(8,128)(2,1)} %shard_map.118) | copy-start | bytes 442372

commit v13 on v12

--- a/solution.py
+++ b/solution.py
@@ -201,11 +201,11 @@
 
     def pack(states_part, coef_part):
         states_flat = states_part.reshape(-1, cols)
-        states_high = states_flat.astype(jnp.bfloat16)
-        states_low = (states_flat - states_high.astype(jnp.float32)).astype(jnp.bfloat16)
+        states_high = lax.reduce_precision(states_flat, exponent_bits=8, mantissa_bits=7)
+        states_low = states_flat - states_high
         return jnp.concatenate(
-            [states_high, states_low, coef_part.reshape(-1, cols).astype(jnp.bfloat16)], axis=0
-        )
+            [states_high, states_low, coef_part.reshape(-1, cols)], axis=0
+        ).astype(jnp.bfloat16)
 
     low = lax.ppermute(
         pack(

time: 63.5 us -> 63.5 us (level)
  no operation moved by 1% of the time
where the time goes in v13:
time: 63.5 us; the launch traced here: 62.4 us
  starting transfers between devices  17.1 us (27%)
  local copies, waits for them, and re-layouts  14.3 us (23%)
  Pallas kernels  11 us (17%)
  waiting for transfers between devices  8.18 us (13%)
  other arithmetic  6.16 us (10%)
  matrix products  5.01 us (8%)
  between operations  0.73 us (1%)
    pallas_call x1, Pallas kernels, post_block(): pl.pallas_call(functools.partial(attention_kernel, chunk=chunk, heads=hea...  11 us
    dot_general x18, matrix products, convolve(): jnp.einsum('oc,mcij->moij', kernel[row_stencil * 3 + column_stencil], shi...  5.01 us
    all_to_all x1, starting transfers between devices, on_device(): lax.all_to_all(by_chunk, 'mem', split_axis=0, concat_axis=0, tiled=True)  4.54 us
    unnamed x46, local copies, waits for them, and re-layouts  4.16 us
    ppermute x1, starting transfers between devices, row_padded(): high = lax.ppermute(block[..., :width, :].reshape(flat), 'row', backward)  4.15 us
    ppermute x1, waiting for transfers between devices, row_padded(): high = lax.ppermute(block[..., :width, :].reshape(flat), 'row', backward)  4.13 us
    all_to_all x1, waiting for transfers between devices, on_device(): lax.all_to_all(by_chunk, 'mem', split_axis=0, concat_axis=0, tiled=True)  3.72 us
    ppermute x1, starting transfers between devices, on_device(): lax.ppermute(pack(starting_states[:, :, row_total - state_halo:], coeffic...  3.12 us
  transfers between devices with their start and end apart: 5, of which 3 were waited for; matrix products, arithmetic and copies ran while one was open for 13% of the time, Pallas kernels for 0%

profile of v13, /device:TPU:9, one launch (start us, length us, event | category | flops | bytes accessed | tf_op | source)
XLA Modules:
  0.0 62.4 jit_solution(12748896436954495539)
XLA Ops:
  0.0 1.1 %maximum_convert_fusion = bf16[3,8,8,512]{3,2,1,0:T(8,128)(2,1)S(1)} fusion(f32[1,8,8,512]{3,2,1,0:T(8,128)} %bitcast.199, f32[1,8,8,512]{3,2,1,0:T(8,128)} %bitcast.201, f32[1,8,8,512]{3,2,1,0:T(8,128)} %bitcast.203), kind=kLoop, calls=%fused_computation.47 | loop fusion | flops 196608 | bytes 589824 | tf_op jit(solution)/shard_map/convert.9
  1.5 3.1 %collective-permute-start = (bf16[200,512]{1,0:T(8,128)(2,1)S(1)}, bf16[200,512]{1,0:T(8,128)(2,1)S(1)}, u32[]{:S(2)}, u32[]{:S(2)}) collective-permute-start(bf16[200,512]{1,0:T(8,128)(2,1)S(1)} %pad_maximum_fusion.5), channel_id=1, source_target_pairs={{0,1},{1,2},{2,3},{3,4},{4,5},{5,6},{6,7},{8,9},{9,10},{10,11},{11... | collective-permute-start | bytes 614408 | tf_op jit(solution)/shard_map/ppermute | solution.py:210
  4.8 3.1 %collective-permute-start.1 = (bf16[200,512]{1,0:T(8,128)(2,1)S(1)}, bf16[200,512]{1,0:T(8,128)(2,1)S(1)}, u32[]{:S(2)}, u32[]{:S(2)}) collective-permute-start(bf16[200,512]{1,0:T(8,128)(2,1)S(1)} %pad_maximum_fusion.6), channel_id=1, source_target_pairs={{1,0},{2,1},{3,2},{4,3},{5,4},{6,5},{7,6},{9,8},{10,9},{11,10},{12... | collective-permute-start | bytes 614408 | tf_op jit(solution)/shard_map/ppermute | solution.py:218
  8.2 0.7 %gather_fusion = bf16[64,3,64]{2,1,0:T(4,128)(2,1)S(1)} fusion(bf16[3,64,64]{2,0,1:T(4,128)(2,1)S(1)} %copy.46, s32[1024]{0:T(1024)S(1)} %pad_clamp_fusion), kind=kCustom, calls=%fused_computation | custom fusion | bytes 49408 | tf_op jit(solution)/shard_map/gather | solution.py:138
  8.9 0.6 copy.47
  9.5 0.6 %gather_fusion.1 = bf16[64,64]{1,0:T(8,128)(2,1)S(1)} fusion(bf16[64,64]{0,1:T(8,128)(2,1)S(1)} %bitcast.197, s32[1024]{0:T(1024)S(1)} %pad_clamp_fusion), kind=kCustom, calls=%fused_computation.1 | custom fusion | bytes 16640 | tf_op jit(solution)/shard_map/gather | solution.py:139
  10.1 0.7 %copy.48 = bf16[64,64]{0,1:T(8,128)(2,1)} copy(bf16[64,64]{1,0:T(8,128)(2,1)S(1)} %gather_fusion.1) | data formatting | bytes 16384 | tf_op jit(solution)/shard_map/gather | solution.py:139
  10.8 0.7 %copy.50.gain_ref = f32[64,1]{1,0:T(8,128)} copy(f32[64,1]{0,1:T(1,128)S(1)} %bitcast.214) | data formatting | bytes 512 | tf_op jit(solution)/shard_map/reshape | solution.py:148
  11.5 0.7 %copy.44 = bf16[8,64]{0,1:T(8,128)(2,1)} copy(bf16[8,64]{1,0:T(8,128)(2,1)S(1)} %copy-done.10) | data formatting | bytes 2048 | tf_op args[4]
  12.2 0.7 %reshape_tile.4.hs_ref = f32[8,1]{1,0:T(8,128)} reshape(f32[2,4]{1,0:T(2,128)S(1)} %tile.2) | data formatting | bytes 64 | tf_op jit(solution)/shard_map/reshape;tile | solution.py:140
  13.7 0.1 copy.102
  13.8 0.1 copy.103
  13.9 0.1 copy.104
  14.1 0.1 copy.105
  15.0 0.1 copy.111
  15.1 0.1 copy.112
  15.3 0.1 copy.113
  15.4 0.1 copy.114
  15.8 0.1 pad_maximum_fusion
  16.3 0.7 %reshape.188 = f32[2,8,4,512]{3,2,1,0:T(4,128)} reshape(f32[64,512]{1,0:T(8,128)S(1)} %slice_add_fusion.1) | data formatting | bytes 262144 | tf_op jit(solution)/shard_map/reshape | solution.py:233
  17.1 1.0 %pad_maximum_fusion.2 = f32[2,8,16,512]{3,2,1,0:T(8,128)S(1)} fusion(f32[2,8,4,512]{3,2,1,0:T(4,128)S(1)} %reshape.191, f32[2,8,8,512]{3,2,1,0:T(8,128)S(1)} %copy-done.7, f32[2,8,4,512]{3,2,1,0:T(4,128)} %reshape.188), kind=kLoop, calls=%fused_computation.41 | loop fusion | flops 262144 | bytes 1048576 | tf_op jit(solution)/shard_map/concatenate | solution.py:232
  18.2 0.5 add_select_fusion.2
  18.8 0.5 add_select_fusion.1
  19.4 0.5 add_select_fusion
  20.0 0.3 select_convert_fusion.1
  20.6 0.2 reshape.198
  20.8 0.7 %pad_maximum_fusion.7 = bf16[4,9,8,256]{3,2,1,0:T(8,128)(2,1)} fusion(bf16[4,1,8,256]{3,2,1,0:T(8,128)(2,1)S(1)} %reshape.198, bf16[4,8,8,256]{3,2,1,0:T(8,128)(2,1)S(1)} %bitcast.207), kind=kLoop, calls=%fused_computation.69 | loop fusion | flops 73728 | bytes 294912 | tf_op jit(solution)/shard_map/concatenate | solution.py:265
  21.5 4.5 %all-to-all-start = ((bf16[4,9,8,256]{3,2,1,0:T(8,128)(2,1)}), bf16[4,9,8,256]{3,2,1,0:T(8,128)(2,1)S(1)}, u32[]{:S(2)}, u32[]{:S(2)}) async-start(bf16[4,9,8,256]{3,2,1,0:T(8,128)(2,1)} %pad_maximum_fusion.7), calls=%async_computation | async-start | bytes 294912 | tf_op jit(solution)/shard_map/all_to_all | solution.py:266
  26.1 3.7 %all-to-all-done.x_ref = bf16[4,9,8,256]{3,2,1,0:T(8,128)(2,1)S(1)} async-done(((bf16[4,9,8,256]{3,2,1,0:T(8,128)(2,1)}), bf16[4,9,8,256]{3,2,1,0:T(8,128)(2,1)S(1)}, u32[]{:S(2)}, u32[]{:S(2)}) %all-to-all-start) | async-done | bytes 147488 | tf_op jit(solution)/shard_map/all_to_all | solution.py:266
  29.8 0.7 %copy-done.8 = bf16[4,9,8,256]{3,2,1,0:T(8,128)(2,1)} copy-done((bf16[4,9,8,256]{3,2,1,0:T(8,128)(2,1)}, bf16[4,9,8,256]{3,2,1,0:T(8,128)(2,1)S(1)}, u32[]{:S(2)}) %copy-start.8) | copy-done | bytes 147480
  30.4 11.0 %shard_map.118 = bf16[9,8,1024]{2,1,0:T(8,128)(2,1)} custom-call(f32[8,1]{1,0:T(8,128)} %reshape_tile.4.hs_ref, bf16[4,9,8,256]{3,2,1,0:T(8,128)(2,1)} %copy-done.8, bf16[64,8]{1,0:T(8,128)(2,1)} %bitcast.212, f32[64,1]{1,0:T(8,128)} %copy.50.gain_ref, bf16[192,64]{1,0:T(8,128)(2,1)} %bitcast.209, bf16[64,64]{1,0:T(8,128)(2,1)} %bitcast.211, ...), custom_call_target="tpu_custom_call" | custom-call | tf_op jit(solution)/shard_map/pallas_call | solution.py:141
  41.4 0.7 %slice.384 = bf16[1,8,1024]{2,1,0:T(8,128)(2,1)S(1)} slice(bf16[9,8,1024]{2,1,0:T(8,128)(2,1)} %shard_map.118), slice={[8:9], [0:8], [0:1024]} | slice | bytes 32768 | tf_op jit(solution)/shard_map/slice | solution.py:281
  42.1 0.9 %copy_bitcast_fusion.2 = bf16[8,8,8,128]{3,1,2,0:T(8,128)(2,1)S(1)} fusion(bf16[9,8,1024]{2,1,0:T(8,128)(2,1)} %shard_map.118), kind=kLoop, calls=%fused_computation.92 | loop fusion | bytes 262144 | tf_op jit(solution)/shard_map/transpose | solution.py:280
  43.1 0.1 reshape_squeeze.3
  43.4 0.2 pad_maximum_fusion.4
  43.7 0.3 reshape.207
  43.9 2.2 %collective-permute-start.2 = (bf16[8,8,1152]{2,1,0:T(8,128)(2,1)S(1)}, bf16[8,8,1152]{2,1,0:T(8,128)(2,1)S(1)}, u32[]{:S(2)}, u32[]{:S(2)}) collective-permute-start(bf16[8,8,1152]{2,1,0:T(8,128)(2,1)S(1)} %reshape.207), channel_id=1, source_target_pairs={{0,1},{1,2},{2,3},{3,4},{4,5},{5,6},{6,7},{8,9},{9,10},{10,11},{11... | collective-permute-start | bytes 442376 | tf_op jit(solution)/shard_map/ppermute | solution.py:34
  46.2 4.1 %collective-permute-start.3 = (bf16[8,8,1152]{2,1,0:T(8,128)(2,1)S(1)}, bf16[8,8,1152]{2,1,0:T(8,128)(2,1)S(1)}, u32[]{:S(2)}, u32[]{:S(2)}) collective-permute-start(bf16[8,8,1152]{2,1,0:T(8,128)(2,1)S(1)} %reshape.207), channel_id=1, source_target_pairs={{1,0},{2,1},{3,2},{4,3},{5,4},{6,5},{7,6},{9,8},{10,9},{11,10},{12... | collective-permute-start | bytes 442376 | tf_op jit(solution)/shard_map/ppermute | solution.py:35
  50.4 0.3 collective-permute-done.2
  50.7 0.4 reshape.208
  51.2 4.1 %collective-permute-done.3 = bf16[8,8,1152]{2,1,0:T(8,128)(2,1)S(1)} collective-permute-done((bf16[8,8,1152]{2,1,0:T(8,128)(2,1)S(1)}, bf16[8,8,1152]{2,1,0:T(8,128)(2,1)S(1)}, u32[]{:S(2)}, u32[]{:S(2)}) %collective-permute-start.3) | collective-permute-done | bytes 147488 | tf_op jit(solution)/shard_map/ppermute | solution.py:35
  55.3 0.4 reshape.209
  55.7 0.2 pad_maximum_fusion.1
  55.9 0.4 pad_maximum_fusion.3
  56.3 0.3 fusion.12
  56.6 0.4 convolution_add_fusion.7
  57.0 0.4 convolution_add_fusion.6
  57.3 0.3 convolution_add_fusion.5
  57.6 0.4 convolution_add_fusion.4
  58.0 0.4 convolution_add_fusion.3
  58.3 0.3 convolution_add_fusion.2
  58.6 0.4 convolution_add_fusion.1
  59.0 0.5 select_convert_fusion
  59.5 0.2 fusion.26
  59.7 0.2 convolution_add_fusion.15
  59.9 0.2 convolution_add_fusion.14
  60.2 0.2 convolution_add_fusion.13
  60.3 0.2 convolution_add_fusion.12
  60.6 0.2 convolution_add_fusion.11
  60.8 0.2 convolution_add_fusion.10
  61.0 0.2 convolution_add_fusion.9
  61.2 0.3 copy-done.3
  61.5 0.2 fusion.3
  61.7 0.7 %copy.76 = bf16[8,8,8,128]{3,2,1,0:T(8,128)(2,1)} copy(bf16[8,8,8,128]{3,1,2,0:T(8,128)(2,1)S(1)} %fusion.3) | data formatting | bytes 262144 | tf_op jit(solution)/shard_map/convert_element_type | solution.py:296
  (87 shorter events, 3.9 us)
Async XLA Ops:
  0.0 9.5 %copy-start = (bf16[64,64]{1,0:T(8,128)(2,1)S(1)}, bf16[64,64]{1,0:T(8,128)(2,1)}, u32[]{:S(2)}) copy-start(bf16[64,64]{1,0:T(8,128)(2,1)} %param.20) | copy-start | bytes 24580
  0.0 1.3 %copy-start.7 = (f32[2,8,8,512]{3,2,1,0:T(8,128)S(1)}, f32[2,8,8,512]{3,2,1,0:T(8,128)}, u32[]{:S(2)}) copy-start(f32[2,8,8,512]{3,2,1,0:T(8,128)} %param.12) | copy-start | bytes 786436
  1.3 6.7 %copy-start.9 = (bf16[64,192]{1,0:T(8,128)(2,1)S(1)}, bf16[64,192]{1,0:T(8,128)(2,1)}, u32[]{:S(2)}) copy-start(bf16[64,192]{1,0:T(8,128)(2,1)} %param.18) | copy-start | bytes 73732
  1.4 9.4 %copy-start.11 = (f32[64]{0:T(128)S(1)}, f32[64]{0:T(128)}, u32[]{:S(2)}) copy-start(f32[64]{0:T(128)} %param.17) | copy-start | bytes 772
  1.4 10.1 %copy-start.10 = (bf16[8,64]{1,0:T(8,128)(2,1)S(1)}, bf16[8,64]{1,0:T(8,128)(2,1)}, u32[]{:S(2)}) copy-start(bf16[8,64]{1,0:T(8,128)(2,1)} %param.16) | copy-start | bytes 3076
  1.4 10.8 %copy-start.12 = (f32[4]{0:T(128)S(1)}, f32[4]{0:T(128)}, u32[]{:S(2)}) copy-start(f32[4]{0:T(128)} %param.19) | copy-start | bytes 52
  1.4 11.5 %copy-start.1 = (bf16[9,8,8]{0,2,1:T(8,128)(2,1)S(1)}, bf16[9,8,8]{0,2,1:T(8,128)(2,1)}, u32[]{:S(2)}) copy-start(bf16[9,8,8]{0,2,1:T(8,128)(2,1)} %param.22) | copy-start | bytes 3460
  1.5 14.1 %collective-permute-start = (bf16[200,512]{1,0:T(8,128)(2,1)S(1)}, bf16[200,512]{1,0:T(8,128)(2,1)S(1)}, u32[]{:S(2)}, u32[]{:S(2)}) collective-permute-start(bf16[200,512]{1,0:T(8,128)(2,1)S(1)} %pad_maximum_fusion.5), channel_id=1, source_target_pairs={{0,1},{1,2},{2,3},{3,4},{4,5},{5,6},{6,7},{8,9},{9,10},{10,11},{11... | collective-permute-start | bytes 614408 | tf_op jit(solution)/shard_map/ppermute | solution.py:210
  4.7 9.5 %copy-start.2 = (bf16[9,8,8]{0,2,1:T(8,128)(2,1)S(1)}, bf16[9,8,8]{0,2,1:T(8,128)(2,1)}, u32[]{:S(2)}) copy-start(bf16[9,8,8]{0,2,1:T(8,128)(2,1)} %param.23) | copy-start | bytes 3460
  4.8 10.9 %collective-permute-start.1 = (bf16[200,512]{1,0:T(8,128)(2,1)S(1)}, bf16[200,512]{1,0:T(8,128)(2,1)S(1)}, u32[]{:S(2)}, u32[]{:S(2)}) collective-permute-start(bf16[200,512]{1,0:T(8,128)(2,1)S(1)} %pad_maximum_fusion.6), channel_id=1, source_target_pairs={{1,0},{2,1},{3,2},{4,3},{5,4},{6,5},{7,6},{9,8},{10,9},{11,10},{12... | collective-permute-start | bytes 614408 | tf_op jit(solution)/shard_map/ppermute | solution.py:218
  12.9 2.9 %copy-start.4 = (f32[8,8,512]{2,1,0:T(8,128)S(1)}, f32[8,8,512]{2,1,0:T(8,128)}, u32[]{:S(2)}) copy-start(f32[8,8,512]{2,1,0:T(8,128)} %param.15) | copy-start | bytes 393220
  12.9 2.9 %copy-start.5 = (f32[8,8,512]{2,1,0:T(8,128)S(1)}, f32[8,8,512]{2,1,0:T(8,128)}, u32[]{:S(2)}) copy-start(f32[8,8,512]{2,1,0:T(8,128)} %param.14) | copy-start | bytes 393220
  12.9 2.9 %copy-start.6 = (f32[8,8,512]{2,1,0:T(8,128)S(1)}, f32[8,8,512]{2,1,0:T(8,128)}, u32[]{:S(2)}) copy-start(f32[8,8,512]{2,1,0:T(8,128)} %param.13) | copy-start | bytes 393220
  21.5 8.3 %all-to-all-start = ((bf16[4,9,8,256]{3,2,1,0:T(8,128)(2,1)}), bf16[4,9,8,256]{3,2,1,0:T(8,128)(2,1)S(1)}, u32[]{:S(2)}, u32[]{:S(2)}) async-start(bf16[4,9,8,256]{3,2,1,0:T(8,128)(2,1)} %pad_maximum_fusion.7), calls=%async_computation | async-start | bytes 294912 | tf_op jit(solution)/shard_map/all_to_all | solution.py:266
  29.8 0.7 %copy-start.8 = (bf16[4,9,8,256]{3,2,1,0:T(8,128)(2,1)}, bf16[4,9,8,256]{3,2,1,0:T(8,128)(2,1)S(1)}, u32[]{:S(2)}) copy-start(bf16[4,9,8,256]{3,2,1,0:T(8,128)(2,1)S(1)} %all-to-all-done.x_ref) | copy-start | bytes 442372
  43.9 6.8 %collective-permute-start.2 = (bf16[8,8,1152]{2,1,0:T(8,128)(2,1)S(1)}, bf16[8,8,1152]{2,1,0:T(8,128)(2,1)S(1)}, u32[]{:S(2)}, u32[]{:S(2)}) collective-permute-start(bf16[8,8,1152]{2,1,0:T(8,128)(2,1)S(1)} %reshape.207), channel_id=1, source_target_pairs={{0,1},{1,2},{2,3},{3,4},{4,5},{5,6},{6,7},{8,9},{9,10},{10,11},{11... | collective-permute-start | bytes 442376 | tf_op jit(solution)/shard_map/ppermute | solution.py:34
  46.2 9.1 %collective-permute-start.3 = (bf16[8,8,1152]{2,1,0:T(8,128)(2,1)S(1)}, bf16[8,8,1152]{2,1,0:T(8,128)(2,1)S(1)}, u32[]{:S(2)}, u32[]{:S(2)}) collective-permute-start(bf16[8,8,1152]{2,1,0:T(8,128)(2,1)S(1)} %reshape.207), channel_id=1, source_target_pairs={{1,0},{2,1},{3,2},{4,3},{5,4},{6,5},{7,6},{9,8},{10,9},{11,10},{12... | collective-permute-start | bytes 442376 | tf_op jit(solution)/shard_map/ppermute | solution.py:35
  60.6 0.9 %copy-start.3 = (bf16[9,8,1024]{2,1,0:T(8,128)(2,1)S(1)}, bf16[9,8,1024]{2,1,0:T(8,128)(2,1)}, u32[]{:S(2)}) copy-start(bf16[9,8,1024]{2,1,0:T(8,128)(2,1)} %shard_map.118) | copy-start | bytes 442372

commit v14 on v10

--- a/solution.py
+++ b/solution.py
@@ -252,18 +252,24 @@
         chunks, 1, levels_count, members_here * tile_rows * 2 * halo
     )
     by_chunk = jnp.concatenate([by_chunk, edges], axis=1)
-    by_source = lax.all_to_all(by_chunk, "mem", split_axis=0, concat_axis=0, tiled=True)
     members = chunks * members_here
-    step_result = post_block(
-        by_source,
-        tile_cols,
-        embed_weight,
-        norm_gain,
-        project_weight,
-        head_scale,
-        output_weight,
-        readout_weight,
-    )
+    first_half = (tile_rows + 1) // 2
+    step_parts = []
+    for part in (by_chunk[:, :first_half], by_chunk[:, first_half:]):
+        by_source = lax.all_to_all(part, "mem", split_axis=0, concat_axis=0, tiled=True)
+        step_parts.append(
+            post_block(
+                by_source,
+                tile_cols,
+                embed_weight,
+                norm_gain,
+                project_weight,
+                head_scale,
+                output_weight,
+                readout_weight,
+            )
+        )
+    step_result = jnp.concatenate(step_parts, axis=0)
     feat = readout_weight.shape[1]
     inner = step_result[:tile_rows].reshape(tile_rows, feat, members, tile_cols)
     inner = jnp.transpose(inner, (2, 1, 0, 3))

time: 65.5 us -> 70.7 us (1.079)
  starting transfers between devices: 16.3 us -> 20.4 us
  Pallas kernels: 11 us -> 12.4 us
  other arithmetic: 5.14 us -> 6 us
    all_to_all x1 -> x2, starting transfers between devices: 3.79 us -> 7.87 us  [on_device(): lax.all_to_all(part, 'mem', split_axis=0, concat_axis=0, tiled=True)]
    pallas_call x1 -> x2, Pallas kernels: 11 us -> 12.4 us  [post_block(): pl.pallas_call(functools.partial(attention_kernel, chunk=chunk, heads=hea...]
    ppermute x1, waiting for transfers between devices: 0.33 us -> 1.76 us  [row_padded(): lax.ppermute(block[..., rows - width:, :].reshape(flat), 'row', forward)]
    all_to_all x1 -> x2, waiting for transfers between devices: 3.72 us -> 2.62 us  [on_device(): lax.all_to_all(part, 'mem', split_axis=0, concat_axis=0, tiled=True)]
    ppermute x1, waiting for transfers between devices: 4.13 us -> 3.13 us  [row_padded(): high = lax.ppermute(block[..., :width, :].reshape(flat), 'row', backward)]
    transpose x1 -> x0, local copies, waits for them, and re-layouts: 0.93 us -> none  [on_device(): inner = jnp.transpose(inner, (2, 1, 0, 3))]
    transpose x0 -> x1, other arithmetic: none -> 0.89 us  [on_device(): inner = jnp.transpose(inner, (2, 1, 0, 3))]
    unnamed x48 -> x52, local copies, waits for them, and re-layouts: 4.65 us -> 4.58 us
  transfers between devices with their start and end apart: 5 -> 6, of which waited for: 5 -> 5; matrix products, arithmetic and copies ran while one was open for 13% -> 13% of each run, Pallas kernels for 0% -> 8%
where the time goes in v14:
time: 70.7 us; the launch traced here: 69.9 us
  starting transfers between devices  20.4 us (29%)
  local copies, waits for them, and re-layouts  14.7 us (21%)
  Pallas kernels  12.4 us (18%)
  waiting for transfers between devices  10.6 us (15%)
  other arithmetic  6 us (8%)
  matrix products  5 us (7%)
  between operations  0.73 us (1%)
    pallas_call x2, Pallas kernels, post_block(): pl.pallas_call(functools.partial(attention_kernel, chunk=chunk, heads=hea...  12.4 us
    all_to_all x2, starting transfers between devices, on_device(): lax.all_to_all(part, 'mem', split_axis=0, concat_axis=0, tiled=True)  7.87 us
    dot_general x18, matrix products, convolve(): jnp.einsum('oc,mcij->moij', kernel[row_stencil * 3 + column_stencil], shi...  5 us
    unnamed x52, local copies, waits for them, and re-layouts  4.58 us
    ppermute x1, starting transfers between devices, row_padded(): high = lax.ppermute(block[..., :width, :].reshape(flat), 'row', backward)  4.04 us
    ppermute x1, waiting for transfers between devices, row_padded(): high = lax.ppermute(block[..., :width, :].reshape(flat), 'row', backward)  3.13 us
    ppermute x1, starting transfers between devices, on_device(): lax.ppermute(pack(starting_states[:, :, row_total - state_halo:], coeffic...  3.12 us
    ppermute x1, starting transfers between devices, on_device(): lax.ppermute(pack(starting_states[:, :, :state_halo], coefficients[:, :,...  3.06 us
  transfers between devices with their start and end apart: 6, of which 5 were waited for; matrix products, arithmetic and copies ran while one was open for 13% of the time, Pallas kernels for 8%

profile of v14, /device:TPU:9, one launch (start us, length us, event | category | flops | bytes accessed | tf_op | source)
XLA Modules:
  0.0 69.9 jit_solution(9279315364602023783)
XLA Ops:
  0.0 1.1 %pad_maximum_fusion.4 = f32[3,8,8,512]{3,2,1,0:T(8,128)S(1)} fusion(f32[1,8,8,512]{3,2,1,0:T(8,128)} %bitcast.199, f32[1,8,8,512]{3,2,1,0:T(8,128)} %bitcast.201, f32[1,8,8,512]{3,2,1,0:T(8,128)} %bitcast.203), kind=kLoop, calls=%fused_computation.47 | loop fusion | flops 196608 | bytes 786432 | tf_op jit(solution)/shard_map/stack | solution.py:194
  1.4 3.1 %collective-permute-start = (f32[136,512]{1,0:T(8,128)S(1)}, f32[136,512]{1,0:T(8,128)S(1)}, u32[]{:S(2)}, u32[]{:S(2)}) collective-permute-start(f32[136,512]{1,0:T(8,128)S(1)} %pad_maximum_fusion.5), channel_id=1, source_target_pairs={{0,1},{1,2},{2,3},{3,4},{4,5},{5,6},{6,7},{8,9},{9,10},{10,11},{11... | collective-permute-start | bytes 835592 | tf_op jit(solution)/shard_map/ppermute | solution.py:207
  4.8 3.1 %collective-permute-start.1 = (f32[136,512]{1,0:T(8,128)S(1)}, f32[136,512]{1,0:T(8,128)S(1)}, u32[]{:S(2)}, u32[]{:S(2)}) collective-permute-start(f32[136,512]{1,0:T(8,128)S(1)} %pad_maximum_fusion.6), channel_id=1, source_target_pairs={{1,0},{2,1},{3,2},{4,3},{5,4},{6,5},{7,6},{9,8},{10,9},{11,10},{12... | collective-permute-start | bytes 835592 | tf_op jit(solution)/shard_map/ppermute | solution.py:215
  8.5 0.7 gather_fusion
  9.1 0.6 copy.47
  9.8 0.6 gather_fusion.1
  10.4 0.7 copy.48
  11.1 0.7 copy.50.gain_ref
  11.8 0.7 copy.44
  12.5 0.7 reshape_tile.5.hs_ref
  13.8 0.1 copy.106
  14.0 0.1 copy.107
  14.1 0.1 copy.108
  14.2 0.1 copy.109
  15.8 3.0 %collective-permute-done.1 = f32[136,512]{1,0:T(8,128)S(1)} collective-permute-done((f32[136,512]{1,0:T(8,128)S(1)}, f32[136,512]{1,0:T(8,128)S(1)}, u32[]{:S(2)}, u32[]{:S(2)}) %collective-permute-start.1) | collective-permute-done | bytes 278560 | tf_op jit(solution)/shard_map/ppermute | solution.py:215
  18.9 0.1 pad_maximum_fusion
  19.0 0.4 copy-done.10
  19.8 0.9 %slice.353 = f32[64,512]{1,0:T(8,128)S(1)} slice(f32[136,512]{1,0:T(8,128)} %copy-done.10), slice={[0:64], [0:512]} | slice | bytes 262144 | tf_op jit(solution)/shard_map/slice | solution.py:222
  20.9 0.5 add_select_fusion.2
  21.5 0.5 add_select_fusion.1
  22.2 0.5 add_select_fusion
  22.7 0.3 select_convert_fusion.1
  23.4 0.2 reshape.208
  23.6 0.6 slice.377
  24.3 3.7 %all-to-all-start = ((bf16[4,4,8,256]{3,2,1,0:T(8,128)(2,1)}), bf16[4,4,8,256]{3,2,1,0:T(8,128)(2,1)S(1)}, u32[]{:S(2)}, u32[]{:S(2)}) async-start(bf16[4,4,8,256]{3,2,1,0:T(8,128)(2,1)} %slice.377), calls=%async_computation | async-start | bytes 131072 | tf_op jit(solution)/shard_map/all_to_all | solution.py:259
  28.0 0.6 pad_maximum_fusion.10
  28.6 2.6 %all-to-all-done.x_ref = bf16[4,4,8,256]{3,2,1,0:T(8,128)(2,1)S(1)} async-done(((bf16[4,4,8,256]{3,2,1,0:T(8,128)(2,1)}), bf16[4,4,8,256]{3,2,1,0:T(8,128)(2,1)S(1)}, u32[]{:S(2)}, u32[]{:S(2)}) %all-to-all-start) | async-done | bytes 65568 | tf_op jit(solution)/shard_map/all_to_all | solution.py:259
  31.3 4.1 %all-to-all-start.1 = ((bf16[4,5,8,256]{3,2,1,0:T(8,128)(2,1)}), bf16[4,5,8,256]{3,2,1,0:T(8,128)(2,1)S(1)}, u32[]{:S(2)}, u32[]{:S(2)}) async-start(bf16[4,5,8,256]{3,2,1,0:T(8,128)(2,1)} %pad_maximum_fusion.10), calls=%async_computation.1 | async-start | bytes 163840 | tf_op jit(solution)/shard_map/all_to_all | solution.py:259
  35.4 5.7 %shard_map.118 = bf16[4,8,1024]{2,1,0:T(8,128)(2,1)} custom-call(f32[8,1]{1,0:T(8,128)} %reshape_tile.5.hs_ref, bf16[4,4,8,256]{3,2,1,0:T(8,128)(2,1)} %copy-done.11, bf16[64,8]{1,0:T(8,128)(2,1)} %bitcast.215, f32[64,1]{1,0:T(8,128)} %copy.50.gain_ref, bf16[192,64]{1,0:T(8,128)(2,1)} %bitcast.209, bf16[64,64]{1,0:T(8,128)(2,1)} %bitcast.213, ...), custom_call_target="tpu_custom_call" | custom-call | tf_op jit(solution)/shard_map/pallas_call | solution.py:141
  41.1 0.6 copy-done.9
  41.7 6.7 %shard_map.119 = bf16[5,8,1024]{2,1,0:T(8,128)(2,1)} custom-call(f32[8,1]{1,0:T(8,128)} %reshape_tile.5.hs_ref, bf16[4,5,8,256]{3,2,1,0:T(8,128)(2,1)} %copy-done.9, bf16[64,8]{1,0:T(8,128)(2,1)} %bitcast.216, f32[64,1]{1,0:T(8,128)} %copy.50.gain_ref, bf16[192,64]{1,0:T(8,128)(2,1)} %bitcast.210, bf16[64,64]{1,0:T(8,128)(2,1)} %bitcast.214, ...), custom_call_target="tpu_custom_call" | custom-call | tf_op jit(solution)/shard_map/pallas_call | solution.py:141
  48.5 0.7 %slice.380 = bf16[1,8,1024]{2,1,0:T(8,128)(2,1)S(1)} slice(bf16[5,8,1024]{2,1,0:T(8,128)(2,1)} %shard_map.119), slice={[4:5], [0:8], [0:1024]} | slice | bytes 32768 | tf_op jit(solution)/shard_map/slice | solution.py:276
  49.2 0.9 %copy_bitcast_fusion.2 = bf16[8,8,8,128]{3,1,2,0:T(8,128)(2,1)S(1)} fusion(bf16[5,8,1024]{2,1,0:T(8,128)(2,1)} %shard_map.119, bf16[4,8,1024]{2,1,0:T(8,128)(2,1)} %shard_map.118), kind=kLoop, calls=%fused_computation.84 | loop fusion | flops 65536 | bytes 278528 | tf_op jit(solution)/shard_map/transpose | solution.py:275
  50.1 0.1 reshape_squeeze.3
  50.5 0.2 pad_maximum_fusion.7
  50.7 0.3 reshape.210
  51.0 2.3 %collective-permute-start.2 = (bf16[8,8,1152]{2,1,0:T(8,128)(2,1)S(1)}, bf16[8,8,1152]{2,1,0:T(8,128)(2,1)S(1)}, u32[]{:S(2)}, u32[]{:S(2)}) collective-permute-start(bf16[8,8,1152]{2,1,0:T(8,128)(2,1)S(1)} %reshape.210), channel_id=1, source_target_pairs={{0,1},{1,2},{2,3},{3,4},{4,5},{5,6},{6,7},{8,9},{9,10},{10,11},{11... | collective-permute-start | bytes 442376 | tf_op jit(solution)/shard_map/ppermute | solution.py:34
  53.3 4.0 %collective-permute-start.3 = (bf16[8,8,1152]{2,1,0:T(8,128)(2,1)S(1)}, bf16[8,8,1152]{2,1,0:T(8,128)(2,1)S(1)}, u32[]{:S(2)}, u32[]{:S(2)}) collective-permute-start(bf16[8,8,1152]{2,1,0:T(8,128)(2,1)S(1)} %reshape.210), channel_id=1, source_target_pairs={{1,0},{2,1},{3,2},{4,3},{5,4},{6,5},{7,6},{9,8},{10,9},{11,10},{12... | collective-permute-start | bytes 442376 | tf_op jit(solution)/shard_map/ppermute | solution.py:35
  57.4 1.8 %collective-permute-done.2 = bf16[8,8,1152]{2,1,0:T(8,128)(2,1)S(1)} collective-permute-done((bf16[8,8,1152]{2,1,0:T(8,128)(2,1)S(1)}, bf16[8,8,1152]{2,1,0:T(8,128)(2,1)S(1)}, u32[]{:S(2)}, u32[]{:S(2)}) %collective-permute-start.2) | collective-permute-done | bytes 147488 | tf_op jit(solution)/shard_map/ppermute | solution.py:34
  59.2 0.4 reshape.211
  59.6 3.1 %collective-permute-done.3 = bf16[8,8,1152]{2,1,0:T(8,128)(2,1)S(1)} collective-permute-done((bf16[8,8,1152]{2,1,0:T(8,128)(2,1)S(1)}, bf16[8,8,1152]{2,1,0:T(8,128)(2,1)S(1)}, u32[]{:S(2)}, u32[]{:S(2)}) %collective-permute-start.3) | collective-permute-done | bytes 147488 | tf_op jit(solution)/shard_map/ppermute | solution.py:35
  62.7 0.4 reshape.212
  63.2 0.2 pad_maximum_fusion.1
  63.4 0.4 pad_maximum_fusion.3
  63.8 0.3 fusion.12
  64.1 0.4 convolution_add_fusion.7
  64.4 0.3 convolution_add_fusion.6
  64.8 0.3 convolution_add_fusion.5
  65.1 0.3 convolution_add_fusion.4
  65.4 0.4 convolution_add_fusion.3
  65.8 0.3 convolution_add_fusion.2
  66.1 0.4 convolution_add_fusion.1
  66.5 0.5 select_convert_fusion
  67.0 0.2 fusion.24
  67.2 0.2 convolution_add_fusion.15
  67.4 0.2 convolution_add_fusion.14
  67.6 0.2 convolution_add_fusion.13
  67.8 0.2 convolution_add_fusion.12
  68.1 0.2 convolution_add_fusion.11
  68.3 0.2 convolution_add_fusion.10
  68.5 0.2 convolution_add_fusion.9
  68.7 0.2 copy-done.7
  68.9 0.2 fusion.3
  69.2 0.7 copy.80
  (93 shorter events, 4.6 us)
Async XLA Ops:
  0.0 9.8 %copy-start = (bf16[64,64]{1,0:T(8,128)(2,1)S(1)}, bf16[64,64]{1,0:T(8,128)(2,1)}, u32[]{:S(2)}) copy-start(bf16[64,64]{1,0:T(8,128)(2,1)} %param.20) | copy-start | bytes 24580
  0.0 1.3 %copy-start.6 = (f32[2,8,8,512]{3,2,1,0:T(8,128)S(1)}, f32[2,8,8,512]{3,2,1,0:T(8,128)}, u32[]{:S(2)}) copy-start(f32[2,8,8,512]{3,2,1,0:T(8,128)} %param.12) | copy-start | bytes 786436
  1.3 6.7 %copy-start.1 = (bf16[9,8,8]{0,2,1:T(8,128)(2,1)S(1)}, bf16[9,8,8]{0,2,1:T(8,128)(2,1)}, u32[]{:S(2)}) copy-start(bf16[9,8,8]{0,2,1:T(8,128)(2,1)} %param.22) | copy-start | bytes 3460
  1.4 6.7 %copy-start.2 = (bf16[9,8,8]{0,2,1:T(8,128)(2,1)S(1)}, bf16[9,8,8]{0,2,1:T(8,128)(2,1)}, u32[]{:S(2)}) copy-start(bf16[9,8,8]{0,2,1:T(8,128)(2,1)} %param.23) | copy-start | bytes 3460
  1.4 6.9 %copy-start.12 = (bf16[64,192]{1,0:T(8,128)(2,1)S(1)}, bf16[64,192]{1,0:T(8,128)(2,1)}, u32[]{:S(2)}) copy-start(bf16[64,192]{1,0:T(8,128)(2,1)} %param.18) | copy-start | bytes 73732
  1.4 14.3 %collective-permute-start = (f32[136,512]{1,0:T(8,128)S(1)}, f32[136,512]{1,0:T(8,128)S(1)}, u32[]{:S(2)}, u32[]{:S(2)}) collective-permute-start(f32[136,512]{1,0:T(8,128)S(1)} %pad_maximum_fusion.5), channel_id=1, source_target_pairs={{0,1},{1,2},{2,3},{3,4},{4,5},{5,6},{6,7},{8,9},{9,10},{10,11},{11... | collective-permute-start | bytes 835592 | tf_op jit(solution)/shard_map/ppermute | solution.py:207
  4.7 6.4 %copy-start.14 = (f32[64]{0:T(128)S(1)}, f32[64]{0:T(128)}, u32[]{:S(2)}) copy-start(f32[64]{0:T(128)} %param.17) | copy-start | bytes 772
  4.7 7.1 %copy-start.13 = (bf16[8,64]{1,0:T(8,128)(2,1)S(1)}, bf16[8,64]{1,0:T(8,128)(2,1)}, u32[]{:S(2)}) copy-start(bf16[8,64]{1,0:T(8,128)(2,1)} %param.16) | copy-start | bytes 3076
  4.7 7.8 %copy-start.15 = (f32[4]{0:T(128)S(1)}, f32[4]{0:T(128)}, u32[]{:S(2)}) copy-start(f32[4]{0:T(128)} %param.19) | copy-start | bytes 52
  4.8 14.0 %collective-permute-start.1 = (f32[136,512]{1,0:T(8,128)S(1)}, f32[136,512]{1,0:T(8,128)S(1)}, u32[]{:S(2)}, u32[]{:S(2)}) collective-permute-start(f32[136,512]{1,0:T(8,128)S(1)} %pad_maximum_fusion.6), channel_id=1, source_target_pairs={{1,0},{2,1},{3,2},{4,3},{5,4},{6,5},{7,6},{9,8},{10,9},{11,10},{12... | collective-permute-start | bytes 835592 | tf_op jit(solution)/shard_map/ppermute | solution.py:215
  8.4 10.4 %copy-start.3 = (f32[8,8,512]{2,1,0:T(8,128)S(1)}, f32[8,8,512]{2,1,0:T(8,128)}, u32[]{:S(2)}) copy-start(f32[8,8,512]{2,1,0:T(8,128)} %param.15) | copy-start | bytes 393220
  8.5 10.4 %copy-start.4 = (f32[8,8,512]{2,1,0:T(8,128)S(1)}, f32[8,8,512]{2,1,0:T(8,128)}, u32[]{:S(2)}) copy-start(f32[8,8,512]{2,1,0:T(8,128)} %param.14) | copy-start | bytes 393220
  8.5 10.4 %copy-start.5 = (f32[8,8,512]{2,1,0:T(8,128)S(1)}, f32[8,8,512]{2,1,0:T(8,128)}, u32[]{:S(2)}) copy-start(f32[8,8,512]{2,1,0:T(8,128)} %param.13) | copy-start | bytes 393220
  18.8 0.7 %copy-start.10 = (f32[136,512]{1,0:T(8,128)}, f32[136,512]{1,0:T(8,128)S(1)}, u32[]{:S(2)}) copy-start(f32[136,512]{1,0:T(8,128)S(1)} %collective-permute-done.1) | copy-start | bytes 835588
  24.3 7.0 %all-to-all-start = ((bf16[4,4,8,256]{3,2,1,0:T(8,128)(2,1)}), bf16[4,4,8,256]{3,2,1,0:T(8,128)(2,1)S(1)}, u32[]{:S(2)}, u32[]{:S(2)}) async-start(bf16[4,4,8,256]{3,2,1,0:T(8,128)(2,1)} %slice.377), calls=%async_computation | async-start | bytes 131072 | tf_op jit(solution)/shard_map/all_to_all | solution.py:259
  31.3 4.1 %copy-start.11 = (bf16[4,4,8,256]{3,2,1,0:T(8,128)(2,1)}, bf16[4,4,8,256]{3,2,1,0:T(8,128)(2,1)S(1)}, u32[]{:S(2)}) copy-start(bf16[4,4,8,256]{3,2,1,0:T(8,128)(2,1)S(1)} %all-to-all-done.x_ref) | copy-start | bytes 196612
  31.3 9.8 %all-to-all-start.1 = ((bf16[4,5,8,256]{3,2,1,0:T(8,128)(2,1)}), bf16[4,5,8,256]{3,2,1,0:T(8,128)(2,1)S(1)}, u32[]{:S(2)}, u32[]{:S(2)}) async-start(bf16[4,5,8,256]{3,2,1,0:T(8,128)(2,1)} %pad_maximum_fusion.10), calls=%async_computation.1 | async-start | bytes 163840 | tf_op jit(solution)/shard_map/all_to_all | solution.py:259
  41.1 0.6 copy-start.9
  51.0 8.2 %collective-permute-start.2 = (bf16[8,8,1152]{2,1,0:T(8,128)(2,1)S(1)}, bf16[8,8,1152]{2,1,0:T(8,128)(2,1)S(1)}, u32[]{:S(2)}, u32[]{:S(2)}) collective-permute-start(bf16[8,8,1152]{2,1,0:T(8,128)(2,1)S(1)} %reshape.210), channel_id=1, source_target_pairs={{0,1},{1,2},{2,3},{3,4},{4,5},{5,6},{6,7},{8,9},{9,10},{10,11},{11... | collective-permute-start | bytes 442376 | tf_op jit(solution)/shard_map/ppermute | solution.py:34
  53.3 9.4 %collective-permute-start.3 = (bf16[8,8,1152]{2,1,0:T(8,128)(2,1)S(1)}, bf16[8,8,1152]{2,1,0:T(8,128)(2,1)S(1)}, u32[]{:S(2)}, u32[]{:S(2)}) collective-permute-start(bf16[8,8,1152]{2,1,0:T(8,128)(2,1)S(1)} %reshape.210), channel_id=1, source_target_pairs={{1,0},{2,1},{3,2},{4,3},{5,4},{6,5},{7,6},{9,8},{10,9},{11,10},{12... | collective-permute-start | bytes 442376 | tf_op jit(solution)/shard_map/ppermute | solution.py:35
  68.0 0.9 %copy-start.7 = (bf16[5,8,1024]{2,1,0:T(8,128)(2,1)S(1)}, bf16[5,8,1024]{2,1,0:T(8,128)(2,1)}, u32[]{:S(2)}) copy-start(bf16[5,8,1024]{2,1,0:T(8,128)(2,1)} %shard_map.119) | copy-start | bytes 245764
  68.1 0.9 %copy-start.8 = (bf16[4,8,1024]{2,1,0:T(8,128)(2,1)S(1)}, bf16[4,8,1024]{2,1,0:T(8,128)(2,1)}, u32[]{:S(2)}) copy-start(bf16[4,8,1024]{2,1,0:T(8,128)(2,1)} %shard_map.118) | copy-start | bytes 196612

commit v15 on v10

--- a/solution.py
+++ b/solution.py
@@ -73,6 +73,7 @@
             r, hs_ref, x_ref, w1_ref, gain_ref, pw_ref, ow_ref, rw_ref, out_ref, chunk, heads
         ),
         0,
+        unroll=2,
     )
 
 

time: 65.5 us -> 64.9 us (level)
  no operation moved by 1% of the time
where the time goes in v15:
time: 64.9 us; the launch traced here: 63.9 us
  starting transfers between devices  16.3 us (25%)
  local copies, waits for them, and re-layouts  15 us (23%)
  waiting for transfers between devices  11.3 us (17%)
  Pallas kernels  10.4 us (16%)
  other arithmetic  5.14 us (8%)
  matrix products  5.01 us (8%)
  between operations  0.72 us (1%)
    pallas_call x1, Pallas kernels, post_block(): pl.pallas_call(functools.partial(attention_kernel, chunk=chunk, heads=hea...  10.4 us
    dot_general x18, matrix products, convolve(): jnp.einsum('oc,mcij->moij', kernel[row_stencil * 3 + column_stencil], shi...  5.01 us
    unnamed x48, local copies, waits for them, and re-layouts  4.65 us
    ppermute x1, waiting for transfers between devices, row_padded(): high = lax.ppermute(block[..., :width, :].reshape(flat), 'row', backward)  4.13 us
    ppermute x1, starting transfers between devices, row_padded(): high = lax.ppermute(block[..., :width, :].reshape(flat), 'row', backward)  4.04 us
    all_to_all x1, starting transfers between devices, on_device(): lax.all_to_all(by_chunk, 'mem', split_axis=0, concat_axis=0, tiled=True)  3.79 us
    all_to_all x1, waiting for transfers between devices, on_device(): lax.all_to_all(by_chunk, 'mem', split_axis=0, concat_axis=0, tiled=True)  3.72 us
    ppermute x1, starting transfers between devices, on_device(): lax.ppermute(pack(starting_states[:, :, row_total - state_halo:], coeffic...  3.12 us
  transfers between devices with their start and end apart: 5, of which 5 were waited for; matrix products, arithmetic and copies ran while one was open for 13% of the time, Pallas kernels for 0%

profile of v15, /device:TPU:9, one launch (start us, length us, event | category | flops | bytes accessed | tf_op | source)
XLA Modules:
  0.0 63.9 jit_solution(17947461565074484823)
XLA Ops:
  0.0 1.1 %pad_maximum_fusion.4 = f32[3,8,8,512]{3,2,1,0:T(8,128)S(1)} fusion(f32[1,8,8,512]{3,2,1,0:T(8,128)} %bitcast.199, f32[1,8,8,512]{3,2,1,0:T(8,128)} %bitcast.201, f32[1,8,8,512]{3,2,1,0:T(8,128)} %bitcast.203), kind=kLoop, calls=%fused_computation.47 | loop fusion | flops 196608 | bytes 786432 | tf_op jit(solution)/shard_map/stack | solution.py:195
  1.4 3.1 %collective-permute-start = (f32[136,512]{1,0:T(8,128)S(1)}, f32[136,512]{1,0:T(8,128)S(1)}, u32[]{:S(2)}, u32[]{:S(2)}) collective-permute-start(f32[136,512]{1,0:T(8,128)S(1)} %pad_maximum_fusion.5), channel_id=1, source_target_pairs={{0,1},{1,2},{2,3},{3,4},{4,5},{5,6},{6,7},{8,9},{9,10},{10,11},{11... | collective-permute-start | bytes 835592 | tf_op jit(solution)/shard_map/ppermute | solution.py:208
  4.8 3.1 %collective-permute-start.1 = (f32[136,512]{1,0:T(8,128)S(1)}, f32[136,512]{1,0:T(8,128)S(1)}, u32[]{:S(2)}, u32[]{:S(2)}) collective-permute-start(f32[136,512]{1,0:T(8,128)S(1)} %pad_maximum_fusion.6), channel_id=1, source_target_pairs={{1,0},{2,1},{3,2},{4,3},{5,4},{6,5},{7,6},{9,8},{10,9},{11,10},{12... | collective-permute-start | bytes 835592 | tf_op jit(solution)/shard_map/ppermute | solution.py:216
  8.5 0.7 %gather_fusion = bf16[64,3,64]{2,1,0:T(4,128)(2,1)S(1)} fusion(bf16[3,64,64]{2,0,1:T(4,128)(2,1)S(1)} %copy.46, s32[1024]{0:T(1024)S(1)} %pad_clamp_fusion), kind=kCustom, calls=%fused_computation | custom fusion | bytes 49408 | tf_op jit(solution)/shard_map/gather | solution.py:139
  9.1 0.6 copy.47
  9.8 0.6 gather_fusion.1
  10.4 0.7 %copy.48 = bf16[64,64]{0,1:T(8,128)(2,1)} copy(bf16[64,64]{1,0:T(8,128)(2,1)S(1)} %gather_fusion.1) | data formatting | bytes 16384 | tf_op jit(solution)/shard_map/gather | solution.py:140
  11.1 0.7 %copy.50.gain_ref = f32[64,1]{1,0:T(8,128)} copy(f32[64,1]{0,1:T(1,128)S(1)} %bitcast.214) | data formatting | bytes 512 | tf_op jit(solution)/shard_map/reshape | solution.py:149
  11.8 0.7 %copy.44 = bf16[8,64]{0,1:T(8,128)(2,1)} copy(bf16[8,64]{1,0:T(8,128)(2,1)S(1)} %copy-done.11) | data formatting | bytes 2048 | tf_op args[4]
  12.5 0.7 %reshape_tile.4.hs_ref = f32[8,1]{1,0:T(8,128)} reshape(f32[2,4]{1,0:T(2,128)S(1)} %tile.2) | data formatting | bytes 64 | tf_op jit(solution)/shard_map/reshape;tile | solution.py:141
  13.8 0.1 copy.102
  13.9 0.1 copy.103
  14.1 0.1 copy.104
  14.2 0.1 copy.105
  14.3 0.1 copy.106
  14.6 0.1 copy.108
  14.9 0.1 copy.110
  15.8 3.0 %collective-permute-done.1 = f32[136,512]{1,0:T(8,128)S(1)} collective-permute-done((f32[136,512]{1,0:T(8,128)S(1)}, f32[136,512]{1,0:T(8,128)S(1)}, u32[]{:S(2)}, u32[]{:S(2)}) %collective-permute-start.1) | collective-permute-done | bytes 278560 | tf_op jit(solution)/shard_map/ppermute | solution.py:216
  18.9 0.1 pad_maximum_fusion
  19.0 0.5 copy-done.9
  19.8 0.9 %slice.345 = f32[64,512]{1,0:T(8,128)S(1)} slice(f32[136,512]{1,0:T(8,128)} %copy-done.9), slice={[0:64], [0:512]} | slice | bytes 262144 | tf_op jit(solution)/shard_map/slice | solution.py:223
  21.0 0.5 add_select_fusion.2
  21.6 0.5 add_select_fusion.1
  22.2 0.5 add_select_fusion
  22.7 0.3 select_convert_fusion.1
  23.4 0.2 reshape.196
  23.6 0.7 %pad_maximum_fusion.8 = bf16[4,9,8,256]{3,2,1,0:T(8,128)(2,1)} fusion(bf16[4,1,8,256]{3,2,1,0:T(8,128)(2,1)S(1)} %reshape.196, bf16[4,8,8,256]{3,2,1,0:T(8,128)(2,1)S(1)} %bitcast.207), kind=kLoop, calls=%fused_computation.65 | loop fusion | flops 73728 | bytes 294912 | tf_op jit(solution)/shard_map/concatenate | solution.py:255
  24.3 3.8 %all-to-all-start = ((bf16[4,9,8,256]{3,2,1,0:T(8,128)(2,1)}), bf16[4,9,8,256]{3,2,1,0:T(8,128)(2,1)S(1)}, u32[]{:S(2)}, u32[]{:S(2)}) async-start(bf16[4,9,8,256]{3,2,1,0:T(8,128)(2,1)} %pad_maximum_fusion.8), calls=%async_computation | async-start | bytes 294912 | tf_op jit(solution)/shard_map/all_to_all | solution.py:256
  28.1 3.7 %all-to-all-done.x_ref = bf16[4,9,8,256]{3,2,1,0:T(8,128)(2,1)S(1)} async-done(((bf16[4,9,8,256]{3,2,1,0:T(8,128)(2,1)}), bf16[4,9,8,256]{3,2,1,0:T(8,128)(2,1)S(1)}, u32[]{:S(2)}, u32[]{:S(2)}) %all-to-all-start) | async-done | bytes 147488 | tf_op jit(solution)/shard_map/all_to_all | solution.py:256
  31.8 0.7 %copy-done.8 = bf16[4,9,8,256]{3,2,1,0:T(8,128)(2,1)} copy-done((bf16[4,9,8,256]{3,2,1,0:T(8,128)(2,1)}, bf16[4,9,8,256]{3,2,1,0:T(8,128)(2,1)S(1)}, u32[]{:S(2)}) %copy-start.8) | copy-done | bytes 147480
  32.5 10.4 %shard_map.118 = bf16[9,8,1024]{2,1,0:T(8,128)(2,1)} custom-call(f32[8,1]{1,0:T(8,128)} %reshape_tile.4.hs_ref, bf16[4,9,8,256]{3,2,1,0:T(8,128)(2,1)} %copy-done.8, bf16[64,8]{1,0:T(8,128)(2,1)} %bitcast.212, f32[64,1]{1,0:T(8,128)} %copy.50.gain_ref, bf16[192,64]{1,0:T(8,128)(2,1)} %bitcast.209, bf16[64,64]{1,0:T(8,128)(2,1)} %bitcast.211, ...), custom_call_target="tpu_custom_call" | custom-call | tf_op jit(solution)/shard_map/pallas_call | solution.py:142
  42.9 0.7 %slice.372 = bf16[1,8,1024]{2,1,0:T(8,128)(2,1)S(1)} slice(bf16[9,8,1024]{2,1,0:T(8,128)(2,1)} %shard_map.118), slice={[8:9], [0:8], [0:1024]} | slice | bytes 32768 | tf_op jit(solution)/shard_map/slice | solution.py:271
  43.6 0.9 %copy_bitcast_fusion.2 = bf16[8,8,8,128]{3,1,2,0:T(8,128)(2,1)S(1)} fusion(bf16[9,8,1024]{2,1,0:T(8,128)(2,1)} %shard_map.118), kind=kLoop, calls=%fused_computation.84 | loop fusion | bytes 262144 | tf_op jit(solution)/shard_map/transpose | solution.py:270
  44.5 0.1 reshape_squeeze.3
  44.9 0.2 pad_maximum_fusion.7
  45.2 0.3 reshape.205
  45.4 2.3 %collective-permute-start.2 = (bf16[8,8,1152]{2,1,0:T(8,128)(2,1)S(1)}, bf16[8,8,1152]{2,1,0:T(8,128)(2,1)S(1)}, u32[]{:S(2)}, u32[]{:S(2)}) collective-permute-start(bf16[8,8,1152]{2,1,0:T(8,128)(2,1)S(1)} %reshape.205), channel_id=1, source_target_pairs={{0,1},{1,2},{2,3},{3,4},{4,5},{5,6},{6,7},{8,9},{9,10},{10,11},{11... | collective-permute-start | bytes 442376 | tf_op jit(solution)/shard_map/ppermute | solution.py:34
  47.7 4.0 %collective-permute-start.3 = (bf16[8,8,1152]{2,1,0:T(8,128)(2,1)S(1)}, bf16[8,8,1152]{2,1,0:T(8,128)(2,1)S(1)}, u32[]{:S(2)}, u32[]{:S(2)}) collective-permute-start(bf16[8,8,1152]{2,1,0:T(8,128)(2,1)S(1)} %reshape.205), channel_id=1, source_target_pairs={{1,0},{2,1},{3,2},{4,3},{5,4},{6,5},{7,6},{9,8},{10,9},{11,10},{12... | collective-permute-start | bytes 442376 | tf_op jit(solution)/shard_map/ppermute | solution.py:35
  51.9 0.3 collective-permute-done.2
  52.2 0.4 reshape.206
  52.6 4.1 %collective-permute-done.3 = bf16[8,8,1152]{2,1,0:T(8,128)(2,1)S(1)} collective-permute-done((bf16[8,8,1152]{2,1,0:T(8,128)(2,1)S(1)}, bf16[8,8,1152]{2,1,0:T(8,128)(2,1)S(1)}, u32[]{:S(2)}, u32[]{:S(2)}) %collective-permute-start.3) | collective-permute-done | bytes 147488 | tf_op jit(solution)/shard_map/ppermute | solution.py:35
  56.8 0.4 reshape.207
  57.2 0.2 pad_maximum_fusion.1
  57.4 0.4 pad_maximum_fusion.3
  57.8 0.3 fusion.12
  58.1 0.4 convolution_add_fusion.7
  58.4 0.4 convolution_add_fusion.6
  58.8 0.3 convolution_add_fusion.5
  59.1 0.4 convolution_add_fusion.4
  59.5 0.4 convolution_add_fusion.3
  59.8 0.3 convolution_add_fusion.2
  60.1 0.3 convolution_add_fusion.1
  60.5 0.5 select_convert_fusion
  61.0 0.2 fusion.24
  61.2 0.2 convolution_add_fusion.15
  61.4 0.2 convolution_add_fusion.14
  61.7 0.2 convolution_add_fusion.13
  61.8 0.2 convolution_add_fusion.12
  62.1 0.2 convolution_add_fusion.11
  62.3 0.2 convolution_add_fusion.10
  62.5 0.2 convolution_add_fusion.9
  62.7 0.3 copy-done.3
  63.0 0.2 fusion.3
  63.2 0.7 %copy.76 = bf16[8,8,8,128]{3,2,1,0:T(8,128)(2,1)} copy(bf16[8,8,8,128]{3,1,2,0:T(8,128)(2,1)S(1)} %fusion.3) | data formatting | bytes 262144 | tf_op jit(solution)/shard_map/convert_element_type | solution.py:286
  (85 shorter events, 4.1 us)
Async XLA Ops:
  0.0 9.8 %copy-start = (bf16[64,64]{1,0:T(8,128)(2,1)S(1)}, bf16[64,64]{1,0:T(8,128)(2,1)}, u32[]{:S(2)}) copy-start(bf16[64,64]{1,0:T(8,128)(2,1)} %param.20) | copy-start | bytes 24580
  0.0 1.3 %copy-start.7 = (f32[2,8,8,512]{3,2,1,0:T(8,128)S(1)}, f32[2,8,8,512]{3,2,1,0:T(8,128)}, u32[]{:S(2)}) copy-start(f32[2,8,8,512]{3,2,1,0:T(8,128)} %param.12) | copy-start | bytes 786436
  1.3 6.7 %copy-start.1 = (bf16[9,8,8]{0,2,1:T(8,128)(2,1)S(1)}, bf16[9,8,8]{0,2,1:T(8,128)(2,1)}, u32[]{:S(2)}) copy-start(bf16[9,8,8]{0,2,1:T(8,128)(2,1)} %param.22) | copy-start | bytes 3460
  1.4 6.7 %copy-start.2 = (bf16[9,8,8]{0,2,1:T(8,128)(2,1)S(1)}, bf16[9,8,8]{0,2,1:T(8,128)(2,1)}, u32[]{:S(2)}) copy-start(bf16[9,8,8]{0,2,1:T(8,128)(2,1)} %param.23) | copy-start | bytes 3460
  1.4 6.9 %copy-start.10 = (bf16[64,192]{1,0:T(8,128)(2,1)S(1)}, bf16[64,192]{1,0:T(8,128)(2,1)}, u32[]{:S(2)}) copy-start(bf16[64,192]{1,0:T(8,128)(2,1)} %param.18) | copy-start | bytes 73732
  1.4 14.3 %collective-permute-start = (f32[136,512]{1,0:T(8,128)S(1)}, f32[136,512]{1,0:T(8,128)S(1)}, u32[]{:S(2)}, u32[]{:S(2)}) collective-permute-start(f32[136,512]{1,0:T(8,128)S(1)} %pad_maximum_fusion.5), channel_id=1, source_target_pairs={{0,1},{1,2},{2,3},{3,4},{4,5},{5,6},{6,7},{8,9},{9,10},{10,11},{11... | collective-permute-start | bytes 835592 | tf_op jit(solution)/shard_map/ppermute | solution.py:208
  4.7 6.4 %copy-start.12 = (f32[64]{0:T(128)S(1)}, f32[64]{0:T(128)}, u32[]{:S(2)}) copy-start(f32[64]{0:T(128)} %param.17) | copy-start | bytes 772
  4.7 7.1 %copy-start.11 = (bf16[8,64]{1,0:T(8,128)(2,1)S(1)}, bf16[8,64]{1,0:T(8,128)(2,1)}, u32[]{:S(2)}) copy-start(bf16[8,64]{1,0:T(8,128)(2,1)} %param.16) | copy-start | bytes 3076
  4.7 7.8 %copy-start.13 = (f32[4]{0:T(128)S(1)}, f32[4]{0:T(128)}, u32[]{:S(2)}) copy-start(f32[4]{0:T(128)} %param.19) | copy-start | bytes 52
  4.8 14.0 %collective-permute-start.1 = (f32[136,512]{1,0:T(8,128)S(1)}, f32[136,512]{1,0:T(8,128)S(1)}, u32[]{:S(2)}, u32[]{:S(2)}) collective-permute-start(f32[136,512]{1,0:T(8,128)S(1)} %pad_maximum_fusion.6), channel_id=1, source_target_pairs={{1,0},{2,1},{3,2},{4,3},{5,4},{6,5},{7,6},{9,8},{10,9},{11,10},{12... | collective-permute-start | bytes 835592 | tf_op jit(solution)/shard_map/ppermute | solution.py:216
  8.4 10.4 %copy-start.4 = (f32[8,8,512]{2,1,0:T(8,128)S(1)}, f32[8,8,512]{2,1,0:T(8,128)}, u32[]{:S(2)}) copy-start(f32[8,8,512]{2,1,0:T(8,128)} %param.15) | copy-start | bytes 393220
  8.5 10.4 %copy-start.5 = (f32[8,8,512]{2,1,0:T(8,128)S(1)}, f32[8,8,512]{2,1,0:T(8,128)}, u32[]{:S(2)}) copy-start(f32[8,8,512]{2,1,0:T(8,128)} %param.14) | copy-start | bytes 393220
  8.5 10.4 %copy-start.6 = (f32[8,8,512]{2,1,0:T(8,128)S(1)}, f32[8,8,512]{2,1,0:T(8,128)}, u32[]{:S(2)}) copy-start(f32[8,8,512]{2,1,0:T(8,128)} %param.13) | copy-start | bytes 393220
  18.8 0.7 %copy-start.9 = (f32[136,512]{1,0:T(8,128)}, f32[136,512]{1,0:T(8,128)S(1)}, u32[]{:S(2)}) copy-start(f32[136,512]{1,0:T(8,128)S(1)} %collective-permute-done.1) | copy-start | bytes 835588
  24.3 7.5 %all-to-all-start = ((bf16[4,9,8,256]{3,2,1,0:T(8,128)(2,1)}), bf16[4,9,8,256]{3,2,1,0:T(8,128)(2,1)S(1)}, u32[]{:S(2)}, u32[]{:S(2)}) async-start(bf16[4,9,8,256]{3,2,1,0:T(8,128)(2,1)} %pad_maximum_fusion.8), calls=%async_computation | async-start | bytes 294912 | tf_op jit(solution)/shard_map/all_to_all | solution.py:256
  31.8 0.7 %copy-start.8 = (bf16[4,9,8,256]{3,2,1,0:T(8,128)(2,1)}, bf16[4,9,8,256]{3,2,1,0:T(8,128)(2,1)S(1)}, u32[]{:S(2)}) copy-start(bf16[4,9,8,256]{3,2,1,0:T(8,128)(2,1)S(1)} %all-to-all-done.x_ref) | copy-start | bytes 442372
  45.4 6.8 %collective-permute-start.2 = (bf16[8,8,1152]{2,1,0:T(8,128)(2,1)S(1)}, bf16[8,8,1152]{2,1,0:T(8,128)(2,1)S(1)}, u32[]{:S(2)}, u32[]{:S(2)}) collective-permute-start(bf16[8,8,1152]{2,1,0:T(8,128)(2,1)S(1)} %reshape.205), channel_id=1, source_target_pairs={{0,1},{1,2},{2,3},{3,4},{4,5},{5,6},{6,7},{8,9},{9,10},{10,11},{11... | collective-permute-start | bytes 442376 | tf_op jit(solution)/shard_map/ppermute | solution.py:34
  47.7 9.0 %collective-permute-start.3 = (bf16[8,8,1152]{2,1,0:T(8,128)(2,1)S(1)}, bf16[8,8,1152]{2,1,0:T(8,128)(2,1)S(1)}, u32[]{:S(2)}, u32[]{:S(2)}) collective-permute-start(bf16[8,8,1152]{2,1,0:T(8,128)(2,1)S(1)} %reshape.205), channel_id=1, source_target_pairs={{1,0},{2,1},{3,2},{4,3},{5,4},{6,5},{7,6},{9,8},{10,9},{11,10},{12... | collective-permute-start | bytes 442376 | tf_op jit(solution)/shard_map/ppermute | solution.py:35
  62.1 0.9 %copy-start.3 = (bf16[9,8,1024]{2,1,0:T(8,128)(2,1)S(1)}, bf16[9,8,1024]{2,1,0:T(8,128)(2,1)}, u32[]{:S(2)}) copy-start(bf16[9,8,1024]{2,1,0:T(8,128)(2,1)} %shard_map.118) | copy-start | bytes 442372

commit v16 on v15

--- a/solution.py
+++ b/solution.py
@@ -64,20 +64,28 @@
 
 
 def attention_kernel(
-    hs_ref, x_ref, w1_ref, gain_ref, pw_ref, ow_ref, rw_ref, out_ref, *, chunk, heads
+    hs_ref, x_ref, w1_ref, gain_ref, pw_ref, ow_ref, rw_ref, out_ref, edge_ref, *, chunk, heads
 ):
+    weights = (hs_ref, x_ref, w1_ref, gain_ref, pw_ref, ow_ref, rw_ref)
+    tile_rows = out_ref.shape[0]
+
+    def store_row(r, features):
+        out_ref[r] = features
+
+    def store_edge(r, features):
+        edge_ref[...] = features
+
     lax.fori_loop(
         0,
-        x_ref.shape[1],
-        lambda r, carry: attention_row(
-            r, hs_ref, x_ref, w1_ref, gain_ref, pw_ref, ow_ref, rw_ref, out_ref, chunk, heads
-        ),
+        tile_rows,
+        lambda r, carry: attention_row(r, *weights, store_row, chunk, heads),
         0,
         unroll=2,
     )
-
-
-def attention_row(r, hs_ref, x_ref, w1_ref, gain_ref, pw_ref, ow_ref, rw_ref, out_ref, chunk, heads):
+    attention_row(tile_rows, *weights, store_edge, chunk, heads)
+
+
+def attention_row(r, hs_ref, x_ref, w1_ref, gain_ref, pw_ref, ow_ref, rw_ref, store, chunk, heads):
     width = w1_ref.shape[0]
     sources = x_ref.shape[0]
     layers = jnp.concatenate([x_ref[s, r] for s in range(sources)], axis=1)
@@ -114,7 +122,7 @@
     attended = jnp.dot(ow_ref[...], mixed, preferred_element_type=jnp.float32)
     residual = (embedded + attended).astype(jnp.bfloat16)
     features = jnp.dot(rw_ref[...], residual, preferred_element_type=jnp.float32)
-    out_ref[r] = features.astype(out_ref.dtype)
+    store(r, features.astype(jnp.bfloat16))
     return 0
 
 
@@ -141,7 +149,10 @@
     scale = jnp.tile(head_scale, sub // heads).reshape(sub, 1)
     return pl.pallas_call(
         functools.partial(attention_kernel, chunk=chunk, heads=heads),
-        out_shape=jax.ShapeDtypeStruct((row_count, feat, lanes), jnp.bfloat16),
+        out_shape=(
+            jax.ShapeDtypeStruct((row_count - 1, feat, lanes), jnp.bfloat16),
+            jax.ShapeDtypeStruct((feat, lanes), jnp.bfloat16),
+        ),
     )(
         scale,
         by_source,
@@ -255,7 +266,7 @@
     by_chunk = jnp.concatenate([by_chunk, edges], axis=1)
     by_source = lax.all_to_all(by_chunk, "mem", split_axis=0, concat_axis=0, tiled=True)
     members = chunks * members_here
-    step_result = post_block(
+    step_rows, step_edges = post_block(
         by_source,
         tile_cols,
         embed_weight,
@@ -266,9 +277,9 @@
         readout_weight,
     )
     feat = readout_weight.shape[1]
-    inner = step_result[:tile_rows].reshape(tile_rows, feat, members, tile_cols)
+    inner = step_rows.reshape(tile_rows, feat, members, tile_cols)
     inner = jnp.transpose(inner, (2, 1, 0, 3))
-    outer = step_result[tile_rows].reshape(feat, members, tile_rows, 2 * halo)
+    outer = step_edges.reshape(feat, members, tile_rows, 2 * halo)
     outer = jnp.transpose(outer, (1, 0, 2, 3))
     mem_index = lax.axis_index("mem")
     left = jnp.where(mem_index > 0, outer[..., :halo], 0)

time: 64.9 us -> 64.8 us (level)
    reshape x0 -> x2, local copies, waits for them, and re-layouts: none -> 0.97 us  [on_device(): outer = step_edges.reshape(feat, members, tile_rows, 2 * halo)]
    slice x1 -> x0, local copies, waits for them, and re-layouts: 0.72 us -> none  [on_device(): outer = step_result[tile_rows].reshape(feat, members, tile_rows, 2 * halo)]
where the time goes in v16:
time: 64.8 us; the launch traced here: 63.8 us
  starting transfers between devices  16.3 us (25%)
  local copies, waits for them, and re-layouts  15 us (23%)
  waiting for transfers between devices  11.3 us (17%)
  Pallas kernels  10.3 us (16%)
  other arithmetic  5.13 us (8%)
  matrix products  5 us (8%)
  between operations  0.72 us (1%)
    pallas_call x1, Pallas kernels, post_block(): pl.pallas_call(functools.partial(attention_kernel, chunk=chunk, heads=hea...  10.3 us
    dot_general x18, matrix products, convolve(): jnp.einsum('oc,mcij->moij', kernel[row_stencil * 3 + column_stencil], shi...  5 us
    unnamed x48, local copies, waits for them, and re-layouts  4.62 us
    ppermute x1, waiting for transfers between devices, row_padded(): high = lax.ppermute(block[..., :width, :].reshape(flat), 'row', backward)  4.13 us
    ppermute x1, starting transfers between devices, row_padded(): high = lax.ppermute(block[..., :width, :].reshape(flat), 'row', backward)  4.04 us
    all_to_all x1, starting transfers between devices, on_device(): lax.all_to_all(by_chunk, 'mem', split_axis=0, concat_axis=0, tiled=True)  3.79 us
    all_to_all x1, waiting for transfers between devices, on_device(): lax.all_to_all(by_chunk, 'mem', split_axis=0, concat_axis=0, tiled=True)  3.72 us
    ppermute x1, starting transfers between devices, on_device(): lax.ppermute(pack(starting_states[:, :, row_total - state_halo:], coeffic...  3.12 us
  transfers between devices with their start and end apart: 5, of which 5 were waited for; matrix products, arithmetic and copies ran while one was open for 13% of the time, Pallas kernels for 0%

profile of v16, /device:TPU:9, one launch (start us, length us, event | category | flops | bytes accessed | tf_op | source)
XLA Modules:
  0.0 63.8 jit_solution(4991134878959197800)
XLA Ops:
  0.0 1.1 %pad_maximum_fusion.4 = f32[3,8,8,512]{3,2,1,0:T(8,128)S(1)} fusion(f32[1,8,8,512]{3,2,1,0:T(8,128)} %bitcast.200, f32[1,8,8,512]{3,2,1,0:T(8,128)} %bitcast.202, f32[1,8,8,512]{3,2,1,0:T(8,128)} %bitcast.204), kind=kLoop, calls=%fused_computation.47 | loop fusion | flops 196608 | bytes 786432 | tf_op jit(solution)/shard_map/stack | solution.py:206
  1.4 3.1 %collective-permute-start = (f32[136,512]{1,0:T(8,128)S(1)}, f32[136,512]{1,0:T(8,128)S(1)}, u32[]{:S(2)}, u32[]{:S(2)}) collective-permute-start(f32[136,512]{1,0:T(8,128)S(1)} %pad_maximum_fusion.5), channel_id=1, source_target_pairs={{0,1},{1,2},{2,3},{3,4},{4,5},{5,6},{6,7},{8,9},{9,10},{10,11},{11... | collective-permute-start | bytes 835592 | tf_op jit(solution)/shard_map/ppermute | solution.py:219
  4.8 3.1 %collective-permute-start.1 = (f32[136,512]{1,0:T(8,128)S(1)}, f32[136,512]{1,0:T(8,128)S(1)}, u32[]{:S(2)}, u32[]{:S(2)}) collective-permute-start(f32[136,512]{1,0:T(8,128)S(1)} %pad_maximum_fusion.6), channel_id=1, source_target_pairs={{1,0},{2,1},{3,2},{4,3},{5,4},{6,5},{7,6},{9,8},{10,9},{11,10},{12... | collective-permute-start | bytes 835592 | tf_op jit(solution)/shard_map/ppermute | solution.py:227
  8.5 0.7 %gather_fusion = bf16[64,3,64]{2,1,0:T(4,128)(2,1)S(1)} fusion(bf16[3,64,64]{2,0,1:T(4,128)(2,1)S(1)} %copy.46, s32[1024]{0:T(1024)S(1)} %pad_clamp_fusion), kind=kCustom, calls=%fused_computation | custom fusion | bytes 49408 | tf_op jit(solution)/shard_map/gather | solution.py:147
  9.1 0.6 copy.47
  9.8 0.6 gather_fusion.1
  10.4 0.7 %copy.48 = bf16[64,64]{0,1:T(8,128)(2,1)} copy(bf16[64,64]{1,0:T(8,128)(2,1)S(1)} %gather_fusion.1) | data formatting | bytes 16384 | tf_op jit(solution)/shard_map/gather | solution.py:148
  11.1 0.7 %copy.50.gain_ref = f32[64,1]{1,0:T(8,128)} copy(f32[64,1]{0,1:T(1,128)S(1)} %bitcast.215) | data formatting | bytes 512 | tf_op jit(solution)/shard_map/reshape | solution.py:160
  11.8 0.7 %copy.44 = bf16[8,64]{0,1:T(8,128)(2,1)} copy(bf16[8,64]{1,0:T(8,128)(2,1)S(1)} %copy-done.11) | data formatting | bytes 2048 | tf_op args[4]
  12.5 0.7 %reshape_tile.4.hs_ref = f32[8,1]{1,0:T(8,128)} reshape(f32[2,4]{1,0:T(2,128)S(1)} %tile.2) | data formatting | bytes 64 | tf_op jit(solution)/shard_map/reshape;tile | solution.py:149
  13.8 0.1 copy.102
  14.0 0.1 copy.103
  14.1 0.1 copy.104
  14.2 0.1 copy.105
  14.4 0.1 copy.106
  14.8 0.1 copy.109
  15.0 0.1 copy.111
  15.3 0.1 copy.113
  15.8 3.0 %collective-permute-done.1 = f32[136,512]{1,0:T(8,128)S(1)} collective-permute-done((f32[136,512]{1,0:T(8,128)S(1)}, f32[136,512]{1,0:T(8,128)S(1)}, u32[]{:S(2)}, u32[]{:S(2)}) %collective-permute-start.1) | collective-permute-done | bytes 278560 | tf_op jit(solution)/shard_map/ppermute | solution.py:227
  18.9 0.1 pad_maximum_fusion
  19.0 0.4 copy-done.9
  19.8 0.9 %slice.337 = f32[64,512]{1,0:T(8,128)S(1)} slice(f32[136,512]{1,0:T(8,128)} %copy-done.9), slice={[0:64], [0:512]} | slice | bytes 262144 | tf_op jit(solution)/shard_map/slice | solution.py:234
  20.9 0.5 add_select_fusion.2
  21.5 0.5 add_select_fusion.1
  22.1 0.5 add_select_fusion
  22.7 0.3 select_convert_fusion.1
  23.4 0.2 reshape.199
  23.6 0.7 %pad_maximum_fusion.8 = bf16[4,9,8,256]{3,2,1,0:T(8,128)(2,1)} fusion(bf16[4,1,8,256]{3,2,1,0:T(8,128)(2,1)S(1)} %reshape.199, bf16[4,8,8,256]{3,2,1,0:T(8,128)(2,1)S(1)} %bitcast.208), kind=kLoop, calls=%fused_computation.65 | loop fusion | flops 73728 | bytes 294912 | tf_op jit(solution)/shard_map/concatenate | solution.py:266
  24.3 3.8 %all-to-all-start = ((bf16[4,9,8,256]{3,2,1,0:T(8,128)(2,1)}), bf16[4,9,8,256]{3,2,1,0:T(8,128)(2,1)S(1)}, u32[]{:S(2)}, u32[]{:S(2)}) async-start(bf16[4,9,8,256]{3,2,1,0:T(8,128)(2,1)} %pad_maximum_fusion.8), calls=%async_computation | async-start | bytes 294912 | tf_op jit(solution)/shard_map/all_to_all | solution.py:267
  28.1 3.7 %all-to-all-done.x_ref = bf16[4,9,8,256]{3,2,1,0:T(8,128)(2,1)S(1)} async-done(((bf16[4,9,8,256]{3,2,1,0:T(8,128)(2,1)}), bf16[4,9,8,256]{3,2,1,0:T(8,128)(2,1)S(1)}, u32[]{:S(2)}, u32[]{:S(2)}) %all-to-all-start) | async-done | bytes 147488 | tf_op jit(solution)/shard_map/all_to_all | solution.py:267
  31.8 0.7 %copy-done.7 = bf16[4,9,8,256]{3,2,1,0:T(8,128)(2,1)} copy-done((bf16[4,9,8,256]{3,2,1,0:T(8,128)(2,1)}, bf16[4,9,8,256]{3,2,1,0:T(8,128)(2,1)S(1)}, u32[]{:S(2)}) %copy-start.7) | copy-done | bytes 147480
  32.5 10.3 %shard_map.118 = (bf16[8,8,1024]{2,1,0:T(8,128)(2,1)}, bf16[8,1024]{1,0:T(8,128)(2,1)}) custom-call(f32[8,1]{1,0:T(8,128)} %reshape_tile.4.hs_ref, bf16[4,9,8,256]{3,2,1,0:T(8,128)(2,1)} %copy-done.7, bf16[64,8]{1,0:T(8,128)(2,1)} %bitcast.213, f32[64,1]{1,0:T(8,128)} %copy.50.gain_ref, bf16[192,64]{1,0:T(8,128)(2,1)} %bitcast.210, ...), custom_call_target="tpu_custom_call" | custom-call | tf_op jit(solution)/shard_map/pallas_call | solution.py:150
  42.8 0.9 %reshape.208 = bf16[8,8,8,16]{3,2,1,0:T(8,128)(2,1)S(1)} reshape(bf16[8,1024]{1,0:T(8,128)(2,1)} %get-tuple-element.8) | data formatting | bytes 32768 | tf_op jit(solution)/shard_map/reshape | solution.py:282
  43.8 0.9 %copy_bitcast_fusion.2 = bf16[8,8,8,128]{3,1,2,0:T(8,128)(2,1)S(1)} fusion(bf16[8,8,1024]{2,1,0:T(8,128)(2,1)} %get-tuple-element.7), kind=kLoop, calls=%fused_computation.83 | loop fusion | bytes 262144 | tf_op jit(solution)/shard_map/transpose | solution.py:281
  44.8 0.2 pad_maximum_fusion.7
  45.1 0.3 reshape.209
  45.3 2.3 %collective-permute-start.2 = (bf16[8,8,1152]{2,1,0:T(8,128)(2,1)S(1)}, bf16[8,8,1152]{2,1,0:T(8,128)(2,1)S(1)}, u32[]{:S(2)}, u32[]{:S(2)}) collective-permute-start(bf16[8,8,1152]{2,1,0:T(8,128)(2,1)S(1)} %reshape.209), channel_id=1, source_target_pairs={{0,1},{1,2},{2,3},{3,4},{4,5},{5,6},{6,7},{8,9},{9,10},{10,11},{11... | collective-permute-start | bytes 442376 | tf_op jit(solution)/shard_map/ppermute | solution.py:34
  47.7 4.0 %collective-permute-start.3 = (bf16[8,8,1152]{2,1,0:T(8,128)(2,1)S(1)}, bf16[8,8,1152]{2,1,0:T(8,128)(2,1)S(1)}, u32[]{:S(2)}, u32[]{:S(2)}) collective-permute-start(bf16[8,8,1152]{2,1,0:T(8,128)(2,1)S(1)} %reshape.209), channel_id=1, source_target_pairs={{1,0},{2,1},{3,2},{4,3},{5,4},{6,5},{7,6},{9,8},{10,9},{11,10},{12... | collective-permute-start | bytes 442376 | tf_op jit(solution)/shard_map/ppermute | solution.py:35
  51.8 0.3 collective-permute-done.2
  52.1 0.4 reshape.210
  52.6 4.1 %collective-permute-done.3 = bf16[8,8,1152]{2,1,0:T(8,128)(2,1)S(1)} collective-permute-done((bf16[8,8,1152]{2,1,0:T(8,128)(2,1)S(1)}, bf16[8,8,1152]{2,1,0:T(8,128)(2,1)S(1)}, u32[]{:S(2)}, u32[]{:S(2)}) %collective-permute-start.3) | collective-permute-done | bytes 147488 | tf_op jit(solution)/shard_map/ppermute | solution.py:35
  56.7 0.4 reshape.211
  57.1 0.2 pad_maximum_fusion.1
  57.3 0.4 pad_maximum_fusion.3
  57.7 0.3 fusion.12
  58.0 0.4 convolution_add_fusion.7
  58.4 0.3 convolution_add_fusion.6
  58.7 0.3 convolution_add_fusion.5
  59.0 0.3 convolution_add_fusion.4
  59.4 0.4 convolution_add_fusion.3
  59.7 0.3 convolution_add_fusion.2
  60.0 0.4 convolution_add_fusion.1
  60.4 0.5 select_convert_fusion
  60.9 0.2 fusion.24
  61.1 0.2 convolution_add_fusion.15
  61.3 0.2 convolution_add_fusion.14
  61.6 0.2 convolution_add_fusion.13
  61.7 0.2 convolution_add_fusion.12
  62.0 0.2 convolution_add_fusion.11
  62.2 0.2 convolution_add_fusion.10
  62.4 0.2 convolution_add_fusion.9
  62.6 0.3 copy-done.8
  62.9 0.2 fusion.3
  63.1 0.7 %copy.76 = bf16[8,8,8,128]{3,2,1,0:T(8,128)(2,1)} copy(bf16[8,8,8,128]{3,1,2,0:T(8,128)(2,1)S(1)} %fusion.3) | data formatting | bytes 262144 | tf_op jit(solution)/shard_map/convert_element_type | solution.py:297
  (84 shorter events, 4.0 us)
Async XLA Ops:
  0.0 9.8 %copy-start = (bf16[64,64]{1,0:T(8,128)(2,1)S(1)}, bf16[64,64]{1,0:T(8,128)(2,1)}, u32[]{:S(2)}) copy-start(bf16[64,64]{1,0:T(8,128)(2,1)} %param.20) | copy-start | bytes 24580
  0.0 1.3 %copy-start.6 = (f32[2,8,8,512]{3,2,1,0:T(8,128)S(1)}, f32[2,8,8,512]{3,2,1,0:T(8,128)}, u32[]{:S(2)}) copy-start(f32[2,8,8,512]{3,2,1,0:T(8,128)} %param.12) | copy-start | bytes 786436
  1.3 6.7 %copy-start.1 = (bf16[9,8,8]{0,2,1:T(8,128)(2,1)S(1)}, bf16[9,8,8]{0,2,1:T(8,128)(2,1)}, u32[]{:S(2)}) copy-start(bf16[9,8,8]{0,2,1:T(8,128)(2,1)} %param.22) | copy-start | bytes 3460
  1.4 6.7 %copy-start.2 = (bf16[9,8,8]{0,2,1:T(8,128)(2,1)S(1)}, bf16[9,8,8]{0,2,1:T(8,128)(2,1)}, u32[]{:S(2)}) copy-start(bf16[9,8,8]{0,2,1:T(8,128)(2,1)} %param.23) | copy-start | bytes 3460
  1.4 6.9 %copy-start.10 = (bf16[64,192]{1,0:T(8,128)(2,1)S(1)}, bf16[64,192]{1,0:T(8,128)(2,1)}, u32[]{:S(2)}) copy-start(bf16[64,192]{1,0:T(8,128)(2,1)} %param.18) | copy-start | bytes 73732
  1.4 14.3 %collective-permute-start = (f32[136,512]{1,0:T(8,128)S(1)}, f32[136,512]{1,0:T(8,128)S(1)}, u32[]{:S(2)}, u32[]{:S(2)}) collective-permute-start(f32[136,512]{1,0:T(8,128)S(1)} %pad_maximum_fusion.5), channel_id=1, source_target_pairs={{0,1},{1,2},{2,3},{3,4},{4,5},{5,6},{6,7},{8,9},{9,10},{10,11},{11... | collective-permute-start | bytes 835592 | tf_op jit(solution)/shard_map/ppermute | solution.py:219
  4.7 6.4 %copy-start.12 = (f32[64]{0:T(128)S(1)}, f32[64]{0:T(128)}, u32[]{:S(2)}) copy-start(f32[64]{0:T(128)} %param.17) | copy-start | bytes 772
  4.7 7.1 %copy-start.11 = (bf16[8,64]{1,0:T(8,128)(2,1)S(1)}, bf16[8,64]{1,0:T(8,128)(2,1)}, u32[]{:S(2)}) copy-start(bf16[8,64]{1,0:T(8,128)(2,1)} %param.16) | copy-start | bytes 3076
  4.7 7.8 %copy-start.13 = (f32[4]{0:T(128)S(1)}, f32[4]{0:T(128)}, u32[]{:S(2)}) copy-start(f32[4]{0:T(128)} %param.19) | copy-start | bytes 52
  4.8 14.0 %collective-permute-start.1 = (f32[136,512]{1,0:T(8,128)S(1)}, f32[136,512]{1,0:T(8,128)S(1)}, u32[]{:S(2)}, u32[]{:S(2)}) collective-permute-start(f32[136,512]{1,0:T(8,128)S(1)} %pad_maximum_fusion.6), channel_id=1, source_target_pairs={{1,0},{2,1},{3,2},{4,3},{5,4},{6,5},{7,6},{9,8},{10,9},{11,10},{12... | collective-permute-start | bytes 835592 | tf_op jit(solution)/shard_map/ppermute | solution.py:227
  8.4 10.4 %copy-start.3 = (f32[8,8,512]{2,1,0:T(8,128)S(1)}, f32[8,8,512]{2,1,0:T(8,128)}, u32[]{:S(2)}) copy-start(f32[8,8,512]{2,1,0:T(8,128)} %param.15) | copy-start | bytes 393220
  8.5 10.4 %copy-start.4 = (f32[8,8,512]{2,1,0:T(8,128)S(1)}, f32[8,8,512]{2,1,0:T(8,128)}, u32[]{:S(2)}) copy-start(f32[8,8,512]{2,1,0:T(8,128)} %param.14) | copy-start | bytes 393220
  8.5 10.4 %copy-start.5 = (f32[8,8,512]{2,1,0:T(8,128)S(1)}, f32[8,8,512]{2,1,0:T(8,128)}, u32[]{:S(2)}) copy-start(f32[8,8,512]{2,1,0:T(8,128)} %param.13) | copy-start | bytes 393220
  18.8 0.7 %copy-start.9 = (f32[136,512]{1,0:T(8,128)}, f32[136,512]{1,0:T(8,128)S(1)}, u32[]{:S(2)}) copy-start(f32[136,512]{1,0:T(8,128)S(1)} %collective-permute-done.1) | copy-start | bytes 835588
  24.3 7.5 %all-to-all-start = ((bf16[4,9,8,256]{3,2,1,0:T(8,128)(2,1)}), bf16[4,9,8,256]{3,2,1,0:T(8,128)(2,1)S(1)}, u32[]{:S(2)}, u32[]{:S(2)}) async-start(bf16[4,9,8,256]{3,2,1,0:T(8,128)(2,1)} %pad_maximum_fusion.8), calls=%async_computation | async-start | bytes 294912 | tf_op jit(solution)/shard_map/all_to_all | solution.py:267
  31.8 0.7 %copy-start.7 = (bf16[4,9,8,256]{3,2,1,0:T(8,128)(2,1)}, bf16[4,9,8,256]{3,2,1,0:T(8,128)(2,1)S(1)}, u32[]{:S(2)}) copy-start(bf16[4,9,8,256]{3,2,1,0:T(8,128)(2,1)S(1)} %all-to-all-done.x_ref) | copy-start | bytes 442372
  45.3 6.8 %collective-permute-start.2 = (bf16[8,8,1152]{2,1,0:T(8,128)(2,1)S(1)}, bf16[8,8,1152]{2,1,0:T(8,128)(2,1)S(1)}, u32[]{:S(2)}, u32[]{:S(2)}) collective-permute-start(bf16[8,8,1152]{2,1,0:T(8,128)(2,1)S(1)} %reshape.209), channel_id=1, source_target_pairs={{0,1},{1,2},{2,3},{3,4},{4,5},{5,6},{6,7},{8,9},{9,10},{10,11},{11... | collective-permute-start | bytes 442376 | tf_op jit(solution)/shard_map/ppermute | solution.py:34
  47.7 9.0 %collective-permute-start.3 = (bf16[8,8,1152]{2,1,0:T(8,128)(2,1)S(1)}, bf16[8,8,1152]{2,1,0:T(8,128)(2,1)S(1)}, u32[]{:S(2)}, u32[]{:S(2)}) collective-permute-start(bf16[8,8,1152]{2,1,0:T(8,128)(2,1)S(1)} %reshape.209), channel_id=1, source_target_pairs={{1,0},{2,1},{3,2},{4,3},{5,4},{6,5},{7,6},{9,8},{10,9},{11,10},{12... | collective-permute-start | bytes 442376 | tf_op jit(solution)/shard_map/ppermute | solution.py:35
  62.0 0.9 %copy-start.8 = (bf16[8,8,1024]{2,1,0:T(8,128)(2,1)S(1)}, bf16[8,8,1024]{2,1,0:T(8,128)(2,1)}, u32[]{:S(2)}) copy-start(bf16[8,8,1024]{2,1,0:T(8,128)(2,1)} %get-tuple-element.7) | copy-start | bytes 393220

commit v17 on v10

--- a/solution.py
+++ b/solution.py
@@ -73,6 +73,7 @@
             r, hs_ref, x_ref, w1_ref, gain_ref, pw_ref, ow_ref, rw_ref, out_ref, chunk, heads
         ),
         0,
+        unroll=3,
     )
 
 

time: 65.5 us -> 64.8 us (0.989)
  Pallas kernels: 11 us -> 10.3 us
    pallas_call x1, Pallas kernels: 11 us -> 10.3 us  [post_block(): pl.pallas_call(functools.partial(attention_kernel, chunk=chunk, heads=hea...]
where the time goes in v17:
time: 64.8 us; the launch traced here: 63.8 us
  starting transfers between devices  16.3 us (25%)
  local copies, waits for them, and re-layouts  15 us (23%)
  waiting for transfers between devices  11.3 us (17%)
  Pallas kernels  10.3 us (16%)
  other arithmetic  5.14 us (8%)
  matrix products  5.01 us (8%)
  between operations  0.72 us (1%)
    pallas_call x1, Pallas kernels, post_block(): pl.pallas_call(functools.partial(attention_kernel, chunk=chunk, heads=hea...  10.3 us
    dot_general x18, matrix products, convolve(): jnp.einsum('oc,mcij->moij', kernel[row_stencil * 3 + column_stencil], shi...  5.01 us
    unnamed x48, local copies, waits for them, and re-layouts  4.65 us
    ppermute x1, waiting for transfers between devices, row_padded(): high = lax.ppermute(block[..., :width, :].reshape(flat), 'row', backward)  4.13 us
    ppermute x1, starting transfers between devices, row_padded(): high = lax.ppermute(block[..., :width, :].reshape(flat), 'row', backward)  4.04 us
    all_to_all x1, starting transfers between devices, on_device(): lax.all_to_all(by_chunk, 'mem', split_axis=0, concat_axis=0, tiled=True)  3.79 us
    all_to_all x1, waiting for transfers between devices, on_device(): lax.all_to_all(by_chunk, 'mem', split_axis=0, concat_axis=0, tiled=True)  3.72 us
    ppermute x1, starting transfers between devices, on_device(): lax.ppermute(pack(starting_states[:, :, row_total - state_halo:], coeffic...  3.12 us
  transfers between devices with their start and end apart: 5, of which 5 were waited for; matrix products, arithmetic and copies ran while one was open for 13% of the time, Pallas kernels for 0%

profile of v17, /device:TPU:9, one launch (start us, length us, event | category | flops | bytes accessed | tf_op | source)
XLA Modules:
  0.0 63.8 jit_solution(8461573474876262574)
XLA Ops:
  0.0 1.1 %pad_maximum_fusion.4 = f32[3,8,8,512]{3,2,1,0:T(8,128)S(1)} fusion(f32[1,8,8,512]{3,2,1,0:T(8,128)} %bitcast.199, f32[1,8,8,512]{3,2,1,0:T(8,128)} %bitcast.201, f32[1,8,8,512]{3,2,1,0:T(8,128)} %bitcast.203), kind=kLoop, calls=%fused_computation.47 | loop fusion | flops 196608 | bytes 786432 | tf_op jit(solution)/shard_map/stack | solution.py:195
  1.4 3.1 %collective-permute-start = (f32[136,512]{1,0:T(8,128)S(1)}, f32[136,512]{1,0:T(8,128)S(1)}, u32[]{:S(2)}, u32[]{:S(2)}) collective-permute-start(f32[136,512]{1,0:T(8,128)S(1)} %pad_maximum_fusion.5), channel_id=1, source_target_pairs={{0,1},{1,2},{2,3},{3,4},{4,5},{5,6},{6,7},{8,9},{9,10},{10,11},{11... | collective-permute-start | bytes 835592 | tf_op jit(solution)/shard_map/ppermute | solution.py:208
  4.8 3.1 %collective-permute-start.1 = (f32[136,512]{1,0:T(8,128)S(1)}, f32[136,512]{1,0:T(8,128)S(1)}, u32[]{:S(2)}, u32[]{:S(2)}) collective-permute-start(f32[136,512]{1,0:T(8,128)S(1)} %pad_maximum_fusion.6), channel_id=1, source_target_pairs={{1,0},{2,1},{3,2},{4,3},{5,4},{6,5},{7,6},{9,8},{10,9},{11,10},{12... | collective-permute-start | bytes 835592 | tf_op jit(solution)/shard_map/ppermute | solution.py:216
  8.5 0.7 %gather_fusion = bf16[64,3,64]{2,1,0:T(4,128)(2,1)S(1)} fusion(bf16[3,64,64]{2,0,1:T(4,128)(2,1)S(1)} %copy.46, s32[1024]{0:T(1024)S(1)} %pad_clamp_fusion), kind=kCustom, calls=%fused_computation | custom fusion | bytes 49408 | tf_op jit(solution)/shard_map/gather | solution.py:139
  9.1 0.6 copy.47
  9.8 0.6 gather_fusion.1
  10.4 0.7 %copy.48 = bf16[64,64]{0,1:T(8,128)(2,1)} copy(bf16[64,64]{1,0:T(8,128)(2,1)S(1)} %gather_fusion.1) | data formatting | bytes 16384 | tf_op jit(solution)/shard_map/gather | solution.py:140
  11.1 0.7 %copy.50.gain_ref = f32[64,1]{1,0:T(8,128)} copy(f32[64,1]{0,1:T(1,128)S(1)} %bitcast.214) | data formatting | bytes 512 | tf_op jit(solution)/shard_map/reshape | solution.py:149
  11.8 0.7 %copy.44 = bf16[8,64]{0,1:T(8,128)(2,1)} copy(bf16[8,64]{1,0:T(8,128)(2,1)S(1)} %copy-done.11) | data formatting | bytes 2048 | tf_op args[4]
  12.5 0.7 %reshape_tile.4.hs_ref = f32[8,1]{1,0:T(8,128)} reshape(f32[2,4]{1,0:T(2,128)S(1)} %tile.2) | data formatting | bytes 64 | tf_op jit(solution)/shard_map/reshape;tile | solution.py:141
  13.8 0.1 copy.102
  13.9 0.1 copy.103
  14.1 0.1 copy.104
  14.2 0.1 copy.105
  14.3 0.1 copy.106
  14.6 0.1 copy.108
  14.9 0.1 copy.110
  15.8 3.0 %collective-permute-done.1 = f32[136,512]{1,0:T(8,128)S(1)} collective-permute-done((f32[136,512]{1,0:T(8,128)S(1)}, f32[136,512]{1,0:T(8,128)S(1)}, u32[]{:S(2)}, u32[]{:S(2)}) %collective-permute-start.1) | collective-permute-done | bytes 278560 | tf_op jit(solution)/shard_map/ppermute | solution.py:216
  18.9 0.1 pad_maximum_fusion
  19.0 0.5 copy-done.9
  19.8 0.9 %slice.345 = f32[64,512]{1,0:T(8,128)S(1)} slice(f32[136,512]{1,0:T(8,128)} %copy-done.9), slice={[0:64], [0:512]} | slice | bytes 262144 | tf_op jit(solution)/shard_map/slice | solution.py:223
  21.0 0.5 add_select_fusion.2
  21.6 0.5 add_select_fusion.1
  22.2 0.5 add_select_fusion
  22.7 0.3 select_convert_fusion.1
  23.4 0.2 reshape.196
  23.6 0.7 %pad_maximum_fusion.8 = bf16[4,9,8,256]{3,2,1,0:T(8,128)(2,1)} fusion(bf16[4,1,8,256]{3,2,1,0:T(8,128)(2,1)S(1)} %reshape.196, bf16[4,8,8,256]{3,2,1,0:T(8,128)(2,1)S(1)} %bitcast.207), kind=kLoop, calls=%fused_computation.65 | loop fusion | flops 73728 | bytes 294912 | tf_op jit(solution)/shard_map/concatenate | solution.py:255
  24.3 3.8 %all-to-all-start = ((bf16[4,9,8,256]{3,2,1,0:T(8,128)(2,1)}), bf16[4,9,8,256]{3,2,1,0:T(8,128)(2,1)S(1)}, u32[]{:S(2)}, u32[]{:S(2)}) async-start(bf16[4,9,8,256]{3,2,1,0:T(8,128)(2,1)} %pad_maximum_fusion.8), calls=%async_computation | async-start | bytes 294912 | tf_op jit(solution)/shard_map/all_to_all | solution.py:256
  28.1 3.7 %all-to-all-done.x_ref = bf16[4,9,8,256]{3,2,1,0:T(8,128)(2,1)S(1)} async-done(((bf16[4,9,8,256]{3,2,1,0:T(8,128)(2,1)}), bf16[4,9,8,256]{3,2,1,0:T(8,128)(2,1)S(1)}, u32[]{:S(2)}, u32[]{:S(2)}) %all-to-all-start) | async-done | bytes 147488 | tf_op jit(solution)/shard_map/all_to_all | solution.py:256
  31.8 0.7 %copy-done.8 = bf16[4,9,8,256]{3,2,1,0:T(8,128)(2,1)} copy-done((bf16[4,9,8,256]{3,2,1,0:T(8,128)(2,1)}, bf16[4,9,8,256]{3,2,1,0:T(8,128)(2,1)S(1)}, u32[]{:S(2)}) %copy-start.8) | copy-done | bytes 147480
  32.5 10.3 %shard_map.118 = bf16[9,8,1024]{2,1,0:T(8,128)(2,1)} custom-call(f32[8,1]{1,0:T(8,128)} %reshape_tile.4.hs_ref, bf16[4,9,8,256]{3,2,1,0:T(8,128)(2,1)} %copy-done.8, bf16[64,8]{1,0:T(8,128)(2,1)} %bitcast.212, f32[64,1]{1,0:T(8,128)} %copy.50.gain_ref, bf16[192,64]{1,0:T(8,128)(2,1)} %bitcast.209, bf16[64,64]{1,0:T(8,128)(2,1)} %bitcast.211, ...), custom_call_target="tpu_custom_call" | custom-call | tf_op jit(solution)/shard_map/pallas_call | solution.py:142
  42.8 0.7 %slice.372 = bf16[1,8,1024]{2,1,0:T(8,128)(2,1)S(1)} slice(bf16[9,8,1024]{2,1,0:T(8,128)(2,1)} %shard_map.118), slice={[8:9], [0:8], [0:1024]} | slice | bytes 32768 | tf_op jit(solution)/shard_map/slice | solution.py:271
  43.5 0.9 %copy_bitcast_fusion.2 = bf16[8,8,8,128]{3,1,2,0:T(8,128)(2,1)S(1)} fusion(bf16[9,8,1024]{2,1,0:T(8,128)(2,1)} %shard_map.118), kind=kLoop, calls=%fused_computation.84 | loop fusion | bytes 262144 | tf_op jit(solution)/shard_map/transpose | solution.py:270
  44.4 0.1 reshape_squeeze.3
  44.8 0.2 pad_maximum_fusion.7
  45.1 0.3 reshape.205
  45.3 2.3 %collective-permute-start.2 = (bf16[8,8,1152]{2,1,0:T(8,128)(2,1)S(1)}, bf16[8,8,1152]{2,1,0:T(8,128)(2,1)S(1)}, u32[]{:S(2)}, u32[]{:S(2)}) collective-permute-start(bf16[8,8,1152]{2,1,0:T(8,128)(2,1)S(1)} %reshape.205), channel_id=1, source_target_pairs={{0,1},{1,2},{2,3},{3,4},{4,5},{5,6},{6,7},{8,9},{9,10},{10,11},{11... | collective-permute-start | bytes 442376 | tf_op jit(solution)/shard_map/ppermute | solution.py:34
  47.6 4.0 %collective-permute-start.3 = (bf16[8,8,1152]{2,1,0:T(8,128)(2,1)S(1)}, bf16[8,8,1152]{2,1,0:T(8,128)(2,1)S(1)}, u32[]{:S(2)}, u32[]{:S(2)}) collective-permute-start(bf16[8,8,1152]{2,1,0:T(8,128)(2,1)S(1)} %reshape.205), channel_id=1, source_target_pairs={{1,0},{2,1},{3,2},{4,3},{5,4},{6,5},{7,6},{9,8},{10,9},{11,10},{12... | collective-permute-start | bytes 442376 | tf_op jit(solution)/shard_map/ppermute | solution.py:35
  51.8 0.3 collective-permute-done.2
  52.1 0.4 reshape.206
  52.5 4.1 %collective-permute-done.3 = bf16[8,8,1152]{2,1,0:T(8,128)(2,1)S(1)} collective-permute-done((bf16[8,8,1152]{2,1,0:T(8,128)(2,1)S(1)}, bf16[8,8,1152]{2,1,0:T(8,128)(2,1)S(1)}, u32[]{:S(2)}, u32[]{:S(2)}) %collective-permute-start.3) | collective-permute-done | bytes 147488 | tf_op jit(solution)/shard_map/ppermute | solution.py:35
  56.7 0.4 reshape.207
  57.1 0.2 pad_maximum_fusion.1
  57.3 0.4 pad_maximum_fusion.3
  57.7 0.3 fusion.12
  58.0 0.4 convolution_add_fusion.7
  58.4 0.4 convolution_add_fusion.6
  58.7 0.3 convolution_add_fusion.5
  59.0 0.4 convolution_add_fusion.4
  59.4 0.4 convolution_add_fusion.3
  59.7 0.3 convolution_add_fusion.2
  60.0 0.3 convolution_add_fusion.1
  60.4 0.5 select_convert_fusion
  60.9 0.2 fusion.24
  61.1 0.2 convolution_add_fusion.15
  61.3 0.2 convolution_add_fusion.14
  61.6 0.2 convolution_add_fusion.13
  61.7 0.2 convolution_add_fusion.12
  62.0 0.2 convolution_add_fusion.11
  62.2 0.2 convolution_add_fusion.10
  62.4 0.2 convolution_add_fusion.9
  62.6 0.3 copy-done.3
  62.9 0.2 fusion.3
  63.1 0.7 %copy.76 = bf16[8,8,8,128]{3,2,1,0:T(8,128)(2,1)} copy(bf16[8,8,8,128]{3,1,2,0:T(8,128)(2,1)S(1)} %fusion.3) | data formatting | bytes 262144 | tf_op jit(solution)/shard_map/convert_element_type | solution.py:286
  (85 shorter events, 4.1 us)
Async XLA Ops:
  0.0 9.8 %copy-start = (bf16[64,64]{1,0:T(8,128)(2,1)S(1)}, bf16[64,64]{1,0:T(8,128)(2,1)}, u32[]{:S(2)}) copy-start(bf16[64,64]{1,0:T(8,128)(2,1)} %param.20) | copy-start | bytes 24580
  0.0 1.3 %copy-start.7 = (f32[2,8,8,512]{3,2,1,0:T(8,128)S(1)}, f32[2,8,8,512]{3,2,1,0:T(8,128)}, u32[]{:S(2)}) copy-start(f32[2,8,8,512]{3,2,1,0:T(8,128)} %param.12) | copy-start | bytes 786436
  1.3 6.7 %copy-start.1 = (bf16[9,8,8]{0,2,1:T(8,128)(2,1)S(1)}, bf16[9,8,8]{0,2,1:T(8,128)(2,1)}, u32[]{:S(2)}) copy-start(bf16[9,8,8]{0,2,1:T(8,128)(2,1)} %param.22) | copy-start | bytes 3460
  1.4 6.7 %copy-start.2 = (bf16[9,8,8]{0,2,1:T(8,128)(2,1)S(1)}, bf16[9,8,8]{0,2,1:T(8,128)(2,1)}, u32[]{:S(2)}) copy-start(bf16[9,8,8]{0,2,1:T(8,128)(2,1)} %param.23) | copy-start | bytes 3460
  1.4 6.9 %copy-start.10 = (bf16[64,192]{1,0:T(8,128)(2,1)S(1)}, bf16[64,192]{1,0:T(8,128)(2,1)}, u32[]{:S(2)}) copy-start(bf16[64,192]{1,0:T(8,128)(2,1)} %param.18) | copy-start | bytes 73732
  1.4 14.3 %collective-permute-start = (f32[136,512]{1,0:T(8,128)S(1)}, f32[136,512]{1,0:T(8,128)S(1)}, u32[]{:S(2)}, u32[]{:S(2)}) collective-permute-start(f32[136,512]{1,0:T(8,128)S(1)} %pad_maximum_fusion.5), channel_id=1, source_target_pairs={{0,1},{1,2},{2,3},{3,4},{4,5},{5,6},{6,7},{8,9},{9,10},{10,11},{11... | collective-permute-start | bytes 835592 | tf_op jit(solution)/shard_map/ppermute | solution.py:208
  4.7 6.4 %copy-start.12 = (f32[64]{0:T(128)S(1)}, f32[64]{0:T(128)}, u32[]{:S(2)}) copy-start(f32[64]{0:T(128)} %param.17) | copy-start | bytes 772
  4.7 7.1 %copy-start.11 = (bf16[8,64]{1,0:T(8,128)(2,1)S(1)}, bf16[8,64]{1,0:T(8,128)(2,1)}, u32[]{:S(2)}) copy-start(bf16[8,64]{1,0:T(8,128)(2,1)} %param.16) | copy-start | bytes 3076
  4.7 7.8 %copy-start.13 = (f32[4]{0:T(128)S(1)}, f32[4]{0:T(128)}, u32[]{:S(2)}) copy-start(f32[4]{0:T(128)} %param.19) | copy-start | bytes 52
  4.8 14.0 %collective-permute-start.1 = (f32[136,512]{1,0:T(8,128)S(1)}, f32[136,512]{1,0:T(8,128)S(1)}, u32[]{:S(2)}, u32[]{:S(2)}) collective-permute-start(f32[136,512]{1,0:T(8,128)S(1)} %pad_maximum_fusion.6), channel_id=1, source_target_pairs={{1,0},{2,1},{3,2},{4,3},{5,4},{6,5},{7,6},{9,8},{10,9},{11,10},{12... | collective-permute-start | bytes 835592 | tf_op jit(solution)/shard_map/ppermute | solution.py:216
  8.4 10.4 %copy-start.4 = (f32[8,8,512]{2,1,0:T(8,128)S(1)}, f32[8,8,512]{2,1,0:T(8,128)}, u32[]{:S(2)}) copy-start(f32[8,8,512]{2,1,0:T(8,128)} %param.15) | copy-start | bytes 393220
  8.5 10.4 %copy-start.5 = (f32[8,8,512]{2,1,0:T(8,128)S(1)}, f32[8,8,512]{2,1,0:T(8,128)}, u32[]{:S(2)}) copy-start(f32[8,8,512]{2,1,0:T(8,128)} %param.14) | copy-start | bytes 393220
  8.5 10.4 %copy-start.6 = (f32[8,8,512]{2,1,0:T(8,128)S(1)}, f32[8,8,512]{2,1,0:T(8,128)}, u32[]{:S(2)}) copy-start(f32[8,8,512]{2,1,0:T(8,128)} %param.13) | copy-start | bytes 393220
  18.8 0.7 %copy-start.9 = (f32[136,512]{1,0:T(8,128)}, f32[136,512]{1,0:T(8,128)S(1)}, u32[]{:S(2)}) copy-start(f32[136,512]{1,0:T(8,128)S(1)} %collective-permute-done.1) | copy-start | bytes 835588
  24.3 7.5 %all-to-all-start = ((bf16[4,9,8,256]{3,2,1,0:T(8,128)(2,1)}), bf16[4,9,8,256]{3,2,1,0:T(8,128)(2,1)S(1)}, u32[]{:S(2)}, u32[]{:S(2)}) async-start(bf16[4,9,8,256]{3,2,1,0:T(8,128)(2,1)} %pad_maximum_fusion.8), calls=%async_computation | async-start | bytes 294912 | tf_op jit(solution)/shard_map/all_to_all | solution.py:256
  31.8 0.7 %copy-start.8 = (bf16[4,9,8,256]{3,2,1,0:T(8,128)(2,1)}, bf16[4,9,8,256]{3,2,1,0:T(8,128)(2,1)S(1)}, u32[]{:S(2)}) copy-start(bf16[4,9,8,256]{3,2,1,0:T(8,128)(2,1)S(1)} %all-to-all-done.x_ref) | copy-start | bytes 442372
  45.3 6.8 %collective-permute-start.2 = (bf16[8,8,1152]{2,1,0:T(8,128)(2,1)S(1)}, bf16[8,8,1152]{2,1,0:T(8,128)(2,1)S(1)}, u32[]{:S(2)}, u32[]{:S(2)}) collective-permute-start(bf16[8,8,1152]{2,1,0:T(8,128)(2,1)S(1)} %reshape.205), channel_id=1, source_target_pairs={{0,1},{1,2},{2,3},{3,4},{4,5},{5,6},{6,7},{8,9},{9,10},{10,11},{11... | collective-permute-start | bytes 442376 | tf_op jit(solution)/shard_map/ppermute | solution.py:34
  47.6 9.0 %collective-permute-start.3 = (bf16[8,8,1152]{2,1,0:T(8,128)(2,1)S(1)}, bf16[8,8,1152]{2,1,0:T(8,128)(2,1)S(1)}, u32[]{:S(2)}, u32[]{:S(2)}) collective-permute-start(bf16[8,8,1152]{2,1,0:T(8,128)(2,1)S(1)} %reshape.205), channel_id=1, source_target_pairs={{1,0},{2,1},{3,2},{4,3},{5,4},{6,5},{7,6},{9,8},{10,9},{11,10},{12... | collective-permute-start | bytes 442376 | tf_op jit(solution)/shard_map/ppermute | solution.py:35
  62.0 0.9 %copy-start.3 = (bf16[9,8,1024]{2,1,0:T(8,128)(2,1)S(1)}, bf16[9,8,1024]{2,1,0:T(8,128)(2,1)}, u32[]{:S(2)}) copy-start(bf16[9,8,1024]{2,1,0:T(8,128)(2,1)} %shard_map.118) | copy-start | bytes 442372

commit v18 on v15

--- a/solution.py
+++ b/solution.py
@@ -154,26 +154,18 @@
 
 
 def convolve(padded_field, kernel):
-    row_total = padded_field.shape[2] - 2 * DILATION_SPAN
-    column_total = padded_field.shape[3] - 2 * DILATION_SPAN
-    summed = jnp.zeros(
-        (padded_field.shape[0], kernel.shape[1], row_total, column_total), jnp.float32
-    )
-    for row_stencil in range(3):
-        for column_stencil in range(3):
-            shifted_field = padded_field[
-                :,
-                :,
-                row_stencil * DILATION_SPAN : row_stencil * DILATION_SPAN + row_total,
-                column_stencil * DILATION_SPAN : column_stencil * DILATION_SPAN + column_total,
-            ]
-            summed = summed + jnp.einsum(
-                "oc,mcij->moij",
-                kernel[row_stencil * 3 + column_stencil],
-                shifted_field,
-                preferred_element_type=jnp.float32,
-            )
-    return summed
+    taps, outputs, inputs = kernel.shape
+    side = int(round(taps**0.5))
+    weights = jnp.transpose(kernel.reshape(side, side, outputs, inputs), (2, 3, 0, 1))
+    return lax.conv_general_dilated(
+        padded_field,
+        weights,
+        window_strides=(1, 1),
+        padding="VALID",
+        rhs_dilation=(DILATION_SPAN, DILATION_SPAN),
+        dimension_numbers=("NCHW", "OIHW", "NCHW"),
+        preferred_element_type=jnp.float32,
+    )
 
 
 def on_device(

time: 64.9 us -> 90.9 us (1.40)
  matrix products: 5.01 us -> 20.2 us
  local copies, waits for them, and re-layouts: 15 us -> 23 us
  waiting for transfers between devices: 11.3 us -> 13.8 us
    conv_general_dilated x0 -> x2, matrix products: none -> 20.2 us  [convolve(): lax.conv_general_dilated(padded_field, weights, window_strides=(1, 1), pa...]
    concatenate x1, local copies, waits for them, and re-layouts: 0.05 us -> 7.09 us  [row_padded(): jnp.concatenate([low.reshape(shape), block, high.reshape(shape)], axis=-2)]
    dot_general x18 -> x0, matrix products: 5.01 us -> none  [convolve(): jnp.einsum('oc,mcij->moij', kernel[row_stencil * 3 + column_stencil], shi...]
    conv_general_dilated x0 -> x1, local copies, waits for them, and re-layouts: none -> 3.32 us  [convolve(): lax.conv_general_dilated(padded_field, weights, window_strides=(1, 1), pa...]
    ppermute x1, waiting for transfers between devices: 0.09 us -> 2.56 us  [on_device(): lax.ppermute(pack(starting_states[:, :, row_total - state_halo:], coeffic...]
    unnamed x48 -> x30, local copies, waits for them, and re-layouts: 4.65 us -> 2.2 us
    slice x1, local copies, waits for them, and re-layouts: 0.04 us -> 1.08 us  [on_device(): starting_states[:, :, row_total - state_halo:]]
    reshape x0 -> x2, local copies, waits for them, and re-layouts: none -> 1 us  [on_device(): inner = step_result[:tile_rows].reshape(tile_rows, feat, members, tile_cols)]
  transfers between devices with their start and end apart: 5 -> 5, of which waited for: 5 -> 5; matrix products, arithmetic and copies ran while one was open for 13% -> 7% of each run, Pallas kernels for 0% -> 0%
where the time goes in v18:
time: 90.9 us; the launch traced here: 89.9 us
  local copies, waits for them, and re-layouts  23 us (25%)
  matrix products  20.2 us (22%)
  starting transfers between devices  16.3 us (18%)
  waiting for transfers between devices  13.8 us (15%)
  Pallas kernels  10.4 us (11%)
  other arithmetic  5.63 us (6%)
    conv_general_dilated x2, matrix products, convolve(): lax.conv_general_dilated(padded_field, weights, window_strides=(1, 1), pa...  20.2 us
    pallas_call x1, Pallas kernels, post_block(): pl.pallas_call(functools.partial(attention_kernel, chunk=chunk, heads=hea...  10.4 us
    concatenate x1, local copies, waits for them, and re-layouts, row_padded(): jnp.concatenate([low.reshape(shape), block, high.reshape(shape)], axis=-2)  7.09 us
    ppermute x1, waiting for transfers between devices, row_padded(): high = lax.ppermute(block[..., :width, :].reshape(flat), 'row', backward)  4.19 us
    ppermute x1, starting transfers between devices, row_padded(): high = lax.ppermute(block[..., :width, :].reshape(flat), 'row', backward)  4.05 us
    all_to_all x1, starting transfers between devices, on_device(): lax.all_to_all(by_chunk, 'mem', split_axis=0, concat_axis=0, tiled=True)  3.79 us
    all_to_all x1, waiting for transfers between devices, on_device(): lax.all_to_all(by_chunk, 'mem', split_axis=0, concat_axis=0, tiled=True)  3.72 us
    conv_general_dilated x1, local copies, waits for them, and re-layouts, convolve(): lax.conv_general_dilated(padded_field, weights, window_strides=(1, 1), pa...  3.32 us
  transfers between devices with their start and end apart: 5, of which 5 were waited for; matrix products, arithmetic and copies ran while one was open for 7% of the time, Pallas kernels for 0%

profile of v18, /device:TPU:9, one launch (start us, length us, event | category | flops | bytes accessed | tf_op | source)
XLA Modules:
  0.0 89.9 jit_solution(3006232164261021896)
XLA Ops:
  0.1 1.2 %pad_maximum_fusion.3 = f32[3,8,8,512]{3,2,1,0:T(8,128)S(1)} fusion(f32[1,8,8,512]{3,2,1,0:T(8,128)} %bitcast.75, f32[1,8,8,512]{3,2,1,0:T(8,128)} %bitcast.77, f32[1,8,8,512]{3,2,1,0:T(8,128)} %bitcast.79), kind=kLoop, calls=%fused_computation.16 | loop fusion | flops 196608 | bytes 786432 | tf_op jit(solution)/shard_map/stack | solution.py:187
  1.3 0.1 fusion.6
  1.4 0.1 reshape.191
  1.5 1.1 %fusion.7 = (f32[2,8,4,512]{3,2,1,0:T(4,128)S(1)}, f32[2,8,4,512]{3,2,1,0:T(4,128)S(1)}) fusion(f32[2,8,8,512]{3,2,1,0:T(8,128)} %param.12), kind=kLoop, calls=%fused_computation.60 | loop fusion | bytes 524288 | tf_op jit(solution)/shard_map/slice | solution.py:202
  2.6 3.1 %collective-permute-start = (f32[136,512]{1,0:T(8,128)S(1)}, f32[136,512]{1,0:T(8,128)S(1)}, u32[]{:S(2)}, u32[]{:S(2)}) collective-permute-start(f32[136,512]{1,0:T(8,128)S(1)} %pad_maximum_fusion.4), channel_id=1, source_target_pairs={{0,1},{1,2},{2,3},{3,4},{4,5},{5,6},{6,7},{8,9},{9,10},{10,11},{11... | collective-permute-start | bytes 835592 | tf_op jit(solution)/shard_map/ppermute | solution.py:200
  5.8 0.1 reshape.194
  5.9 3.1 %collective-permute-start.1 = (f32[136,512]{1,0:T(8,128)S(1)}, f32[136,512]{1,0:T(8,128)S(1)}, u32[]{:S(2)}, u32[]{:S(2)}) collective-permute-start(f32[136,512]{1,0:T(8,128)S(1)} %pad_maximum_fusion.5), channel_id=1, source_target_pairs={{1,0},{2,1},{3,2},{4,3},{5,4},{6,5},{7,6},{9,8},{10,9},{11,10},{12... | collective-permute-start | bytes 835592 | tf_op jit(solution)/shard_map/ppermute | solution.py:208
  9.1 0.1 reshape.208
  9.2 0.1 copy.61
  9.4 0.7 gather_fusion
  10.0 0.6 copy.63
  10.7 0.6 gather_fusion.1
  11.3 0.7 copy.64
  12.0 0.7 copy.66.gain_ref
  12.7 0.7 copy.60
  13.4 0.7 reshape_tile.4.hs_ref
  14.0 0.1 copy.69
  14.2 0.1 copy.71
  14.3 2.6 %collective-permute-done = f32[136,512]{1,0:T(8,128)S(1)} collective-permute-done((f32[136,512]{1,0:T(8,128)S(1)}, f32[136,512]{1,0:T(8,128)S(1)}, u32[]{:S(2)}, u32[]{:S(2)}) %collective-permute-start) | collective-permute-done | bytes 278560 | tf_op jit(solution)/shard_map/ppermute | solution.py:200
  16.9 0.1 reshape.196
  17.0 3.0 %collective-permute-done.1 = f32[136,512]{1,0:T(8,128)S(1)} collective-permute-done((f32[136,512]{1,0:T(8,128)S(1)}, f32[136,512]{1,0:T(8,128)S(1)}, u32[]{:S(2)}, u32[]{:S(2)}) %collective-permute-start.1) | collective-permute-done | bytes 278560 | tf_op jit(solution)/shard_map/ppermute | solution.py:208
  20.0 0.1 reshape.197
  20.1 0.1 pad_maximum_fusion
  20.2 0.4 copy-done.6
  20.7 0.1 slice_bitcast_fusion.5
  20.8 0.1 slice_bitcast_fusion.2
  21.0 0.9 %slice.195 = f32[64,512]{1,0:T(8,128)S(1)} slice(f32[136,512]{1,0:T(8,128)} %copy-done.6), slice={[0:64], [0:512]} | slice | bytes 262144 | tf_op jit(solution)/shard_map/slice | solution.py:215
  22.0 0.1 pad_maximum_fusion.2
  22.1 0.1 slice.196
  22.1 0.5 add_select_fusion.2
  22.7 0.1 slice.204
  22.7 0.5 add_select_fusion.1
  23.3 0.1 slice.210
  23.4 0.5 add_select_fusion
  23.9 0.3 select_convert_fusion.2
  24.2 0.1 fusion.1
  24.4 0.1 slice.220
  24.5 0.1 copy_bitcast_fusion
  24.6 0.2 reshape.202
  24.8 0.7 pad_maximum_fusion.7
  25.5 3.8 %all-to-all-start = ((bf16[4,9,8,256]{3,2,1,0:T(8,128)(2,1)}), bf16[4,9,8,256]{3,2,1,0:T(8,128)(2,1)S(1)}, u32[]{:S(2)}, u32[]{:S(2)}) async-start(bf16[4,9,8,256]{3,2,1,0:T(8,128)(2,1)} %pad_maximum_fusion.7), calls=%async_computation | async-start | bytes 294912 | tf_op jit(solution)/shard_map/all_to_all | solution.py:248
  29.3 3.7 %all-to-all-done.x_ref = bf16[4,9,8,256]{3,2,1,0:T(8,128)(2,1)S(1)} async-done(((bf16[4,9,8,256]{3,2,1,0:T(8,128)(2,1)}), bf16[4,9,8,256]{3,2,1,0:T(8,128)(2,1)S(1)}, u32[]{:S(2)}, u32[]{:S(2)}) %all-to-all-start) | async-done | bytes 147488 | tf_op jit(solution)/shard_map/all_to_all | solution.py:248
  33.0 0.7 copy-done.5
  33.7 10.4 %shard_map.118 = bf16[9,8,1024]{2,1,0:T(8,128)(2,1)} custom-call(f32[8,1]{1,0:T(8,128)} %reshape_tile.4.hs_ref, bf16[4,9,8,256]{3,2,1,0:T(8,128)(2,1)} %copy-done.5, bf16[64,8]{1,0:T(8,128)(2,1)} %bitcast.90, f32[64,1]{1,0:T(8,128)} %copy.66.gain_ref, bf16[192,64]{1,0:T(8,128)(2,1)} %bitcast.87, bf16[64,64]{1,0:T(8,128)(2,1)} %bitcast.89, bf16[8,64]{1,0:T(8,128)(2,1)} %bitcast.93), custom_call_target="tpu_custom_call" | custom-call | tf_op jit(solution)/shard_map/pallas_call | solution.py:142
  44.1 0.7 slice.222
  44.8 0.9 %slice_bitcast_fusion.9 = bf16[8,8,8,128]{3,1,2,0:T(8,128)(2,1)S(1)} fusion(bf16[9,8,1024]{2,1,0:T(8,128)(2,1)} %shard_map.118), kind=kLoop, calls=%fused_computation.40 | loop fusion | bytes 262144 | tf_op jit(solution)/shard_map/reshape | solution.py:261
  45.7 0.1 reshape_squeeze.3
  45.9 0.1 copy.83
  46.0 0.1 slice_select_fusion.1
  46.1 0.2 pad_maximum_fusion.6
  46.3 0.3 reshape.211
  46.6 2.3 %collective-permute-start.2 = (bf16[8,8,1152]{2,1,0:T(8,128)(2,1)S(1)}, bf16[8,8,1152]{2,1,0:T(8,128)(2,1)S(1)}, u32[]{:S(2)}, u32[]{:S(2)}) collective-permute-start(bf16[8,8,1152]{2,1,0:T(8,128)(2,1)S(1)} %reshape.211), channel_id=1, source_target_pairs={{0,1},{1,2},{2,3},{3,4},{4,5},{5,6},{6,7},{8,9},{9,10},{10,11},{11... | collective-permute-start | bytes 442376 | tf_op jit(solution)/shard_map/ppermute | solution.py:34
  48.9 4.1 %collective-permute-start.3 = (bf16[8,8,1152]{2,1,0:T(8,128)(2,1)S(1)}, bf16[8,8,1152]{2,1,0:T(8,128)(2,1)S(1)}, u32[]{:S(2)}, u32[]{:S(2)}) collective-permute-start(bf16[8,8,1152]{2,1,0:T(8,128)(2,1)S(1)} %reshape.211), channel_id=1, source_target_pairs={{1,0},{2,1},{3,2},{4,3},{5,4},{6,5},{7,6},{9,8},{10,9},{11,10},{12... | collective-permute-start | bytes 442376 | tf_op jit(solution)/shard_map/ppermute | solution.py:35
  52.9 0.1 broadcast_and_fusion
  53.0 0.3 collective-permute-done.2
  53.3 0.4 reshape.212
  53.7 4.2 %collective-permute-done.3 = bf16[8,8,1152]{2,1,0:T(8,128)(2,1)S(1)} collective-permute-done((bf16[8,8,1152]{2,1,0:T(8,128)(2,1)S(1)}, bf16[8,8,1152]{2,1,0:T(8,128)(2,1)S(1)}, u32[]{:S(2)}, u32[]{:S(2)}) %collective-permute-start.3) | collective-permute-done | bytes 147488 | tf_op jit(solution)/shard_map/ppermute | solution.py:35
  57.9 0.4 reshape.213
  58.3 0.2 pad_maximum_fusion.1
  58.5 7.1 %copy.70 = bf16[8,8,24,144]{1,0,3,2:T(8,128)(2,1)} copy(bf16[8,8,24,144]{3,2,1,0:T(8,128)(2,1)S(1)} %pad_maximum_fusion.1) | data formatting | bytes 884736 | tf_op jit(solution)/shard_map/concatenate | solution.py:36
  65.6 13.7 %select_convert_fusion.5 = bf16[8,8,16,136]{1,0,3,2:T(8,128)(2,1)S(1)} fusion(pred[16,136]{1,0:T(8,128)(4,1)S(1)} %broadcast_and_fusion, bf16[8,8,24,144]{1,0,3,2:T(8,128)(2,1)} %copy.70, bf16[3,3,8,8]{3,2,1,0:T(8,128)(2,1)S(1)} %bitcast.92), kind=kOutput, calls=%fused_computation.2.clone.clone.1 | convolution fusion | flops 20889600 | bytes 724224 | tf_op jit(solution)/shard_map/conv_general_dilated | solution.py:160
  79.3 6.5 %fusion = f32[8,8,8,128]{1,0,3,2:T(8,128)} fusion(bf16[3,3,8,8]{3,2,1,0:T(8,128)(2,1)S(1)} %bitcast.91, bf16[8,8,16,136]{1,0,3,2:T(8,128)(2,1)S(1)} %select_convert_fusion.5), kind=kOutput, calls=%fused_computation.3 | convolution fusion | flops 9437184 | bytes 541824 | tf_op jit(solution)/shard_map/conv_general_dilated | solution.py:160
  85.8 3.3 %copy.72 = f32[8,8,8,128]{3,2,1,0:T(8,128)S(1)} copy(f32[8,8,8,128]{1,0,3,2:T(8,128)} %fusion) | data formatting | bytes 524288 | tf_op jit(solution)/shard_map/conv_general_dilated | solution.py:160
  89.1 0.7 add_convert_fusion
  (48 shorter events, 0.6 us)
Async XLA Ops:
  0.0 10.6 %copy-start = (bf16[64,64]{1,0:T(8,128)(2,1)S(1)}, bf16[64,64]{1,0:T(8,128)(2,1)}, u32[]{:S(2)}) copy-start(bf16[64,64]{1,0:T(8,128)(2,1)} %param.20) | copy-start | bytes 24580
  0.0 20.1 %copy-start.3 = (f32[8,8,512]{2,1,0:T(8,128)S(1)}, f32[8,8,512]{2,1,0:T(8,128)}, u32[]{:S(2)}) copy-start(f32[8,8,512]{2,1,0:T(8,128)} %param.13) | copy-start | bytes 393220
  0.0 20.1 %copy-start.2 = (f32[8,8,512]{2,1,0:T(8,128)S(1)}, f32[8,8,512]{2,1,0:T(8,128)}, u32[]{:S(2)}) copy-start(f32[8,8,512]{2,1,0:T(8,128)} %param.14) | copy-start | bytes 393220
  0.0 20.1 %copy-start.1 = (f32[8,8,512]{2,1,0:T(8,128)S(1)}, f32[8,8,512]{2,1,0:T(8,128)}, u32[]{:S(2)}) copy-start(f32[8,8,512]{2,1,0:T(8,128)} %param.15) | copy-start | bytes 393220
  0.0 9.2 %copy-start.7 = (bf16[64,192]{1,0:T(8,128)(2,1)S(1)}, bf16[64,192]{1,0:T(8,128)(2,1)}, u32[]{:S(2)}) copy-start(bf16[64,192]{1,0:T(8,128)(2,1)} %param.18) | copy-start | bytes 73732
  0.0 11.9 %copy-start.11 = (f32[64]{0:T(128)S(1)}, f32[64]{0:T(128)}, u32[]{:S(2)}) copy-start(f32[64]{0:T(128)} %param.17) | copy-start | bytes 772
  0.0 12.6 %copy-start.10 = (bf16[8,64]{1,0:T(8,128)(2,1)S(1)}, bf16[8,64]{1,0:T(8,128)(2,1)}, u32[]{:S(2)}) copy-start(bf16[8,64]{1,0:T(8,128)(2,1)} %param.16) | copy-start | bytes 3076
  0.1 13.3 %copy-start.12 = (f32[4]{0:T(128)S(1)}, f32[4]{0:T(128)}, u32[]{:S(2)}) copy-start(f32[4]{0:T(128)} %param.19) | copy-start | bytes 52
  0.1 14.0 %copy-start.8 = (bf16[9,8,8]{0,2,1:T(8,128)(2,1)S(1)}, bf16[9,8,8]{0,2,1:T(8,128)(2,1)}, u32[]{:S(2)}) copy-start(bf16[9,8,8]{0,2,1:T(8,128)(2,1)} %param.22) | copy-start | bytes 3460
  0.1 14.1 %copy-start.9 = (bf16[9,8,8]{0,2,1:T(8,128)(2,1)S(1)}, bf16[9,8,8]{0,2,1:T(8,128)(2,1)}, u32[]{:S(2)}) copy-start(bf16[9,8,8]{0,2,1:T(8,128)(2,1)} %param.23) | copy-start | bytes 3460
  2.6 14.3 %collective-permute-start = (f32[136,512]{1,0:T(8,128)S(1)}, f32[136,512]{1,0:T(8,128)S(1)}, u32[]{:S(2)}, u32[]{:S(2)}) collective-permute-start(f32[136,512]{1,0:T(8,128)S(1)} %pad_maximum_fusion.4), channel_id=1, source_target_pairs={{0,1},{1,2},{2,3},{3,4},{4,5},{5,6},{6,7},{8,9},{9,10},{10,11},{11... | collective-permute-start | bytes 835592 | tf_op jit(solution)/shard_map/ppermute | solution.py:200
  5.9 14.0 %collective-permute-start.1 = (f32[136,512]{1,0:T(8,128)S(1)}, f32[136,512]{1,0:T(8,128)S(1)}, u32[]{:S(2)}, u32[]{:S(2)}) collective-permute-start(f32[136,512]{1,0:T(8,128)S(1)} %pad_maximum_fusion.5), channel_id=1, source_target_pairs={{1,0},{2,1},{3,2},{4,3},{5,4},{6,5},{7,6},{9,8},{10,9},{11,10},{12... | collective-permute-start | bytes 835592 | tf_op jit(solution)/shard_map/ppermute | solution.py:208
  10.6 11.3 %copy-start.4 = (f32[2,8,8,512]{3,2,1,0:T(8,128)S(1)}, f32[2,8,8,512]{3,2,1,0:T(8,128)}, u32[]{:S(2)}) copy-start(f32[2,8,8,512]{3,2,1,0:T(8,128)} %param.12) | copy-start | bytes 786436
  20.0 0.7 copy-start.6
  25.5 7.5 %all-to-all-start = ((bf16[4,9,8,256]{3,2,1,0:T(8,128)(2,1)}), bf16[4,9,8,256]{3,2,1,0:T(8,128)(2,1)S(1)}, u32[]{:S(2)}, u32[]{:S(2)}) async-start(bf16[4,9,8,256]{3,2,1,0:T(8,128)(2,1)} %pad_maximum_fusion.7), calls=%async_computation | async-start | bytes 294912 | tf_op jit(solution)/shard_map/all_to_all | solution.py:248
  33.0 0.7 copy-start.5
  46.6 6.8 %collective-permute-start.2 = (bf16[8,8,1152]{2,1,0:T(8,128)(2,1)S(1)}, bf16[8,8,1152]{2,1,0:T(8,128)(2,1)S(1)}, u32[]{:S(2)}, u32[]{:S(2)}) collective-permute-start(bf16[8,8,1152]{2,1,0:T(8,128)(2,1)S(1)} %reshape.211), channel_id=1, source_target_pairs={{0,1},{1,2},{2,3},{3,4},{4,5},{5,6},{6,7},{8,9},{9,10},{10,11},{11... | collective-permute-start | bytes 442376 | tf_op jit(solution)/shard_map/ppermute | solution.py:34
  48.9 9.0 %collective-permute-start.3 = (bf16[8,8,1152]{2,1,0:T(8,128)(2,1)S(1)}, bf16[8,8,1152]{2,1,0:T(8,128)(2,1)S(1)}, u32[]{:S(2)}, u32[]{:S(2)}) collective-permute-start(bf16[8,8,1152]{2,1,0:T(8,128)(2,1)S(1)} %reshape.211), channel_id=1, source_target_pairs={{1,0},{2,1},{3,2},{4,3},{5,4},{6,5},{7,6},{9,8},{10,9},{11,10},{12... | collective-permute-start | bytes 442376 | tf_op jit(solution)/shard_map/ppermute | solution.py:35

commit v19 on v15

--- a/solution.py
+++ b/solution.py
@@ -200,32 +200,48 @@
     backward = [(target, source) for source, target in forward]
     cols = starting_states.shape[3]
 
+    levels = coefficients.shape[1]
+    half = levels // 2
+    pair = lax.axis_index("mem") % 2
+    own = lax.dynamic_slice_in_dim(coefficients, pair * half, half, axis=1)
+
     def pack(states_part, coef_part):
         return jnp.concatenate(
             [states_part.reshape(-1, cols), coef_part.reshape(-1, cols)], axis=0
         )
 
     low = lax.ppermute(
-        pack(
-            starting_states[:, :, row_total - state_halo :],
-            coefficients[:, :, row_total - coef_halo :],
-        ),
+        pack(starting_states[:, :, row_total - state_halo :], own[:, :, row_total - coef_halo :]),
         "row",
         forward,
     )
     high = lax.ppermute(
-        pack(starting_states[:, :, :state_halo], coefficients[:, :, :coef_halo]), "row", backward
+        pack(starting_states[:, :, :state_halo], own[:, :, :coef_halo]), "row", backward
     )
     split = members_here * starting_states.shape[1] * state_halo
     state_shape = starting_states.shape[:2] + (state_halo, cols)
-    coef_shape = coefficients.shape[:2] + (coef_halo, cols)
+    half_shape = (coefficients.shape[0], half, coef_halo, cols)
+    own_halos = jnp.concatenate([low[split:], high[split:]], axis=0)
+    pairs = [(i, i ^ 1) for i in range(lax.axis_size("mem"))]
+    other_halos = lax.ppermute(own_halos, "mem", pairs)
+    count_low = low.shape[0] - split
+
+    def levels_of(own_part, other_part):
+        own_part = own_part.reshape(half_shape)
+        other_part = other_part.reshape(half_shape)
+        return jnp.where(
+            pair == 0,
+            jnp.concatenate([own_part, other_part], axis=1),
+            jnp.concatenate([other_part, own_part], axis=1),
+        )
+
+    coef_low = levels_of(own_halos[:count_low], other_halos[:count_low])
+    coef_high = levels_of(own_halos[count_low:], other_halos[count_low:])
     gridded_quantity_list = jnp.concatenate(
         [low[:split].reshape(state_shape), starting_states, high[:split].reshape(state_shape)],
         axis=2,
     )
-    coef_rows = jnp.concatenate(
-        [low[split:].reshape(coef_shape), coefficients, high[split:].reshape(coef_shape)], axis=2
-    )
+    coef_rows = jnp.concatenate([coef_low, coefficients, coef_high], axis=2)
     first_row = lax.axis_index("row") * row_total - STEPS
     all_rows = lax.axis_size("row") * row_total
     for section in range(STEPS):

time: 64.9 us -> 68.9 us (1.062)
  waiting for transfers between devices: 11.3 us -> 15.9 us
  local copies, waits for them, and re-layouts: 15 us -> 14.3 us
    ppermute x2 -> x3, waiting for transfers between devices: 3.09 us -> 7.72 us  [the longest x1 5.61 us: on_device(): lax.ppermute(pack(starting_states[:, :, :state_halo], own[:, :, :coef_hal...]
    slice x1, local copies, waits for them, and re-layouts: 0.91 us -> 0.01 us  [on_device(): high[:split].reshape(state_shape)]
    ppermute x2 -> x3, starting transfers between devices: 6.18 us -> 6.74 us  [the longest x1 3.12 us: on_device(): lax.ppermute(pack(starting_states[:, :, row_total - state_halo:], own[:,...]
    unnamed x48 -> x46, local copies, waits for them, and re-layouts: 4.65 us -> 4.9 us
  transfers between devices with their start and end apart: 5 -> 6, of which waited for: 5 -> 5; matrix products, arithmetic and copies ran while one was open for 13% -> 13% of each run, Pallas kernels for 0% -> 0%
where the time goes in v19:
time: 68.9 us; the launch traced here: 67.8 us
  starting transfers between devices  16.4 us (24%)
  waiting for transfers between devices  15.9 us (23%)
  local copies, waits for them, and re-layouts  14.3 us (21%)
  Pallas kernels  10.4 us (15%)
  other arithmetic  5.06 us (7%)
  matrix products  5 us (7%)
  between operations  0.74 us (1%)
    pallas_call x1, Pallas kernels, post_block(): pl.pallas_call(functools.partial(attention_kernel, chunk=chunk, heads=hea...  10.4 us
    ppermute x1, waiting for transfers between devices, on_device(): lax.ppermute(pack(starting_states[:, :, :state_halo], own[:, :, :coef_hal...  5.61 us
    dot_general x18, matrix products, convolve(): jnp.einsum('oc,mcij->moij', kernel[row_stencil * 3 + column_stencil], shi...  5 us
    unnamed x46, local copies, waits for them, and re-layouts  4.9 us
    ppermute x1, waiting for transfers between devices, row_padded(): high = lax.ppermute(block[..., :width, :].reshape(flat), 'row', backward)  4.11 us
    ppermute x1, starting transfers between devices, row_padded(): high = lax.ppermute(block[..., :width, :].reshape(flat), 'row', backward)  4.11 us
    all_to_all x1, waiting for transfers between devices, on_device(): lax.all_to_all(by_chunk, 'mem', split_axis=0, concat_axis=0, tiled=True)  3.72 us
    all_to_all x1, starting transfers between devices, on_device(): lax.all_to_all(by_chunk, 'mem', split_axis=0, concat_axis=0, tiled=True)  3.34 us
  transfers between devices with their start and end apart: 6, of which 5 were waited for; matrix products, arithmetic and copies ran while one was open for 13% of the time, Pallas kernels for 0%

profile of v19, /device:TPU:9, one launch (start us, length us, event | category | flops | bytes accessed | tf_op | source)
XLA Modules:
  0.0 67.8 jit_solution(14888569607747560507)
XLA Ops:
  0.0 1.0 %fusion.15 = f32[3,4,8,512]{3,2,1,0:T(8,128)S(1)} fusion(s32[]{:T(128)S(6)} %select_n.70, f32[1,8,8,512]{3,2,1,0:T(8,128)} %bitcast.199, f32[1,8,8,512]{3,2,1,0:T(8,128)} %bitcast.201, f32[1,8,8,512]{3,2,1,0:T(8,128)} %bitcast.203), kind=kLoop, calls=%fused_computation.66 | loop fusion | flops 98304 | bytes 589828 | tf_op jit(solution)/shard_map/stack | solution.py:195
  1.2 3.1 %collective-permute-start = (f32[100,512]{1,0:T(8,128)S(1)}, f32[100,512]{1,0:T(8,128)S(1)}, u32[]{:S(2)}, u32[]{:S(2)}) collective-permute-start(f32[100,512]{1,0:T(8,128)S(1)} %pad_maximum_fusion.5), channel_id=1, source_target_pairs={{0,1},{1,2},{2,3},{3,4},{4,5},{5,6},{6,7},{8,9},{9,10},{10,11},{11... | collective-permute-start | bytes 614408 | tf_op jit(solution)/shard_map/ppermute | solution.py:213
  4.5 3.1 %collective-permute-start.1 = (f32[100,512]{1,0:T(8,128)S(1)}, f32[100,512]{1,0:T(8,128)S(1)}, u32[]{:S(2)}, u32[]{:S(2)}) collective-permute-start(f32[100,512]{1,0:T(8,128)S(1)} %pad_maximum_fusion.6), channel_id=1, source_target_pairs={{1,0},{2,1},{3,2},{4,3},{5,4},{6,5},{7,6},{9,8},{10,9},{11,10},{12... | collective-permute-start | bytes 614408 | tf_op jit(solution)/shard_map/ppermute | solution.py:218
  8.0 2.1 %collective-permute-done = f32[100,512]{1,0:T(8,128)S(1)} collective-permute-done((f32[100,512]{1,0:T(8,128)S(1)}, f32[100,512]{1,0:T(8,128)S(1)}, u32[]{:S(2)}, u32[]{:S(2)}) %collective-permute-start) | collective-permute-done | bytes 204832 | tf_op jit(solution)/shard_map/ppermute | solution.py:213
  10.1 5.6 %collective-permute-done.1 = f32[100,512]{1,0:T(8,128)S(1)} collective-permute-done((f32[100,512]{1,0:T(8,128)S(1)}, f32[100,512]{1,0:T(8,128)S(1)}, u32[]{:S(2)}, u32[]{:S(2)}) %collective-permute-start.1) | collective-permute-done | bytes 204832 | tf_op jit(solution)/shard_map/ppermute | solution.py:218
  15.8 0.6 collective-permute-start.2
  16.5 0.7 gather_fusion
  17.2 0.6 copy.47
  17.8 0.6 gather_fusion.1
  18.4 0.7 %copy.48 = bf16[64,64]{0,1:T(8,128)(2,1)} copy(bf16[64,64]{1,0:T(8,128)(2,1)S(1)} %gather_fusion.1) | data formatting | bytes 16384 | tf_op jit(solution)/shard_map/gather | solution.py:140
  19.1 0.7 %copy.50.gain_ref = f32[64,1]{1,0:T(8,128)} copy(f32[64,1]{0,1:T(1,128)S(1)} %bitcast.214) | data formatting | bytes 512 | tf_op jit(solution)/shard_map/reshape | solution.py:149
  19.8 0.7 %copy.44 = bf16[8,64]{0,1:T(8,128)(2,1)} copy(bf16[8,64]{1,0:T(8,128)(2,1)S(1)} %copy-done.10) | data formatting | bytes 2048 | tf_op args[4]
  20.5 0.7 reshape_tile.4.hs_ref
  21.9 0.1 copy.102
  22.0 0.1 copy.103
  22.1 0.1 copy.104
  22.5 0.1 copy.107
  22.8 0.1 copy.109
  23.1 0.1 copy.111
  24.3 0.6 copy-done.4
  25.0 0.1 pad_maximum_fusion
  25.4 0.5 add_select_fusion.2
  26.0 0.5 add_select_fusion.1
  26.6 0.5 add_select_fusion
  27.1 0.3 select_convert_fusion.1
  27.8 0.2 reshape.204
  28.0 0.7 %pad_maximum_fusion.8 = bf16[4,9,8,256]{3,2,1,0:T(8,128)(2,1)} fusion(bf16[4,1,8,256]{3,2,1,0:T(8,128)(2,1)S(1)} %reshape.204, bf16[4,8,8,256]{3,2,1,0:T(8,128)(2,1)S(1)} %bitcast.207), kind=kLoop, calls=%fused_computation.72 | loop fusion | flops 73728 | bytes 294912 | tf_op jit(solution)/shard_map/concatenate | solution.py:271
  28.7 3.3 %all-to-all-start = ((bf16[4,9,8,256]{3,2,1,0:T(8,128)(2,1)}), bf16[4,9,8,256]{3,2,1,0:T(8,128)(2,1)S(1)}, u32[]{:S(2)}, u32[]{:S(2)}) async-start(bf16[4,9,8,256]{3,2,1,0:T(8,128)(2,1)} %pad_maximum_fusion.8), calls=%async_computation | async-start | bytes 294912 | tf_op jit(solution)/shard_map/all_to_all | solution.py:272
  32.1 3.7 %all-to-all-done.x_ref = bf16[4,9,8,256]{3,2,1,0:T(8,128)(2,1)S(1)} async-done(((bf16[4,9,8,256]{3,2,1,0:T(8,128)(2,1)}), bf16[4,9,8,256]{3,2,1,0:T(8,128)(2,1)S(1)}, u32[]{:S(2)}, u32[]{:S(2)}) %all-to-all-start) | async-done | bytes 147488 | tf_op jit(solution)/shard_map/all_to_all | solution.py:272
  35.8 0.7 copy-done.8
  36.5 10.4 %shard_map.118 = bf16[9,8,1024]{2,1,0:T(8,128)(2,1)} custom-call(f32[8,1]{1,0:T(8,128)} %reshape_tile.4.hs_ref, bf16[4,9,8,256]{3,2,1,0:T(8,128)(2,1)} %copy-done.8, bf16[64,8]{1,0:T(8,128)(2,1)} %bitcast.212, f32[64,1]{1,0:T(8,128)} %copy.50.gain_ref, bf16[192,64]{1,0:T(8,128)(2,1)} %bitcast.209, bf16[64,64]{1,0:T(8,128)(2,1)} %bitcast.211, ...), custom_call_target="tpu_custom_call" | custom-call | tf_op jit(solution)/shard_map/pallas_call | solution.py:142
  46.8 0.7 %slice.382 = bf16[1,8,1024]{2,1,0:T(8,128)(2,1)S(1)} slice(bf16[9,8,1024]{2,1,0:T(8,128)(2,1)} %shard_map.118), slice={[8:9], [0:8], [0:1024]} | slice | bytes 32768 | tf_op jit(solution)/shard_map/slice | solution.py:287
  47.6 0.9 %copy_bitcast_fusion.2 = bf16[8,8,8,128]{3,1,2,0:T(8,128)(2,1)S(1)} fusion(bf16[9,8,1024]{2,1,0:T(8,128)(2,1)} %shard_map.118), kind=kLoop, calls=%fused_computation.91 | loop fusion | bytes 262144 | tf_op jit(solution)/shard_map/transpose | solution.py:286
  48.5 0.1 reshape_squeeze.3
  48.9 0.2 pad_maximum_fusion.4
  49.1 0.3 reshape.213
  49.4 2.2 %collective-permute-start.3 = (bf16[8,8,1152]{2,1,0:T(8,128)(2,1)S(1)}, bf16[8,8,1152]{2,1,0:T(8,128)(2,1)S(1)}, u32[]{:S(2)}, u32[]{:S(2)}) collective-permute-start(bf16[8,8,1152]{2,1,0:T(8,128)(2,1)S(1)} %reshape.213), channel_id=1, source_target_pairs={{0,1},{1,2},{2,3},{3,4},{4,5},{5,6},{6,7},{8,9},{9,10},{10,11},{11... | collective-permute-start | bytes 442376 | tf_op jit(solution)/shard_map/ppermute | solution.py:34
  51.6 4.1 %collective-permute-start.4 = (bf16[8,8,1152]{2,1,0:T(8,128)(2,1)S(1)}, bf16[8,8,1152]{2,1,0:T(8,128)(2,1)S(1)}, u32[]{:S(2)}, u32[]{:S(2)}) collective-permute-start(bf16[8,8,1152]{2,1,0:T(8,128)(2,1)S(1)} %reshape.213), channel_id=1, source_target_pairs={{1,0},{2,1},{3,2},{4,3},{5,4},{6,5},{7,6},{9,8},{10,9},{11,10},{12... | collective-permute-start | bytes 442376 | tf_op jit(solution)/shard_map/ppermute | solution.py:35
  55.8 0.3 collective-permute-done.3
  56.2 0.4 reshape.214
  56.6 4.1 %collective-permute-done.4 = bf16[8,8,1152]{2,1,0:T(8,128)(2,1)S(1)} collective-permute-done((bf16[8,8,1152]{2,1,0:T(8,128)(2,1)S(1)}, bf16[8,8,1152]{2,1,0:T(8,128)(2,1)S(1)}, u32[]{:S(2)}, u32[]{:S(2)}) %collective-permute-start.4) | collective-permute-done | bytes 147488 | tf_op jit(solution)/shard_map/ppermute | solution.py:35
  60.7 0.4 reshape.215
  61.1 0.2 pad_maximum_fusion.1
  61.4 0.4 pad_maximum_fusion.3
  61.7 0.3 fusion.12
  62.0 0.4 convolution_add_fusion.7
  62.4 0.3 convolution_add_fusion.6
  62.7 0.3 convolution_add_fusion.5
  63.0 0.3 convolution_add_fusion.4
  63.4 0.4 convolution_add_fusion.3
  63.8 0.3 convolution_add_fusion.2
  64.0 0.4 convolution_add_fusion.1
  64.4 0.5 select_convert_fusion
  64.9 0.2 fusion.26
  65.1 0.2 convolution_add_fusion.15
  65.3 0.2 convolution_add_fusion.14
  65.6 0.2 convolution_add_fusion.13
  65.8 0.2 convolution_add_fusion.12
  66.0 0.2 convolution_add_fusion.11
  66.2 0.2 convolution_add_fusion.10
  66.4 0.2 convolution_add_fusion.9
  66.6 0.3 copy-done.3
  66.9 0.2 fusion.3
  67.1 0.7 %copy.76 = bf16[8,8,8,128]{3,2,1,0:T(8,128)(2,1)} copy(bf16[8,8,8,128]{3,1,2,0:T(8,128)(2,1)S(1)} %fusion.3) | data formatting | bytes 262144 | tf_op jit(solution)/shard_map/convert_element_type | solution.py:302
  (90 shorter events, 4.3 us)
Async XLA Ops:
  0.0 17.8 %copy-start = (bf16[64,64]{1,0:T(8,128)(2,1)S(1)}, bf16[64,64]{1,0:T(8,128)(2,1)}, u32[]{:S(2)}) copy-start(bf16[64,64]{1,0:T(8,128)(2,1)} %param.20) | copy-start | bytes 24580
  0.0 1.1 %copy-start.7 = (f32[2,8,8,512]{3,2,1,0:T(8,128)S(1)}, f32[2,8,8,512]{3,2,1,0:T(8,128)}, u32[]{:S(2)}) copy-start(f32[2,8,8,512]{3,2,1,0:T(8,128)} %param.12) | copy-start | bytes 786436
  1.1 6.7 %copy-start.1 = (bf16[9,8,8]{0,2,1:T(8,128)(2,1)S(1)}, bf16[9,8,8]{0,2,1:T(8,128)(2,1)}, u32[]{:S(2)}) copy-start(bf16[9,8,8]{0,2,1:T(8,128)(2,1)} %param.22) | copy-start | bytes 3460
  1.1 6.8 %copy-start.2 = (bf16[9,8,8]{0,2,1:T(8,128)(2,1)S(1)}, bf16[9,8,8]{0,2,1:T(8,128)(2,1)}, u32[]{:S(2)}) copy-start(bf16[9,8,8]{0,2,1:T(8,128)(2,1)} %param.23) | copy-start | bytes 3460
  1.2 8.9 %collective-permute-start = (f32[100,512]{1,0:T(8,128)S(1)}, f32[100,512]{1,0:T(8,128)S(1)}, u32[]{:S(2)}, u32[]{:S(2)}) collective-permute-start(f32[100,512]{1,0:T(8,128)S(1)} %pad_maximum_fusion.5), channel_id=1, source_target_pairs={{0,1},{1,2},{2,3},{3,4},{4,5},{5,6},{6,7},{8,9},{9,10},{10,11},{11... | collective-permute-start | bytes 614408 | tf_op jit(solution)/shard_map/ppermute | solution.py:213
  4.3 12.0 %copy-start.9 = (bf16[64,192]{1,0:T(8,128)(2,1)S(1)}, bf16[64,192]{1,0:T(8,128)(2,1)}, u32[]{:S(2)}) copy-start(bf16[64,192]{1,0:T(8,128)(2,1)} %param.18) | copy-start | bytes 73732
  4.5 14.7 %copy-start.11 = (f32[64]{0:T(128)S(1)}, f32[64]{0:T(128)}, u32[]{:S(2)}) copy-start(f32[64]{0:T(128)} %param.17) | copy-start | bytes 772
  4.5 15.3 %copy-start.10 = (bf16[8,64]{1,0:T(8,128)(2,1)S(1)}, bf16[8,64]{1,0:T(8,128)(2,1)}, u32[]{:S(2)}) copy-start(bf16[8,64]{1,0:T(8,128)(2,1)} %param.16) | copy-start | bytes 3076
  4.5 16.0 %copy-start.12 = (f32[4]{0:T(128)S(1)}, f32[4]{0:T(128)}, u32[]{:S(2)}) copy-start(f32[4]{0:T(128)} %param.19) | copy-start | bytes 52
  4.5 11.2 %collective-permute-start.1 = (f32[100,512]{1,0:T(8,128)S(1)}, f32[100,512]{1,0:T(8,128)S(1)}, u32[]{:S(2)}, u32[]{:S(2)}) collective-permute-start(f32[100,512]{1,0:T(8,128)S(1)} %pad_maximum_fusion.6), channel_id=1, source_target_pairs={{1,0},{2,1},{3,2},{4,3},{5,4},{6,5},{7,6},{9,8},{10,9},{11,10},{12... | collective-permute-start | bytes 614408 | tf_op jit(solution)/shard_map/ppermute | solution.py:218
  15.8 8.3 %collective-permute-start.2 = (f32[72,512]{1,0:T(8,128)S(1)}, f32[72,512]{1,0:T(8,128)S(1)}, u32[]{:S(2)}, u32[]{:S(2)}) collective-permute-start(f32[72,512]{1,0:T(8,128)S(1)} %pad_maximum_fusion.7), channel_id=1, source_target_pairs={{0,8},{8,0},{16,24},{24,16},{1,9},{9,1},{17,25},{25,17},{2,10},{10... | collective-permute-start | bytes 442376 | tf_op jit(solution)/shard_map/ppermute | solution.py:226
  23.9 0.9 %copy-start.4 = (f32[8,8,512]{2,1,0:T(8,128)S(1)}, f32[8,8,512]{2,1,0:T(8,128)}, u32[]{:S(2)}) copy-start(f32[8,8,512]{2,1,0:T(8,128)} %param.13) | copy-start | bytes 393220
  24.0 1.0 %copy-start.5 = (f32[8,8,512]{2,1,0:T(8,128)S(1)}, f32[8,8,512]{2,1,0:T(8,128)}, u32[]{:S(2)}) copy-start(f32[8,8,512]{2,1,0:T(8,128)} %param.14) | copy-start | bytes 393220
  24.0 1.0 %copy-start.6 = (f32[8,8,512]{2,1,0:T(8,128)S(1)}, f32[8,8,512]{2,1,0:T(8,128)}, u32[]{:S(2)}) copy-start(f32[8,8,512]{2,1,0:T(8,128)} %param.15) | copy-start | bytes 393220
  28.7 7.1 %all-to-all-start = ((bf16[4,9,8,256]{3,2,1,0:T(8,128)(2,1)}), bf16[4,9,8,256]{3,2,1,0:T(8,128)(2,1)S(1)}, u32[]{:S(2)}, u32[]{:S(2)}) async-start(bf16[4,9,8,256]{3,2,1,0:T(8,128)(2,1)} %pad_maximum_fusion.8), calls=%async_computation | async-start | bytes 294912 | tf_op jit(solution)/shard_map/all_to_all | solution.py:272
  35.8 0.7 copy-start.8
  49.4 6.8 %collective-permute-start.3 = (bf16[8,8,1152]{2,1,0:T(8,128)(2,1)S(1)}, bf16[8,8,1152]{2,1,0:T(8,128)(2,1)S(1)}, u32[]{:S(2)}, u32[]{:S(2)}) collective-permute-start(bf16[8,8,1152]{2,1,0:T(8,128)(2,1)S(1)} %reshape.213), channel_id=1, source_target_pairs={{0,1},{1,2},{2,3},{3,4},{4,5},{5,6},{6,7},{8,9},{9,10},{10,11},{11... | collective-permute-start | bytes 442376 | tf_op jit(solution)/shard_map/ppermute | solution.py:34
  51.6 9.1 %collective-permute-start.4 = (bf16[8,8,1152]{2,1,0:T(8,128)(2,1)S(1)}, bf16[8,8,1152]{2,1,0:T(8,128)(2,1)S(1)}, u32[]{:S(2)}, u32[]{:S(2)}) collective-permute-start(bf16[8,8,1152]{2,1,0:T(8,128)(2,1)S(1)} %reshape.213), channel_id=1, source_target_pairs={{1,0},{2,1},{3,2},{4,3},{5,4},{6,5},{7,6},{9,8},{10,9},{11,10},{12... | collective-permute-start | bytes 442376 | tf_op jit(solution)/shard_map/ppermute | solution.py:35
  66.0 0.9 %copy-start.3 = (bf16[9,8,1024]{2,1,0:T(8,128)(2,1)S(1)}, bf16[9,8,1024]{2,1,0:T(8,128)(2,1)}, u32[]{:S(2)}) copy-start(bf16[9,8,1024]{2,1,0:T(8,128)(2,1)} %shard_map.118) | copy-start | bytes 442372

commit v20 on v19

--- a/solution.py
+++ b/solution.py
@@ -118,20 +118,8 @@
     return 0
 
 
-def post_block(
-    by_source,
-    chunk,
-    embed_weight,
-    norm_gain,
-    project_weight,
-    head_scale,
-    output_weight,
-    readout_weight,
-):
-    sources, row_count, levels_count, source_lanes = by_source.shape
-    lanes = sources * source_lanes
+def prepare_weights(embed_weight, norm_gain, project_weight, head_scale, output_weight, readout_weight):
     width = embed_weight.shape[1]
-    feat = readout_weight.shape[1]
     heads = head_scale.shape[0]
     head_size = width // heads
     sub = 8
@@ -139,18 +127,26 @@
     project_t = project_weight.T.reshape(3, width, width)[:, order].reshape(3 * width, width)
     output_t = output_weight.T[:, order]
     scale = jnp.tile(head_scale, sub // heads).reshape(sub, 1)
-    return pl.pallas_call(
-        functools.partial(attention_kernel, chunk=chunk, heads=heads),
-        out_shape=jax.ShapeDtypeStruct((row_count, feat, lanes), jnp.bfloat16),
-    )(
+    return (
         scale,
-        by_source,
         embed_weight.T,
         norm_gain.reshape(width, 1),
         project_t,
         output_t,
         readout_weight.T,
     )
+
+
+def post_block(by_source, chunk, prepared):
+    scale, embed_t, gain, project_t, output_t, readout_t = prepared
+    sources, row_count, levels_count, source_lanes = by_source.shape
+    lanes = sources * source_lanes
+    feat = readout_t.shape[0]
+    heads = scale.shape[0] // 2
+    return pl.pallas_call(
+        functools.partial(attention_kernel, chunk=chunk, heads=heads),
+        out_shape=jax.ShapeDtypeStruct((row_count, feat, lanes), jnp.bfloat16),
+    )(scale, by_source, embed_t, gain, project_t, output_t, readout_t)
 
 
 def convolve(padded_field, kernel):
@@ -223,6 +219,10 @@
     half_shape = (coefficients.shape[0], half, coef_halo, cols)
     own_halos = jnp.concatenate([low[split:], high[split:]], axis=0)
     pairs = [(i, i ^ 1) for i in range(lax.axis_size("mem"))]
+    prepared = prepare_weights(
+        embed_weight, norm_gain, project_weight, head_scale, output_weight, readout_weight
+    )
+    own_halos, prepared = lax.optimization_barrier((own_halos, prepared))
     other_halos = lax.ppermute(own_halos, "mem", pairs)
     count_low = low.shape[0] - split
 
@@ -271,16 +271,7 @@
     by_chunk = jnp.concatenate([by_chunk, edges], axis=1)
     by_source = lax.all_to_all(by_chunk, "mem", split_axis=0, concat_axis=0, tiled=True)
     members = chunks * members_here
-    step_result = post_block(
-        by_source,
-        tile_cols,
-        embed_weight,
-        norm_gain,
-        project_weight,
-        head_scale,
-        output_weight,
-        readout_weight,
-    )
+    step_result = post_block(by_source, tile_cols, prepared)
     feat = readout_weight.shape[1]
     inner = step_result[:tile_rows].reshape(tile_rows, feat, members, tile_cols)
     inner = jnp.transpose(inner, (2, 1, 0, 3))

time: 68.9 us -> 61.8 us (0.90)
  waiting for transfers between devices: 15.9 us -> 9.11 us
    ppermute x1, waiting for transfers between devices: 5.61 us -> 1.75 us  [on_device(): lax.ppermute(pack(starting_states[:, :, :state_halo], own[:, :, :coef_hal...]
    ppermute x1, waiting for transfers between devices: 2.1 us -> 0.01 us  [on_device(): lax.ppermute(pack(starting_states[:, :, row_total - state_halo:], own[:,...]
    all_to_all x1, waiting for transfers between devices: 3.72 us -> 2.34 us  [on_device(): lax.all_to_all(by_chunk, 'mem', split_axis=0, concat_axis=0, tiled=True)]
    optimization_barrier x0 -> x2, local copies, waits for them, and re-layouts: none -> 1.38 us  [on_device(): own_halos, prepared = lax.optimization_barrier((own_halos, prepared))]
    reshape x3 -> x2, local copies, waits for them, and re-layouts: 0.83 us -> 0.14 us  [the longest x1 0.08 us: prepare_weights(): order = jnp.arange(width).reshape(heads, head_size).T.reshape(width)]
  transfers between devices with their start and end apart: 6 -> 6, of which waited for: 5 -> 5; matrix products, arithmetic and copies ran while one was open for 13% -> 14% of each run, Pallas kernels for 0% -> 0%
where the time goes in v20:
time: 61.8 us; the launch traced here: 60.8 us
  starting transfers between devices  16.6 us (27%)
  local copies, waits for them, and re-layouts  13.8 us (22%)
  Pallas kernels  10.4 us (17%)
  waiting for transfers between devices  9.11 us (15%)
  other arithmetic  5.05 us (8%)
  matrix products  5 us (8%)
  between operations  0.74 us (1%)
    pallas_call x1, Pallas kernels, post_block(): pl.pallas_call(functools.partial(attention_kernel, chunk=chunk, heads=hea...  10.4 us
    dot_general x18, matrix products, convolve(): jnp.einsum('oc,mcij->moij', kernel[row_stencil * 3 + column_stencil], shi...  5 us
    unnamed x46, local copies, waits for them, and re-layouts  4.32 us
    ppermute x1, waiting for transfers between devices, row_padded(): high = lax.ppermute(block[..., :width, :].reshape(flat), 'row', backward)  4.11 us
    ppermute x1, starting transfers between devices, row_padded(): high = lax.ppermute(block[..., :width, :].reshape(flat), 'row', backward)  4.11 us
    all_to_all x1, starting transfers between devices, on_device(): lax.all_to_all(by_chunk, 'mem', split_axis=0, concat_axis=0, tiled=True)  3.55 us
    ppermute x1, starting transfers between devices, on_device(): lax.ppermute(pack(starting_states[:, :, row_total - state_halo:], own[:,...  3.12 us
    ppermute x1, starting transfers between devices, on_device(): lax.ppermute(pack(starting_states[:, :, :state_halo], own[:, :, :coef_hal...  3.06 us
  transfers between devices with their start and end apart: 6, of which 5 were waited for; matrix products, arithmetic and copies ran while one was open for 14% of the time, Pallas kernels for 0%

profile of v20, /device:TPU:9, one launch (start us, length us, event | category | flops | bytes accessed | tf_op | source)
XLA Modules:
  0.0 60.8 jit_solution(4349024019183619577)
XLA Ops:
  0.0 1.0 %fusion.15 = f32[3,4,8,512]{3,2,1,0:T(8,128)S(1)} fusion(s32[]{:T(128)S(6)} %select_n.70, f32[1,8,8,512]{3,2,1,0:T(8,128)} %bitcast.199, f32[1,8,8,512]{3,2,1,0:T(8,128)} %bitcast.201, f32[1,8,8,512]{3,2,1,0:T(8,128)} %bitcast.203), kind=kLoop, calls=%fused_computation.66 | loop fusion | flops 98304 | bytes 589828 | tf_op jit(solution)/shard_map/stack | solution.py:191
  1.3 3.1 %collective-permute-start = (f32[100,512]{1,0:T(8,128)S(1)}, f32[100,512]{1,0:T(8,128)S(1)}, u32[]{:S(2)}, u32[]{:S(2)}) collective-permute-start(f32[100,512]{1,0:T(8,128)S(1)} %pad_maximum_fusion.5), channel_id=1, source_target_pairs={{0,1},{1,2},{2,3},{3,4},{4,5},{5,6},{6,7},{8,9},{9,10},{10,11},{11... | collective-permute-start | bytes 614408 | tf_op jit(solution)/shard_map/ppermute | solution.py:209
  4.5 3.1 %collective-permute-start.1 = (f32[100,512]{1,0:T(8,128)S(1)}, f32[100,512]{1,0:T(8,128)S(1)}, u32[]{:S(2)}, u32[]{:S(2)}) collective-permute-start(f32[100,512]{1,0:T(8,128)S(1)} %pad_maximum_fusion.6), channel_id=1, source_target_pairs={{1,0},{2,1},{3,2},{4,3},{5,4},{6,5},{7,6},{9,8},{10,9},{11,10},{12... | collective-permute-start | bytes 614408 | tf_op jit(solution)/shard_map/ppermute | solution.py:214
  7.9 0.7 %gather_fusion = bf16[64,3,64]{2,1,0:T(4,128)(2,1)S(1)} fusion(bf16[3,64,64]{2,0,1:T(4,128)(2,1)S(1)} %copy.43, s32[1024]{0:T(1024)S(1)} %pad_clamp_fusion), kind=kCustom, calls=%fused_computation | custom fusion | bytes 49408 | tf_op jit(solution)/shard_map/gather | solution.py:127
  8.5 0.6 %copy.44 = bf16[3,64,64]{2,1,0:T(8,128)(2,1)} copy(bf16[3,64,64]{2,0,1:T(4,128)(2,1)S(1)} %bitcast.208) | data formatting | bytes 49152 | tf_op jit(solution)/shard_map/gather | solution.py:127
  9.2 0.6 %gather_fusion.1 = bf16[64,64]{1,0:T(8,128)(2,1)S(1)} fusion(bf16[64,64]{0,1:T(8,128)(2,1)S(1)} %bitcast.197, s32[1024]{0:T(1024)S(1)} %pad_clamp_fusion), kind=kCustom, calls=%fused_computation.1 | custom fusion | bytes 16640 | tf_op jit(solution)/shard_map/gather | solution.py:128
  9.8 0.7 %copy.45 = bf16[64,64]{0,1:T(8,128)(2,1)} copy(bf16[64,64]{1,0:T(8,128)(2,1)S(1)} %gather_fusion.1) | data formatting | bytes 16384 | tf_op jit(solution)/shard_map/gather | solution.py:128
  10.5 0.7 %copy.41 = bf16[8,64]{0,1:T(8,128)(2,1)} copy(bf16[8,64]{1,0:T(8,128)(2,1)S(1)} %copy-done.10) | data formatting | bytes 2048 | tf_op args[4]
  12.1 0.1 copy.102
  12.2 0.1 copy.103
  12.4 0.1 copy.104
  12.5 0.1 copy.105
  13.4 0.1 copy.111
  13.6 0.1 copy.112
  13.7 0.1 copy.113
  14.0 1.7 %collective-permute-done.1 = f32[100,512]{1,0:T(8,128)S(1)} collective-permute-done((f32[100,512]{1,0:T(8,128)S(1)}, f32[100,512]{1,0:T(8,128)S(1)}, u32[]{:S(2)}, u32[]{:S(2)}) %collective-permute-start.1) | collective-permute-done | bytes 204832 | tf_op jit(solution)/shard_map/ppermute | solution.py:214
  15.8 0.6 collective-permute-start.2
  16.8 0.6 collective-permute-done.2
  17.7 0.1 pad_maximum_fusion
  18.1 0.5 add_select_fusion.2
  18.7 0.5 add_select_fusion.1
  19.3 0.5 add_select_fusion
  19.9 0.3 select_convert_fusion.1
  20.6 0.2 reshape.211
  20.8 0.7 %pad_maximum_fusion.8 = bf16[4,9,8,256]{3,2,1,0:T(8,128)(2,1)} fusion(bf16[4,1,8,256]{3,2,1,0:T(8,128)(2,1)S(1)} %reshape.211, bf16[4,8,8,256]{3,2,1,0:T(8,128)(2,1)S(1)} %bitcast.207), kind=kLoop, calls=%fused_computation.72 | loop fusion | flops 73728 | bytes 294912 | tf_op jit(solution)/shard_map/concatenate | solution.py:271
  21.5 3.5 %all-to-all-start = ((bf16[4,9,8,256]{3,2,1,0:T(8,128)(2,1)}), bf16[4,9,8,256]{3,2,1,0:T(8,128)(2,1)S(1)}, u32[]{:S(2)}, u32[]{:S(2)}) async-start(bf16[4,9,8,256]{3,2,1,0:T(8,128)(2,1)} %pad_maximum_fusion.8), calls=%async_computation | async-start | bytes 294912 | tf_op jit(solution)/shard_map/all_to_all | solution.py:272
  25.0 0.7 %copy.50.gain_ref = f32[64,1]{1,0:T(8,128)} copy(f32[64,1]{0,1:T(1,128)S(1)} %bitcast.214) | data formatting | bytes 512 | tf_op jit(solution)/shard_map/optimization_barrier | solution.py:225
  25.7 0.7 %copy.49.hs_ref = f32[8,1]{1,0:T(8,128)} copy(f32[8,1]{0,1:T(1,128)S(1)} %reshape_tile.3) | data formatting | bytes 64 | tf_op jit(solution)/shard_map/optimization_barrier | solution.py:225
  26.4 2.3 %all-to-all-done.x_ref = bf16[4,9,8,256]{3,2,1,0:T(8,128)(2,1)S(1)} async-done(((bf16[4,9,8,256]{3,2,1,0:T(8,128)(2,1)}), bf16[4,9,8,256]{3,2,1,0:T(8,128)(2,1)S(1)}, u32[]{:S(2)}, u32[]{:S(2)}) %all-to-all-start) | async-done | bytes 147488 | tf_op jit(solution)/shard_map/all_to_all | solution.py:272
  28.7 0.7 %copy-done.8 = bf16[4,9,8,256]{3,2,1,0:T(8,128)(2,1)} copy-done((bf16[4,9,8,256]{3,2,1,0:T(8,128)(2,1)}, bf16[4,9,8,256]{3,2,1,0:T(8,128)(2,1)S(1)}, u32[]{:S(2)}) %copy-start.8) | copy-done | bytes 147480
  29.4 10.4 %shard_map.118 = bf16[9,8,1024]{2,1,0:T(8,128)(2,1)} custom-call(f32[8,1]{1,0:T(8,128)} %copy.49.hs_ref, bf16[4,9,8,256]{3,2,1,0:T(8,128)(2,1)} %copy-done.8, bf16[64,8]{1,0:T(8,128)(2,1)} %bitcast.212, f32[64,1]{1,0:T(8,128)} %copy.50.gain_ref, bf16[192,64]{1,0:T(8,128)(2,1)} %bitcast.209, bf16[64,64]{1,0:T(8,128)(2,1)} %bitcast.211, bf16[8,64]{1,0:T(8,128)(2,1)} %bitcast.213), custom_call_target="tpu_custom_call" | custom-call | tf_op jit(solution)/shard_map/pallas_call | solution.py:146
  39.8 0.7 %slice.390 = bf16[1,8,1024]{2,1,0:T(8,128)(2,1)S(1)} slice(bf16[9,8,1024]{2,1,0:T(8,128)(2,1)} %shard_map.118), slice={[8:9], [0:8], [0:1024]} | slice | bytes 32768 | tf_op jit(solution)/shard_map/slice | solution.py:278
  40.5 0.9 %copy_bitcast_fusion.2 = bf16[8,8,8,128]{3,1,2,0:T(8,128)(2,1)S(1)} fusion(bf16[9,8,1024]{2,1,0:T(8,128)(2,1)} %shard_map.118), kind=kLoop, calls=%fused_computation.91 | loop fusion | bytes 262144 | tf_op jit(solution)/shard_map/transpose | solution.py:277
  41.4 0.1 reshape_squeeze.3
  41.8 0.2 pad_maximum_fusion.4
  42.1 0.3 reshape.213
  42.3 2.2 %collective-permute-start.3 = (bf16[8,8,1152]{2,1,0:T(8,128)(2,1)S(1)}, bf16[8,8,1152]{2,1,0:T(8,128)(2,1)S(1)}, u32[]{:S(2)}, u32[]{:S(2)}) collective-permute-start(bf16[8,8,1152]{2,1,0:T(8,128)(2,1)S(1)} %reshape.213), channel_id=1, source_target_pairs={{0,1},{1,2},{2,3},{3,4},{4,5},{5,6},{6,7},{8,9},{9,10},{10,11},{11... | collective-permute-start | bytes 442376 | tf_op jit(solution)/shard_map/ppermute | solution.py:34
  44.6 4.1 %collective-permute-start.4 = (bf16[8,8,1152]{2,1,0:T(8,128)(2,1)S(1)}, bf16[8,8,1152]{2,1,0:T(8,128)(2,1)S(1)}, u32[]{:S(2)}, u32[]{:S(2)}) collective-permute-start(bf16[8,8,1152]{2,1,0:T(8,128)(2,1)S(1)} %reshape.213), channel_id=1, source_target_pairs={{1,0},{2,1},{3,2},{4,3},{5,4},{6,5},{7,6},{9,8},{10,9},{11,10},{12... | collective-permute-start | bytes 442376 | tf_op jit(solution)/shard_map/ppermute | solution.py:35
  48.8 0.3 collective-permute-done.3
  49.1 0.4 reshape.214
  49.5 4.1 %collective-permute-done.4 = bf16[8,8,1152]{2,1,0:T(8,128)(2,1)S(1)} collective-permute-done((bf16[8,8,1152]{2,1,0:T(8,128)(2,1)S(1)}, bf16[8,8,1152]{2,1,0:T(8,128)(2,1)S(1)}, u32[]{:S(2)}, u32[]{:S(2)}) %collective-permute-start.4) | collective-permute-done | bytes 147488 | tf_op jit(solution)/shard_map/ppermute | solution.py:35
  53.6 0.4 reshape.215
  54.1 0.2 pad_maximum_fusion.1
  54.3 0.4 pad_maximum_fusion.3
  54.7 0.3 fusion.12
  55.0 0.3 convolution_add_fusion.7
  55.3 0.4 convolution_add_fusion.6
  55.7 0.3 convolution_add_fusion.5
  56.0 0.4 convolution_add_fusion.4
  56.4 0.4 convolution_add_fusion.3
  56.7 0.3 convolution_add_fusion.2
  57.0 0.4 convolution_add_fusion.1
  57.4 0.5 select_convert_fusion
  57.9 0.2 fusion.26
  58.1 0.2 convolution_add_fusion.15
  58.3 0.2 convolution_add_fusion.14
  58.5 0.2 convolution_add_fusion.13
  58.7 0.2 convolution_add_fusion.12
  59.0 0.2 convolution_add_fusion.11
  59.2 0.2 convolution_add_fusion.10
  59.4 0.2 convolution_add_fusion.9
  59.6 0.3 copy-done.3
  59.9 0.2 fusion.3
  60.1 0.7 %copy.76 = bf16[8,8,8,128]{3,2,1,0:T(8,128)(2,1)} copy(bf16[8,8,8,128]{3,1,2,0:T(8,128)(2,1)S(1)} %fusion.3) | data formatting | bytes 262144 | tf_op jit(solution)/shard_map/convert_element_type | solution.py:293
  (92 shorter events, 4.3 us)
Async XLA Ops:
  0.0 9.2 %copy-start = (bf16[64,64]{1,0:T(8,128)(2,1)S(1)}, bf16[64,64]{1,0:T(8,128)(2,1)}, u32[]{:S(2)}) copy-start(bf16[64,64]{1,0:T(8,128)(2,1)} %param.20) | copy-start | bytes 24580
  0.0 1.1 %copy-start.7 = (f32[2,8,8,512]{3,2,1,0:T(8,128)S(1)}, f32[2,8,8,512]{3,2,1,0:T(8,128)}, u32[]{:S(2)}) copy-start(f32[2,8,8,512]{3,2,1,0:T(8,128)} %param.12) | copy-start | bytes 786436
  1.1 6.6 %copy-start.9 = (bf16[64,192]{1,0:T(8,128)(2,1)S(1)}, bf16[64,192]{1,0:T(8,128)(2,1)}, u32[]{:S(2)}) copy-start(bf16[64,192]{1,0:T(8,128)(2,1)} %param.18) | copy-start | bytes 73732
  1.1 9.4 %copy-start.10 = (bf16[8,64]{1,0:T(8,128)(2,1)S(1)}, bf16[8,64]{1,0:T(8,128)(2,1)}, u32[]{:S(2)}) copy-start(bf16[8,64]{1,0:T(8,128)(2,1)} %param.16) | copy-start | bytes 3076
  1.1 10.1 %copy-start.12 = (f32[4]{0:T(128)S(1)}, f32[4]{0:T(128)}, u32[]{:S(2)}) copy-start(f32[4]{0:T(128)} %param.19) | copy-start | bytes 52
  1.2 10.2 %copy-start.1 = (bf16[9,8,8]{0,2,1:T(8,128)(2,1)S(1)}, bf16[9,8,8]{0,2,1:T(8,128)(2,1)}, u32[]{:S(2)}) copy-start(bf16[9,8,8]{0,2,1:T(8,128)(2,1)} %param.22) | copy-start | bytes 3460
  1.2 11.4 %copy-start.2 = (bf16[9,8,8]{0,2,1:T(8,128)(2,1)S(1)}, bf16[9,8,8]{0,2,1:T(8,128)(2,1)}, u32[]{:S(2)}) copy-start(bf16[9,8,8]{0,2,1:T(8,128)(2,1)} %param.23) | copy-start | bytes 3460
  1.3 12.8 %collective-permute-start = (f32[100,512]{1,0:T(8,128)S(1)}, f32[100,512]{1,0:T(8,128)S(1)}, u32[]{:S(2)}, u32[]{:S(2)}) collective-permute-start(f32[100,512]{1,0:T(8,128)S(1)} %pad_maximum_fusion.5), channel_id=1, source_target_pairs={{0,1},{1,2},{2,3},{3,4},{4,5},{5,6},{6,7},{8,9},{9,10},{10,11},{11... | collective-permute-start | bytes 614408 | tf_op jit(solution)/shard_map/ppermute | solution.py:209
  4.5 11.3 %collective-permute-start.1 = (f32[100,512]{1,0:T(8,128)S(1)}, f32[100,512]{1,0:T(8,128)S(1)}, u32[]{:S(2)}, u32[]{:S(2)}) collective-permute-start(f32[100,512]{1,0:T(8,128)S(1)} %pad_maximum_fusion.6), channel_id=1, source_target_pairs={{1,0},{2,1},{3,2},{4,3},{5,4},{6,5},{7,6},{9,8},{10,9},{11,10},{12... | collective-permute-start | bytes 614408 | tf_op jit(solution)/shard_map/ppermute | solution.py:214
  15.8 1.6 %collective-permute-start.2 = (f32[72,512]{1,0:T(8,128)S(1)}, f32[72,512]{1,0:T(8,128)S(1)}, u32[]{:S(2)}, u32[]{:S(2)}) collective-permute-start(f32[72,512]{1,0:T(8,128)S(1)} %pad_maximum_fusion.7), channel_id=1, source_target_pairs={{0,8},{8,0},{16,24},{24,16},{1,9},{9,1},{17,25},{25,17},{2,10},{10... | collective-permute-start | bytes 442376 | tf_op jit(solution)/shard_map/ppermute | solution.py:226
  16.7 0.9 %copy-start.4 = (f32[8,8,512]{2,1,0:T(8,128)S(1)}, f32[8,8,512]{2,1,0:T(8,128)}, u32[]{:S(2)}) copy-start(f32[8,8,512]{2,1,0:T(8,128)} %param.13) | copy-start | bytes 393220
  16.7 1.0 %copy-start.5 = (f32[8,8,512]{2,1,0:T(8,128)S(1)}, f32[8,8,512]{2,1,0:T(8,128)}, u32[]{:S(2)}) copy-start(f32[8,8,512]{2,1,0:T(8,128)} %param.14) | copy-start | bytes 393220
  16.7 1.0 %copy-start.6 = (f32[8,8,512]{2,1,0:T(8,128)S(1)}, f32[8,8,512]{2,1,0:T(8,128)}, u32[]{:S(2)}) copy-start(f32[8,8,512]{2,1,0:T(8,128)} %param.15) | copy-start | bytes 393220
  20.2 4.8 %copy-start.11 = (f32[64]{0:T(128)S(1)}, f32[64]{0:T(128)}, u32[]{:S(2)}) copy-start(f32[64]{0:T(128)} %param.17) | copy-start | bytes 772
  21.5 7.3 %all-to-all-start = ((bf16[4,9,8,256]{3,2,1,0:T(8,128)(2,1)}), bf16[4,9,8,256]{3,2,1,0:T(8,128)(2,1)S(1)}, u32[]{:S(2)}, u32[]{:S(2)}) async-start(bf16[4,9,8,256]{3,2,1,0:T(8,128)(2,1)} %pad_maximum_fusion.8), calls=%async_computation | async-start | bytes 294912 | tf_op jit(solution)/shard_map/all_to_all | solution.py:272
  28.7 0.7 %copy-start.8 = (bf16[4,9,8,256]{3,2,1,0:T(8,128)(2,1)}, bf16[4,9,8,256]{3,2,1,0:T(8,128)(2,1)S(1)}, u32[]{:S(2)}) copy-start(bf16[4,9,8,256]{3,2,1,0:T(8,128)(2,1)S(1)} %all-to-all-done.x_ref) | copy-start | bytes 442372
  42.3 6.8 %collective-permute-start.3 = (bf16[8,8,1152]{2,1,0:T(8,128)(2,1)S(1)}, bf16[8,8,1152]{2,1,0:T(8,128)(2,1)S(1)}, u32[]{:S(2)}, u32[]{:S(2)}) collective-permute-start(bf16[8,8,1152]{2,1,0:T(8,128)(2,1)S(1)} %reshape.213), channel_id=1, source_target_pairs={{0,1},{1,2},{2,3},{3,4},{4,5},{5,6},{6,7},{8,9},{9,10},{10,11},{11... | collective-permute-start | bytes 442376 | tf_op jit(solution)/shard_map/ppermute | solution.py:34
  44.6 9.1 %collective-permute-start.4 = (bf16[8,8,1152]{2,1,0:T(8,128)(2,1)S(1)}, bf16[8,8,1152]{2,1,0:T(8,128)(2,1)S(1)}, u32[]{:S(2)}, u32[]{:S(2)}) collective-permute-start(bf16[8,8,1152]{2,1,0:T(8,128)(2,1)S(1)} %reshape.213), channel_id=1, source_target_pairs={{1,0},{2,1},{3,2},{4,3},{5,4},{6,5},{7,6},{9,8},{10,9},{11,10},{12... | collective-permute-start | bytes 442376 | tf_op jit(solution)/shard_map/ppermute | solution.py:35
  59.0 0.9 %copy-start.3 = (bf16[9,8,1024]{2,1,0:T(8,128)(2,1)S(1)}, bf16[9,8,1024]{2,1,0:T(8,128)(2,1)}, u32[]{:S(2)}) copy-start(bf16[9,8,1024]{2,1,0:T(8,128)(2,1)} %shard_map.118) | copy-start | bytes 442372

commit v21 on v20

--- a/solution.py
+++ b/solution.py
@@ -273,16 +273,28 @@
     members = chunks * members_here
     step_result = post_block(by_source, tile_cols, prepared)
     feat = readout_weight.shape[1]
-    inner = step_result[:tile_rows].reshape(tile_rows, feat, members, tile_cols)
-    inner = jnp.transpose(inner, (2, 1, 0, 3))
-    outer = step_result[tile_rows].reshape(feat, members, tile_rows, 2 * halo)
-    outer = jnp.transpose(outer, (1, 0, 2, 3))
     mem_index = lax.axis_index("mem")
-    left = jnp.where(mem_index > 0, outer[..., :halo], 0)
-    right = jnp.where(mem_index < chunks - 1, outer[..., halo:], 0)
-    features_wide = jnp.concatenate([left, inner, right], axis=-1)
+
+    def widen(result):
+        inner = result[:tile_rows].reshape(tile_rows, feat, members, tile_cols)
+        inner = jnp.transpose(inner, (2, 1, 0, 3))
+        outer = result[tile_rows].reshape(feat, members, tile_rows, 2 * halo)
+        outer = jnp.transpose(outer, (1, 0, 2, 3))
+        left = jnp.where(mem_index > 0, outer[..., :halo], 0)
+        right = jnp.where(mem_index < chunks - 1, outer[..., halo:], 0)
+        return inner, jnp.concatenate([left, inner, right], axis=-1)
+
+    inner, features_wide = widen(step_result)
     span = DILATION_SPAN
-    padded_feature = row_padded(features_wide, halo)
+    if halo == tile_rows:
+        count = lax.axis_size("row")
+        forward = [(i, i + 1) for i in range(count - 1)]
+        backward = [(target, source) for source, target in forward]
+        _, from_low = widen(lax.ppermute(step_result, "row", forward))
+        _, from_high = widen(lax.ppermute(step_result, "row", backward))
+        padded_feature = jnp.concatenate([from_low, features_wide, from_high], axis=2)
+    else:
+        padded_feature = row_padded(features_wide, halo)
     first = jax.nn.silu(convolve(padded_feature, first_kernel))
     row_ids = lax.axis_index("row") * tile_rows - span + jnp.arange(tile_rows + 2 * span)
     col_ids = mem_index * tile_cols - span + jnp.arange(tile_cols + 2 * span)

time: 61.8 us -> 60 us (0.971)
  local copies, waits for them, and re-layouts: 13.8 us -> 12.1 us
    ppermute x1, waiting for transfers between devices: 1.75 us -> 4.15 us  [on_device(): lax.ppermute(pack(starting_states[:, :, :state_halo], own[:, :, :coef_hal...]
    all_to_all x1, waiting for transfers between devices: 2.34 us -> 0.01 us  [on_device(): lax.all_to_all(by_chunk, 'mem', split_axis=0, concat_axis=0, tiled=True)]
    reshape x5 -> x0, local copies, waits for them, and re-layouts: 1.07 us -> none  [the longest x2 0.41 us: row_padded(): high.reshape(shape)]
    transpose x1 -> x3, local copies, waits for them, and re-layouts: 0.93 us -> 0.07 us  [widen(): inner = jnp.transpose(inner, (2, 1, 0, 3))]
  transfers between devices with their start and end apart: 6 -> 6, of which waited for: 5 -> 3; matrix products, arithmetic and copies ran while one was open for 14% -> 16% of each run, Pallas kernels for 0% -> 0%
where the time goes in v21:
time: 60 us; the launch traced here: 59.2 us
  starting transfers between devices  16.8 us (28%)
  local copies, waits for them, and re-layouts  12.1 us (20%)
  Pallas kernels  10.4 us (17%)
  waiting for transfers between devices  8.61 us (14%)
  other arithmetic  5.56 us (9%)
  matrix products  5.01 us (8%)
  between operations  0.77 us (1%)
    pallas_call x1, Pallas kernels, post_block(): pl.pallas_call(functools.partial(attention_kernel, chunk=chunk, heads=hea...  10.4 us
    dot_general x18, matrix products, convolve(): jnp.einsum('oc,mcij->moij', kernel[row_stencil * 3 + column_stencil], shi...  5.01 us
    ppermute x1, waiting for transfers between devices, on_device(): lax.ppermute(pack(starting_states[:, :, :state_halo], own[:, :, :coef_hal...  4.15 us
    ppermute x1, starting transfers between devices, on_device(): _, from_high = widen(lax.ppermute(step_result, 'row', backward))  4.12 us
    unnamed x46, local copies, waits for them, and re-layouts  4.08 us
    ppermute x1, waiting for transfers between devices, on_device(): _, from_high = widen(lax.ppermute(step_result, 'row', backward))  3.87 us
    all_to_all x1, starting transfers between devices, on_device(): lax.all_to_all(by_chunk, 'mem', split_axis=0, concat_axis=0, tiled=True)  3.55 us
    ppermute x1, starting transfers between devices, on_device(): lax.ppermute(pack(starting_states[:, :, row_total - state_halo:], own[:,...  3.12 us
  transfers between devices with their start and end apart: 6, of which 3 were waited for; matrix products, arithmetic and copies ran while one was open for 16% of the time, Pallas kernels for 0%

profile of v21, /device:TPU:9, one launch (start us, length us, event | category | flops | bytes accessed | tf_op | source)
XLA Modules:
  0.0 59.2 jit_solution(3817106555701733104)
XLA Ops:
  0.0 1.0 %fusion.15 = f32[3,4,8,512]{3,2,1,0:T(8,128)S(1)} fusion(s32[]{:T(128)S(6)} %select_n.86, f32[1,8,8,512]{3,2,1,0:T(8,128)} %bitcast.213, f32[1,8,8,512]{3,2,1,0:T(8,128)} %bitcast.215, f32[1,8,8,512]{3,2,1,0:T(8,128)} %bitcast.217), kind=kLoop, calls=%fused_computation.65 | loop fusion | flops 98304 | bytes 589828 | tf_op jit(solution)/shard_map/stack | solution.py:191
  1.3 3.1 %collective-permute-start = (f32[100,512]{1,0:T(8,128)S(1)}, f32[100,512]{1,0:T(8,128)S(1)}, u32[]{:S(2)}, u32[]{:S(2)}) collective-permute-start(f32[100,512]{1,0:T(8,128)S(1)} %pad_maximum_fusion.2), channel_id=1, source_target_pairs={{0,1},{1,2},{2,3},{3,4},{4,5},{5,6},{6,7},{8,9},{9,10},{10,11},{11... | collective-permute-start | bytes 614408 | tf_op jit(solution)/shard_map/ppermute | solution.py:209
  4.5 3.1 %collective-permute-start.1 = (f32[100,512]{1,0:T(8,128)S(1)}, f32[100,512]{1,0:T(8,128)S(1)}, u32[]{:S(2)}, u32[]{:S(2)}) collective-permute-start(f32[100,512]{1,0:T(8,128)S(1)} %pad_maximum_fusion.3), channel_id=1, source_target_pairs={{1,0},{2,1},{3,2},{4,3},{5,4},{6,5},{7,6},{9,8},{10,9},{11,10},{12... | collective-permute-start | bytes 614408 | tf_op jit(solution)/shard_map/ppermute | solution.py:214
  7.9 0.7 %gather_fusion = bf16[64,3,64]{2,1,0:T(4,128)(2,1)S(1)} fusion(bf16[3,64,64]{2,0,1:T(4,128)(2,1)S(1)} %copy.47, s32[1024]{0:T(1024)S(1)} %pad_clamp_fusion), kind=kCustom, calls=%fused_computation | custom fusion | bytes 49408 | tf_op jit(solution)/shard_map/gather | solution.py:127
  8.5 0.6 %copy.48 = bf16[3,64,64]{2,1,0:T(8,128)(2,1)} copy(bf16[3,64,64]{2,0,1:T(4,128)(2,1)S(1)} %bitcast.224) | data formatting | bytes 49152 | tf_op jit(solution)/shard_map/gather | solution.py:127
  9.2 0.6 %gather_fusion.1 = bf16[64,64]{1,0:T(8,128)(2,1)S(1)} fusion(bf16[64,64]{0,1:T(8,128)(2,1)S(1)} %bitcast.211, s32[1024]{0:T(1024)S(1)} %pad_clamp_fusion), kind=kCustom, calls=%fused_computation.1 | custom fusion | bytes 16640 | tf_op jit(solution)/shard_map/gather | solution.py:128
  9.8 0.7 %copy.49 = bf16[64,64]{0,1:T(8,128)(2,1)} copy(bf16[64,64]{1,0:T(8,128)(2,1)S(1)} %gather_fusion.1) | data formatting | bytes 16384 | tf_op jit(solution)/shard_map/gather | solution.py:128
  10.5 0.7 %copy.45 = bf16[8,64]{0,1:T(8,128)(2,1)} copy(bf16[8,64]{1,0:T(8,128)(2,1)S(1)} %copy-done.10) | data formatting | bytes 2048 | tf_op args[4]
  11.6 4.2 %collective-permute-done.1 = f32[100,512]{1,0:T(8,128)S(1)} collective-permute-done((f32[100,512]{1,0:T(8,128)S(1)}, f32[100,512]{1,0:T(8,128)S(1)}, u32[]{:S(2)}, u32[]{:S(2)}) %collective-permute-start.1) | collective-permute-done | bytes 204832 | tf_op jit(solution)/shard_map/ppermute | solution.py:214
  15.8 0.6 collective-permute-start.2
  16.8 0.6 collective-permute-done.2
  17.7 0.1 pad_maximum_fusion
  18.1 0.5 add_select_fusion.2
  18.7 0.5 add_select_fusion.1
  19.3 0.5 add_select_fusion
  19.9 0.3 select_convert_fusion.1
  20.6 0.2 reshape.207
  20.8 0.7 %pad_maximum_fusion.5 = bf16[4,9,8,256]{3,2,1,0:T(8,128)(2,1)} fusion(bf16[4,1,8,256]{3,2,1,0:T(8,128)(2,1)S(1)} %reshape.207, bf16[4,8,8,256]{3,2,1,0:T(8,128)(2,1)S(1)} %bitcast.223), kind=kLoop, calls=%fused_computation.71 | loop fusion | flops 73728 | bytes 294912 | tf_op jit(solution)/shard_map/concatenate | solution.py:271
  21.5 3.5 %all-to-all-start = ((bf16[4,9,8,256]{3,2,1,0:T(8,128)(2,1)}), bf16[4,9,8,256]{3,2,1,0:T(8,128)(2,1)S(1)}, u32[]{:S(2)}, u32[]{:S(2)}) async-start(bf16[4,9,8,256]{3,2,1,0:T(8,128)(2,1)} %pad_maximum_fusion.5), calls=%async_computation | async-start | bytes 294912 | tf_op jit(solution)/shard_map/all_to_all | solution.py:272
  25.7 0.1 copy.105
  25.9 0.1 copy.106
  26.0 0.1 copy.107
  26.1 0.1 copy.108
  26.3 0.1 copy.109
  26.4 0.1 copy.110
  26.6 0.1 copy.111
  26.7 0.1 copy.112
  26.8 0.1 copy.113
  27.0 0.1 copy.114
  27.1 0.1 copy.115
  27.2 0.1 copy.116
  27.4 0.1 copy.117
  27.5 0.7 %copy.54.gain_ref = f32[64,1]{1,0:T(8,128)} copy(f32[64,1]{0,1:T(1,128)S(1)} %bitcast.230) | data formatting | bytes 512 | tf_op jit(solution)/shard_map/optimization_barrier | solution.py:225
  28.2 0.7 %copy.53.hs_ref = f32[8,1]{1,0:T(8,128)} copy(f32[8,1]{0,1:T(1,128)S(1)} %reshape_tile.3) | data formatting | bytes 64 | tf_op jit(solution)/shard_map/optimization_barrier | solution.py:225
  28.9 0.7 %copy-done.8 = bf16[4,9,8,256]{3,2,1,0:T(8,128)(2,1)} copy-done((bf16[4,9,8,256]{3,2,1,0:T(8,128)(2,1)}, bf16[4,9,8,256]{3,2,1,0:T(8,128)(2,1)S(1)}, u32[]{:S(2)}) %copy-start.8) | copy-done | bytes 147480
  29.6 10.4 %shard_map.118 = bf16[9,8,1024]{2,1,0:T(8,128)(2,1)} custom-call(f32[8,1]{1,0:T(8,128)} %copy.53.hs_ref, bf16[4,9,8,256]{3,2,1,0:T(8,128)(2,1)} %copy-done.8, bf16[64,8]{1,0:T(8,128)(2,1)} %bitcast.228, f32[64,1]{1,0:T(8,128)} %copy.54.gain_ref, bf16[192,64]{1,0:T(8,128)(2,1)} %bitcast.225, bf16[64,64]{1,0:T(8,128)(2,1)} %bitcast.227, bf16[8,64]{1,0:T(8,128)(2,1)} %bitcast.229), custom_call_target="tpu_custom_call" | custom-call | tf_op jit(solution)/shard_map/pallas_call | solution.py:146
  39.9 2.4 %collective-permute-start.3 = (bf16[9,8,1024]{2,1,0:T(8,128)(2,1)}, bf16[9,8,1024]{2,1,0:T(8,128)(2,1)S(1)}, u32[]{:S(2)}, u32[]{:S(2)}) collective-permute-start(bf16[9,8,1024]{2,1,0:T(8,128)(2,1)} %shard_map.118), channel_id=1, source_target_pairs={{0,1},{1,2},{2,3},{3,4},{4,5},{5,6},{6,7},{8,9},{9,10},{10,11},{11... | collective-permute-start | bytes 442376 | tf_op jit(solution)/shard_map/ppermute | solution.py:293
  42.3 4.1 %collective-permute-start.4 = (bf16[9,8,1024]{2,1,0:T(8,128)(2,1)}, bf16[9,8,1024]{2,1,0:T(8,128)(2,1)S(1)}, u32[]{:S(2)}, u32[]{:S(2)}) collective-permute-start(bf16[9,8,1024]{2,1,0:T(8,128)(2,1)} %shard_map.118), channel_id=1, source_target_pairs={{1,0},{2,1},{3,2},{4,3},{5,4},{6,5},{7,6},{9,8},{10,9},{11,10},{12... | collective-permute-start | bytes 442376 | tf_op jit(solution)/shard_map/ppermute | solution.py:294
  46.4 0.7 %slice.426 = bf16[1,8,1024]{2,1,0:T(8,128)(2,1)S(1)} slice(bf16[9,8,1024]{2,1,0:T(8,128)(2,1)} %shard_map.118), slice={[8:9], [0:8], [0:1024]} | slice | bytes 32768 | tf_op jit(solution)/shard_map/slice | solution.py:281
  47.2 0.2 reshape_squeeze.10
  47.6 0.1 reshape_squeeze.9
  48.0 3.9 %collective-permute-done.4 = bf16[9,8,1024]{2,1,0:T(8,128)(2,1)S(1)} collective-permute-done((bf16[9,8,1024]{2,1,0:T(8,128)(2,1)}, bf16[9,8,1024]{2,1,0:T(8,128)(2,1)S(1)}, u32[]{:S(2)}, u32[]{:S(2)}) %collective-permute-start.4) | collective-permute-done | bytes 147488 | tf_op jit(solution)/shard_map/ppermute | solution.py:294
  51.8 0.2 reshape_squeeze.11
  52.3 0.5 maximum_maximum_fusion
  52.7 0.6 %maximum_maximum_fusion.2 = (bf16[8,8,16,144]{3,1,2,0:T(8,128)(2,1)S(1)}, bf16[8,8,16,144]{3,1,2,0:T(8,128)(2,1)S(1)}) fusion(bf16[8,8,8,8]{3,1,2,0:T(8,128)(2,1)S(1)} %get-tuple-element.39, bf16[8,8,8,128]{3,1,2,0:T(8,128)(2,1)S(1)} %copy_bitcast_fusion.1, bf16[8,8,8,8]{3,1,2,0:T(8,128)(2,1)S(1)} %get-tuple-element.38, ...), kind=kLoop, calls=%fused_computation.43 | loop fusion | flops 3538944 | bytes 1032192 | tf_op jit(solution)/shard_map/concatenate | solution.py:295
  53.4 0.3 fusion.12
  53.7 0.4 convolution_add_fusion.7
  54.0 0.3 convolution_add_fusion.6
  54.4 0.3 convolution_add_fusion.5
  54.7 0.3 convolution_add_fusion.4
  55.0 0.4 convolution_add_fusion.3
  55.4 0.3 convolution_add_fusion.2
  55.7 0.4 convolution_add_fusion.1
  56.0 0.5 select_convert_fusion
  56.6 0.2 fusion.26
  56.8 0.2 convolution_add_fusion.15
  57.0 0.2 convolution_add_fusion.14
  57.2 0.2 convolution_add_fusion.13
  57.4 0.2 convolution_add_fusion.12
  57.6 0.2 convolution_add_fusion.11
  57.9 0.2 convolution_add_fusion.10
  58.0 0.2 convolution_add_fusion.9
  58.3 0.2 fusion.3
  58.5 0.7 %copy.79 = bf16[8,8,8,128]{3,2,1,0:T(8,128)(2,1)} copy(bf16[8,8,8,128]{3,1,2,0:T(8,128)(2,1)S(1)} %fusion.3) | data formatting | bytes 262144 | tf_op jit(solution)/shard_map/convert_element_type | solution.py:305
  (95 shorter events, 3.8 us)
Async XLA Ops:
  0.0 9.2 %copy-start = (bf16[64,64]{1,0:T(8,128)(2,1)S(1)}, bf16[64,64]{1,0:T(8,128)(2,1)}, u32[]{:S(2)}) copy-start(bf16[64,64]{1,0:T(8,128)(2,1)} %param.20) | copy-start | bytes 24580
  0.0 1.1 %copy-start.7 = (f32[2,8,8,512]{3,2,1,0:T(8,128)S(1)}, f32[2,8,8,512]{3,2,1,0:T(8,128)}, u32[]{:S(2)}) copy-start(f32[2,8,8,512]{3,2,1,0:T(8,128)} %param.12) | copy-start | bytes 786436
  1.1 6.6 %copy-start.9 = (bf16[64,192]{1,0:T(8,128)(2,1)S(1)}, bf16[64,192]{1,0:T(8,128)(2,1)}, u32[]{:S(2)}) copy-start(bf16[64,192]{1,0:T(8,128)(2,1)} %param.18) | copy-start | bytes 73732
  1.1 9.4 %copy-start.10 = (bf16[8,64]{1,0:T(8,128)(2,1)S(1)}, bf16[8,64]{1,0:T(8,128)(2,1)}, u32[]{:S(2)}) copy-start(bf16[8,64]{1,0:T(8,128)(2,1)} %param.16) | copy-start | bytes 3076
  1.1 10.1 %copy-start.12 = (f32[4]{0:T(128)S(1)}, f32[4]{0:T(128)}, u32[]{:S(2)}) copy-start(f32[4]{0:T(128)} %param.19) | copy-start | bytes 52
  1.2 10.2 %copy-start.1 = (bf16[9,8,8]{0,2,1:T(8,128)(2,1)S(1)}, bf16[9,8,8]{0,2,1:T(8,128)(2,1)}, u32[]{:S(2)}) copy-start(bf16[9,8,8]{0,2,1:T(8,128)(2,1)} %param.22) | copy-start | bytes 3460
  1.2 10.3 %copy-start.2 = (bf16[9,8,8]{0,2,1:T(8,128)(2,1)S(1)}, bf16[9,8,8]{0,2,1:T(8,128)(2,1)}, u32[]{:S(2)}) copy-start(bf16[9,8,8]{0,2,1:T(8,128)(2,1)} %param.23) | copy-start | bytes 3460
  1.3 10.4 %collective-permute-start = (f32[100,512]{1,0:T(8,128)S(1)}, f32[100,512]{1,0:T(8,128)S(1)}, u32[]{:S(2)}, u32[]{:S(2)}) collective-permute-start(f32[100,512]{1,0:T(8,128)S(1)} %pad_maximum_fusion.2), channel_id=1, source_target_pairs={{0,1},{1,2},{2,3},{3,4},{4,5},{5,6},{6,7},{8,9},{9,10},{10,11},{11... | collective-permute-start | bytes 614408 | tf_op jit(solution)/shard_map/ppermute | solution.py:209
  4.5 11.3 %collective-permute-start.1 = (f32[100,512]{1,0:T(8,128)S(1)}, f32[100,512]{1,0:T(8,128)S(1)}, u32[]{:S(2)}, u32[]{:S(2)}) collective-permute-start(f32[100,512]{1,0:T(8,128)S(1)} %pad_maximum_fusion.3), channel_id=1, source_target_pairs={{1,0},{2,1},{3,2},{4,3},{5,4},{6,5},{7,6},{9,8},{10,9},{11,10},{12... | collective-permute-start | bytes 614408 | tf_op jit(solution)/shard_map/ppermute | solution.py:214
  15.8 1.6 %collective-permute-start.2 = (f32[72,512]{1,0:T(8,128)S(1)}, f32[72,512]{1,0:T(8,128)S(1)}, u32[]{:S(2)}, u32[]{:S(2)}) collective-permute-start(f32[72,512]{1,0:T(8,128)S(1)} %pad_maximum_fusion.4), channel_id=1, source_target_pairs={{0,8},{8,0},{16,24},{24,16},{1,9},{9,1},{17,25},{25,17},{2,10},{10... | collective-permute-start | bytes 442376 | tf_op jit(solution)/shard_map/ppermute | solution.py:226
  16.7 0.9 %copy-start.4 = (f32[8,8,512]{2,1,0:T(8,128)S(1)}, f32[8,8,512]{2,1,0:T(8,128)}, u32[]{:S(2)}) copy-start(f32[8,8,512]{2,1,0:T(8,128)} %param.13) | copy-start | bytes 393220
  16.7 1.0 %copy-start.5 = (f32[8,8,512]{2,1,0:T(8,128)S(1)}, f32[8,8,512]{2,1,0:T(8,128)}, u32[]{:S(2)}) copy-start(f32[8,8,512]{2,1,0:T(8,128)} %param.14) | copy-start | bytes 393220
  16.7 1.0 %copy-start.6 = (f32[8,8,512]{2,1,0:T(8,128)S(1)}, f32[8,8,512]{2,1,0:T(8,128)}, u32[]{:S(2)}) copy-start(f32[8,8,512]{2,1,0:T(8,128)} %param.15) | copy-start | bytes 393220
  20.3 7.2 %copy-start.11 = (f32[64]{0:T(128)S(1)}, f32[64]{0:T(128)}, u32[]{:S(2)}) copy-start(f32[64]{0:T(128)} %param.17) | copy-start | bytes 772
  21.5 7.4 %all-to-all-start = ((bf16[4,9,8,256]{3,2,1,0:T(8,128)(2,1)}), bf16[4,9,8,256]{3,2,1,0:T(8,128)(2,1)S(1)}, u32[]{:S(2)}, u32[]{:S(2)}) async-start(bf16[4,9,8,256]{3,2,1,0:T(8,128)(2,1)} %pad_maximum_fusion.5), calls=%async_computation | async-start | bytes 294912 | tf_op jit(solution)/shard_map/all_to_all | solution.py:272
  28.9 0.7 %copy-start.8 = (bf16[4,9,8,256]{3,2,1,0:T(8,128)(2,1)}, bf16[4,9,8,256]{3,2,1,0:T(8,128)(2,1)S(1)}, u32[]{:S(2)}) copy-start(bf16[4,9,8,256]{3,2,1,0:T(8,128)(2,1)S(1)} %all-to-all-done.x_ref) | copy-start | bytes 442372
  39.9 7.6 %copy-start.3 = (bf16[9,8,1024]{2,1,0:T(8,128)(2,1)S(1)}, bf16[9,8,1024]{2,1,0:T(8,128)(2,1)}, u32[]{:S(2)}) copy-start(bf16[9,8,1024]{2,1,0:T(8,128)(2,1)} %shard_map.118) | copy-start | bytes 442372
  39.9 7.6 %collective-permute-start.3 = (bf16[9,8,1024]{2,1,0:T(8,128)(2,1)}, bf16[9,8,1024]{2,1,0:T(8,128)(2,1)S(1)}, u32[]{:S(2)}, u32[]{:S(2)}) collective-permute-start(bf16[9,8,1024]{2,1,0:T(8,128)(2,1)} %shard_map.118), channel_id=1, source_target_pairs={{0,1},{1,2},{2,3},{3,4},{4,5},{5,6},{6,7},{8,9},{9,10},{10,11},{11... | collective-permute-start | bytes 442376 | tf_op jit(solution)/shard_map/ppermute | solution.py:293
  42.3 9.5 %collective-permute-start.4 = (bf16[9,8,1024]{2,1,0:T(8,128)(2,1)}, bf16[9,8,1024]{2,1,0:T(8,128)(2,1)S(1)}, u32[]{:S(2)}, u32[]{:S(2)}) collective-permute-start(bf16[9,8,1024]{2,1,0:T(8,128)(2,1)} %shard_map.118), channel_id=1, source_target_pairs={{1,0},{2,1},{3,2},{4,3},{5,4},{6,5},{7,6},{9,8},{10,9},{11,10},{12... | collective-permute-start | bytes 442376 | tf_op jit(solution)/shard_map/ppermute | solution.py:294

commit v22 on v21

--- a/solution.py
+++ b/solution.py
@@ -34,6 +34,24 @@
     low = lax.ppermute(block[..., rows - width :, :].reshape(flat), "row", forward)
     high = lax.ppermute(block[..., :width, :].reshape(flat), "row", backward)
     return jnp.concatenate([low.reshape(shape), block, high.reshape(shape)], axis=-2)
+
+
+def advance_rows_first(padded_field, wind_east, wind_north, diffusivity):
+    middle = padded_field[1:-1]
+    northern = padded_field[2:]
+    southern = padded_field[:-2]
+    widths = [(0, 0)] * (middle.ndim - 1) + [(1, 1)]
+    widened = jnp.pad(middle, widths)
+    eastern = widened[..., 2:]
+    western = widened[..., :-2]
+    drifting = 0.2 * jnp.tanh(middle)
+    laplace = northern + southern + eastern + western - 4.0 * middle
+    return (
+        middle
+        - (wind_east + drifting) * (eastern - western) * 0.5
+        - (wind_north + drifting) * (northern - southern) * 0.5
+        + diffusivity * laplace
+    )
 
 
 def advance(padded_field, wind_east, wind_north, diffusivity):
@@ -237,35 +255,44 @@
 
     coef_low = levels_of(own_halos[:count_low], other_halos[:count_low])
     coef_high = levels_of(own_halos[count_low:], other_halos[count_low:])
+    rows_first = lambda x: jnp.transpose(x, (2, 0, 1, 3))
     gridded_quantity_list = jnp.concatenate(
-        [low[:split].reshape(state_shape), starting_states, high[:split].reshape(state_shape)],
-        axis=2,
-    )
-    coef_rows = jnp.concatenate([coef_low, coefficients, coef_high], axis=2)
+        [
+            rows_first(low[:split].reshape(state_shape)),
+            rows_first(starting_states),
+            rows_first(high[:split].reshape(state_shape)),
+        ],
+        axis=0,
+    )
+    coef_rows = jnp.concatenate(
+        [rows_first(coef_low), rows_first(coefficients), rows_first(coef_high)], axis=0
+    )
     first_row = lax.axis_index("row") * row_total - STEPS
     all_rows = lax.axis_size("row") * row_total
     for section in range(STEPS):
         out_rows = row_total + 2 * (STEPS - section - 1)
         offset = section + 1
-        window = coef_rows[:, :, section : section + out_rows]
-        gridded_quantity_list = advance(gridded_quantity_list, window[0], window[1], window[2])
+        window = coef_rows[section : section + out_rows]
+        gridded_quantity_list = advance_rows_first(
+            gridded_quantity_list, window[:, 0:1], window[:, 1:2], window[:, 2:3]
+        )
         row_ids = first_row + offset + jnp.arange(out_rows)
         inside = (row_ids >= 0) & (row_ids < all_rows)
-        gridded_quantity_list = jnp.where(inside[None, None, :, None], gridded_quantity_list, 0.0)
+        gridded_quantity_list = jnp.where(inside[:, None, None, None], gridded_quantity_list, 0.0)
     predicted_states = gridded_quantity_list.astype(jnp.bfloat16)
     chunks = lax.axis_size("mem")
-    _, levels_count, tile_rows, cols_all = predicted_states.shape
+    tile_rows, _, levels_count, cols_all = predicted_states.shape
     tile_cols = cols_all // chunks
     halo = 2 * DILATION_SPAN
-    by_chunk = predicted_states.reshape(members_here, levels_count, tile_rows, chunks, tile_cols)
-    by_chunk = jnp.transpose(by_chunk, (3, 2, 1, 0, 4)).reshape(
+    split_cols = (tile_rows, members_here, levels_count, chunks, tile_cols)
+    by_chunk = jnp.transpose(predicted_states.reshape(split_cols), (3, 0, 2, 1, 4)).reshape(
         chunks, tile_rows, levels_count, members_here * tile_cols
     )
     wide = jnp.pad(predicted_states, ((0, 0), (0, 0), (0, 0), (halo, halo)))
-    lefts = wide[..., :cols_all].reshape(members_here, levels_count, tile_rows, chunks, tile_cols)
-    rights = wide[..., 2 * halo :].reshape(members_here, levels_count, tile_rows, chunks, tile_cols)
+    lefts = wide[..., :cols_all].reshape(split_cols)
+    rights = wide[..., 2 * halo :].reshape(split_cols)
     edges = jnp.concatenate([lefts[..., :halo], rights[..., tile_cols - halo :]], axis=-1)
-    edges = jnp.transpose(edges, (3, 1, 0, 2, 4)).reshape(
+    edges = jnp.transpose(edges, (3, 2, 1, 0, 4)).reshape(
         chunks, 1, levels_count, members_here * tile_rows * 2 * halo
     )
     by_chunk = jnp.concatenate([by_chunk, edges], axis=1)

time: 60 us -> 60.1 us (level)
    transpose x1 -> x3, other arithmetic: 0.11 us -> 1.37 us  [the longest x2 1.26 us: on_device(): rows_first = lambda x: jnp.transpose(x, (2, 0, 1, 3))]
    another operation x1 -> x0, other arithmetic: 0.96 us -> none  [on_device(): coefficients = jnp.stack([wind_east, wind_north, diffusivity])]
    unnamed x46 -> x40, local copies, waits for them, and re-layouts: 4.08 us -> 3.91 us
    select_n x4 -> x3, other arithmetic: 1.66 us -> 1.56 us  [on_device(): jnp.where(inside[:, None, None, None], gridded_quantity_list, 0.0)]
where the time goes in v22:
time: 60.1 us; the launch traced here: 59.3 us
  starting transfers between devices  16.9 us (28%)
  local copies, waits for them, and re-layouts  12 us (20%)
  Pallas kernels  10.4 us (17%)
  waiting for transfers between devices  8.57 us (14%)
  other arithmetic  5.76 us (10%)
  matrix products  5 us (8%)
  between operations  0.76 us (1%)
    pallas_call x1, Pallas kernels, post_block(): pl.pallas_call(functools.partial(attention_kernel, chunk=chunk, heads=hea...  10.4 us
    dot_general x18, matrix products, convolve(): jnp.einsum('oc,mcij->moij', kernel[row_stencil * 3 + column_stencil], shi...  5 us
    ppermute x1, starting transfers between devices, on_device(): _, from_high = widen(lax.ppermute(step_result, 'row', backward))  4.11 us
    ppermute x1, waiting for transfers between devices, on_device(): lax.ppermute(pack(starting_states[:, :, :state_halo], own[:, :, :coef_hal...  4.09 us
    unnamed x40, local copies, waits for them, and re-layouts  3.91 us
    ppermute x1, waiting for transfers between devices, on_device(): _, from_high = widen(lax.ppermute(step_result, 'row', backward))  3.86 us
    all_to_all x1, starting transfers between devices, on_device(): lax.all_to_all(by_chunk, 'mem', split_axis=0, concat_axis=0, tiled=True)  3.66 us
    ppermute x1, starting transfers between devices, on_device(): lax.ppermute(pack(starting_states[:, :, row_total - state_halo:], own[:,...  3.12 us
  transfers between devices with their start and end apart: 6, of which 3 were waited for; matrix products, arithmetic and copies ran while one was open for 16% of the time, Pallas kernels for 0%

profile of v22, /device:TPU:9, one launch (start us, length us, event | category | flops | bytes accessed | tf_op | source)
XLA Modules:
  0.0 59.3 jit_solution(4563266428585399460)
XLA Ops:
  0.0 1.2 %fusion.47 = (f32[8,3,8,512]{3,0,2,1:T(8,128)S(1)}, f32[3,8,8,512]{3,2,1,0:T(8,128)S(1)}) fusion(f32[1,8,8,512]{3,2,1,0:T(8,128)} %bitcast.239, f32[1,8,8,512]{3,2,1,0:T(8,128)} %bitcast.240, f32[1,8,8,512]{3,2,1,0:T(8,128)} %bitcast.241), kind=kLoop, calls=%fused_computation.134 | loop fusion | flops 196608 | bytes 1179648 | tf_op jit(solution)/shard_map/transpose | solution.py:258
  1.4 3.1 %collective-permute-start = (f32[100,512]{1,0:T(8,128)S(1)}, f32[100,512]{1,0:T(8,128)S(1)}, u32[]{:S(2)}, u32[]{:S(2)}) collective-permute-start(f32[100,512]{1,0:T(8,128)S(1)} %pad_maximum_fusion.3), channel_id=1, source_target_pairs={{0,1},{1,2},{2,3},{3,4},{4,5},{5,6},{6,7},{8,9},{9,10},{10,11},{11... | collective-permute-start | bytes 614408 | tf_op jit(solution)/shard_map/ppermute | solution.py:227
  4.7 3.1 %collective-permute-start.1 = (f32[100,512]{1,0:T(8,128)S(1)}, f32[100,512]{1,0:T(8,128)S(1)}, u32[]{:S(2)}, u32[]{:S(2)}) collective-permute-start(f32[100,512]{1,0:T(8,128)S(1)} %pad_maximum_fusion.4), channel_id=1, source_target_pairs={{1,0},{2,1},{3,2},{4,3},{5,4},{6,5},{7,6},{9,8},{10,9},{11,10},{12... | collective-permute-start | bytes 614408 | tf_op jit(solution)/shard_map/ppermute | solution.py:232
  8.1 0.7 %gather_fusion = bf16[64,3,64]{2,1,0:T(4,128)(2,1)S(1)} fusion(bf16[3,64,64]{2,0,1:T(4,128)(2,1)S(1)} %copy.47, s32[1024]{0:T(1024)S(1)} %pad_clamp_fusion), kind=kCustom, calls=%fused_computation | custom fusion | bytes 49408 | tf_op jit(solution)/shard_map/gather | solution.py:145
  8.8 0.6 %copy.48 = bf16[3,64,64]{2,1,0:T(8,128)(2,1)} copy(bf16[3,64,64]{2,0,1:T(4,128)(2,1)S(1)} %bitcast.236) | data formatting | bytes 49152 | tf_op jit(solution)/shard_map/gather | solution.py:145
  9.4 0.6 %gather_fusion.1 = bf16[64,64]{1,0:T(8,128)(2,1)S(1)} fusion(bf16[64,64]{0,1:T(8,128)(2,1)S(1)} %bitcast.226, s32[1024]{0:T(1024)S(1)} %pad_clamp_fusion), kind=kCustom, calls=%fused_computation.1 | custom fusion | bytes 16640 | tf_op jit(solution)/shard_map/gather | solution.py:146
  10.0 0.7 %copy.49 = bf16[64,64]{0,1:T(8,128)(2,1)} copy(bf16[64,64]{1,0:T(8,128)(2,1)S(1)} %gather_fusion.1) | data formatting | bytes 16384 | tf_op jit(solution)/shard_map/gather | solution.py:146
  10.7 0.7 %copy.45 = bf16[8,64]{0,1:T(8,128)(2,1)} copy(bf16[8,64]{1,0:T(8,128)(2,1)S(1)} %copy-done.7) | data formatting | bytes 2048 | tf_op args[4]
  11.9 4.1 %collective-permute-done.1 = f32[100,512]{1,0:T(8,128)S(1)} collective-permute-done((f32[100,512]{1,0:T(8,128)S(1)}, f32[100,512]{1,0:T(8,128)S(1)}, u32[]{:S(2)}, u32[]{:S(2)}) %collective-permute-start.1) | collective-permute-done | bytes 204832 | tf_op jit(solution)/shard_map/ppermute | solution.py:232
  16.0 0.6 collective-permute-start.2
  17.0 0.6 %collective-permute-done.2 = f32[72,512]{1,0:T(8,128)S(1)} collective-permute-done((f32[72,512]{1,0:T(8,128)S(1)}, f32[72,512]{1,0:T(8,128)S(1)}, u32[]{:S(2)}, u32[]{:S(2)}) %collective-permute-start.2) | collective-permute-done | bytes 147488 | tf_op jit(solution)/shard_map/ppermute | solution.py:244
  17.8 0.1 pad_maximum_fusion
  18.2 0.5 add_select_fusion.2
  18.8 0.5 add_select_fusion.1
  19.3 0.5 add_select_fusion
  19.9 0.3 select_convert_fusion.1
  20.6 0.2 reshape.204
  20.8 0.7 %pad_maximum_fusion.6 = bf16[4,9,8,256]{3,2,1,0:T(8,128)(2,1)} fusion(bf16[4,1,8,256]{3,2,1,0:T(8,128)(2,1)S(1)} %reshape.204, bf16[4,8,8,256]{3,2,1,0:T(8,128)(2,1)S(1)} %bitcast.233), kind=kLoop, calls=%fused_computation.69 | loop fusion | flops 73728 | bytes 294912 | tf_op jit(solution)/shard_map/concatenate | solution.py:298
  21.5 3.7 %all-to-all-start = ((bf16[4,9,8,256]{3,2,1,0:T(8,128)(2,1)}), bf16[4,9,8,256]{3,2,1,0:T(8,128)(2,1)S(1)}, u32[]{:S(2)}, u32[]{:S(2)}) async-start(bf16[4,9,8,256]{3,2,1,0:T(8,128)(2,1)} %pad_maximum_fusion.6), calls=%async_computation | async-start | bytes 294912 | tf_op jit(solution)/shard_map/all_to_all | solution.py:299
  25.9 0.1 copy.105
  26.0 0.1 copy.106
  26.2 0.1 copy.107
  26.3 0.1 copy.108
  26.4 0.1 copy.109
  26.6 0.1 copy.110
  26.7 0.1 copy.111
  26.8 0.1 copy.112
  27.0 0.1 copy.113
  27.1 0.1 copy.114
  27.2 0.1 copy.115
  27.4 0.1 copy.116
  27.5 0.1 copy.117
  27.7 0.7 %copy.54.gain_ref = f32[64,1]{1,0:T(8,128)} copy(f32[64,1]{0,1:T(1,128)S(1)} %bitcast.245) | data formatting | bytes 512 | tf_op jit(solution)/shard_map/optimization_barrier | solution.py:243
  28.4 0.7 %copy.53.hs_ref = f32[8,1]{1,0:T(8,128)} copy(f32[8,1]{0,1:T(1,128)S(1)} %reshape_tile.3) | data formatting | bytes 64 | tf_op jit(solution)/shard_map/optimization_barrier | solution.py:243
  29.0 0.7 %copy-done.5 = bf16[4,9,8,256]{3,2,1,0:T(8,128)(2,1)} copy-done((bf16[4,9,8,256]{3,2,1,0:T(8,128)(2,1)}, bf16[4,9,8,256]{3,2,1,0:T(8,128)(2,1)S(1)}, u32[]{:S(2)}) %copy-start.5) | copy-done | bytes 147480
  29.7 10.4 %shard_map.118 = bf16[9,8,1024]{2,1,0:T(8,128)(2,1)} custom-call(f32[8,1]{1,0:T(8,128)} %copy.53.hs_ref, bf16[4,9,8,256]{3,2,1,0:T(8,128)(2,1)} %copy-done.5, bf16[64,8]{1,0:T(8,128)(2,1)} %bitcast.243, f32[64,1]{1,0:T(8,128)} %copy.54.gain_ref, bf16[192,64]{1,0:T(8,128)(2,1)} %bitcast.237, bf16[64,64]{1,0:T(8,128)(2,1)} %bitcast.242, bf16[8,64]{1,0:T(8,128)(2,1)} %bitcast.244), custom_call_target="tpu_custom_call" | custom-call | tf_op jit(solution)/shard_map/pallas_call | solution.py:164
  40.1 2.4 %collective-permute-start.3 = (bf16[9,8,1024]{2,1,0:T(8,128)(2,1)}, bf16[9,8,1024]{2,1,0:T(8,128)(2,1)S(1)}, u32[]{:S(2)}, u32[]{:S(2)}) collective-permute-start(bf16[9,8,1024]{2,1,0:T(8,128)(2,1)} %shard_map.118), channel_id=1, source_target_pairs={{0,1},{1,2},{2,3},{3,4},{4,5},{5,6},{6,7},{8,9},{9,10},{10,11},{11... | collective-permute-start | bytes 442376 | tf_op jit(solution)/shard_map/ppermute | solution.py:320
  42.5 4.1 %collective-permute-start.4 = (bf16[9,8,1024]{2,1,0:T(8,128)(2,1)}, bf16[9,8,1024]{2,1,0:T(8,128)(2,1)S(1)}, u32[]{:S(2)}, u32[]{:S(2)}) collective-permute-start(bf16[9,8,1024]{2,1,0:T(8,128)(2,1)} %shard_map.118), channel_id=1, source_target_pairs={{1,0},{2,1},{3,2},{4,3},{5,4},{6,5},{7,6},{9,8},{10,9},{11,10},{12... | collective-permute-start | bytes 442376 | tf_op jit(solution)/shard_map/ppermute | solution.py:321
  46.6 0.7 %slice.439 = bf16[1,8,1024]{2,1,0:T(8,128)(2,1)S(1)} slice(bf16[9,8,1024]{2,1,0:T(8,128)(2,1)} %shard_map.118), slice={[8:9], [0:8], [0:1024]} | slice | bytes 32768 | tf_op jit(solution)/shard_map/slice | solution.py:308
  47.3 0.2 reshape_squeeze.10
  47.7 0.1 reshape_squeeze.9
  48.1 3.9 %collective-permute-done.4 = bf16[9,8,1024]{2,1,0:T(8,128)(2,1)S(1)} collective-permute-done((bf16[9,8,1024]{2,1,0:T(8,128)(2,1)}, bf16[9,8,1024]{2,1,0:T(8,128)(2,1)S(1)}, u32[]{:S(2)}, u32[]{:S(2)}) %collective-permute-start.4) | collective-permute-done | bytes 147488 | tf_op jit(solution)/shard_map/ppermute | solution.py:321
  52.0 0.2 reshape_squeeze.11
  52.4 0.5 maximum_maximum_fusion
  52.9 0.6 %maximum_maximum_fusion.2 = (bf16[8,8,16,144]{3,1,2,0:T(8,128)(2,1)S(1)}, bf16[8,8,16,144]{3,1,2,0:T(8,128)(2,1)S(1)}) fusion(bf16[8,8,8,8]{3,1,2,0:T(8,128)(2,1)S(1)} %get-tuple-element.44, bf16[8,8,8,128]{3,1,2,0:T(8,128)(2,1)S(1)} %copy_bitcast_fusion.1, bf16[8,8,8,8]{3,1,2,0:T(8,128)(2,1)S(1)} %get-tuple-element.43, ...), kind=kLoop, calls=%fused_computation.43 | loop fusion | flops 3538944 | bytes 1032192 | tf_op jit(solution)/shard_map/concatenate | solution.py:322
  53.5 0.3 fusion.12
  53.8 0.4 convolution_add_fusion.7
  54.2 0.3 convolution_add_fusion.6
  54.5 0.3 convolution_add_fusion.5
  54.8 0.3 convolution_add_fusion.4
  55.2 0.4 convolution_add_fusion.3
  55.5 0.3 convolution_add_fusion.2
  55.8 0.4 convolution_add_fusion.1
  56.2 0.5 select_convert_fusion
  56.7 0.2 fusion.26
  56.9 0.2 convolution_add_fusion.15
  57.1 0.2 convolution_add_fusion.14
  57.4 0.2 convolution_add_fusion.13
  57.5 0.2 convolution_add_fusion.12
  57.8 0.2 convolution_add_fusion.11
  58.0 0.2 convolution_add_fusion.10
  58.2 0.2 convolution_add_fusion.9
  58.4 0.2 fusion.3
  58.7 0.7 %copy.79 = bf16[8,8,8,128]{3,2,1,0:T(8,128)(2,1)} copy(bf16[8,8,8,128]{3,1,2,0:T(8,128)(2,1)S(1)} %fusion.3) | data formatting | bytes 262144 | tf_op jit(solution)/shard_map/convert_element_type | solution.py:332
  (90 shorter events, 3.7 us)
Async XLA Ops:
  0.0 9.4 %copy-start = (bf16[64,64]{1,0:T(8,128)(2,1)S(1)}, bf16[64,64]{1,0:T(8,128)(2,1)}, u32[]{:S(2)}) copy-start(bf16[64,64]{1,0:T(8,128)(2,1)} %param.20) | copy-start | bytes 24580
  0.0 1.3 %copy-start.4 = (f32[2,8,8,512]{3,2,1,0:T(8,128)S(1)}, f32[2,8,8,512]{3,2,1,0:T(8,128)}, u32[]{:S(2)}) copy-start(f32[2,8,8,512]{3,2,1,0:T(8,128)} %param.12) | copy-start | bytes 786436
  1.3 6.6 %copy-start.6 = (bf16[64,192]{1,0:T(8,128)(2,1)S(1)}, bf16[64,192]{1,0:T(8,128)(2,1)}, u32[]{:S(2)}) copy-start(bf16[64,192]{1,0:T(8,128)(2,1)} %param.18) | copy-start | bytes 73732
  1.3 9.4 %copy-start.7 = (bf16[8,64]{1,0:T(8,128)(2,1)S(1)}, bf16[8,64]{1,0:T(8,128)(2,1)}, u32[]{:S(2)}) copy-start(bf16[8,64]{1,0:T(8,128)(2,1)} %param.16) | copy-start | bytes 3076
  1.3 10.1 %copy-start.9 = (f32[4]{0:T(128)S(1)}, f32[4]{0:T(128)}, u32[]{:S(2)}) copy-start(f32[4]{0:T(128)} %param.19) | copy-start | bytes 52
  1.4 10.4 %collective-permute-start = (f32[100,512]{1,0:T(8,128)S(1)}, f32[100,512]{1,0:T(8,128)S(1)}, u32[]{:S(2)}, u32[]{:S(2)}) collective-permute-start(f32[100,512]{1,0:T(8,128)S(1)} %pad_maximum_fusion.3), channel_id=1, source_target_pairs={{0,1},{1,2},{2,3},{3,4},{4,5},{5,6},{6,7},{8,9},{9,10},{10,11},{11... | collective-permute-start | bytes 614408 | tf_op jit(solution)/shard_map/ppermute | solution.py:227
  4.6 7.0 %copy-start.1 = (bf16[9,8,8]{0,2,1:T(8,128)(2,1)S(1)}, bf16[9,8,8]{0,2,1:T(8,128)(2,1)}, u32[]{:S(2)}) copy-start(bf16[9,8,8]{0,2,1:T(8,128)(2,1)} %param.22) | copy-start | bytes 3460
  4.7 7.1 %copy-start.2 = (bf16[9,8,8]{0,2,1:T(8,128)(2,1)S(1)}, bf16[9,8,8]{0,2,1:T(8,128)(2,1)}, u32[]{:S(2)}) copy-start(bf16[9,8,8]{0,2,1:T(8,128)(2,1)} %param.23) | copy-start | bytes 3460
  4.7 11.3 %collective-permute-start.1 = (f32[100,512]{1,0:T(8,128)S(1)}, f32[100,512]{1,0:T(8,128)S(1)}, u32[]{:S(2)}, u32[]{:S(2)}) collective-permute-start(f32[100,512]{1,0:T(8,128)S(1)} %pad_maximum_fusion.4), channel_id=1, source_target_pairs={{1,0},{2,1},{3,2},{4,3},{5,4},{6,5},{7,6},{9,8},{10,9},{11,10},{12... | collective-permute-start | bytes 614408 | tf_op jit(solution)/shard_map/ppermute | solution.py:232
  16.0 1.6 %collective-permute-start.2 = (f32[72,512]{1,0:T(8,128)S(1)}, f32[72,512]{1,0:T(8,128)S(1)}, u32[]{:S(2)}, u32[]{:S(2)}) collective-permute-start(f32[72,512]{1,0:T(8,128)S(1)} %pad_maximum_fusion.5), channel_id=1, source_target_pairs={{0,8},{8,0},{16,24},{24,16},{1,9},{9,1},{17,25},{25,17},{2,10},{10... | collective-permute-start | bytes 442376 | tf_op jit(solution)/shard_map/ppermute | solution.py:244
  20.4 7.3 %copy-start.8 = (f32[64]{0:T(128)S(1)}, f32[64]{0:T(128)}, u32[]{:S(2)}) copy-start(f32[64]{0:T(128)} %param.17) | copy-start | bytes 772
  21.5 7.6 %all-to-all-start = ((bf16[4,9,8,256]{3,2,1,0:T(8,128)(2,1)}), bf16[4,9,8,256]{3,2,1,0:T(8,128)(2,1)S(1)}, u32[]{:S(2)}, u32[]{:S(2)}) async-start(bf16[4,9,8,256]{3,2,1,0:T(8,128)(2,1)} %pad_maximum_fusion.6), calls=%async_computation | async-start | bytes 294912 | tf_op jit(solution)/shard_map/all_to_all | solution.py:299
  29.0 0.7 %copy-start.5 = (bf16[4,9,8,256]{3,2,1,0:T(8,128)(2,1)}, bf16[4,9,8,256]{3,2,1,0:T(8,128)(2,1)S(1)}, u32[]{:S(2)}) copy-start(bf16[4,9,8,256]{3,2,1,0:T(8,128)(2,1)S(1)} %all-to-all-done.x_ref) | copy-start | bytes 442372
  40.1 7.6 %copy-start.3 = (bf16[9,8,1024]{2,1,0:T(8,128)(2,1)S(1)}, bf16[9,8,1024]{2,1,0:T(8,128)(2,1)}, u32[]{:S(2)}) copy-start(bf16[9,8,1024]{2,1,0:T(8,128)(2,1)} %shard_map.118) | copy-start | bytes 442372
  40.1 7.6 %collective-permute-start.3 = (bf16[9,8,1024]{2,1,0:T(8,128)(2,1)}, bf16[9,8,1024]{2,1,0:T(8,128)(2,1)S(1)}, u32[]{:S(2)}, u32[]{:S(2)}) collective-permute-start(bf16[9,8,1024]{2,1,0:T(8,128)(2,1)} %shard_map.118), channel_id=1, source_target_pairs={{0,1},{1,2},{2,3},{3,4},{4,5},{5,6},{6,7},{8,9},{9,10},{10,11},{11... | collective-permute-start | bytes 442376 | tf_op jit(solution)/shard_map/ppermute | solution.py:320
  42.5 9.5 %collective-permute-start.4 = (bf16[9,8,1024]{2,1,0:T(8,128)(2,1)}, bf16[9,8,1024]{2,1,0:T(8,128)(2,1)S(1)}, u32[]{:S(2)}, u32[]{:S(2)}) collective-permute-start(bf16[9,8,1024]{2,1,0:T(8,128)(2,1)} %shard_map.118), channel_id=1, source_target_pairs={{1,0},{2,1},{3,2},{4,3},{5,4},{6,5},{7,6},{9,8},{10,9},{11,10},{12... | collective-permute-start | bytes 442376 | tf_op jit(solution)/shard_map/ppermute | solution.py:321

commit v23 on v21

--- a/solution.py
+++ b/solution.py
@@ -64,23 +64,37 @@
 
 
 def attention_kernel(
-    hs_ref, x_ref, w1_ref, gain_ref, pw_ref, ow_ref, rw_ref, out_ref, *, chunk, heads
+    hs_ref, x_hbm, w1_ref, gain_ref, pw_ref, ow_ref, rw_ref, out_ref, x_buf, sems, *, chunk, heads
 ):
-    lax.fori_loop(
-        0,
-        x_ref.shape[1],
-        lambda r, carry: attention_row(
-            r, hs_ref, x_ref, w1_ref, gain_ref, pw_ref, ow_ref, rw_ref, out_ref, chunk, heads
-        ),
-        0,
-        unroll=2,
-    )
+    rows = x_hbm.shape[1]
+
+    def fetch(r, slot):
+        return pltpu.make_async_copy(
+            x_hbm.at[:, pl.ds(r, 1)], x_buf.at[slot], sems.at[slot]
+        )
+
+    fetch(0, 0).start()
+
+    def body(r, carry):
+        slot = r % 2
+        fetch(r, slot).wait()
+
+        @pl.when(r + 1 < rows)
+        def _():
+            fetch(r + 1, 1 - slot).start()
+
+        return attention_row(
+            r, hs_ref, x_buf.at[slot], w1_ref, gain_ref, pw_ref, ow_ref, rw_ref, out_ref,
+            chunk, heads,
+        )
+
+    lax.fori_loop(0, rows, body, 0, unroll=2)
 
 
 def attention_row(r, hs_ref, x_ref, w1_ref, gain_ref, pw_ref, ow_ref, rw_ref, out_ref, chunk, heads):
     width = w1_ref.shape[0]
     sources = x_ref.shape[0]
-    layers = jnp.concatenate([x_ref[s, r] for s in range(sources)], axis=1)
+    layers = jnp.concatenate([x_ref[s, 0] for s in range(sources)], axis=1)
     lanes = layers.shape[1]
     members = lanes // chunk
     embedded = jnp.dot(w1_ref[...], layers, preferred_element_type=jnp.float32)
@@ -146,6 +160,13 @@
     return pl.pallas_call(
         functools.partial(attention_kernel, chunk=chunk, heads=heads),
         out_shape=jax.ShapeDtypeStruct((row_count, feat, lanes), jnp.bfloat16),
+        in_specs=[pl.BlockSpec(memory_space=pltpu.VMEM)]
+        + [pl.BlockSpec(memory_space=pl.ANY)]
+        + [pl.BlockSpec(memory_space=pltpu.VMEM)] * 5,
+        scratch_shapes=[
+            pltpu.VMEM((2, sources, 1, levels_count, source_lanes), by_source.dtype),
+            pltpu.SemaphoreType.DMA((2,)),
+        ],
     )(scale, by_source, embed_t, gain, project_t, output_t, readout_t)
 
 

time: 60 us -> 61.3 us (1.022)
  Pallas kernels: 10.4 us -> 11.6 us
    pallas_call x1, Pallas kernels: 10.4 us -> 11.6 us  [post_block(): pl.pallas_call(functools.partial(attention_kernel, chunk=chunk, heads=hea...]
where the time goes in v23:
time: 61.3 us; the launch traced here: 60.5 us
  starting transfers between devices  16.8 us (27%)
  local copies, waits for them, and re-layouts  12.1 us (20%)
  Pallas kernels  11.6 us (19%)
  waiting for transfers between devices  8.61 us (14%)
  other arithmetic  5.56 us (9%)
  matrix products  5.01 us (8%)
  between operations  0.78 us (1%)
    pallas_call x1, Pallas kernels, post_block(): pl.pallas_call(functools.partial(attention_kernel, chunk=chunk, heads=hea...  11.6 us
    dot_general x18, matrix products, convolve(): jnp.einsum('oc,mcij->moij', kernel[row_stencil * 3 + column_stencil], shi...  5.01 us
    ppermute x1, waiting for transfers between devices, on_device(): lax.ppermute(pack(starting_states[:, :, :state_halo], own[:, :, :coef_hal...  4.15 us
    ppermute x1, starting transfers between devices, on_device(): _, from_high = widen(lax.ppermute(step_result, 'row', backward))  4.11 us
    unnamed x46, local copies, waits for them, and re-layouts  4.08 us
    ppermute x1, waiting for transfers between devices, on_device(): _, from_high = widen(lax.ppermute(step_result, 'row', backward))  3.87 us
    all_to_all x1, starting transfers between devices, on_device(): lax.all_to_all(by_chunk, 'mem', split_axis=0, concat_axis=0, tiled=True)  3.55 us
    ppermute x1, starting transfers between devices, on_device(): lax.ppermute(pack(starting_states[:, :, row_total - state_halo:], own[:,...  3.12 us
  transfers between devices with their start and end apart: 6, of which 3 were waited for; matrix products, arithmetic and copies ran while one was open for 16% of the time, Pallas kernels for 0%

profile of v23, /device:TPU:9, one launch (start us, length us, event | category | flops | bytes accessed | tf_op | source)
XLA Modules:
  0.0 60.5 jit_solution(7709230060848612003)
XLA Ops:
  0.0 1.0 %fusion.15 = f32[3,4,8,512]{3,2,1,0:T(8,128)S(1)} fusion(s32[]{:T(128)S(6)} %select_n.86, f32[1,8,8,512]{3,2,1,0:T(8,128)} %bitcast.213, f32[1,8,8,512]{3,2,1,0:T(8,128)} %bitcast.215, f32[1,8,8,512]{3,2,1,0:T(8,128)} %bitcast.217), kind=kLoop, calls=%fused_computation.65 | loop fusion | flops 98304 | bytes 589828 | tf_op jit(solution)/shard_map/stack | solution.py:212
  1.3 3.1 %collective-permute-start = (f32[100,512]{1,0:T(8,128)S(1)}, f32[100,512]{1,0:T(8,128)S(1)}, u32[]{:S(2)}, u32[]{:S(2)}) collective-permute-start(f32[100,512]{1,0:T(8,128)S(1)} %pad_maximum_fusion.2), channel_id=1, source_target_pairs={{0,1},{1,2},{2,3},{3,4},{4,5},{5,6},{6,7},{8,9},{9,10},{10,11},{11... | collective-permute-start | bytes 614408 | tf_op jit(solution)/shard_map/ppermute | solution.py:230
  4.5 3.1 %collective-permute-start.1 = (f32[100,512]{1,0:T(8,128)S(1)}, f32[100,512]{1,0:T(8,128)S(1)}, u32[]{:S(2)}, u32[]{:S(2)}) collective-permute-start(f32[100,512]{1,0:T(8,128)S(1)} %pad_maximum_fusion.3), channel_id=1, source_target_pairs={{1,0},{2,1},{3,2},{4,3},{5,4},{6,5},{7,6},{9,8},{10,9},{11,10},{12... | collective-permute-start | bytes 614408 | tf_op jit(solution)/shard_map/ppermute | solution.py:235
  7.9 0.7 %gather_fusion = bf16[64,3,64]{2,1,0:T(4,128)(2,1)S(1)} fusion(bf16[3,64,64]{2,0,1:T(4,128)(2,1)S(1)} %copy.47, s32[1024]{0:T(1024)S(1)} %pad_clamp_fusion), kind=kCustom, calls=%fused_computation | custom fusion | bytes 49408 | tf_op jit(solution)/shard_map/gather | solution.py:141
  8.5 0.6 %copy.48 = bf16[3,64,64]{2,1,0:T(8,128)(2,1)} copy(bf16[3,64,64]{2,0,1:T(4,128)(2,1)S(1)} %bitcast.224) | data formatting | bytes 49152 | tf_op jit(solution)/shard_map/gather | solution.py:141
  9.2 0.6 %gather_fusion.1 = bf16[64,64]{1,0:T(8,128)(2,1)S(1)} fusion(bf16[64,64]{0,1:T(8,128)(2,1)S(1)} %bitcast.211, s32[1024]{0:T(1024)S(1)} %pad_clamp_fusion), kind=kCustom, calls=%fused_computation.1 | custom fusion | bytes 16640 | tf_op jit(solution)/shard_map/gather | solution.py:142
  9.8 0.7 %copy.49 = bf16[64,64]{0,1:T(8,128)(2,1)} copy(bf16[64,64]{1,0:T(8,128)(2,1)S(1)} %gather_fusion.1) | data formatting | bytes 16384 | tf_op jit(solution)/shard_map/gather | solution.py:142
  10.5 0.7 %copy.45 = bf16[8,64]{0,1:T(8,128)(2,1)} copy(bf16[8,64]{1,0:T(8,128)(2,1)S(1)} %copy-done.10) | data formatting | bytes 2048 | tf_op args[4]
  11.6 4.2 %collective-permute-done.1 = f32[100,512]{1,0:T(8,128)S(1)} collective-permute-done((f32[100,512]{1,0:T(8,128)S(1)}, f32[100,512]{1,0:T(8,128)S(1)}, u32[]{:S(2)}, u32[]{:S(2)}) %collective-permute-start.1) | collective-permute-done | bytes 204832 | tf_op jit(solution)/shard_map/ppermute | solution.py:235
  15.8 0.6 collective-permute-start.2
  16.8 0.6 collective-permute-done.2
  17.7 0.1 pad_maximum_fusion
  18.1 0.5 add_select_fusion.2
  18.7 0.5 add_select_fusion.1
  19.3 0.5 add_select_fusion
  19.9 0.3 select_convert_fusion.1
  20.6 0.2 reshape.207
  20.8 0.7 %pad_maximum_fusion.5 = bf16[4,9,8,256]{3,2,1,0:T(8,128)(2,1)} fusion(bf16[4,1,8,256]{3,2,1,0:T(8,128)(2,1)S(1)} %reshape.207, bf16[4,8,8,256]{3,2,1,0:T(8,128)(2,1)S(1)} %bitcast.223), kind=kLoop, calls=%fused_computation.71 | loop fusion | flops 73728 | bytes 294912 | tf_op jit(solution)/shard_map/concatenate | solution.py:292
  21.5 3.5 %all-to-all-start = ((bf16[4,9,8,256]{3,2,1,0:T(8,128)(2,1)}), bf16[4,9,8,256]{3,2,1,0:T(8,128)(2,1)S(1)}, u32[]{:S(2)}, u32[]{:S(2)}) async-start(bf16[4,9,8,256]{3,2,1,0:T(8,128)(2,1)} %pad_maximum_fusion.5), calls=%async_computation | async-start | bytes 294912 | tf_op jit(solution)/shard_map/all_to_all | solution.py:293
  25.7 0.1 copy.105
  25.9 0.1 copy.106
  26.0 0.1 copy.107
  26.1 0.1 copy.108
  26.3 0.1 copy.109
  26.4 0.1 copy.110
  26.6 0.1 copy.111
  26.7 0.1 copy.112
  26.8 0.1 copy.113
  27.0 0.1 copy.114
  27.1 0.1 copy.115
  27.2 0.1 copy.116
  27.4 0.1 copy.117
  27.5 0.7 %copy.54.gain_ref = f32[64,1]{1,0:T(8,128)} copy(f32[64,1]{0,1:T(1,128)S(1)} %bitcast.230) | data formatting | bytes 512 | tf_op jit(solution)/shard_map/optimization_barrier | solution.py:246
  28.2 0.7 %copy.53.hs_ref = f32[8,1]{1,0:T(8,128)} copy(f32[8,1]{0,1:T(1,128)S(1)} %reshape_tile.3) | data formatting | bytes 64 | tf_op jit(solution)/shard_map/optimization_barrier | solution.py:246
  28.9 0.7 %copy-done.8 = bf16[4,9,8,256]{3,2,1,0:T(8,128)(2,1)} copy-done((bf16[4,9,8,256]{3,2,1,0:T(8,128)(2,1)}, bf16[4,9,8,256]{3,2,1,0:T(8,128)(2,1)S(1)}, u32[]{:S(2)}) %copy-start.8) | copy-done | bytes 147480
  29.6 11.6 %shard_map.118 = bf16[9,8,1024]{2,1,0:T(8,128)(2,1)} custom-call(f32[8,1]{1,0:T(8,128)} %copy.53.hs_ref, bf16[4,9,8,256]{3,2,1,0:T(8,128)(2,1)} %copy-done.8, bf16[64,8]{1,0:T(8,128)(2,1)} %bitcast.228, f32[64,1]{1,0:T(8,128)} %copy.54.gain_ref, bf16[192,64]{1,0:T(8,128)(2,1)} %bitcast.225, bf16[64,64]{1,0:T(8,128)(2,1)} %bitcast.227, bf16[8,64]{1,0:T(8,128)(2,1)} %bitcast.229), custom_call_target="tpu_custom_call" | custom-call | tf_op jit(solution)/shard_map/pallas_call | solution.py:160
  41.2 2.4 %collective-permute-start.3 = (bf16[9,8,1024]{2,1,0:T(8,128)(2,1)}, bf16[9,8,1024]{2,1,0:T(8,128)(2,1)S(1)}, u32[]{:S(2)}, u32[]{:S(2)}) collective-permute-start(bf16[9,8,1024]{2,1,0:T(8,128)(2,1)} %shard_map.118), channel_id=1, source_target_pairs={{0,1},{1,2},{2,3},{3,4},{4,5},{5,6},{6,7},{8,9},{9,10},{10,11},{11... | collective-permute-start | bytes 442376 | tf_op jit(solution)/shard_map/ppermute | solution.py:314
  43.6 4.1 %collective-permute-start.4 = (bf16[9,8,1024]{2,1,0:T(8,128)(2,1)}, bf16[9,8,1024]{2,1,0:T(8,128)(2,1)S(1)}, u32[]{:S(2)}, u32[]{:S(2)}) collective-permute-start(bf16[9,8,1024]{2,1,0:T(8,128)(2,1)} %shard_map.118), channel_id=1, source_target_pairs={{1,0},{2,1},{3,2},{4,3},{5,4},{6,5},{7,6},{9,8},{10,9},{11,10},{12... | collective-permute-start | bytes 442376 | tf_op jit(solution)/shard_map/ppermute | solution.py:315
  47.7 0.7 %slice.426 = bf16[1,8,1024]{2,1,0:T(8,128)(2,1)S(1)} slice(bf16[9,8,1024]{2,1,0:T(8,128)(2,1)} %shard_map.118), slice={[8:9], [0:8], [0:1024]} | slice | bytes 32768 | tf_op jit(solution)/shard_map/slice | solution.py:302
  48.4 0.2 reshape_squeeze.10
  48.8 0.1 reshape_squeeze.9
  49.2 3.9 %collective-permute-done.4 = bf16[9,8,1024]{2,1,0:T(8,128)(2,1)S(1)} collective-permute-done((bf16[9,8,1024]{2,1,0:T(8,128)(2,1)}, bf16[9,8,1024]{2,1,0:T(8,128)(2,1)S(1)}, u32[]{:S(2)}, u32[]{:S(2)}) %collective-permute-start.4) | collective-permute-done | bytes 147488 | tf_op jit(solution)/shard_map/ppermute | solution.py:315
  53.1 0.2 reshape_squeeze.11
  53.5 0.5 maximum_maximum_fusion
  54.0 0.6 %maximum_maximum_fusion.2 = (bf16[8,8,16,144]{3,1,2,0:T(8,128)(2,1)S(1)}, bf16[8,8,16,144]{3,1,2,0:T(8,128)(2,1)S(1)}) fusion(bf16[8,8,8,8]{3,1,2,0:T(8,128)(2,1)S(1)} %get-tuple-element.39, bf16[8,8,8,128]{3,1,2,0:T(8,128)(2,1)S(1)} %copy_bitcast_fusion.1, bf16[8,8,8,8]{3,1,2,0:T(8,128)(2,1)S(1)} %get-tuple-element.38, ...), kind=kLoop, calls=%fused_computation.43 | loop fusion | flops 3538944 | bytes 1032192 | tf_op jit(solution)/shard_map/concatenate | solution.py:316
  54.6 0.3 fusion.12
  54.9 0.4 convolution_add_fusion.7
  55.3 0.4 convolution_add_fusion.6
  55.6 0.3 convolution_add_fusion.5
  55.9 0.4 convolution_add_fusion.4
  56.3 0.4 convolution_add_fusion.3
  56.6 0.3 convolution_add_fusion.2
  56.9 0.4 convolution_add_fusion.1
  57.3 0.5 select_convert_fusion
  57.8 0.2 fusion.26
  58.0 0.2 convolution_add_fusion.15
  58.2 0.2 convolution_add_fusion.14
  58.5 0.2 convolution_add_fusion.13
  58.6 0.2 convolution_add_fusion.12
  58.9 0.2 convolution_add_fusion.11
  59.1 0.2 convolution_add_fusion.10
  59.3 0.2 convolution_add_fusion.9
  59.5 0.2 fusion.3
  59.8 0.7 %copy.79 = bf16[8,8,8,128]{3,2,1,0:T(8,128)(2,1)} copy(bf16[8,8,8,128]{3,1,2,0:T(8,128)(2,1)S(1)} %fusion.3) | data formatting | bytes 262144 | tf_op jit(solution)/shard_map/convert_element_type | solution.py:326
  (95 shorter events, 3.8 us)
Async XLA Ops:
  0.0 9.2 %copy-start = (bf16[64,64]{1,0:T(8,128)(2,1)S(1)}, bf16[64,64]{1,0:T(8,128)(2,1)}, u32[]{:S(2)}) copy-start(bf16[64,64]{1,0:T(8,128)(2,1)} %param.20) | copy-start | bytes 24580
  0.0 1.1 %copy-start.7 = (f32[2,8,8,512]{3,2,1,0:T(8,128)S(1)}, f32[2,8,8,512]{3,2,1,0:T(8,128)}, u32[]{:S(2)}) copy-start(f32[2,8,8,512]{3,2,1,0:T(8,128)} %param.12) | copy-start | bytes 786436
  1.1 6.6 %copy-start.9 = (bf16[64,192]{1,0:T(8,128)(2,1)S(1)}, bf16[64,192]{1,0:T(8,128)(2,1)}, u32[]{:S(2)}) copy-start(bf16[64,192]{1,0:T(8,128)(2,1)} %param.18) | copy-start | bytes 73732
  1.1 9.4 %copy-start.10 = (bf16[8,64]{1,0:T(8,128)(2,1)S(1)}, bf16[8,64]{1,0:T(8,128)(2,1)}, u32[]{:S(2)}) copy-start(bf16[8,64]{1,0:T(8,128)(2,1)} %param.16) | copy-start | bytes 3076
  1.1 10.1 %copy-start.12 = (f32[4]{0:T(128)S(1)}, f32[4]{0:T(128)}, u32[]{:S(2)}) copy-start(f32[4]{0:T(128)} %param.19) | copy-start | bytes 52
  1.2 10.2 %copy-start.1 = (bf16[9,8,8]{0,2,1:T(8,128)(2,1)S(1)}, bf16[9,8,8]{0,2,1:T(8,128)(2,1)}, u32[]{:S(2)}) copy-start(bf16[9,8,8]{0,2,1:T(8,128)(2,1)} %param.22) | copy-start | bytes 3460
  1.2 10.3 %copy-start.2 = (bf16[9,8,8]{0,2,1:T(8,128)(2,1)S(1)}, bf16[9,8,8]{0,2,1:T(8,128)(2,1)}, u32[]{:S(2)}) copy-start(bf16[9,8,8]{0,2,1:T(8,128)(2,1)} %param.23) | copy-start | bytes 3460
  1.3 10.4 %collective-permute-start = (f32[100,512]{1,0:T(8,128)S(1)}, f32[100,512]{1,0:T(8,128)S(1)}, u32[]{:S(2)}, u32[]{:S(2)}) collective-permute-start(f32[100,512]{1,0:T(8,128)S(1)} %pad_maximum_fusion.2), channel_id=1, source_target_pairs={{0,1},{1,2},{2,3},{3,4},{4,5},{5,6},{6,7},{8,9},{9,10},{10,11},{11... | collective-permute-start | bytes 614408 | tf_op jit(solution)/shard_map/ppermute | solution.py:230
  4.5 11.3 %collective-permute-start.1 = (f32[100,512]{1,0:T(8,128)S(1)}, f32[100,512]{1,0:T(8,128)S(1)}, u32[]{:S(2)}, u32[]{:S(2)}) collective-permute-start(f32[100,512]{1,0:T(8,128)S(1)} %pad_maximum_fusion.3), channel_id=1, source_target_pairs={{1,0},{2,1},{3,2},{4,3},{5,4},{6,5},{7,6},{9,8},{10,9},{11,10},{12... | collective-permute-start | bytes 614408 | tf_op jit(solution)/shard_map/ppermute | solution.py:235
  15.8 1.6 %collective-permute-start.2 = (f32[72,512]{1,0:T(8,128)S(1)}, f32[72,512]{1,0:T(8,128)S(1)}, u32[]{:S(2)}, u32[]{:S(2)}) collective-permute-start(f32[72,512]{1,0:T(8,128)S(1)} %pad_maximum_fusion.4), channel_id=1, source_target_pairs={{0,8},{8,0},{16,24},{24,16},{1,9},{9,1},{17,25},{25,17},{2,10},{10... | collective-permute-start | bytes 442376 | tf_op jit(solution)/shard_map/ppermute | solution.py:247
  16.7 0.9 %copy-start.4 = (f32[8,8,512]{2,1,0:T(8,128)S(1)}, f32[8,8,512]{2,1,0:T(8,128)}, u32[]{:S(2)}) copy-start(f32[8,8,512]{2,1,0:T(8,128)} %param.13) | copy-start | bytes 393220
  16.7 1.0 %copy-start.5 = (f32[8,8,512]{2,1,0:T(8,128)S(1)}, f32[8,8,512]{2,1,0:T(8,128)}, u32[]{:S(2)}) copy-start(f32[8,8,512]{2,1,0:T(8,128)} %param.14) | copy-start | bytes 393220
  16.7 1.0 %copy-start.6 = (f32[8,8,512]{2,1,0:T(8,128)S(1)}, f32[8,8,512]{2,1,0:T(8,128)}, u32[]{:S(2)}) copy-start(f32[8,8,512]{2,1,0:T(8,128)} %param.15) | copy-start | bytes 393220
  20.3 7.2 %copy-start.11 = (f32[64]{0:T(128)S(1)}, f32[64]{0:T(128)}, u32[]{:S(2)}) copy-start(f32[64]{0:T(128)} %param.17) | copy-start | bytes 772
  21.5 7.4 %all-to-all-start = ((bf16[4,9,8,256]{3,2,1,0:T(8,128)(2,1)}), bf16[4,9,8,256]{3,2,1,0:T(8,128)(2,1)S(1)}, u32[]{:S(2)}, u32[]{:S(2)}) async-start(bf16[4,9,8,256]{3,2,1,0:T(8,128)(2,1)} %pad_maximum_fusion.5), calls=%async_computation | async-start | bytes 294912 | tf_op jit(solution)/shard_map/all_to_all | solution.py:293
  28.9 0.7 %copy-start.8 = (bf16[4,9,8,256]{3,2,1,0:T(8,128)(2,1)}, bf16[4,9,8,256]{3,2,1,0:T(8,128)(2,1)S(1)}, u32[]{:S(2)}) copy-start(bf16[4,9,8,256]{3,2,1,0:T(8,128)(2,1)S(1)} %all-to-all-done.x_hbm) | copy-start | bytes 442372
  41.2 7.6 %copy-start.3 = (bf16[9,8,1024]{2,1,0:T(8,128)(2,1)S(1)}, bf16[9,8,1024]{2,1,0:T(8,128)(2,1)}, u32[]{:S(2)}) copy-start(bf16[9,8,1024]{2,1,0:T(8,128)(2,1)} %shard_map.118) | copy-start | bytes 442372
  41.2 7.6 %collective-permute-start.3 = (bf16[9,8,1024]{2,1,0:T(8,128)(2,1)}, bf16[9,8,1024]{2,1,0:T(8,128)(2,1)S(1)}, u32[]{:S(2)}, u32[]{:S(2)}) collective-permute-start(bf16[9,8,1024]{2,1,0:T(8,128)(2,1)} %shard_map.118), channel_id=1, source_target_pairs={{0,1},{1,2},{2,3},{3,4},{4,5},{5,6},{6,7},{8,9},{9,10},{10,11},{11... | collective-permute-start | bytes 442376 | tf_op jit(solution)/shard_map/ppermute | solution.py:314
  43.6 9.5 %collective-permute-start.4 = (bf16[9,8,1024]{2,1,0:T(8,128)(2,1)}, bf16[9,8,1024]{2,1,0:T(8,128)(2,1)S(1)}, u32[]{:S(2)}, u32[]{:S(2)}) collective-permute-start(bf16[9,8,1024]{2,1,0:T(8,128)(2,1)} %shard_map.118), channel_id=1, source_target_pairs={{1,0},{2,1},{3,2},{4,3},{5,4},{6,5},{7,6},{9,8},{10,9},{11,10},{12... | collective-permute-start | bytes 442376 | tf_op jit(solution)/shard_map/ppermute | solution.py:315

commit v24 on v21

--- a/solution.py
+++ b/solution.py
@@ -172,6 +172,44 @@
     return summed
 
 
+def convolve_split(padded_field, local_field, kernel, halo):
+    span = DILATION_SPAN
+    row_total = padded_field.shape[2] - 2 * span
+    column_total = padded_field.shape[3] - 2 * span
+    local_rows = local_field.shape[2]
+    middle = jnp.zeros(
+        (local_field.shape[0], kernel.shape[1], local_rows, column_total), jnp.float32
+    )
+    for column_stencil in range(3):
+        middle = middle + jnp.einsum(
+            "oc,mcij->moij",
+            kernel[3 + column_stencil],
+            local_field[:, :, :, column_stencil * span : column_stencil * span + column_total],
+            preferred_element_type=jnp.float32,
+        )
+    start = halo - span
+    summed = jnp.pad(middle, ((0, 0), (0, 0), (start, row_total - start - local_rows), (0, 0)))
+    for row_stencil in range(3):
+        for column_stencil in range(3):
+            shifted_field = padded_field[
+                :,
+                :,
+                row_stencil * span : row_stencil * span + row_total,
+                column_stencil * span : column_stencil * span + column_total,
+            ]
+            if row_stencil == 1:
+                rows = jnp.arange(row_total)
+                keep = (rows < start) | (rows >= start + local_rows)
+                shifted_field = jnp.where(keep[:, None], shifted_field, 0)
+            summed = summed + jnp.einsum(
+                "oc,mcij->moij",
+                kernel[row_stencil * 3 + column_stencil],
+                shifted_field,
+                preferred_element_type=jnp.float32,
+            )
+    return summed
+
+
 def on_device(
     starting_states,
     wind_east,
@@ -295,7 +333,7 @@
         padded_feature = jnp.concatenate([from_low, features_wide, from_high], axis=2)
     else:
         padded_feature = row_padded(features_wide, halo)
-    first = jax.nn.silu(convolve(padded_feature, first_kernel))
+    first = jax.nn.silu(convolve_split(padded_feature, features_wide, first_kernel, halo))
     row_ids = lax.axis_index("row") * tile_rows - span + jnp.arange(tile_rows + 2 * span)
     col_ids = mem_index * tile_cols - span + jnp.arange(tile_cols + 2 * span)
     row_in = (row_ids >= 0) & (row_ids < lax.axis_size("row") * tile_rows)

time: 60 us -> 59.5 us (level)
  the two profiles are of different devices: /device:TPU:9 before, /device:TPU:0 now
where the time goes in v24:
time: 59.5 us; the launch traced here: 59 us
  starting transfers between devices  16 us (27%)
  local copies, waits for them, and re-layouts  13.1 us (22%)
  Pallas kernels  10.4 us (17%)
  waiting for transfers between devices  7.14 us (12%)
  matrix products  6.02 us (10%)
  other arithmetic  5.58 us (9%)
  between operations  0.82 us (1%)
    pallas_call x1, Pallas kernels, post_block(): pl.pallas_call(functools.partial(attention_kernel, chunk=chunk, heads=hea...  10.4 us
    ppermute x1, starting transfers between devices, on_device(): _, from_low = widen(lax.ppermute(step_result, 'row', forward))  5.17 us
    ppermute x1, starting transfers between devices, on_device(): lax.ppermute(pack(starting_states[:, :, row_total - state_halo:], own[:,...  4.86 us
    unnamed x46, local copies, waits for them, and re-layouts  4.16 us
    all_to_all x1, waiting for transfers between devices, on_device(): lax.all_to_all(by_chunk, 'mem', split_axis=0, concat_axis=0, tiled=True)  3.38 us
    all_to_all x1, starting transfers between devices, on_device(): lax.all_to_all(by_chunk, 'mem', split_axis=0, concat_axis=0, tiled=True)  3.33 us
    dot_general x9, matrix products, convolve_split(): jnp.einsum('oc,mcij->moij', kernel[row_stencil * 3 + column_stencil], shi...  3.33 us
    dot_general x9, matrix products, convolve(): jnp.einsum('oc,mcij->moij', kernel[row_stencil * 3 + column_stencil], shi...  1.86 us
  transfers between devices with their start and end apart: 6, of which 4 were waited for; matrix products, arithmetic and copies ran while one was open for 19% of the time, Pallas kernels for 0%

profile of v24, /device:TPU:0, one launch (start us, length us, event | category | flops | bytes accessed | tf_op | source)
XLA Modules:
  0.0 59.0 jit_solution(4365333204688021375)
XLA Ops:
  0.0 1.0 %fusion.34 = f32[3,4,8,512]{3,2,1,0:T(8,128)S(1)} fusion(s32[]{:T(128)S(6)} %select_n.96, f32[1,8,8,512]{3,2,1,0:T(8,128)} %bitcast.255, f32[1,8,8,512]{3,2,1,0:T(8,128)} %bitcast.257, f32[1,8,8,512]{3,2,1,0:T(8,128)} %bitcast.259), kind=kLoop, calls=%fused_computation.92 | loop fusion | flops 98304 | bytes 589828 | tf_op jit(solution)/shard_map/stack | solution.py:229
  1.3 4.9 %collective-permute-start = (f32[100,512]{1,0:T(8,128)S(1)}, f32[100,512]{1,0:T(8,128)S(1)}, u32[]{:S(2)}, u32[]{:S(2)}) collective-permute-start(f32[100,512]{1,0:T(8,128)S(1)} %pad_maximum_fusion.6), channel_id=1, source_target_pairs={{0,1},{1,2},{2,3},{3,4},{4,5},{5,6},{6,7},{8,9},{9,10},{10,11},{11... | collective-permute-start | bytes 614408 | tf_op jit(solution)/shard_map/ppermute | solution.py:247
  6.2 1.3 %collective-permute-start.1 = (f32[100,512]{1,0:T(8,128)S(1)}, f32[100,512]{1,0:T(8,128)S(1)}, u32[]{:S(2)}, u32[]{:S(2)}) collective-permute-start(f32[100,512]{1,0:T(8,128)S(1)} %pad_maximum_fusion.7), channel_id=1, source_target_pairs={{1,0},{2,1},{3,2},{4,3},{5,4},{6,5},{7,6},{9,8},{10,9},{11,10},{12... | collective-permute-start | bytes 614408 | tf_op jit(solution)/shard_map/ppermute | solution.py:252
  7.9 0.7 %gather_fusion = bf16[64,3,64]{2,1,0:T(4,128)(2,1)S(1)} fusion(bf16[3,64,64]{2,0,1:T(4,128)(2,1)S(1)} %copy.47, s32[1024]{0:T(1024)S(1)} %pad_clamp_fusion), kind=kCustom, calls=%fused_computation | custom fusion | bytes 49408 | tf_op jit(solution)/shard_map/gather | solution.py:127
  8.5 0.6 %copy.48 = bf16[3,64,64]{2,1,0:T(8,128)(2,1)} copy(bf16[3,64,64]{2,0,1:T(4,128)(2,1)S(1)} %bitcast.266) | data formatting | bytes 49152 | tf_op jit(solution)/shard_map/gather | solution.py:127
  9.1 0.6 %gather_fusion.1 = bf16[64,64]{1,0:T(8,128)(2,1)S(1)} fusion(bf16[64,64]{0,1:T(8,128)(2,1)S(1)} %bitcast.253, s32[1024]{0:T(1024)S(1)} %pad_clamp_fusion), kind=kCustom, calls=%fused_computation.1 | custom fusion | bytes 16640 | tf_op jit(solution)/shard_map/gather | solution.py:128
  9.8 0.7 %copy.49 = bf16[64,64]{0,1:T(8,128)(2,1)} copy(bf16[64,64]{1,0:T(8,128)(2,1)S(1)} %gather_fusion.1) | data formatting | bytes 16384 | tf_op jit(solution)/shard_map/gather | solution.py:128
  10.5 0.7 %copy.45 = bf16[8,64]{0,1:T(8,128)(2,1)} copy(bf16[8,64]{1,0:T(8,128)(2,1)S(1)} %copy-done.10) | data formatting | bytes 2048 | tf_op args[4]
  12.1 0.1 copy.105
  12.2 0.1 copy.106
  12.4 0.1 copy.107
  13.4 0.1 copy.114
  13.6 0.1 copy.115
  13.7 0.1 copy.116
  13.8 0.1 copy.117
  14.1 1.1 %collective-permute-done = f32[100,512]{1,0:T(8,128)S(1)} collective-permute-done((f32[100,512]{1,0:T(8,128)S(1)}, f32[100,512]{1,0:T(8,128)S(1)}, u32[]{:S(2)}, u32[]{:S(2)}) %collective-permute-start) | collective-permute-done | bytes 204832 | tf_op jit(solution)/shard_map/ppermute | solution.py:247
  15.8 0.9 %collective-permute-done.2 = f32[72,512]{1,0:T(8,128)S(1)} collective-permute-done((f32[72,512]{1,0:T(8,128)S(1)}, f32[72,512]{1,0:T(8,128)S(1)}, u32[]{:S(2)}, u32[]{:S(2)}) %collective-permute-start.2) | collective-permute-done | bytes 147488 | tf_op jit(solution)/shard_map/ppermute | solution.py:264
  16.9 0.1 pad_maximum_fusion
  17.3 0.5 add_select_fusion.2
  17.9 0.5 add_select_fusion.1
  18.5 0.5 add_select_fusion
  19.1 0.3 select_convert_fusion.1
  19.4 0.1 fusion.35
  19.8 0.2 reshape.207
  20.0 0.7 %pad_maximum_fusion.9 = bf16[4,9,8,256]{3,2,1,0:T(8,128)(2,1)} fusion(bf16[4,1,8,256]{3,2,1,0:T(8,128)(2,1)S(1)} %reshape.207, bf16[4,8,8,256]{3,2,1,0:T(8,128)(2,1)S(1)} %bitcast.265), kind=kLoop, calls=%fused_computation.98 | loop fusion | flops 73728 | bytes 294912 | tf_op jit(solution)/shard_map/concatenate | solution.py:309
  20.6 3.3 %all-to-all-start = ((bf16[4,9,8,256]{3,2,1,0:T(8,128)(2,1)}), bf16[4,9,8,256]{3,2,1,0:T(8,128)(2,1)S(1)}, u32[]{:S(2)}, u32[]{:S(2)}) async-start(bf16[4,9,8,256]{3,2,1,0:T(8,128)(2,1)} %pad_maximum_fusion.9), calls=%async_computation | async-start | bytes 294912 | tf_op jit(solution)/shard_map/all_to_all | solution.py:310
  24.0 0.7 %copy.54.gain_ref = f32[64,1]{1,0:T(8,128)} copy(f32[64,1]{0,1:T(1,128)S(1)} %bitcast.272) | data formatting | bytes 512 | tf_op jit(solution)/shard_map/optimization_barrier | solution.py:263
  24.7 0.7 %copy.53.hs_ref = f32[8,1]{1,0:T(8,128)} copy(f32[8,1]{0,1:T(1,128)S(1)} %reshape_tile.3) | data formatting | bytes 64 | tf_op jit(solution)/shard_map/optimization_barrier | solution.py:263
  25.4 3.4 %all-to-all-done.x_ref = bf16[4,9,8,256]{3,2,1,0:T(8,128)(2,1)S(1)} async-done(((bf16[4,9,8,256]{3,2,1,0:T(8,128)(2,1)}), bf16[4,9,8,256]{3,2,1,0:T(8,128)(2,1)S(1)}, u32[]{:S(2)}, u32[]{:S(2)}) %all-to-all-start) | async-done | bytes 147488 | tf_op jit(solution)/shard_map/all_to_all | solution.py:310
  28.8 0.7 %copy-done.8 = bf16[4,9,8,256]{3,2,1,0:T(8,128)(2,1)} copy-done((bf16[4,9,8,256]{3,2,1,0:T(8,128)(2,1)}, bf16[4,9,8,256]{3,2,1,0:T(8,128)(2,1)S(1)}, u32[]{:S(2)}) %copy-start.8) | copy-done | bytes 147480
  29.4 10.4 %shard_map.118 = bf16[9,8,1024]{2,1,0:T(8,128)(2,1)} custom-call(f32[8,1]{1,0:T(8,128)} %copy.53.hs_ref, bf16[4,9,8,256]{3,2,1,0:T(8,128)(2,1)} %copy-done.8, bf16[64,8]{1,0:T(8,128)(2,1)} %bitcast.270, f32[64,1]{1,0:T(8,128)} %copy.54.gain_ref, bf16[192,64]{1,0:T(8,128)(2,1)} %bitcast.267, bf16[64,64]{1,0:T(8,128)(2,1)} %bitcast.269, bf16[8,64]{1,0:T(8,128)(2,1)} %bitcast.271), custom_call_target="tpu_custom_call" | custom-call | tf_op jit(solution)/shard_map/pallas_call | solution.py:146
  39.8 1.3 %collective-permute-start.4 = (bf16[9,8,1024]{2,1,0:T(8,128)(2,1)}, bf16[9,8,1024]{2,1,0:T(8,128)(2,1)S(1)}, u32[]{:S(2)}, u32[]{:S(2)}) collective-permute-start(bf16[9,8,1024]{2,1,0:T(8,128)(2,1)} %shard_map.118), channel_id=1, source_target_pairs={{1,0},{2,1},{3,2},{4,3},{5,4},{6,5},{7,6},{9,8},{10,9},{11,10},{12... | collective-permute-start | bytes 442376 | tf_op jit(solution)/shard_map/ppermute | solution.py:332
  41.1 5.2 %collective-permute-start.3 = (bf16[9,8,1024]{2,1,0:T(8,128)(2,1)}, bf16[9,8,1024]{2,1,0:T(8,128)(2,1)S(1)}, u32[]{:S(2)}, u32[]{:S(2)}) collective-permute-start(bf16[9,8,1024]{2,1,0:T(8,128)(2,1)} %shard_map.118), channel_id=1, source_target_pairs={{0,1},{1,2},{2,3},{3,4},{4,5},{5,6},{6,7},{8,9},{9,10},{10,11},{11... | collective-permute-start | bytes 442376 | tf_op jit(solution)/shard_map/ppermute | solution.py:331
  46.3 0.7 %slice.433 = bf16[1,8,1024]{2,1,0:T(8,128)(2,1)S(1)} slice(bf16[9,8,1024]{2,1,0:T(8,128)(2,1)} %shard_map.118), slice={[8:9], [0:8], [0:1024]} | slice | bytes 32768 | tf_op jit(solution)/shard_map/slice | solution.py:319
  47.0 0.9 %copy_bitcast_fusion.6 = bf16[8,8,8,128]{3,1,2,0:T(8,128)(2,1)S(1)} fusion(bf16[9,8,1024]{2,1,0:T(8,128)(2,1)} %shard_map.118), kind=kLoop, calls=%fused_computation.127 | loop fusion | bytes 262144 | tf_op jit(solution)/shard_map/transpose | solution.py:318
  47.9 0.1 reshape_squeeze.9
  48.3 0.3 fusion.23
  48.6 0.3 convolution_add_fusion.1
  48.9 0.2 fusion.9
  49.1 0.1 reshape_squeeze.11
  49.5 1.7 %collective-permute-done.3 = bf16[9,8,1024]{2,1,0:T(8,128)(2,1)S(1)} collective-permute-done((bf16[9,8,1024]{2,1,0:T(8,128)(2,1)}, bf16[9,8,1024]{2,1,0:T(8,128)(2,1)S(1)}, u32[]{:S(2)}, u32[]{:S(2)}) %collective-permute-start.3) | collective-permute-done | bytes 147488 | tf_op jit(solution)/shard_map/ppermute | solution.py:331
  51.2 0.2 reshape_squeeze.10
  51.6 0.5 maximum_maximum_fusion
  52.1 0.6 %maximum_maximum_fusion.2 = (bf16[8,8,16,144]{3,1,2,0:T(8,128)(2,1)S(1)}, bf16[8,8,16,144]{3,1,2,0:T(8,128)(2,1)S(1)}) fusion(bf16[8,8,8,8]{3,1,2,0:T(8,128)(2,1)S(1)} %get-tuple-element.39, bf16[8,8,8,128]{3,1,2,0:T(8,128)(2,1)S(1)} %copy_bitcast_fusion.1, bf16[8,8,8,8]{3,1,2,0:T(8,128)(2,1)S(1)} %get-tuple-element.38, ...), kind=kLoop, calls=%fused_computation.54 | loop fusion | flops 3538944 | bytes 1032192 | tf_op jit(solution)/shard_map/concatenate | solution.py:333
  52.8 0.3 fusion.8
  53.0 0.3 fusion.7
  53.4 0.4 fusion.6
  53.8 0.3 fusion.5
  54.1 0.4 fusion.4
  54.5 0.4 fusion.3
  55.0 0.3 fusion.2
  55.2 0.4 fusion.1
  55.6 0.5 select_convert_fusion
  56.2 0.2 fusion.45
  56.3 0.2 convolution_add_fusion.9
  56.6 0.2 convolution_add_fusion.8
  56.8 0.2 convolution_add_fusion.7
  57.0 0.2 convolution_add_fusion.6
  57.2 0.2 convolution_add_fusion.5
  57.4 0.2 convolution_add_fusion.4
  57.6 0.2 convolution_add_fusion.3
  57.9 0.3 copy-done.3
  58.1 0.2 fusion.12
  58.3 0.7 %copy.79 = bf16[8,8,8,128]{3,2,1,0:T(8,128)(2,1)} copy(bf16[8,8,8,128]{3,1,2,0:T(8,128)(2,1)S(1)} %fusion.12) | data formatting | bytes 262144 | tf_op jit(solution)/shard_map/convert_element_type | solution.py:343
  (99 shorter events, 4.4 us)
Async XLA Ops:
  0.0 9.1 %copy-start = (bf16[64,64]{1,0:T(8,128)(2,1)S(1)}, bf16[64,64]{1,0:T(8,128)(2,1)}, u32[]{:S(2)}) copy-start(bf16[64,64]{1,0:T(8,128)(2,1)} %param.20) | copy-start | bytes 24580
  0.0 1.1 %copy-start.7 = (f32[2,8,8,512]{3,2,1,0:T(8,128)S(1)}, f32[2,8,8,512]{3,2,1,0:T(8,128)}, u32[]{:S(2)}) copy-start(f32[2,8,8,512]{3,2,1,0:T(8,128)} %param.12) | copy-start | bytes 786436
  1.1 6.6 %copy-start.9 = (bf16[64,192]{1,0:T(8,128)(2,1)S(1)}, bf16[64,192]{1,0:T(8,128)(2,1)}, u32[]{:S(2)}) copy-start(bf16[64,192]{1,0:T(8,128)(2,1)} %param.18) | copy-start | bytes 73732
  1.1 9.3 %copy-start.10 = (bf16[8,64]{1,0:T(8,128)(2,1)S(1)}, bf16[8,64]{1,0:T(8,128)(2,1)}, u32[]{:S(2)}) copy-start(bf16[8,64]{1,0:T(8,128)(2,1)} %param.16) | copy-start | bytes 3076
  1.1 10.0 %copy-start.12 = (f32[4]{0:T(128)S(1)}, f32[4]{0:T(128)}, u32[]{:S(2)}) copy-start(f32[4]{0:T(128)} %param.19) | copy-start | bytes 52
  1.2 10.2 %copy-start.1 = (bf16[9,8,8]{0,2,1:T(8,128)(2,1)S(1)}, bf16[9,8,8]{0,2,1:T(8,128)(2,1)}, u32[]{:S(2)}) copy-start(bf16[9,8,8]{0,2,1:T(8,128)(2,1)} %param.22) | copy-start | bytes 3460
  1.2 11.4 %copy-start.2 = (bf16[9,8,8]{0,2,1:T(8,128)(2,1)S(1)}, bf16[9,8,8]{0,2,1:T(8,128)(2,1)}, u32[]{:S(2)}) copy-start(bf16[9,8,8]{0,2,1:T(8,128)(2,1)} %param.23) | copy-start | bytes 3460
  1.3 13.9 %collective-permute-start = (f32[100,512]{1,0:T(8,128)S(1)}, f32[100,512]{1,0:T(8,128)S(1)}, u32[]{:S(2)}, u32[]{:S(2)}) collective-permute-start(f32[100,512]{1,0:T(8,128)S(1)} %pad_maximum_fusion.6), channel_id=1, source_target_pairs={{0,1},{1,2},{2,3},{3,4},{4,5},{5,6},{6,7},{8,9},{9,10},{10,11},{11... | collective-permute-start | bytes 614408 | tf_op jit(solution)/shard_map/ppermute | solution.py:247
  6.2 9.0 %collective-permute-start.1 = (f32[100,512]{1,0:T(8,128)S(1)}, f32[100,512]{1,0:T(8,128)S(1)}, u32[]{:S(2)}, u32[]{:S(2)}) collective-permute-start(f32[100,512]{1,0:T(8,128)S(1)} %pad_maximum_fusion.7), channel_id=1, source_target_pairs={{1,0},{2,1},{3,2},{4,3},{5,4},{6,5},{7,6},{9,8},{10,9},{11,10},{12... | collective-permute-start | bytes 614408 | tf_op jit(solution)/shard_map/ppermute | solution.py:252
  15.2 1.4 %collective-permute-start.2 = (f32[72,512]{1,0:T(8,128)S(1)}, f32[72,512]{1,0:T(8,128)S(1)}, u32[]{:S(2)}, u32[]{:S(2)}) collective-permute-start(f32[72,512]{1,0:T(8,128)S(1)} %pad_maximum_fusion.8), channel_id=1, source_target_pairs={{0,8},{8,0},{16,24},{24,16},{1,9},{9,1},{17,25},{25,17},{2,10},{10... | collective-permute-start | bytes 442376 | tf_op jit(solution)/shard_map/ppermute | solution.py:264
  15.7 1.2 %copy-start.4 = (f32[8,8,512]{2,1,0:T(8,128)S(1)}, f32[8,8,512]{2,1,0:T(8,128)}, u32[]{:S(2)}) copy-start(f32[8,8,512]{2,1,0:T(8,128)} %param.13) | copy-start | bytes 393220
  15.7 1.2 %copy-start.5 = (f32[8,8,512]{2,1,0:T(8,128)S(1)}, f32[8,8,512]{2,1,0:T(8,128)}, u32[]{:S(2)}) copy-start(f32[8,8,512]{2,1,0:T(8,128)} %param.14) | copy-start | bytes 393220
  15.7 1.2 %copy-start.6 = (f32[8,8,512]{2,1,0:T(8,128)S(1)}, f32[8,8,512]{2,1,0:T(8,128)}, u32[]{:S(2)}) copy-start(f32[8,8,512]{2,1,0:T(8,128)} %param.15) | copy-start | bytes 393220
  19.4 4.6 %copy-start.11 = (f32[64]{0:T(128)S(1)}, f32[64]{0:T(128)}, u32[]{:S(2)}) copy-start(f32[64]{0:T(128)} %param.17) | copy-start | bytes 772
  20.6 8.1 %all-to-all-start = ((bf16[4,9,8,256]{3,2,1,0:T(8,128)(2,1)}), bf16[4,9,8,256]{3,2,1,0:T(8,128)(2,1)S(1)}, u32[]{:S(2)}, u32[]{:S(2)}) async-start(bf16[4,9,8,256]{3,2,1,0:T(8,128)(2,1)} %pad_maximum_fusion.9), calls=%async_computation | async-start | bytes 294912 | tf_op jit(solution)/shard_map/all_to_all | solution.py:310
  28.8 0.7 %copy-start.8 = (bf16[4,9,8,256]{3,2,1,0:T(8,128)(2,1)}, bf16[4,9,8,256]{3,2,1,0:T(8,128)(2,1)S(1)}, u32[]{:S(2)}) copy-start(bf16[4,9,8,256]{3,2,1,0:T(8,128)(2,1)S(1)} %all-to-all-done.x_ref) | copy-start | bytes 442372
  39.8 9.3 %collective-permute-start.4 = (bf16[9,8,1024]{2,1,0:T(8,128)(2,1)}, bf16[9,8,1024]{2,1,0:T(8,128)(2,1)S(1)}, u32[]{:S(2)}, u32[]{:S(2)}) collective-permute-start(bf16[9,8,1024]{2,1,0:T(8,128)(2,1)} %shard_map.118), channel_id=1, source_target_pairs={{1,0},{2,1},{3,2},{4,3},{5,4},{6,5},{7,6},{9,8},{10,9},{11,10},{12... | collective-permute-start | bytes 442376 | tf_op jit(solution)/shard_map/ppermute | solution.py:332
  41.1 10.1 %collective-permute-start.3 = (bf16[9,8,1024]{2,1,0:T(8,128)(2,1)}, bf16[9,8,1024]{2,1,0:T(8,128)(2,1)S(1)}, u32[]{:S(2)}, u32[]{:S(2)}) collective-permute-start(bf16[9,8,1024]{2,1,0:T(8,128)(2,1)} %shard_map.118), channel_id=1, source_target_pairs={{0,1},{1,2},{2,3},{3,4},{4,5},{5,6},{6,7},{8,9},{9,10},{10,11},{11... | collective-permute-start | bytes 442376 | tf_op jit(solution)/shard_map/ppermute | solution.py:331
  57.2 0.9 %copy-start.3 = (bf16[9,8,1024]{2,1,0:T(8,128)(2,1)S(1)}, bf16[9,8,1024]{2,1,0:T(8,128)(2,1)}, u32[]{:S(2)}) copy-start(bf16[9,8,1024]{2,1,0:T(8,128)(2,1)} %shard_map.118) | copy-start | bytes 442372

commit v25 on v24

--- a/solution.py
+++ b/solution.py
@@ -177,19 +177,30 @@
     row_total = padded_field.shape[2] - 2 * span
     column_total = padded_field.shape[3] - 2 * span
     local_rows = local_field.shape[2]
-    middle = jnp.zeros(
-        (local_field.shape[0], kernel.shape[1], local_rows, column_total), jnp.float32
-    )
-    for column_stencil in range(3):
-        middle = middle + jnp.einsum(
-            "oc,mcij->moij",
-            kernel[3 + column_stencil],
-            local_field[:, :, :, column_stencil * span : column_stencil * span + column_total],
-            preferred_element_type=jnp.float32,
-        )
-    start = halo - span
-    summed = jnp.pad(middle, ((0, 0), (0, 0), (start, row_total - start - local_rows), (0, 0)))
+    rows = jnp.arange(row_total)
+    summed = jnp.zeros(
+        (padded_field.shape[0], kernel.shape[1], row_total, column_total), jnp.float32
+    )
+    bands = []
     for row_stencil in range(3):
+        start = halo - row_stencil * span
+        band = jnp.zeros(
+            (local_field.shape[0], kernel.shape[1], local_rows, column_total), jnp.float32
+        )
+        for column_stencil in range(3):
+            band = band + jnp.einsum(
+                "oc,mcij->moij",
+                kernel[row_stencil * 3 + column_stencil],
+                local_field[:, :, :, column_stencil * span : column_stencil * span + column_total],
+                preferred_element_type=jnp.float32,
+            )
+        summed = summed + jnp.pad(
+            band, ((0, 0), (0, 0), (start, row_total - start - local_rows), (0, 0))
+        )
+        bands.append(start)
+    for row_stencil in range(3):
+        start = bands[row_stencil]
+        keep = (rows < start) | (rows >= start + local_rows)
         for column_stencil in range(3):
             shifted_field = padded_field[
                 :,
@@ -197,10 +208,7 @@
                 row_stencil * span : row_stencil * span + row_total,
                 column_stencil * span : column_stencil * span + column_total,
             ]
-            if row_stencil == 1:
-                rows = jnp.arange(row_total)
-                keep = (rows < start) | (rows >= start + local_rows)
-                shifted_field = jnp.where(keep[:, None], shifted_field, 0)
+            shifted_field = jnp.where(keep[:, None], shifted_field, 0)
             summed = summed + jnp.einsum(
                 "oc,mcij->moij",
                 kernel[row_stencil * 3 + column_stencil],

time: 59.5 us -> 59.8 us (level)
  matrix products: 6.02 us -> 7.99 us
  waiting for transfers between devices: 7.14 us -> 5.44 us
    ppermute x1, waiting for transfers between devices: 1.7 us -> 0.03 us  [on_device(): _, from_low = widen(lax.ppermute(step_result, 'row', forward))]
    dot_general x3 -> x9, matrix products: 0.83 us -> 2.49 us  [convolve_split(): jnp.einsum('oc,mcij->moij', kernel[row_stencil * 3 + column_stencil], loc...]
  transfers between devices with their start and end apart: 6 -> 6, of which waited for: 4 -> 3; matrix products, arithmetic and copies ran while one was open for 19% -> 22% of each run, Pallas kernels for 0% -> 0%
where the time goes in v25:
time: 59.8 us; the launch traced here: 59.3 us
  starting transfers between devices  16 us (27%)
  local copies, waits for them, and re-layouts  13.1 us (22%)
  Pallas kernels  10.4 us (17%)
  matrix products  7.99 us (13%)
  other arithmetic  5.59 us (9%)
  waiting for transfers between devices  5.44 us (9%)
  between operations  0.85 us (1%)
    pallas_call x1, Pallas kernels, post_block(): pl.pallas_call(functools.partial(attention_kernel, chunk=chunk, heads=hea...  10.4 us
    ppermute x1, starting transfers between devices, on_device(): _, from_low = widen(lax.ppermute(step_result, 'row', forward))  5.17 us
    ppermute x1, starting transfers between devices, on_device(): lax.ppermute(pack(starting_states[:, :, row_total - state_halo:], own[:,...  4.86 us
    unnamed x46, local copies, waits for them, and re-layouts  4.16 us
    dot_general x9, matrix products, convolve_split(): jnp.einsum('oc,mcij->moij', kernel[row_stencil * 3 + column_stencil], shi...  3.64 us
    all_to_all x1, waiting for transfers between devices, on_device(): lax.all_to_all(by_chunk, 'mem', split_axis=0, concat_axis=0, tiled=True)  3.38 us
    all_to_all x1, starting transfers between devices, on_device(): lax.all_to_all(by_chunk, 'mem', split_axis=0, concat_axis=0, tiled=True)  3.33 us
    dot_general x9, matrix products, convolve_split(): jnp.einsum('oc,mcij->moij', kernel[row_stencil * 3 + column_stencil], loc...  2.49 us
  transfers between devices with their start and end apart: 6, of which 3 were waited for; matrix products, arithmetic and copies ran while one was open for 22% of the time, Pallas kernels for 0%

profile of v25, /device:TPU:0, one launch (start us, length us, event | category | flops | bytes accessed | tf_op | source)
XLA Modules:
  0.0 59.3 jit_solution(2100525998511944777)
XLA Ops:
  0.0 1.0 %fusion.34 = f32[3,4,8,512]{3,2,1,0:T(8,128)S(1)} fusion(s32[]{:T(128)S(6)} %select_n.114, f32[1,8,8,512]{3,2,1,0:T(8,128)} %bitcast.271, f32[1,8,8,512]{3,2,1,0:T(8,128)} %bitcast.273, f32[1,8,8,512]{3,2,1,0:T(8,128)} %bitcast.275), kind=kLoop, calls=%fused_computation.104 | loop fusion | flops 98304 | bytes 589828 | tf_op jit(solution)/shard_map/stack | solution.py:237
  1.3 4.9 %collective-permute-start = (f32[100,512]{1,0:T(8,128)S(1)}, f32[100,512]{1,0:T(8,128)S(1)}, u32[]{:S(2)}, u32[]{:S(2)}) collective-permute-start(f32[100,512]{1,0:T(8,128)S(1)} %pad_maximum_fusion.6), channel_id=1, source_target_pairs={{0,1},{1,2},{2,3},{3,4},{4,5},{5,6},{6,7},{8,9},{9,10},{10,11},{11... | collective-permute-start | bytes 614408 | tf_op jit(solution)/shard_map/ppermute | solution.py:255
  6.2 1.3 %collective-permute-start.1 = (f32[100,512]{1,0:T(8,128)S(1)}, f32[100,512]{1,0:T(8,128)S(1)}, u32[]{:S(2)}, u32[]{:S(2)}) collective-permute-start(f32[100,512]{1,0:T(8,128)S(1)} %pad_maximum_fusion.7), channel_id=1, source_target_pairs={{1,0},{2,1},{3,2},{4,3},{5,4},{6,5},{7,6},{9,8},{10,9},{11,10},{12... | collective-permute-start | bytes 614408 | tf_op jit(solution)/shard_map/ppermute | solution.py:260
  7.9 0.7 %gather_fusion = bf16[64,3,64]{2,1,0:T(4,128)(2,1)S(1)} fusion(bf16[3,64,64]{2,0,1:T(4,128)(2,1)S(1)} %copy.47, s32[1024]{0:T(1024)S(1)} %pad_clamp_fusion), kind=kCustom, calls=%fused_computation | custom fusion | bytes 49408 | tf_op jit(solution)/shard_map/gather | solution.py:127
  8.5 0.6 %copy.48 = bf16[3,64,64]{2,1,0:T(8,128)(2,1)} copy(bf16[3,64,64]{2,0,1:T(4,128)(2,1)S(1)} %bitcast.282) | data formatting | bytes 49152 | tf_op jit(solution)/shard_map/gather | solution.py:127
  9.2 0.6 %gather_fusion.1 = bf16[64,64]{1,0:T(8,128)(2,1)S(1)} fusion(bf16[64,64]{0,1:T(8,128)(2,1)S(1)} %bitcast.269, s32[1024]{0:T(1024)S(1)} %pad_clamp_fusion), kind=kCustom, calls=%fused_computation.1 | custom fusion | bytes 16640 | tf_op jit(solution)/shard_map/gather | solution.py:128
  9.8 0.7 %copy.49 = bf16[64,64]{0,1:T(8,128)(2,1)} copy(bf16[64,64]{1,0:T(8,128)(2,1)S(1)} %gather_fusion.1) | data formatting | bytes 16384 | tf_op jit(solution)/shard_map/gather | solution.py:128
  10.5 0.7 %copy.45 = bf16[8,64]{0,1:T(8,128)(2,1)} copy(bf16[8,64]{1,0:T(8,128)(2,1)S(1)} %copy-done.10) | data formatting | bytes 2048 | tf_op args[4]
  12.1 0.1 copy.105
  12.2 0.1 copy.106
  12.5 0.1 copy.108
  14.1 1.1 %collective-permute-done = f32[100,512]{1,0:T(8,128)S(1)} collective-permute-done((f32[100,512]{1,0:T(8,128)S(1)}, f32[100,512]{1,0:T(8,128)S(1)}, u32[]{:S(2)}, u32[]{:S(2)}) %collective-permute-start) | collective-permute-done | bytes 204832 | tf_op jit(solution)/shard_map/ppermute | solution.py:255
  15.8 0.9 %collective-permute-done.2 = f32[72,512]{1,0:T(8,128)S(1)} collective-permute-done((f32[72,512]{1,0:T(8,128)S(1)}, f32[72,512]{1,0:T(8,128)S(1)}, u32[]{:S(2)}, u32[]{:S(2)}) %collective-permute-start.2) | collective-permute-done | bytes 147488 | tf_op jit(solution)/shard_map/ppermute | solution.py:272
  16.9 0.1 pad_maximum_fusion
  17.3 0.5 add_select_fusion.2
  17.9 0.5 add_select_fusion.1
  18.5 0.5 add_select_fusion
  19.1 0.3 select_convert_fusion.1
  19.8 0.2 reshape.207
  20.0 0.7 %pad_maximum_fusion.9 = bf16[4,9,8,256]{3,2,1,0:T(8,128)(2,1)} fusion(bf16[4,1,8,256]{3,2,1,0:T(8,128)(2,1)S(1)} %reshape.207, bf16[4,8,8,256]{3,2,1,0:T(8,128)(2,1)S(1)} %bitcast.281), kind=kLoop, calls=%fused_computation.110 | loop fusion | flops 73728 | bytes 294912 | tf_op jit(solution)/shard_map/concatenate | solution.py:317
  20.6 3.3 %all-to-all-start = ((bf16[4,9,8,256]{3,2,1,0:T(8,128)(2,1)}), bf16[4,9,8,256]{3,2,1,0:T(8,128)(2,1)S(1)}, u32[]{:S(2)}, u32[]{:S(2)}) async-start(bf16[4,9,8,256]{3,2,1,0:T(8,128)(2,1)} %pad_maximum_fusion.9), calls=%async_computation | async-start | bytes 294912 | tf_op jit(solution)/shard_map/all_to_all | solution.py:318
  24.0 0.7 %copy.54.gain_ref = f32[64,1]{1,0:T(8,128)} copy(f32[64,1]{0,1:T(1,128)S(1)} %bitcast.288) | data formatting | bytes 512 | tf_op jit(solution)/shard_map/optimization_barrier | solution.py:271
  24.7 0.7 %copy.53.hs_ref = f32[8,1]{1,0:T(8,128)} copy(f32[8,1]{0,1:T(1,128)S(1)} %reshape_tile.3) | data formatting | bytes 64 | tf_op jit(solution)/shard_map/optimization_barrier | solution.py:271
  25.4 3.4 %all-to-all-done.x_ref = bf16[4,9,8,256]{3,2,1,0:T(8,128)(2,1)S(1)} async-done(((bf16[4,9,8,256]{3,2,1,0:T(8,128)(2,1)}), bf16[4,9,8,256]{3,2,1,0:T(8,128)(2,1)S(1)}, u32[]{:S(2)}, u32[]{:S(2)}) %all-to-all-start) | async-done | bytes 147488 | tf_op jit(solution)/shard_map/all_to_all | solution.py:318
  28.8 0.7 %copy-done.8 = bf16[4,9,8,256]{3,2,1,0:T(8,128)(2,1)} copy-done((bf16[4,9,8,256]{3,2,1,0:T(8,128)(2,1)}, bf16[4,9,8,256]{3,2,1,0:T(8,128)(2,1)S(1)}, u32[]{:S(2)}) %copy-start.8) | copy-done | bytes 147480
  29.4 10.4 %shard_map.118 = bf16[9,8,1024]{2,1,0:T(8,128)(2,1)} custom-call(f32[8,1]{1,0:T(8,128)} %copy.53.hs_ref, bf16[4,9,8,256]{3,2,1,0:T(8,128)(2,1)} %copy-done.8, bf16[64,8]{1,0:T(8,128)(2,1)} %bitcast.286, f32[64,1]{1,0:T(8,128)} %copy.54.gain_ref, bf16[192,64]{1,0:T(8,128)(2,1)} %bitcast.283, bf16[64,64]{1,0:T(8,128)(2,1)} %bitcast.285, bf16[8,64]{1,0:T(8,128)(2,1)} %bitcast.287), custom_call_target="tpu_custom_call" | custom-call | tf_op jit(solution)/shard_map/pallas_call | solution.py:146
  39.8 1.3 %collective-permute-start.4 = (bf16[9,8,1024]{2,1,0:T(8,128)(2,1)}, bf16[9,8,1024]{2,1,0:T(8,128)(2,1)S(1)}, u32[]{:S(2)}, u32[]{:S(2)}) collective-permute-start(bf16[9,8,1024]{2,1,0:T(8,128)(2,1)} %shard_map.118), channel_id=1, source_target_pairs={{1,0},{2,1},{3,2},{4,3},{5,4},{6,5},{7,6},{9,8},{10,9},{11,10},{12... | collective-permute-start | bytes 442376 | tf_op jit(solution)/shard_map/ppermute | solution.py:340
  41.1 5.2 %collective-permute-start.3 = (bf16[9,8,1024]{2,1,0:T(8,128)(2,1)}, bf16[9,8,1024]{2,1,0:T(8,128)(2,1)S(1)}, u32[]{:S(2)}, u32[]{:S(2)}) collective-permute-start(bf16[9,8,1024]{2,1,0:T(8,128)(2,1)} %shard_map.118), channel_id=1, source_target_pairs={{0,1},{1,2},{2,3},{3,4},{4,5},{5,6},{6,7},{8,9},{9,10},{10,11},{11... | collective-permute-start | bytes 442376 | tf_op jit(solution)/shard_map/ppermute | solution.py:339
  46.3 0.7 %slice.445 = bf16[1,8,1024]{2,1,0:T(8,128)(2,1)S(1)} slice(bf16[9,8,1024]{2,1,0:T(8,128)(2,1)} %shard_map.118), slice={[8:9], [0:8], [0:1024]} | slice | bytes 32768 | tf_op jit(solution)/shard_map/slice | solution.py:327
  47.0 0.9 %copy_bitcast_fusion.6 = bf16[8,8,8,128]{3,1,2,0:T(8,128)(2,1)S(1)} fusion(bf16[9,8,1024]{2,1,0:T(8,128)(2,1)} %shard_map.118), kind=kLoop, calls=%fused_computation.139 | loop fusion | bytes 262144 | tf_op jit(solution)/shard_map/transpose | solution.py:326
  47.9 0.1 reshape_squeeze.9
  48.3 0.3 fusion.49
  48.6 0.3 fusion.48
  48.9 0.3 fusion.47
  49.1 0.3 convolution_add_fusion.5
  49.5 0.2 fusion.9
  49.7 0.3 convolution_add_fusion.3
  50.0 0.2 fusion.10
  50.2 0.3 convolution_add_fusion.1
  50.6 0.2 fusion.11
  50.8 0.1 reshape_squeeze.11
  51.2 0.2 reshape_squeeze.10
  51.6 0.5 maximum_maximum_fusion
  52.1 0.6 %maximum_maximum_fusion.2 = (bf16[8,8,16,144]{3,1,2,0:T(8,128)(2,1)S(1)}, bf16[8,8,16,144]{3,1,2,0:T(8,128)(2,1)S(1)}) fusion(bf16[8,8,8,8]{3,1,2,0:T(8,128)(2,1)S(1)} %get-tuple-element.39, bf16[8,8,8,128]{3,1,2,0:T(8,128)(2,1)S(1)} %copy_bitcast_fusion.1, bf16[8,8,8,8]{3,1,2,0:T(8,128)(2,1)S(1)} %get-tuple-element.38, ...), kind=kLoop, calls=%fused_computation.60 | loop fusion | flops 3538944 | bytes 1032192 | tf_op jit(solution)/shard_map/concatenate | solution.py:341
  52.8 0.3 fusion.8
  53.1 0.4 fusion.7
  53.5 0.4 fusion.6
  54.0 0.3 fusion.5
  54.3 0.4 fusion.4
  54.7 0.4 fusion.3
  55.1 0.3 fusion.2
  55.5 0.4 fusion.1
  55.9 0.5 select_convert_fusion
  56.5 0.2 fusion.45
  56.6 0.2 convolution_add_fusion.13
  56.9 0.2 convolution_add_fusion.12
  57.1 0.2 convolution_add_fusion.11
  57.3 0.2 convolution_add_fusion.10
  57.5 0.2 convolution_add_fusion.9
  57.8 0.2 convolution_add_fusion.8
  57.9 0.2 convolution_add_fusion.7
  58.2 0.3 copy-done.3
  58.4 0.2 fusion.14
  58.7 0.7 %copy.79 = bf16[8,8,8,128]{3,2,1,0:T(8,128)(2,1)} copy(bf16[8,8,8,128]{3,1,2,0:T(8,128)(2,1)S(1)} %fusion.14) | data formatting | bytes 262144 | tf_op jit(solution)/shard_map/convert_element_type | solution.py:351
  (107 shorter events, 5.1 us)
Async XLA Ops:
  0.0 9.2 %copy-start = (bf16[64,64]{1,0:T(8,128)(2,1)S(1)}, bf16[64,64]{1,0:T(8,128)(2,1)}, u32[]{:S(2)}) copy-start(bf16[64,64]{1,0:T(8,128)(2,1)} %param.20) | copy-start | bytes 24580
  0.0 1.1 %copy-start.7 = (f32[2,8,8,512]{3,2,1,0:T(8,128)S(1)}, f32[2,8,8,512]{3,2,1,0:T(8,128)}, u32[]{:S(2)}) copy-start(f32[2,8,8,512]{3,2,1,0:T(8,128)} %param.12) | copy-start | bytes 786436
  1.1 6.6 %copy-start.9 = (bf16[64,192]{1,0:T(8,128)(2,1)S(1)}, bf16[64,192]{1,0:T(8,128)(2,1)}, u32[]{:S(2)}) copy-start(bf16[64,192]{1,0:T(8,128)(2,1)} %param.18) | copy-start | bytes 73732
  1.1 9.4 %copy-start.10 = (bf16[8,64]{1,0:T(8,128)(2,1)S(1)}, bf16[8,64]{1,0:T(8,128)(2,1)}, u32[]{:S(2)}) copy-start(bf16[8,64]{1,0:T(8,128)(2,1)} %param.16) | copy-start | bytes 3076
  1.1 10.1 %copy-start.12 = (f32[4]{0:T(128)S(1)}, f32[4]{0:T(128)}, u32[]{:S(2)}) copy-start(f32[4]{0:T(128)} %param.19) | copy-start | bytes 52
  1.2 10.1 %copy-start.1 = (bf16[9,8,8]{0,2,1:T(8,128)(2,1)S(1)}, bf16[9,8,8]{0,2,1:T(8,128)(2,1)}, u32[]{:S(2)}) copy-start(bf16[9,8,8]{0,2,1:T(8,128)(2,1)} %param.22) | copy-start | bytes 3460
  1.2 11.5 %copy-start.2 = (bf16[9,8,8]{0,2,1:T(8,128)(2,1)S(1)}, bf16[9,8,8]{0,2,1:T(8,128)(2,1)}, u32[]{:S(2)}) copy-start(bf16[9,8,8]{0,2,1:T(8,128)(2,1)} %param.23) | copy-start | bytes 3460
  1.3 13.9 %collective-permute-start = (f32[100,512]{1,0:T(8,128)S(1)}, f32[100,512]{1,0:T(8,128)S(1)}, u32[]{:S(2)}, u32[]{:S(2)}) collective-permute-start(f32[100,512]{1,0:T(8,128)S(1)} %pad_maximum_fusion.6), channel_id=1, source_target_pairs={{0,1},{1,2},{2,3},{3,4},{4,5},{5,6},{6,7},{8,9},{9,10},{10,11},{11... | collective-permute-start | bytes 614408 | tf_op jit(solution)/shard_map/ppermute | solution.py:255
  6.2 9.0 %collective-permute-start.1 = (f32[100,512]{1,0:T(8,128)S(1)}, f32[100,512]{1,0:T(8,128)S(1)}, u32[]{:S(2)}, u32[]{:S(2)}) collective-permute-start(f32[100,512]{1,0:T(8,128)S(1)} %pad_maximum_fusion.7), channel_id=1, source_target_pairs={{1,0},{2,1},{3,2},{4,3},{5,4},{6,5},{7,6},{9,8},{10,9},{11,10},{12... | collective-permute-start | bytes 614408 | tf_op jit(solution)/shard_map/ppermute | solution.py:260
  15.2 1.4 %collective-permute-start.2 = (f32[72,512]{1,0:T(8,128)S(1)}, f32[72,512]{1,0:T(8,128)S(1)}, u32[]{:S(2)}, u32[]{:S(2)}) collective-permute-start(f32[72,512]{1,0:T(8,128)S(1)} %pad_maximum_fusion.8), channel_id=1, source_target_pairs={{0,8},{8,0},{16,24},{24,16},{1,9},{9,1},{17,25},{25,17},{2,10},{10... | collective-permute-start | bytes 442376 | tf_op jit(solution)/shard_map/ppermute | solution.py:272
  15.7 1.2 %copy-start.4 = (f32[8,8,512]{2,1,0:T(8,128)S(1)}, f32[8,8,512]{2,1,0:T(8,128)}, u32[]{:S(2)}) copy-start(f32[8,8,512]{2,1,0:T(8,128)} %param.13) | copy-start | bytes 393220
  15.7 1.2 %copy-start.5 = (f32[8,8,512]{2,1,0:T(8,128)S(1)}, f32[8,8,512]{2,1,0:T(8,128)}, u32[]{:S(2)}) copy-start(f32[8,8,512]{2,1,0:T(8,128)} %param.14) | copy-start | bytes 393220
  15.7 1.2 %copy-start.6 = (f32[8,8,512]{2,1,0:T(8,128)S(1)}, f32[8,8,512]{2,1,0:T(8,128)}, u32[]{:S(2)}) copy-start(f32[8,8,512]{2,1,0:T(8,128)} %param.15) | copy-start | bytes 393220
  19.4 4.6 %copy-start.11 = (f32[64]{0:T(128)S(1)}, f32[64]{0:T(128)}, u32[]{:S(2)}) copy-start(f32[64]{0:T(128)} %param.17) | copy-start | bytes 772
  20.6 8.1 %all-to-all-start = ((bf16[4,9,8,256]{3,2,1,0:T(8,128)(2,1)}), bf16[4,9,8,256]{3,2,1,0:T(8,128)(2,1)S(1)}, u32[]{:S(2)}, u32[]{:S(2)}) async-start(bf16[4,9,8,256]{3,2,1,0:T(8,128)(2,1)} %pad_maximum_fusion.9), calls=%async_computation | async-start | bytes 294912 | tf_op jit(solution)/shard_map/all_to_all | solution.py:318
  28.8 0.7 %copy-start.8 = (bf16[4,9,8,256]{3,2,1,0:T(8,128)(2,1)}, bf16[4,9,8,256]{3,2,1,0:T(8,128)(2,1)S(1)}, u32[]{:S(2)}) copy-start(bf16[4,9,8,256]{3,2,1,0:T(8,128)(2,1)S(1)} %all-to-all-done.x_ref) | copy-start | bytes 442372
  39.8 11.0 %collective-permute-start.4 = (bf16[9,8,1024]{2,1,0:T(8,128)(2,1)}, bf16[9,8,1024]{2,1,0:T(8,128)(2,1)S(1)}, u32[]{:S(2)}, u32[]{:S(2)}) collective-permute-start(bf16[9,8,1024]{2,1,0:T(8,128)(2,1)} %shard_map.118), channel_id=1, source_target_pairs={{1,0},{2,1},{3,2},{4,3},{5,4},{6,5},{7,6},{9,8},{10,9},{11,10},{12... | collective-permute-start | bytes 442376 | tf_op jit(solution)/shard_map/ppermute | solution.py:340
  41.1 10.1 %collective-permute-start.3 = (bf16[9,8,1024]{2,1,0:T(8,128)(2,1)}, bf16[9,8,1024]{2,1,0:T(8,128)(2,1)S(1)}, u32[]{:S(2)}, u32[]{:S(2)}) collective-permute-start(bf16[9,8,1024]{2,1,0:T(8,128)(2,1)} %shard_map.118), channel_id=1, source_target_pairs={{0,1},{1,2},{2,3},{3,4},{4,5},{5,6},{6,7},{8,9},{9,10},{10,11},{11... | collective-permute-start | bytes 442376 | tf_op jit(solution)/shard_map/ppermute | solution.py:339
  57.5 0.9 %copy-start.3 = (bf16[9,8,1024]{2,1,0:T(8,128)(2,1)S(1)}, bf16[9,8,1024]{2,1,0:T(8,128)(2,1)}, u32[]{:S(2)}) copy-start(bf16[9,8,1024]{2,1,0:T(8,128)(2,1)} %shard_map.118) | copy-start | bytes 442372

commit v26 on v24

--- a/solution.py
+++ b/solution.py
@@ -188,8 +188,27 @@
             preferred_element_type=jnp.float32,
         )
     start = halo - span
-    summed = jnp.pad(middle, ((0, 0), (0, 0), (start, row_total - start - local_rows), (0, 0)))
-    for row_stencil in range(3):
+    end = start + local_rows
+    lead = middle.shape[:2]
+    outer = [
+        jnp.zeros(lead + (start, column_total), jnp.float32),
+        jnp.zeros(lead + (row_total - end, column_total), jnp.float32),
+    ]
+    for column_stencil in range(3):
+        for part, (low, high) in enumerate(((0, start), (end, row_total))):
+            outer[part] = outer[part] + jnp.einsum(
+                "oc,mcij->moij",
+                kernel[3 + column_stencil],
+                padded_field[
+                    :,
+                    :,
+                    span + low : span + high,
+                    column_stencil * span : column_stencil * span + column_total,
+                ],
+                preferred_element_type=jnp.float32,
+            )
+    summed = jnp.concatenate([outer[0], middle, outer[1]], axis=2)
+    for row_stencil in (0, 2):
         for column_stencil in range(3):
             shifted_field = padded_field[
                 :,
@@ -197,10 +216,6 @@
                 row_stencil * span : row_stencil * span + row_total,
                 column_stencil * span : column_stencil * span + column_total,
             ]
-            if row_stencil == 1:
-                rows = jnp.arange(row_total)
-                keep = (rows < start) | (rows >= start + local_rows)
-                shifted_field = jnp.where(keep[:, None], shifted_field, 0)
             summed = summed + jnp.einsum(
                 "oc,mcij->moij",
                 kernel[row_stencil * 3 + column_stencil],

time: 59.5 us -> 62.8 us (1.055)
  the two profiles are of different devices: /device:TPU:0 before, /device:TPU:9 now
where the time goes in v26:
time: 62.8 us; the launch traced here: 61.9 us
  starting transfers between devices  16.8 us (27%)
  local copies, waits for them, and re-layouts  16.3 us (26%)
  Pallas kernels  10.4 us (17%)
  waiting for transfers between devices  6.53 us (10%)
  matrix products  6.14 us (10%)
  other arithmetic  5.07 us (8%)
  between operations  0.73 us (1%)
    pallas_call x1, Pallas kernels, post_block(): pl.pallas_call(functools.partial(attention_kernel, chunk=chunk, heads=hea...  10.4 us
    unnamed x46, local copies, waits for them, and re-layouts  7.42 us
    ppermute x1, starting transfers between devices, on_device(): _, from_high = widen(lax.ppermute(step_result, 'row', backward))  4.11 us
    all_to_all x1, starting transfers between devices, on_device(): lax.all_to_all(by_chunk, 'mem', split_axis=0, concat_axis=0, tiled=True)  3.66 us
    ppermute x1, waiting for transfers between devices, on_device(): lax.ppermute(pack(starting_states[:, :, :state_halo], own[:, :, :coef_hal...  3.57 us
    ppermute x1, starting transfers between devices, on_device(): lax.ppermute(pack(starting_states[:, :, row_total - state_halo:], own[:,...  3.12 us
    ppermute x1, starting transfers between devices, on_device(): lax.ppermute(pack(starting_states[:, :, :state_halo], own[:, :, :coef_hal...  3.06 us
    ppermute x1, waiting for transfers between devices, on_device(): _, from_high = widen(lax.ppermute(step_result, 'row', backward))  2.34 us
  transfers between devices with their start and end apart: 6, of which 3 were waited for; matrix products, arithmetic and copies ran while one was open for 18% of the time, Pallas kernels for 0%

profile of v26, /device:TPU:9, one launch (start us, length us, event | category | flops | bytes accessed | tf_op | source)
XLA Modules:
  0.0 61.9 jit_solution(10408950647397606142)
XLA Ops:
  0.0 0.9 %fusion.39 = f32[3,4,8,512]{3,2,1,0:T(8,128)S(1)} fusion(s32[]{:T(128)S(6)} %select_n.86, f32[1,8,8,512]{3,2,1,0:T(8,128)} %bitcast.253, f32[1,8,8,512]{3,2,1,0:T(8,128)} %bitcast.255, f32[1,8,8,512]{3,2,1,0:T(8,128)} %bitcast.257), kind=kLoop, calls=%fused_computation.94 | loop fusion | flops 98304 | bytes 589828 | tf_op jit(solution)/shard_map/stack | solution.py:244
  1.0 0.9 %copy-done.7 = f32[2,8,8,512]{3,2,1,0:T(8,128)S(1)} copy-done((f32[2,8,8,512]{3,2,1,0:T(8,128)S(1)}, f32[2,8,8,512]{3,2,1,0:T(8,128)}, u32[]{:S(2)}) %copy-start.7) | copy-done | bytes 262168
  2.0 3.1 %collective-permute-start = (f32[100,512]{1,0:T(8,128)S(1)}, f32[100,512]{1,0:T(8,128)S(1)}, u32[]{:S(2)}, u32[]{:S(2)}) collective-permute-start(f32[100,512]{1,0:T(8,128)S(1)} %pad_maximum_fusion.6), channel_id=1, source_target_pairs={{0,1},{1,2},{2,3},{3,4},{4,5},{5,6},{6,7},{8,9},{9,10},{10,11},{11... | collective-permute-start | bytes 614408 | tf_op jit(solution)/shard_map/ppermute | solution.py:262
  5.3 3.1 %collective-permute-start.1 = (f32[100,512]{1,0:T(8,128)S(1)}, f32[100,512]{1,0:T(8,128)S(1)}, u32[]{:S(2)}, u32[]{:S(2)}) collective-permute-start(f32[100,512]{1,0:T(8,128)S(1)} %pad_maximum_fusion.7), channel_id=1, source_target_pairs={{1,0},{2,1},{3,2},{4,3},{5,4},{6,5},{7,6},{9,8},{10,9},{11,10},{12... | collective-permute-start | bytes 614408 | tf_op jit(solution)/shard_map/ppermute | solution.py:267
  8.7 0.7 %gather_fusion = bf16[64,3,64]{2,1,0:T(4,128)(2,1)S(1)} fusion(bf16[3,64,64]{2,0,1:T(4,128)(2,1)S(1)} %copy.47, s32[1024]{0:T(1024)S(1)} %pad_clamp_fusion), kind=kCustom, calls=%fused_computation | custom fusion | bytes 49408 | tf_op jit(solution)/shard_map/gather | solution.py:127
  9.3 0.6 %copy.48 = bf16[3,64,64]{2,1,0:T(8,128)(2,1)} copy(bf16[3,64,64]{2,0,1:T(4,128)(2,1)S(1)} %bitcast.264) | data formatting | bytes 49152 | tf_op jit(solution)/shard_map/gather | solution.py:127
  9.9 0.6 %gather_fusion.1 = bf16[64,64]{1,0:T(8,128)(2,1)S(1)} fusion(bf16[64,64]{0,1:T(8,128)(2,1)S(1)} %bitcast.251, s32[1024]{0:T(1024)S(1)} %pad_clamp_fusion), kind=kCustom, calls=%fused_computation.1 | custom fusion | bytes 16640 | tf_op jit(solution)/shard_map/gather | solution.py:128
  10.6 0.7 %copy.49 = bf16[64,64]{0,1:T(8,128)(2,1)} copy(bf16[64,64]{1,0:T(8,128)(2,1)S(1)} %gather_fusion.1) | data formatting | bytes 16384 | tf_op jit(solution)/shard_map/gather | solution.py:128
  11.3 0.7 %copy.45 = bf16[8,64]{0,1:T(8,128)(2,1)} copy(bf16[8,64]{1,0:T(8,128)(2,1)S(1)} %copy-done.10) | data formatting | bytes 2048 | tf_op args[4]
  12.3 0.6 copy-done.2
  13.0 3.6 %collective-permute-done.1 = f32[100,512]{1,0:T(8,128)S(1)} collective-permute-done((f32[100,512]{1,0:T(8,128)S(1)}, f32[100,512]{1,0:T(8,128)S(1)}, u32[]{:S(2)}, u32[]{:S(2)}) %collective-permute-start.1) | collective-permute-done | bytes 204832 | tf_op jit(solution)/shard_map/ppermute | solution.py:267
  16.6 0.6 collective-permute-start.2
  17.5 0.6 collective-permute-done.2
  18.4 0.8 %copy-done.4 = f32[8,8,512]{2,1,0:T(8,128)S(1)} copy-done((f32[8,8,512]{2,1,0:T(8,128)S(1)}, f32[8,8,512]{2,1,0:T(8,128)}, u32[]{:S(2)}) %copy-start.4) | copy-done | bytes 131096
  19.3 0.1 pad_maximum_fusion
  19.7 0.5 add_select_fusion.2
  20.3 0.5 add_select_fusion.1
  20.9 0.5 add_select_fusion
  21.4 0.3 select_convert_fusion.1
  22.1 0.2 reshape.207
  22.3 0.7 %pad_maximum_fusion.9 = bf16[4,9,8,256]{3,2,1,0:T(8,128)(2,1)} fusion(bf16[4,1,8,256]{3,2,1,0:T(8,128)(2,1)S(1)} %reshape.207, bf16[4,8,8,256]{3,2,1,0:T(8,128)(2,1)S(1)} %bitcast.263), kind=kLoop, calls=%fused_computation.100 | loop fusion | flops 73728 | bytes 294912 | tf_op jit(solution)/shard_map/concatenate | solution.py:324
  23.0 3.7 %all-to-all-start = ((bf16[4,9,8,256]{3,2,1,0:T(8,128)(2,1)}), bf16[4,9,8,256]{3,2,1,0:T(8,128)(2,1)S(1)}, u32[]{:S(2)}, u32[]{:S(2)}) async-start(bf16[4,9,8,256]{3,2,1,0:T(8,128)(2,1)} %pad_maximum_fusion.9), calls=%async_computation | async-start | bytes 294912 | tf_op jit(solution)/shard_map/all_to_all | solution.py:325
  27.4 0.1 copy.105
  29.0 0.1 copy.117
  29.2 0.5 copy-done.11
  29.7 0.7 %copy.54.gain_ref = f32[64,1]{1,0:T(8,128)} copy(f32[64,1]{0,1:T(1,128)S(1)} %bitcast.270) | data formatting | bytes 512 | tf_op jit(solution)/shard_map/optimization_barrier | solution.py:278
  30.4 0.7 %copy.53.hs_ref = f32[8,1]{1,0:T(8,128)} copy(f32[8,1]{0,1:T(1,128)S(1)} %reshape_tile.3) | data formatting | bytes 64 | tf_op jit(solution)/shard_map/optimization_barrier | solution.py:278
  31.1 0.7 %copy-done.8 = bf16[4,9,8,256]{3,2,1,0:T(8,128)(2,1)} copy-done((bf16[4,9,8,256]{3,2,1,0:T(8,128)(2,1)}, bf16[4,9,8,256]{3,2,1,0:T(8,128)(2,1)S(1)}, u32[]{:S(2)}) %copy-start.8) | copy-done | bytes 147480
  31.7 10.4 %shard_map.118 = bf16[9,8,1024]{2,1,0:T(8,128)(2,1)} custom-call(f32[8,1]{1,0:T(8,128)} %copy.53.hs_ref, bf16[4,9,8,256]{3,2,1,0:T(8,128)(2,1)} %copy-done.8, bf16[64,8]{1,0:T(8,128)(2,1)} %bitcast.268, f32[64,1]{1,0:T(8,128)} %copy.54.gain_ref, bf16[192,64]{1,0:T(8,128)(2,1)} %bitcast.265, bf16[64,64]{1,0:T(8,128)(2,1)} %bitcast.267, bf16[8,64]{1,0:T(8,128)(2,1)} %bitcast.269), custom_call_target="tpu_custom_call" | custom-call | tf_op jit(solution)/shard_map/pallas_call | solution.py:146
  42.1 2.2 %collective-permute-start.3 = (bf16[9,8,1024]{2,1,0:T(8,128)(2,1)}, bf16[9,8,1024]{2,1,0:T(8,128)(2,1)S(1)}, u32[]{:S(2)}, u32[]{:S(2)}) collective-permute-start(bf16[9,8,1024]{2,1,0:T(8,128)(2,1)} %shard_map.118), channel_id=1, source_target_pairs={{0,1},{1,2},{2,3},{3,4},{4,5},{5,6},{6,7},{8,9},{9,10},{10,11},{11... | collective-permute-start | bytes 442376 | tf_op jit(solution)/shard_map/ppermute | solution.py:346
  44.4 4.1 %collective-permute-start.4 = (bf16[9,8,1024]{2,1,0:T(8,128)(2,1)}, bf16[9,8,1024]{2,1,0:T(8,128)(2,1)S(1)}, u32[]{:S(2)}, u32[]{:S(2)}) collective-permute-start(bf16[9,8,1024]{2,1,0:T(8,128)(2,1)} %shard_map.118), channel_id=1, source_target_pairs={{1,0},{2,1},{3,2},{4,3},{5,4},{6,5},{7,6},{9,8},{10,9},{11,10},{12... | collective-permute-start | bytes 442376 | tf_op jit(solution)/shard_map/ppermute | solution.py:347
  48.5 0.7 %slice.456 = bf16[1,8,1024]{2,1,0:T(8,128)(2,1)S(1)} slice(bf16[9,8,1024]{2,1,0:T(8,128)(2,1)} %shard_map.118), slice={[8:9], [0:8], [0:1024]} | slice | bytes 32768 | tf_op jit(solution)/shard_map/slice | solution.py:334
  49.2 0.9 %copy_bitcast_fusion.6 = bf16[8,8,8,128]{3,1,2,0:T(8,128)(2,1)S(1)} fusion(bf16[9,8,1024]{2,1,0:T(8,128)(2,1)} %shard_map.118), kind=kLoop, calls=%fused_computation.137 | loop fusion | bytes 262144 | tf_op jit(solution)/shard_map/transpose | solution.py:333
  50.1 0.1 reshape_squeeze.10
  50.5 0.3 fusion.25
  50.8 0.3 convolution_add_fusion.1
  51.1 0.2 fusion.6
  51.3 0.1 reshape_squeeze.9
  51.7 2.3 %collective-permute-done.4 = bf16[9,8,1024]{2,1,0:T(8,128)(2,1)S(1)} collective-permute-done((bf16[9,8,1024]{2,1,0:T(8,128)(2,1)}, bf16[9,8,1024]{2,1,0:T(8,128)(2,1)S(1)}, u32[]{:S(2)}, u32[]{:S(2)}) %collective-permute-start.4) | collective-permute-done | bytes 147488 | tf_op jit(solution)/shard_map/ppermute | solution.py:347
  54.0 0.2 reshape_squeeze.11
  54.4 0.3 fusion.54
  54.7 0.6 %maximum_maximum_fusion.1 = (bf16[8,8,16,144]{3,1,2,0:T(8,128)(2,1)S(1)}, bf16[8,8,16,144]{3,1,2,0:T(8,128)(2,1)S(1)}) fusion(bf16[8,8,8,8]{3,1,2,0:T(8,128)(2,1)S(1)} %get-tuple-element.43, bf16[8,8,8,128]{3,1,2,0:T(8,128)(2,1)S(1)} %copy_bitcast_fusion.1, bf16[8,8,8,8]{3,1,2,0:T(8,128)(2,1)S(1)} %get-tuple-element.42, ...), kind=kLoop, calls=%fused_computation.50 | loop fusion | flops 3538944 | bytes 1032192 | tf_op jit(solution)/shard_map/concatenate | solution.py:348
  55.4 0.3 fusion.52
  55.6 0.2 convolution_add_fusion.5
  55.9 0.2 fusion.8
  56.0 0.2 convolution_add_fusion.3
  56.3 0.2 fusion.7
  56.4 0.3 fusion.5
  56.7 0.3 fusion.4
  57.1 0.4 fusion.3
  57.5 0.3 fusion.2
  57.7 0.4 fusion.1
  58.1 0.5 select_convert_fusion
  58.7 0.2 fusion.50
  58.8 0.2 convolution_add_fusion.13
  59.1 0.2 convolution_add_fusion.12
  59.3 0.2 convolution_add_fusion.11
  59.5 0.2 convolution_add_fusion.10
  59.7 0.2 convolution_add_fusion.9
  59.9 0.2 convolution_add_fusion.8
  60.1 0.2 convolution_add_fusion.7
  60.3 0.7 %copy-done.3 = bf16[9,8,1024]{2,1,0:T(8,128)(2,1)S(1)} copy-done((bf16[9,8,1024]{2,1,0:T(8,128)(2,1)S(1)}, bf16[9,8,1024]{2,1,0:T(8,128)(2,1)}, u32[]{:S(2)}) %copy-start.3) | copy-done | bytes 147480
  61.0 0.2 fusion.11
  61.3 0.7 %copy.79 = bf16[8,8,8,128]{3,2,1,0:T(8,128)(2,1)} copy(bf16[8,8,8,128]{3,1,2,0:T(8,128)(2,1)S(1)} %fusion.11) | data formatting | bytes 262144 | tf_op jit(solution)/shard_map/convert_element_type | solution.py:358
  (100 shorter events, 5.2 us)
Async XLA Ops:
  0.0 9.9 %copy-start = (bf16[64,64]{1,0:T(8,128)(2,1)S(1)}, bf16[64,64]{1,0:T(8,128)(2,1)}, u32[]{:S(2)}) copy-start(bf16[64,64]{1,0:T(8,128)(2,1)} %param.20) | copy-start | bytes 24580
  0.9 1.0 %copy-start.7 = (f32[2,8,8,512]{3,2,1,0:T(8,128)S(1)}, f32[2,8,8,512]{3,2,1,0:T(8,128)}, u32[]{:S(2)}) copy-start(f32[2,8,8,512]{3,2,1,0:T(8,128)} %param.12) | copy-start | bytes 786436
  2.0 10.9 %collective-permute-start = (f32[100,512]{1,0:T(8,128)S(1)}, f32[100,512]{1,0:T(8,128)S(1)}, u32[]{:S(2)}, u32[]{:S(2)}) collective-permute-start(f32[100,512]{1,0:T(8,128)S(1)} %pad_maximum_fusion.6), channel_id=1, source_target_pairs={{0,1},{1,2},{2,3},{3,4},{4,5},{5,6},{6,7},{8,9},{9,10},{10,11},{11... | collective-permute-start | bytes 614408 | tf_op jit(solution)/shard_map/ppermute | solution.py:262
  5.2 3.2 %copy-start.9 = (bf16[64,192]{1,0:T(8,128)(2,1)S(1)}, bf16[64,192]{1,0:T(8,128)(2,1)}, u32[]{:S(2)}) copy-start(bf16[64,192]{1,0:T(8,128)(2,1)} %param.18) | copy-start | bytes 73732
  5.3 11.3 %collective-permute-start.1 = (f32[100,512]{1,0:T(8,128)S(1)}, f32[100,512]{1,0:T(8,128)S(1)}, u32[]{:S(2)}, u32[]{:S(2)}) collective-permute-start(f32[100,512]{1,0:T(8,128)S(1)} %pad_maximum_fusion.7), channel_id=1, source_target_pairs={{1,0},{2,1},{3,2},{4,3},{5,4},{6,5},{7,6},{9,8},{10,9},{11,10},{12... | collective-permute-start | bytes 614408 | tf_op jit(solution)/shard_map/ppermute | solution.py:267
  10.6 0.7 %copy-start.10 = (bf16[8,64]{1,0:T(8,128)(2,1)S(1)}, bf16[8,64]{1,0:T(8,128)(2,1)}, u32[]{:S(2)}) copy-start(bf16[8,64]{1,0:T(8,128)(2,1)} %param.16) | copy-start | bytes 3076
  11.3 0.7 %copy-start.12 = (f32[4]{0:T(128)S(1)}, f32[4]{0:T(128)}, u32[]{:S(2)}) copy-start(f32[4]{0:T(128)} %param.19) | copy-start | bytes 52
  11.3 0.8 %copy-start.1 = (bf16[9,8,8]{0,2,1:T(8,128)(2,1)S(1)}, bf16[9,8,8]{0,2,1:T(8,128)(2,1)}, u32[]{:S(2)}) copy-start(bf16[9,8,8]{0,2,1:T(8,128)(2,1)} %param.22) | copy-start | bytes 3460
  12.1 0.7 %copy-start.2 = (bf16[9,8,8]{0,2,1:T(8,128)(2,1)S(1)}, bf16[9,8,8]{0,2,1:T(8,128)(2,1)}, u32[]{:S(2)}) copy-start(bf16[9,8,8]{0,2,1:T(8,128)(2,1)} %param.23) | copy-start | bytes 3460
  16.6 1.6 %collective-permute-start.2 = (f32[72,512]{1,0:T(8,128)S(1)}, f32[72,512]{1,0:T(8,128)S(1)}, u32[]{:S(2)}, u32[]{:S(2)}) collective-permute-start(f32[72,512]{1,0:T(8,128)S(1)} %pad_maximum_fusion.8), channel_id=1, source_target_pairs={{0,8},{8,0},{16,24},{24,16},{1,9},{9,1},{17,25},{25,17},{2,10},{10... | collective-permute-start | bytes 442376 | tf_op jit(solution)/shard_map/ppermute | solution.py:279
  18.2 0.9 %copy-start.4 = (f32[8,8,512]{2,1,0:T(8,128)S(1)}, f32[8,8,512]{2,1,0:T(8,128)}, u32[]{:S(2)}) copy-start(f32[8,8,512]{2,1,0:T(8,128)} %param.13) | copy-start | bytes 393220
  18.2 1.0 %copy-start.5 = (f32[8,8,512]{2,1,0:T(8,128)S(1)}, f32[8,8,512]{2,1,0:T(8,128)}, u32[]{:S(2)}) copy-start(f32[8,8,512]{2,1,0:T(8,128)} %param.14) | copy-start | bytes 393220
  18.3 1.0 %copy-start.6 = (f32[8,8,512]{2,1,0:T(8,128)S(1)}, f32[8,8,512]{2,1,0:T(8,128)}, u32[]{:S(2)}) copy-start(f32[8,8,512]{2,1,0:T(8,128)} %param.15) | copy-start | bytes 393220
  23.0 8.1 %all-to-all-start = ((bf16[4,9,8,256]{3,2,1,0:T(8,128)(2,1)}), bf16[4,9,8,256]{3,2,1,0:T(8,128)(2,1)S(1)}, u32[]{:S(2)}, u32[]{:S(2)}) async-start(bf16[4,9,8,256]{3,2,1,0:T(8,128)(2,1)} %pad_maximum_fusion.9), calls=%async_computation | async-start | bytes 294912 | tf_op jit(solution)/shard_map/all_to_all | solution.py:325
  29.0 0.7 %copy-start.11 = (f32[64]{0:T(128)S(1)}, f32[64]{0:T(128)}, u32[]{:S(2)}) copy-start(f32[64]{0:T(128)} %param.17) | copy-start | bytes 772
  31.1 0.7 %copy-start.8 = (bf16[4,9,8,256]{3,2,1,0:T(8,128)(2,1)}, bf16[4,9,8,256]{3,2,1,0:T(8,128)(2,1)S(1)}, u32[]{:S(2)}) copy-start(bf16[4,9,8,256]{3,2,1,0:T(8,128)(2,1)S(1)} %all-to-all-done.x_ref) | copy-start | bytes 442372
  42.1 9.2 %collective-permute-start.3 = (bf16[9,8,1024]{2,1,0:T(8,128)(2,1)}, bf16[9,8,1024]{2,1,0:T(8,128)(2,1)S(1)}, u32[]{:S(2)}, u32[]{:S(2)}) collective-permute-start(bf16[9,8,1024]{2,1,0:T(8,128)(2,1)} %shard_map.118), channel_id=1, source_target_pairs={{0,1},{1,2},{2,3},{3,4},{4,5},{5,6},{6,7},{8,9},{9,10},{10,11},{11... | collective-permute-start | bytes 442376 | tf_op jit(solution)/shard_map/ppermute | solution.py:346
  44.4 9.7 %collective-permute-start.4 = (bf16[9,8,1024]{2,1,0:T(8,128)(2,1)}, bf16[9,8,1024]{2,1,0:T(8,128)(2,1)S(1)}, u32[]{:S(2)}, u32[]{:S(2)}) collective-permute-start(bf16[9,8,1024]{2,1,0:T(8,128)(2,1)} %shard_map.118), channel_id=1, source_target_pairs={{1,0},{2,1},{3,2},{4,3},{5,4},{6,5},{7,6},{9,8},{10,9},{11,10},{12... | collective-permute-start | bytes 442376 | tf_op jit(solution)/shard_map/ppermute | solution.py:347
  60.1 0.9 %copy-start.3 = (bf16[9,8,1024]{2,1,0:T(8,128)(2,1)S(1)}, bf16[9,8,1024]{2,1,0:T(8,128)(2,1)}, u32[]{:S(2)}) copy-start(bf16[9,8,1024]{2,1,0:T(8,128)(2,1)} %shard_map.118) | copy-start | bytes 442372

commit v27 on v24

--- a/solution.py
+++ b/solution.py
@@ -189,18 +189,18 @@
         )
     start = halo - span
     summed = jnp.pad(middle, ((0, 0), (0, 0), (start, row_total - start - local_rows), (0, 0)))
+    rows = jnp.arange(row_total)
+    keep = (rows < start) | (rows >= start + local_rows)
+    middle_rows = jnp.where(keep[:, None], padded_field[:, :, span : span + row_total], 0)
     for row_stencil in range(3):
         for column_stencil in range(3):
-            shifted_field = padded_field[
-                :,
-                :,
-                row_stencil * span : row_stencil * span + row_total,
-                column_stencil * span : column_stencil * span + column_total,
+            if row_stencil == 1:
+                source = middle_rows
+            else:
+                source = padded_field[:, :, row_stencil * span : row_stencil * span + row_total]
+            shifted_field = source[
+                :, :, :, column_stencil * span : column_stencil * span + column_total
             ]
-            if row_stencil == 1:
-                rows = jnp.arange(row_total)
-                keep = (rows < start) | (rows >= start + local_rows)
-                shifted_field = jnp.where(keep[:, None], shifted_field, 0)
             summed = summed + jnp.einsum(
                 "oc,mcij->moij",
                 kernel[row_stencil * 3 + column_stencil],

time: 59.5 us -> 61.7 us (1.037)
  local copies, waits for them, and re-layouts: 13.1 us -> 17 us
  waiting for transfers between devices: 7.14 us -> 5.41 us
    unnamed x46, local copies, waits for them, and re-layouts: 4.16 us -> 8.06 us
    ppermute x1, waiting for transfers between devices: 1.13 us -> 0.01 us  [on_device(): lax.ppermute(pack(starting_states[:, :, row_total - state_halo:], own[:,...]
    all_to_all x1, waiting for transfers between devices: 3.38 us -> 2.75 us  [on_device(): lax.all_to_all(by_chunk, 'mem', split_axis=0, concat_axis=0, tiled=True)]
  transfers between devices with their start and end apart: 6 -> 6, of which waited for: 4 -> 3; matrix products, arithmetic and copies ran while one was open for 19% -> 19% of each run, Pallas kernels for 0% -> 0%
where the time goes in v27:
time: 61.7 us; the launch traced here: 61 us
  local copies, waits for them, and re-layouts  17 us (28%)
  starting transfers between devices  16.2 us (26%)
  Pallas kernels  10.4 us (17%)
  matrix products  5.83 us (9%)
  other arithmetic  5.45 us (9%)
  waiting for transfers between devices  5.41 us (9%)
  between operations  0.76 us (1%)
    pallas_call x1, Pallas kernels, post_block(): pl.pallas_call(functools.partial(attention_kernel, chunk=chunk, heads=hea...  10.4 us
    unnamed x46, local copies, waits for them, and re-layouts  8.06 us
    ppermute x1, starting transfers between devices, on_device(): _, from_low = widen(lax.ppermute(step_result, 'row', forward))  5.36 us
    ppermute x1, starting transfers between devices, on_device(): lax.ppermute(pack(starting_states[:, :, row_total - state_halo:], own[:,...  4.86 us
    all_to_all x1, starting transfers between devices, on_device(): lax.all_to_all(by_chunk, 'mem', split_axis=0, concat_axis=0, tiled=True)  3.33 us
    dot_general x9, matrix products, convolve_split(): jnp.einsum('oc,mcij->moij', kernel[row_stencil * 3 + column_stencil], shi...  3.15 us
    all_to_all x1, waiting for transfers between devices, on_device(): lax.all_to_all(by_chunk, 'mem', split_axis=0, concat_axis=0, tiled=True)  2.75 us
    dot_general x9, matrix products, convolve(): jnp.einsum('oc,mcij->moij', kernel[row_stencil * 3 + column_stencil], shi...  1.86 us
  transfers between devices with their start and end apart: 6, of which 3 were waited for; matrix products, arithmetic and copies ran while one was open for 19% of the time, Pallas kernels for 0%

profile of v27, /device:TPU:0, one launch (start us, length us, event | category | flops | bytes accessed | tf_op | source)
XLA Modules:
  0.0 61.0 jit_solution(15624211953291564198)
XLA Ops:
  0.0 0.9 %fusion.34 = f32[3,4,8,512]{3,2,1,0:T(8,128)S(1)} fusion(s32[]{:T(128)S(6)} %select_n.90, f32[1,8,8,512]{3,2,1,0:T(8,128)} %bitcast.255, f32[1,8,8,512]{3,2,1,0:T(8,128)} %bitcast.257, f32[1,8,8,512]{3,2,1,0:T(8,128)} %bitcast.259), kind=kLoop, calls=%fused_computation.94 | loop fusion | flops 98304 | bytes 589828 | tf_op jit(solution)/shard_map/stack | solution.py:229
  1.0 0.9 %copy-done.7 = f32[2,8,8,512]{3,2,1,0:T(8,128)S(1)} copy-done((f32[2,8,8,512]{3,2,1,0:T(8,128)S(1)}, f32[2,8,8,512]{3,2,1,0:T(8,128)}, u32[]{:S(2)}) %copy-start.7) | copy-done | bytes 262168
  2.0 4.9 %collective-permute-start = (f32[100,512]{1,0:T(8,128)S(1)}, f32[100,512]{1,0:T(8,128)S(1)}, u32[]{:S(2)}, u32[]{:S(2)}) collective-permute-start(f32[100,512]{1,0:T(8,128)S(1)} %pad_maximum_fusion.12), channel_id=1, source_target_pairs={{0,1},{1,2},{2,3},{3,4},{4,5},{5,6},{6,7},{8,9},{9,10},{10,11},{11... | collective-permute-start | bytes 614408 | tf_op jit(solution)/shard_map/ppermute | solution.py:247
  7.0 1.3 %collective-permute-start.1 = (f32[100,512]{1,0:T(8,128)S(1)}, f32[100,512]{1,0:T(8,128)S(1)}, u32[]{:S(2)}, u32[]{:S(2)}) collective-permute-start(f32[100,512]{1,0:T(8,128)S(1)} %pad_maximum_fusion.13), channel_id=1, source_target_pairs={{1,0},{2,1},{3,2},{4,3},{5,4},{6,5},{7,6},{9,8},{10,9},{11,10},{12... | collective-permute-start | bytes 614408 | tf_op jit(solution)/shard_map/ppermute | solution.py:252
  8.6 0.7 %gather_fusion = bf16[64,3,64]{2,1,0:T(4,128)(2,1)S(1)} fusion(bf16[3,64,64]{2,0,1:T(4,128)(2,1)S(1)} %copy.47, s32[1024]{0:T(1024)S(1)} %pad_clamp_fusion), kind=kCustom, calls=%fused_computation | custom fusion | bytes 49408 | tf_op jit(solution)/shard_map/gather | solution.py:127
  9.3 0.6 %copy.48 = bf16[3,64,64]{2,1,0:T(8,128)(2,1)} copy(bf16[3,64,64]{2,0,1:T(4,128)(2,1)S(1)} %bitcast.266) | data formatting | bytes 49152 | tf_op jit(solution)/shard_map/gather | solution.py:127
  9.9 0.6 %gather_fusion.1 = bf16[64,64]{1,0:T(8,128)(2,1)S(1)} fusion(bf16[64,64]{0,1:T(8,128)(2,1)S(1)} %bitcast.253, s32[1024]{0:T(1024)S(1)} %pad_clamp_fusion), kind=kCustom, calls=%fused_computation.1 | custom fusion | bytes 16640 | tf_op jit(solution)/shard_map/gather | solution.py:128
  10.6 0.7 %copy.49 = bf16[64,64]{0,1:T(8,128)(2,1)} copy(bf16[64,64]{1,0:T(8,128)(2,1)S(1)} %gather_fusion.1) | data formatting | bytes 16384 | tf_op jit(solution)/shard_map/gather | solution.py:128
  11.2 0.7 %copy.45 = bf16[8,64]{0,1:T(8,128)(2,1)} copy(bf16[8,64]{1,0:T(8,128)(2,1)S(1)} %copy-done.10) | data formatting | bytes 2048 | tf_op args[4]
  12.1 0.6 copy-done.1
  13.4 0.1 copy.105
  13.6 0.1 copy.106
  13.7 0.1 copy.107
  14.0 0.6 copy-done.2
  15.3 0.1 copy.114
  16.5 1.0 %collective-permute-done.2 = f32[72,512]{1,0:T(8,128)S(1)} collective-permute-done((f32[72,512]{1,0:T(8,128)S(1)}, f32[72,512]{1,0:T(8,128)S(1)}, u32[]{:S(2)}, u32[]{:S(2)}) %collective-permute-start.2) | collective-permute-done | bytes 147488 | tf_op jit(solution)/shard_map/ppermute | solution.py:264
  17.7 0.8 %copy-done.4 = f32[8,8,512]{2,1,0:T(8,128)S(1)} copy-done((f32[8,8,512]{2,1,0:T(8,128)S(1)}, f32[8,8,512]{2,1,0:T(8,128)}, u32[]{:S(2)}) %copy-start.4) | copy-done | bytes 131096
  18.6 0.1 pad_maximum_fusion
  19.0 0.5 add_select_fusion.2
  19.6 0.5 add_select_fusion.1
  20.2 0.5 add_select_fusion
  20.8 0.3 select_convert_fusion.1
  21.4 0.2 reshape.207
  21.7 0.7 %pad_maximum_fusion.15 = bf16[4,9,8,256]{3,2,1,0:T(8,128)(2,1)} fusion(bf16[4,1,8,256]{3,2,1,0:T(8,128)(2,1)S(1)} %reshape.207, bf16[4,8,8,256]{3,2,1,0:T(8,128)(2,1)S(1)} %bitcast.265), kind=kLoop, calls=%fused_computation.100 | loop fusion | flops 73728 | bytes 294912 | tf_op jit(solution)/shard_map/concatenate | solution.py:309
  22.3 3.3 %all-to-all-start = ((bf16[4,9,8,256]{3,2,1,0:T(8,128)(2,1)}), bf16[4,9,8,256]{3,2,1,0:T(8,128)(2,1)S(1)}, u32[]{:S(2)}, u32[]{:S(2)}) async-start(bf16[4,9,8,256]{3,2,1,0:T(8,128)(2,1)} %pad_maximum_fusion.15), calls=%async_computation | async-start | bytes 294912 | tf_op jit(solution)/shard_map/all_to_all | solution.py:310
  25.7 0.6 %copy-done.11 = f32[64]{0:T(128)S(1)} copy-done((f32[64]{0:T(128)S(1)}, f32[64]{0:T(128)}, u32[]{:S(2)}) %copy-start.11) | copy-done | bytes 280
  26.3 0.7 %copy.54.gain_ref = f32[64,1]{1,0:T(8,128)} copy(f32[64,1]{0,1:T(1,128)S(1)} %bitcast.272) | data formatting | bytes 512 | tf_op jit(solution)/shard_map/optimization_barrier | solution.py:263
  27.0 0.7 %copy.53.hs_ref = f32[8,1]{1,0:T(8,128)} copy(f32[8,1]{0,1:T(1,128)S(1)} %reshape_tile.3) | data formatting | bytes 64 | tf_op jit(solution)/shard_map/optimization_barrier | solution.py:263
  27.7 2.7 %all-to-all-done.x_ref = bf16[4,9,8,256]{3,2,1,0:T(8,128)(2,1)S(1)} async-done(((bf16[4,9,8,256]{3,2,1,0:T(8,128)(2,1)}), bf16[4,9,8,256]{3,2,1,0:T(8,128)(2,1)S(1)}, u32[]{:S(2)}, u32[]{:S(2)}) %all-to-all-start) | async-done | bytes 147488 | tf_op jit(solution)/shard_map/all_to_all | solution.py:310
  30.5 0.7 %copy-done.8 = bf16[4,9,8,256]{3,2,1,0:T(8,128)(2,1)} copy-done((bf16[4,9,8,256]{3,2,1,0:T(8,128)(2,1)}, bf16[4,9,8,256]{3,2,1,0:T(8,128)(2,1)S(1)}, u32[]{:S(2)}) %copy-start.8) | copy-done | bytes 147480
  31.1 10.4 %shard_map.118 = bf16[9,8,1024]{2,1,0:T(8,128)(2,1)} custom-call(f32[8,1]{1,0:T(8,128)} %copy.53.hs_ref, bf16[4,9,8,256]{3,2,1,0:T(8,128)(2,1)} %copy-done.8, bf16[64,8]{1,0:T(8,128)(2,1)} %bitcast.270, f32[64,1]{1,0:T(8,128)} %copy.54.gain_ref, bf16[192,64]{1,0:T(8,128)(2,1)} %bitcast.267, bf16[64,64]{1,0:T(8,128)(2,1)} %bitcast.269, bf16[8,64]{1,0:T(8,128)(2,1)} %bitcast.271), custom_call_target="tpu_custom_call" | custom-call | tf_op jit(solution)/shard_map/pallas_call | solution.py:146
  41.5 1.3 %collective-permute-start.4 = (bf16[9,8,1024]{2,1,0:T(8,128)(2,1)}, bf16[9,8,1024]{2,1,0:T(8,128)(2,1)S(1)}, u32[]{:S(2)}, u32[]{:S(2)}) collective-permute-start(bf16[9,8,1024]{2,1,0:T(8,128)(2,1)} %shard_map.118), channel_id=1, source_target_pairs={{1,0},{2,1},{3,2},{4,3},{5,4},{6,5},{7,6},{9,8},{10,9},{11,10},{12... | collective-permute-start | bytes 442376 | tf_op jit(solution)/shard_map/ppermute | solution.py:332
  42.8 5.4 %collective-permute-start.3 = (bf16[9,8,1024]{2,1,0:T(8,128)(2,1)}, bf16[9,8,1024]{2,1,0:T(8,128)(2,1)S(1)}, u32[]{:S(2)}, u32[]{:S(2)}) collective-permute-start(bf16[9,8,1024]{2,1,0:T(8,128)(2,1)} %shard_map.118), channel_id=1, source_target_pairs={{0,1},{1,2},{2,3},{3,4},{4,5},{5,6},{6,7},{8,9},{9,10},{10,11},{11... | collective-permute-start | bytes 442376 | tf_op jit(solution)/shard_map/ppermute | solution.py:331
  48.2 0.7 %slice.441 = bf16[1,8,1024]{2,1,0:T(8,128)(2,1)S(1)} slice(bf16[9,8,1024]{2,1,0:T(8,128)(2,1)} %shard_map.118), slice={[8:9], [0:8], [0:1024]} | slice | bytes 32768 | tf_op jit(solution)/shard_map/slice | solution.py:319
  48.9 0.9 %copy_bitcast_fusion.6 = bf16[8,8,8,128]{3,1,2,0:T(8,128)(2,1)S(1)} fusion(bf16[9,8,1024]{2,1,0:T(8,128)(2,1)} %shard_map.118), kind=kLoop, calls=%fused_computation.129 | loop fusion | bytes 262144 | tf_op jit(solution)/shard_map/transpose | solution.py:318
  49.8 0.1 reshape_squeeze.9
  50.2 0.3 fusion.26
  50.5 0.3 convolution_add_fusion.1
  50.8 0.2 fusion.9
  51.0 0.1 reshape_squeeze.11
  51.4 1.7 %collective-permute-done.3 = bf16[9,8,1024]{2,1,0:T(8,128)(2,1)S(1)} collective-permute-done((bf16[9,8,1024]{2,1,0:T(8,128)(2,1)}, bf16[9,8,1024]{2,1,0:T(8,128)(2,1)S(1)}, u32[]{:S(2)}, u32[]{:S(2)}) %collective-permute-start.3) | collective-permute-done | bytes 147488 | tf_op jit(solution)/shard_map/ppermute | solution.py:331
  53.1 0.2 reshape_squeeze.10
  53.5 0.3 maximum_maximum_fusion
  53.8 0.3 fusion.8
  54.1 0.4 fusion.7
  54.5 0.4 fusion.6
  54.9 0.7 %maximum_maximum_fusion.1 = (bf16[8,8,16,144]{3,1,2,0:T(8,128)(2,1)S(1)}, bf16[8,8,16,144]{3,1,2,0:T(8,128)(2,1)S(1)}) fusion(bf16[8,8,8,8]{3,1,2,0:T(8,128)(2,1)S(1)} %get-tuple-element.39, bf16[8,8,8,128]{3,1,2,0:T(8,128)(2,1)S(1)} %copy_bitcast_fusion.1, bf16[8,8,8,8]{3,1,2,0:T(8,128)(2,1)S(1)} %get-tuple-element.38, ...), kind=kLoop, calls=%fused_computation.62 | loop fusion | flops 4571136 | bytes 1032208 | tf_op jit(solution)/shard_map/concatenate | solution.py:333
  55.5 0.3 fusion.5
  55.8 0.4 fusion.4
  56.2 0.4 fusion.3
  56.5 0.3 fusion.2
  56.8 0.4 fusion.1
  57.2 0.5 select_convert_fusion
  57.7 0.2 fusion.45
  57.9 0.2 convolution_add_fusion.9
  58.1 0.2 convolution_add_fusion.8
  58.4 0.2 convolution_add_fusion.7
  58.6 0.2 convolution_add_fusion.6
  58.8 0.2 convolution_add_fusion.5
  59.0 0.2 convolution_add_fusion.4
  59.2 0.2 convolution_add_fusion.3
  59.4 0.7 %copy-done.3 = bf16[9,8,1024]{2,1,0:T(8,128)(2,1)S(1)} copy-done((bf16[9,8,1024]{2,1,0:T(8,128)(2,1)S(1)}, bf16[9,8,1024]{2,1,0:T(8,128)(2,1)}, u32[]{:S(2)}) %copy-start.3) | copy-done | bytes 147480
  60.1 0.2 fusion.12
  60.3 0.7 %copy.79 = bf16[8,8,8,128]{3,2,1,0:T(8,128)(2,1)} copy(bf16[8,8,8,128]{3,1,2,0:T(8,128)(2,1)S(1)} %fusion.12) | data formatting | bytes 262144 | tf_op jit(solution)/shard_map/convert_element_type | solution.py:343
  (99 shorter events, 5.1 us)
Async XLA Ops:
  0.0 9.9 %copy-start = (bf16[64,64]{1,0:T(8,128)(2,1)S(1)}, bf16[64,64]{1,0:T(8,128)(2,1)}, u32[]{:S(2)}) copy-start(bf16[64,64]{1,0:T(8,128)(2,1)} %param.20) | copy-start | bytes 24580
  0.9 1.0 %copy-start.7 = (f32[2,8,8,512]{3,2,1,0:T(8,128)S(1)}, f32[2,8,8,512]{3,2,1,0:T(8,128)}, u32[]{:S(2)}) copy-start(f32[2,8,8,512]{3,2,1,0:T(8,128)} %param.12) | copy-start | bytes 786436
  2.0 14.0 %collective-permute-start = (f32[100,512]{1,0:T(8,128)S(1)}, f32[100,512]{1,0:T(8,128)S(1)}, u32[]{:S(2)}, u32[]{:S(2)}) collective-permute-start(f32[100,512]{1,0:T(8,128)S(1)} %pad_maximum_fusion.12), channel_id=1, source_target_pairs={{0,1},{1,2},{2,3},{3,4},{4,5},{5,6},{6,7},{8,9},{9,10},{10,11},{11... | collective-permute-start | bytes 614408 | tf_op jit(solution)/shard_map/ppermute | solution.py:247
  7.0 1.5 %copy-start.9 = (bf16[64,192]{1,0:T(8,128)(2,1)S(1)}, bf16[64,192]{1,0:T(8,128)(2,1)}, u32[]{:S(2)}) copy-start(bf16[64,192]{1,0:T(8,128)(2,1)} %param.18) | copy-start | bytes 73732
  7.0 9.0 %collective-permute-start.1 = (f32[100,512]{1,0:T(8,128)S(1)}, f32[100,512]{1,0:T(8,128)S(1)}, u32[]{:S(2)}, u32[]{:S(2)}) collective-permute-start(f32[100,512]{1,0:T(8,128)S(1)} %pad_maximum_fusion.13), channel_id=1, source_target_pairs={{1,0},{2,1},{3,2},{4,3},{5,4},{6,5},{7,6},{9,8},{10,9},{11,10},{12... | collective-permute-start | bytes 614408 | tf_op jit(solution)/shard_map/ppermute | solution.py:252
  10.6 0.7 %copy-start.10 = (bf16[8,64]{1,0:T(8,128)(2,1)S(1)}, bf16[8,64]{1,0:T(8,128)(2,1)}, u32[]{:S(2)}) copy-start(bf16[8,64]{1,0:T(8,128)(2,1)} %param.16) | copy-start | bytes 3076
  11.2 0.7 %copy-start.12 = (f32[4]{0:T(128)S(1)}, f32[4]{0:T(128)}, u32[]{:S(2)}) copy-start(f32[4]{0:T(128)} %param.19) | copy-start | bytes 52
  11.9 0.7 %copy-start.1 = (bf16[9,8,8]{0,2,1:T(8,128)(2,1)S(1)}, bf16[9,8,8]{0,2,1:T(8,128)(2,1)}, u32[]{:S(2)}) copy-start(bf16[9,8,8]{0,2,1:T(8,128)(2,1)} %param.22) | copy-start | bytes 3460
  13.8 0.7 %copy-start.2 = (bf16[9,8,8]{0,2,1:T(8,128)(2,1)S(1)}, bf16[9,8,8]{0,2,1:T(8,128)(2,1)}, u32[]{:S(2)}) copy-start(bf16[9,8,8]{0,2,1:T(8,128)(2,1)} %param.23) | copy-start | bytes 3460
  16.0 1.4 %collective-permute-start.2 = (f32[72,512]{1,0:T(8,128)S(1)}, f32[72,512]{1,0:T(8,128)S(1)}, u32[]{:S(2)}, u32[]{:S(2)}) collective-permute-start(f32[72,512]{1,0:T(8,128)S(1)} %pad_maximum_fusion.14), channel_id=1, source_target_pairs={{0,8},{8,0},{16,24},{24,16},{1,9},{9,1},{17,25},{25,17},{2,10},{10... | collective-permute-start | bytes 442376 | tf_op jit(solution)/shard_map/ppermute | solution.py:264
  17.6 0.9 %copy-start.4 = (f32[8,8,512]{2,1,0:T(8,128)S(1)}, f32[8,8,512]{2,1,0:T(8,128)}, u32[]{:S(2)}) copy-start(f32[8,8,512]{2,1,0:T(8,128)} %param.13) | copy-start | bytes 393220
  17.6 1.0 %copy-start.5 = (f32[8,8,512]{2,1,0:T(8,128)S(1)}, f32[8,8,512]{2,1,0:T(8,128)}, u32[]{:S(2)}) copy-start(f32[8,8,512]{2,1,0:T(8,128)} %param.14) | copy-start | bytes 393220
  17.6 1.0 %copy-start.6 = (f32[8,8,512]{2,1,0:T(8,128)S(1)}, f32[8,8,512]{2,1,0:T(8,128)}, u32[]{:S(2)}) copy-start(f32[8,8,512]{2,1,0:T(8,128)} %param.15) | copy-start | bytes 393220
  22.3 8.1 %all-to-all-start = ((bf16[4,9,8,256]{3,2,1,0:T(8,128)(2,1)}), bf16[4,9,8,256]{3,2,1,0:T(8,128)(2,1)S(1)}, u32[]{:S(2)}, u32[]{:S(2)}) async-start(bf16[4,9,8,256]{3,2,1,0:T(8,128)(2,1)} %pad_maximum_fusion.15), calls=%async_computation | async-start | bytes 294912 | tf_op jit(solution)/shard_map/all_to_all | solution.py:310
  25.7 0.7 %copy-start.11 = (f32[64]{0:T(128)S(1)}, f32[64]{0:T(128)}, u32[]{:S(2)}) copy-start(f32[64]{0:T(128)} %param.17) | copy-start | bytes 772
  30.5 0.7 %copy-start.8 = (bf16[4,9,8,256]{3,2,1,0:T(8,128)(2,1)}, bf16[4,9,8,256]{3,2,1,0:T(8,128)(2,1)S(1)}, u32[]{:S(2)}) copy-start(bf16[4,9,8,256]{3,2,1,0:T(8,128)(2,1)S(1)} %all-to-all-done.x_ref) | copy-start | bytes 442372
  41.5 9.5 %collective-permute-start.4 = (bf16[9,8,1024]{2,1,0:T(8,128)(2,1)}, bf16[9,8,1024]{2,1,0:T(8,128)(2,1)S(1)}, u32[]{:S(2)}, u32[]{:S(2)}) collective-permute-start(bf16[9,8,1024]{2,1,0:T(8,128)(2,1)} %shard_map.118), channel_id=1, source_target_pairs={{1,0},{2,1},{3,2},{4,3},{5,4},{6,5},{7,6},{9,8},{10,9},{11,10},{12... | collective-permute-start | bytes 442376 | tf_op jit(solution)/shard_map/ppermute | solution.py:332
  42.8 10.3 %collective-permute-start.3 = (bf16[9,8,1024]{2,1,0:T(8,128)(2,1)}, bf16[9,8,1024]{2,1,0:T(8,128)(2,1)S(1)}, u32[]{:S(2)}, u32[]{:S(2)}) collective-permute-start(bf16[9,8,1024]{2,1,0:T(8,128)(2,1)} %shard_map.118), channel_id=1, source_target_pairs={{0,1},{1,2},{2,3},{3,4},{4,5},{5,6},{6,7},{8,9},{9,10},{10,11},{11... | collective-permute-start | bytes 442376 | tf_op jit(solution)/shard_map/ppermute | solution.py:331
  59.2 0.9 %copy-start.3 = (bf16[9,8,1024]{2,1,0:T(8,128)(2,1)S(1)}, bf16[9,8,1024]{2,1,0:T(8,128)(2,1)}, u32[]{:S(2)}) copy-start(bf16[9,8,1024]{2,1,0:T(8,128)(2,1)} %shard_map.118) | copy-start | bytes 442372

commit v28 on v25

--- a/solution.py
+++ b/solution.py
@@ -182,7 +182,7 @@
         (padded_field.shape[0], kernel.shape[1], row_total, column_total), jnp.float32
     )
     bands = []
-    for row_stencil in range(3):
+    for row_stencil in range(2):
         start = halo - row_stencil * span
         band = jnp.zeros(
             (local_field.shape[0], kernel.shape[1], local_rows, column_total), jnp.float32
@@ -199,7 +199,7 @@
         )
         bands.append(start)
     for row_stencil in range(3):
-        start = bands[row_stencil]
+        start = bands[row_stencil] if row_stencil < len(bands) else row_total
         keep = (rows < start) | (rows >= start + local_rows)
         for column_stencil in range(3):
             shifted_field = padded_field[

time: 59.8 us -> 59.8 us (level)
  waiting for transfers between devices: 5.44 us -> 6.28 us
  matrix products: 7.99 us -> 7.16 us
    ppermute x1, waiting for transfers between devices: 0.03 us -> 0.86 us  [on_device(): _, from_low = widen(lax.ppermute(step_result, 'row', forward))]
    dot_general x9 -> x6, matrix products: 2.49 us -> 1.66 us  [convolve_split(): jnp.einsum('oc,mcij->moij', kernel[row_stencil * 3 + column_stencil], loc...]
  transfers between devices with their start and end apart: 6 -> 6, of which waited for: 3 -> 4; matrix products, arithmetic and copies ran while one was open for 22% -> 21% of each run, Pallas kernels for 0% -> 0%
where the time goes in v28:
time: 59.8 us; the launch traced here: 59.3 us
  starting transfers between devices  16 us (27%)
  local copies, waits for them, and re-layouts  13.1 us (22%)
  Pallas kernels  10.4 us (17%)
  matrix products  7.16 us (12%)
  waiting for transfers between devices  6.28 us (11%)
  other arithmetic  5.59 us (9%)
  between operations  0.84 us (1%)
    pallas_call x1, Pallas kernels, post_block(): pl.pallas_call(functools.partial(attention_kernel, chunk=chunk, heads=hea...  10.4 us
    ppermute x1, starting transfers between devices, on_device(): _, from_low = widen(lax.ppermute(step_result, 'row', forward))  5.17 us
    ppermute x1, starting transfers between devices, on_device(): lax.ppermute(pack(starting_states[:, :, row_total - state_halo:], own[:,...  4.86 us
    unnamed x46, local copies, waits for them, and re-layouts  4.16 us
    dot_general x9, matrix products, convolve_split(): jnp.einsum('oc,mcij->moij', kernel[row_stencil * 3 + column_stencil], shi...  3.64 us
    all_to_all x1, waiting for transfers between devices, on_device(): lax.all_to_all(by_chunk, 'mem', split_axis=0, concat_axis=0, tiled=True)  3.38 us
    all_to_all x1, starting transfers between devices, on_device(): lax.all_to_all(by_chunk, 'mem', split_axis=0, concat_axis=0, tiled=True)  3.33 us
    dot_general x9, matrix products, convolve(): jnp.einsum('oc,mcij->moij', kernel[row_stencil * 3 + column_stencil], shi...  1.86 us
  transfers between devices with their start and end apart: 6, of which 4 were waited for; matrix products, arithmetic and copies ran while one was open for 21% of the time, Pallas kernels for 0%

profile of v28, /device:TPU:0, one launch (start us, length us, event | category | flops | bytes accessed | tf_op | source)
XLA Modules:
  0.0 59.3 jit_solution(5493743078414411894)
XLA Ops:
  0.0 1.0 %fusion.33 = f32[3,4,8,512]{3,2,1,0:T(8,128)S(1)} fusion(s32[]{:T(128)S(6)} %select_n.114, f32[1,8,8,512]{3,2,1,0:T(8,128)} %bitcast.263, f32[1,8,8,512]{3,2,1,0:T(8,128)} %bitcast.265, f32[1,8,8,512]{3,2,1,0:T(8,128)} %bitcast.267), kind=kLoop, calls=%fused_computation.101 | loop fusion | flops 98304 | bytes 589828 | tf_op jit(solution)/shard_map/stack | solution.py:237
  1.3 4.9 %collective-permute-start = (f32[100,512]{1,0:T(8,128)S(1)}, f32[100,512]{1,0:T(8,128)S(1)}, u32[]{:S(2)}, u32[]{:S(2)}) collective-permute-start(f32[100,512]{1,0:T(8,128)S(1)} %pad_maximum_fusion.6), channel_id=1, source_target_pairs={{0,1},{1,2},{2,3},{3,4},{4,5},{5,6},{6,7},{8,9},{9,10},{10,11},{11... | collective-permute-start | bytes 614408 | tf_op jit(solution)/shard_map/ppermute | solution.py:255
  6.2 1.3 %collective-permute-start.1 = (f32[100,512]{1,0:T(8,128)S(1)}, f32[100,512]{1,0:T(8,128)S(1)}, u32[]{:S(2)}, u32[]{:S(2)}) collective-permute-start(f32[100,512]{1,0:T(8,128)S(1)} %pad_maximum_fusion.7), channel_id=1, source_target_pairs={{1,0},{2,1},{3,2},{4,3},{5,4},{6,5},{7,6},{9,8},{10,9},{11,10},{12... | collective-permute-start | bytes 614408 | tf_op jit(solution)/shard_map/ppermute | solution.py:260
  7.9 0.7 %gather_fusion = bf16[64,3,64]{2,1,0:T(4,128)(2,1)S(1)} fusion(bf16[3,64,64]{2,0,1:T(4,128)(2,1)S(1)} %copy.47, s32[1024]{0:T(1024)S(1)} %pad_clamp_fusion), kind=kCustom, calls=%fused_computation | custom fusion | bytes 49408 | tf_op jit(solution)/shard_map/gather | solution.py:127
  8.5 0.6 %copy.48 = bf16[3,64,64]{2,1,0:T(8,128)(2,1)} copy(bf16[3,64,64]{2,0,1:T(4,128)(2,1)S(1)} %bitcast.274) | data formatting | bytes 49152 | tf_op jit(solution)/shard_map/gather | solution.py:127
  9.2 0.6 %gather_fusion.1 = bf16[64,64]{1,0:T(8,128)(2,1)S(1)} fusion(bf16[64,64]{0,1:T(8,128)(2,1)S(1)} %bitcast.261, s32[1024]{0:T(1024)S(1)} %pad_clamp_fusion), kind=kCustom, calls=%fused_computation.1 | custom fusion | bytes 16640 | tf_op jit(solution)/shard_map/gather | solution.py:128
  9.8 0.7 %copy.49 = bf16[64,64]{0,1:T(8,128)(2,1)} copy(bf16[64,64]{1,0:T(8,128)(2,1)S(1)} %gather_fusion.1) | data formatting | bytes 16384 | tf_op jit(solution)/shard_map/gather | solution.py:128
  10.5 0.7 %copy.45 = bf16[8,64]{0,1:T(8,128)(2,1)} copy(bf16[8,64]{1,0:T(8,128)(2,1)S(1)} %copy-done.10) | data formatting | bytes 2048 | tf_op args[4]
  12.1 0.1 copy.105
  12.2 0.1 copy.106
  12.4 0.1 copy.107
  13.5 0.1 copy.114
  13.6 0.1 copy.115
  14.1 1.1 %collective-permute-done = f32[100,512]{1,0:T(8,128)S(1)} collective-permute-done((f32[100,512]{1,0:T(8,128)S(1)}, f32[100,512]{1,0:T(8,128)S(1)}, u32[]{:S(2)}, u32[]{:S(2)}) %collective-permute-start) | collective-permute-done | bytes 204832 | tf_op jit(solution)/shard_map/ppermute | solution.py:255
  15.8 0.9 %collective-permute-done.2 = f32[72,512]{1,0:T(8,128)S(1)} collective-permute-done((f32[72,512]{1,0:T(8,128)S(1)}, f32[72,512]{1,0:T(8,128)S(1)}, u32[]{:S(2)}, u32[]{:S(2)}) %collective-permute-start.2) | collective-permute-done | bytes 147488 | tf_op jit(solution)/shard_map/ppermute | solution.py:272
  16.9 0.1 pad_maximum_fusion
  17.3 0.5 add_select_fusion.2
  17.9 0.5 add_select_fusion.1
  18.5 0.5 add_select_fusion
  19.1 0.3 select_convert_fusion.1
  19.8 0.2 reshape.207
  20.0 0.7 %pad_maximum_fusion.13 = bf16[4,9,8,256]{3,2,1,0:T(8,128)(2,1)} fusion(bf16[4,1,8,256]{3,2,1,0:T(8,128)(2,1)S(1)} %reshape.207, bf16[4,8,8,256]{3,2,1,0:T(8,128)(2,1)S(1)} %bitcast.273), kind=kLoop, calls=%fused_computation.109 | loop fusion | flops 73728 | bytes 294912 | tf_op jit(solution)/shard_map/concatenate | solution.py:317
  20.6 3.3 %all-to-all-start = ((bf16[4,9,8,256]{3,2,1,0:T(8,128)(2,1)}), bf16[4,9,8,256]{3,2,1,0:T(8,128)(2,1)S(1)}, u32[]{:S(2)}, u32[]{:S(2)}) async-start(bf16[4,9,8,256]{3,2,1,0:T(8,128)(2,1)} %pad_maximum_fusion.13), calls=%async_computation | async-start | bytes 294912 | tf_op jit(solution)/shard_map/all_to_all | solution.py:318
  24.0 0.7 %copy.54.gain_ref = f32[64,1]{1,0:T(8,128)} copy(f32[64,1]{0,1:T(1,128)S(1)} %bitcast.280) | data formatting | bytes 512 | tf_op jit(solution)/shard_map/optimization_barrier | solution.py:271
  24.7 0.7 %copy.53.hs_ref = f32[8,1]{1,0:T(8,128)} copy(f32[8,1]{0,1:T(1,128)S(1)} %reshape_tile.3) | data formatting | bytes 64 | tf_op jit(solution)/shard_map/optimization_barrier | solution.py:271
  25.4 3.4 %all-to-all-done.x_ref = bf16[4,9,8,256]{3,2,1,0:T(8,128)(2,1)S(1)} async-done(((bf16[4,9,8,256]{3,2,1,0:T(8,128)(2,1)}), bf16[4,9,8,256]{3,2,1,0:T(8,128)(2,1)S(1)}, u32[]{:S(2)}, u32[]{:S(2)}) %all-to-all-start) | async-done | bytes 147488 | tf_op jit(solution)/shard_map/all_to_all | solution.py:318
  28.8 0.7 %copy-done.8 = bf16[4,9,8,256]{3,2,1,0:T(8,128)(2,1)} copy-done((bf16[4,9,8,256]{3,2,1,0:T(8,128)(2,1)}, bf16[4,9,8,256]{3,2,1,0:T(8,128)(2,1)S(1)}, u32[]{:S(2)}) %copy-start.8) | copy-done | bytes 147480
  29.4 10.4 %shard_map.118 = bf16[9,8,1024]{2,1,0:T(8,128)(2,1)} custom-call(f32[8,1]{1,0:T(8,128)} %copy.53.hs_ref, bf16[4,9,8,256]{3,2,1,0:T(8,128)(2,1)} %copy-done.8, bf16[64,8]{1,0:T(8,128)(2,1)} %bitcast.278, f32[64,1]{1,0:T(8,128)} %copy.54.gain_ref, bf16[192,64]{1,0:T(8,128)(2,1)} %bitcast.275, bf16[64,64]{1,0:T(8,128)(2,1)} %bitcast.277, bf16[8,64]{1,0:T(8,128)(2,1)} %bitcast.279), custom_call_target="tpu_custom_call" | custom-call | tf_op jit(solution)/shard_map/pallas_call | solution.py:146
  39.8 1.3 %collective-permute-start.4 = (bf16[9,8,1024]{2,1,0:T(8,128)(2,1)}, bf16[9,8,1024]{2,1,0:T(8,128)(2,1)S(1)}, u32[]{:S(2)}, u32[]{:S(2)}) collective-permute-start(bf16[9,8,1024]{2,1,0:T(8,128)(2,1)} %shard_map.118), channel_id=1, source_target_pairs={{1,0},{2,1},{3,2},{4,3},{5,4},{6,5},{7,6},{9,8},{10,9},{11,10},{12... | collective-permute-start | bytes 442376 | tf_op jit(solution)/shard_map/ppermute | solution.py:340
  41.1 5.2 %collective-permute-start.3 = (bf16[9,8,1024]{2,1,0:T(8,128)(2,1)}, bf16[9,8,1024]{2,1,0:T(8,128)(2,1)S(1)}, u32[]{:S(2)}, u32[]{:S(2)}) collective-permute-start(bf16[9,8,1024]{2,1,0:T(8,128)(2,1)} %shard_map.118), channel_id=1, source_target_pairs={{0,1},{1,2},{2,3},{3,4},{4,5},{5,6},{6,7},{8,9},{9,10},{10,11},{11... | collective-permute-start | bytes 442376 | tf_op jit(solution)/shard_map/ppermute | solution.py:339
  46.3 0.7 %slice.439 = bf16[1,8,1024]{2,1,0:T(8,128)(2,1)S(1)} slice(bf16[9,8,1024]{2,1,0:T(8,128)(2,1)} %shard_map.118), slice={[8:9], [0:8], [0:1024]} | slice | bytes 32768 | tf_op jit(solution)/shard_map/slice | solution.py:327
  47.0 0.9 %copy_bitcast_fusion.6 = bf16[8,8,8,128]{3,1,2,0:T(8,128)(2,1)S(1)} fusion(bf16[9,8,1024]{2,1,0:T(8,128)(2,1)} %shard_map.118), kind=kLoop, calls=%fused_computation.138 | loop fusion | bytes 262144 | tf_op jit(solution)/shard_map/transpose | solution.py:326
  47.9 0.1 reshape_squeeze.9
  48.3 0.3 fusion.35
  48.6 0.3 fusion.34
  48.9 0.3 convolution_add_fusion.3
  49.2 0.2 fusion.9
  49.4 0.3 convolution_add_fusion.1
  49.7 0.2 fusion.10
  50.0 0.1 reshape_squeeze.11
  50.3 0.9 %collective-permute-done.3 = bf16[9,8,1024]{2,1,0:T(8,128)(2,1)S(1)} collective-permute-done((bf16[9,8,1024]{2,1,0:T(8,128)(2,1)}, bf16[9,8,1024]{2,1,0:T(8,128)(2,1)S(1)}, u32[]{:S(2)}, u32[]{:S(2)}) %collective-permute-start.3) | collective-permute-done | bytes 147488 | tf_op jit(solution)/shard_map/ppermute | solution.py:339
  51.2 0.2 reshape_squeeze.10
  51.6 0.5 maximum_maximum_fusion
  52.1 0.6 %maximum_maximum_fusion.2 = (bf16[8,8,16,144]{3,1,2,0:T(8,128)(2,1)S(1)}, bf16[8,8,16,144]{3,1,2,0:T(8,128)(2,1)S(1)}) fusion(bf16[8,8,8,8]{3,1,2,0:T(8,128)(2,1)S(1)} %get-tuple-element.39, bf16[8,8,8,128]{3,1,2,0:T(8,128)(2,1)S(1)} %copy_bitcast_fusion.1, bf16[8,8,8,8]{3,1,2,0:T(8,128)(2,1)S(1)} %get-tuple-element.38, ...), kind=kLoop, calls=%fused_computation.57 | loop fusion | flops 3538944 | bytes 1032192 | tf_op jit(solution)/shard_map/concatenate | solution.py:341
  52.8 0.3 fusion.8
  53.1 0.4 fusion.7
  53.5 0.4 fusion.6
  54.0 0.3 fusion.5
  54.3 0.4 fusion.4
  54.7 0.4 fusion.3
  55.1 0.3 fusion.2
  55.5 0.4 fusion.1
  55.9 0.5 select_convert_fusion
  56.5 0.2 fusion.46
  56.6 0.2 convolution_add_fusion.11
  56.9 0.2 convolution_add_fusion.10
  57.1 0.2 convolution_add_fusion.9
  57.3 0.2 convolution_add_fusion.8
  57.5 0.2 convolution_add_fusion.7
  57.8 0.2 convolution_add_fusion.6
  57.9 0.2 convolution_add_fusion.5
  58.2 0.3 copy-done.3
  58.4 0.2 fusion.13
  58.7 0.7 %copy.79 = bf16[8,8,8,128]{3,2,1,0:T(8,128)(2,1)} copy(bf16[8,8,8,128]{3,1,2,0:T(8,128)(2,1)S(1)} %fusion.13) | data formatting | bytes 262144 | tf_op jit(solution)/shard_map/convert_element_type | solution.py:351
  (104 shorter events, 4.8 us)
Async XLA Ops:
  0.0 9.2 %copy-start = (bf16[64,64]{1,0:T(8,128)(2,1)S(1)}, bf16[64,64]{1,0:T(8,128)(2,1)}, u32[]{:S(2)}) copy-start(bf16[64,64]{1,0:T(8,128)(2,1)} %param.20) | copy-start | bytes 24580
  0.0 1.1 %copy-start.7 = (f32[2,8,8,512]{3,2,1,0:T(8,128)S(1)}, f32[2,8,8,512]{3,2,1,0:T(8,128)}, u32[]{:S(2)}) copy-start(f32[2,8,8,512]{3,2,1,0:T(8,128)} %param.12) | copy-start | bytes 786436
  1.1 6.6 %copy-start.9 = (bf16[64,192]{1,0:T(8,128)(2,1)S(1)}, bf16[64,192]{1,0:T(8,128)(2,1)}, u32[]{:S(2)}) copy-start(bf16[64,192]{1,0:T(8,128)(2,1)} %param.18) | copy-start | bytes 73732
  1.1 9.4 %copy-start.10 = (bf16[8,64]{1,0:T(8,128)(2,1)S(1)}, bf16[8,64]{1,0:T(8,128)(2,1)}, u32[]{:S(2)}) copy-start(bf16[8,64]{1,0:T(8,128)(2,1)} %param.16) | copy-start | bytes 3076
  1.1 10.1 %copy-start.12 = (f32[4]{0:T(128)S(1)}, f32[4]{0:T(128)}, u32[]{:S(2)}) copy-start(f32[4]{0:T(128)} %param.19) | copy-start | bytes 52
  1.2 10.1 %copy-start.1 = (bf16[9,8,8]{0,2,1:T(8,128)(2,1)S(1)}, bf16[9,8,8]{0,2,1:T(8,128)(2,1)}, u32[]{:S(2)}) copy-start(bf16[9,8,8]{0,2,1:T(8,128)(2,1)} %param.22) | copy-start | bytes 3460
  1.2 11.5 %copy-start.2 = (bf16[9,8,8]{0,2,1:T(8,128)(2,1)S(1)}, bf16[9,8,8]{0,2,1:T(8,128)(2,1)}, u32[]{:S(2)}) copy-start(bf16[9,8,8]{0,2,1:T(8,128)(2,1)} %param.23) | copy-start | bytes 3460
  1.3 13.9 %collective-permute-start = (f32[100,512]{1,0:T(8,128)S(1)}, f32[100,512]{1,0:T(8,128)S(1)}, u32[]{:S(2)}, u32[]{:S(2)}) collective-permute-start(f32[100,512]{1,0:T(8,128)S(1)} %pad_maximum_fusion.6), channel_id=1, source_target_pairs={{0,1},{1,2},{2,3},{3,4},{4,5},{5,6},{6,7},{8,9},{9,10},{10,11},{11... | collective-permute-start | bytes 614408 | tf_op jit(solution)/shard_map/ppermute | solution.py:255
  6.2 9.0 %collective-permute-start.1 = (f32[100,512]{1,0:T(8,128)S(1)}, f32[100,512]{1,0:T(8,128)S(1)}, u32[]{:S(2)}, u32[]{:S(2)}) collective-permute-start(f32[100,512]{1,0:T(8,128)S(1)} %pad_maximum_fusion.7), channel_id=1, source_target_pairs={{1,0},{2,1},{3,2},{4,3},{5,4},{6,5},{7,6},{9,8},{10,9},{11,10},{12... | collective-permute-start | bytes 614408 | tf_op jit(solution)/shard_map/ppermute | solution.py:260
  15.2 1.4 %collective-permute-start.2 = (f32[72,512]{1,0:T(8,128)S(1)}, f32[72,512]{1,0:T(8,128)S(1)}, u32[]{:S(2)}, u32[]{:S(2)}) collective-permute-start(f32[72,512]{1,0:T(8,128)S(1)} %pad_maximum_fusion.12), channel_id=1, source_target_pairs={{0,8},{8,0},{16,24},{24,16},{1,9},{9,1},{17,25},{25,17},{2,10},{10... | collective-permute-start | bytes 442376 | tf_op jit(solution)/shard_map/ppermute | solution.py:272
  15.7 1.2 %copy-start.4 = (f32[8,8,512]{2,1,0:T(8,128)S(1)}, f32[8,8,512]{2,1,0:T(8,128)}, u32[]{:S(2)}) copy-start(f32[8,8,512]{2,1,0:T(8,128)} %param.13) | copy-start | bytes 393220
  15.7 1.2 %copy-start.5 = (f32[8,8,512]{2,1,0:T(8,128)S(1)}, f32[8,8,512]{2,1,0:T(8,128)}, u32[]{:S(2)}) copy-start(f32[8,8,512]{2,1,0:T(8,128)} %param.14) | copy-start | bytes 393220
  15.7 1.2 %copy-start.6 = (f32[8,8,512]{2,1,0:T(8,128)S(1)}, f32[8,8,512]{2,1,0:T(8,128)}, u32[]{:S(2)}) copy-start(f32[8,8,512]{2,1,0:T(8,128)} %param.15) | copy-start | bytes 393220
  19.4 4.6 %copy-start.11 = (f32[64]{0:T(128)S(1)}, f32[64]{0:T(128)}, u32[]{:S(2)}) copy-start(f32[64]{0:T(128)} %param.17) | copy-start | bytes 772
  20.6 8.1 %all-to-all-start = ((bf16[4,9,8,256]{3,2,1,0:T(8,128)(2,1)}), bf16[4,9,8,256]{3,2,1,0:T(8,128)(2,1)S(1)}, u32[]{:S(2)}, u32[]{:S(2)}) async-start(bf16[4,9,8,256]{3,2,1,0:T(8,128)(2,1)} %pad_maximum_fusion.13), calls=%async_computation | async-start | bytes 294912 | tf_op jit(solution)/shard_map/all_to_all | solution.py:318
  28.8 0.7 %copy-start.8 = (bf16[4,9,8,256]{3,2,1,0:T(8,128)(2,1)}, bf16[4,9,8,256]{3,2,1,0:T(8,128)(2,1)S(1)}, u32[]{:S(2)}) copy-start(bf16[4,9,8,256]{3,2,1,0:T(8,128)(2,1)S(1)} %all-to-all-done.x_ref) | copy-start | bytes 442372
  39.8 10.2 %collective-permute-start.4 = (bf16[9,8,1024]{2,1,0:T(8,128)(2,1)}, bf16[9,8,1024]{2,1,0:T(8,128)(2,1)S(1)}, u32[]{:S(2)}, u32[]{:S(2)}) collective-permute-start(bf16[9,8,1024]{2,1,0:T(8,128)(2,1)} %shard_map.118), channel_id=1, source_target_pairs={{1,0},{2,1},{3,2},{4,3},{5,4},{6,5},{7,6},{9,8},{10,9},{11,10},{12... | collective-permute-start | bytes 442376 | tf_op jit(solution)/shard_map/ppermute | solution.py:340
  41.1 10.1 %collective-permute-start.3 = (bf16[9,8,1024]{2,1,0:T(8,128)(2,1)}, bf16[9,8,1024]{2,1,0:T(8,128)(2,1)S(1)}, u32[]{:S(2)}, u32[]{:S(2)}) collective-permute-start(bf16[9,8,1024]{2,1,0:T(8,128)(2,1)} %shard_map.118), channel_id=1, source_target_pairs={{0,1},{1,2},{2,3},{3,4},{4,5},{5,6},{6,7},{8,9},{9,10},{10,11},{11... | collective-permute-start | bytes 442376 | tf_op jit(solution)/shard_map/ppermute | solution.py:339
  57.5 0.9 %copy-start.3 = (bf16[9,8,1024]{2,1,0:T(8,128)(2,1)S(1)}, bf16[9,8,1024]{2,1,0:T(8,128)(2,1)}, u32[]{:S(2)}) copy-start(bf16[9,8,1024]{2,1,0:T(8,128)(2,1)} %shard_map.118) | copy-start | bytes 442372
